TPU v7x, 256 devices: a whole 4x4x8 slice. The times are simulated.
256 devices in a mesh: seq: 64 (over x, y_hi, z), head: 4 (over y_lo, core).
Axes of the slice: x: 4, y: 4 (y_hi: 2, y_lo: 2; y = y_hi * 2 + y_lo), z: 8, core: 2. Of those that a mesh axis runs over, the one named last changes fastest.
Arguments:
- tokens: bfloat16 [16384, 1024], P('seq'), may hold values from -6 to 6
- queries: bfloat16 [16384, 1024], P('seq', 'head'), may hold values from -8 to 8
- key_rows: bfloat16 [16384, 1024], P('seq', 'head'), may hold values from -8 to 8
- values: bfloat16 [16384, 1024], P('seq', 'head'), may hold values from -6 to 6
- ssm_input: bfloat16 [16384, 2048], P('seq', 'head'), may hold values from -6 to 6
- write_proj: bfloat16 [16384, 128], P('seq'), may hold values from -6 to 6
- read_proj: bfloat16 [16384, 128], P('seq'), may hold values from -6 to 6
- log_decay: float32 [32, 16384], P('head', 'seq'), may hold values from -1 to 0
- attn_project: bfloat16 [1024, 1024], P('head'), may hold values from -0.1875 to 0.1875
- ssm_project: bfloat16 [2048, 1024], P('head'), may hold values from -0.125 to 0.125
- gauss_project: bfloat16 [1024, 768], replicated, may hold values from -0.1875 to 0.1875
- tile_owner: int32 [16384], P('seq'), may hold values from 0 to 3, as said below
Outputs:
- block_out: bfloat16 [16384, 1024], P(('seq', 'head'))
- tile_rows: bfloat16 [64, 4, 4, 32, 768], P('seq', 'head')
Inputs may be any that keep to these rules, and one draw needn't show every extreme that they name: `tile_owner`: in each aligned group of 64 tokens no owner is named by more than 32 tokens; in every block of 256 tokens one owner is named by exactly 32 tokens of each of its groups.
All inputs are finite; a program needn't handle non-finite values.
Results may differ from a plain program's by a relative error of at most 0.023.
Values may be sent and summed in bfloat16 or wider, within the bound.
No kernel may reach another device: no remote copies, remote signals or barrier semaphores. Data moves between devices by JAX's collectives and lax.ppermute only.
A program may use at most 128 MiB of HBM per device.

v0:
```python
import math

import jax
import jax.numpy as jnp
from jax import lax
from jax.sharding import PartitionSpec as P

HDIM = 64


def entering_2(array, axis, combine, identity):
    devices, mine = (lax.axis_size(axis), lax.axis_index(axis))
    everything = jax.tree.map(
        lambda part, kind: lax.all_gather(part.astype(kind), axis),
        array,
        (jnp.bfloat16, jnp.bfloat16),
    )
    start = jax.tree.map(
        lambda part, zero: jnp.broadcast_to(jnp.asarray(zero, part.dtype), part.shape),
        array,
        identity,
    )

    def hop(k, before):
        reached = k < mine
        new = combine(
            before, jax.tree.map(lambda part, own: part[k].astype(own.dtype), everything, array)
        )
        return jax.tree.map(lambda a, b: jnp.where(reached, a, b), new, before)

    return lax.fori_loop(0, devices, hop, start)


def chain_pieces(ssm_input, write_proj, read_proj, log_decay):
    row_count = write_proj.shape[0]
    head_count = log_decay.shape[0]
    head_width = ssm_input.shape[1] // head_count
    cumulative = jnp.cumsum(log_decay, axis=1)
    inputs_heads = ssm_input.reshape(row_count, head_count, head_width)
    later_rows = lax.broadcasted_iota(jnp.int32, (row_count, row_count), 0)
    earlier_cols = lax.broadcasted_iota(jnp.int32, (row_count, row_count), 1)
    log_gaps = cumulative[:, :, None] - cumulative[:, None, :]
    decays = jnp.exp(jnp.where((later_rows >= earlier_cols)[None], log_gaps, -jnp.inf))
    cross_terms = jnp.dot(read_proj, write_proj.T, preferred_element_type=jnp.float32)
    mixing = (decays * cross_terms[None]).astype(jnp.bfloat16)
    inner_part = jnp.einsum(
        "hts,shp->thp", mixing, inputs_heads, preferred_element_type=jnp.float32
    )
    tail_decay = jnp.exp(cumulative[:, -1:] - cumulative)
    tail_inputs = (inputs_heads.astype(jnp.float32) * tail_decay.T[:, :, None]).astype(jnp.bfloat16)
    local_state = jnp.einsum(
        "sn,shp->hnp", write_proj, tail_inputs, preferred_element_type=jnp.float32
    )
    total_decay = jnp.exp(cumulative[:, -1])
    return (cumulative, inner_part, local_state, total_decay)


def chain_output(cumulative, inner_part, entering, read_proj):
    entering_low = entering.astype(jnp.bfloat16)
    outer_part = jnp.einsum(
        "tn,hnp->thp", read_proj, entering_low, preferred_element_type=jnp.float32
    )
    mixture = inner_part + outer_part * jnp.exp(cumulative).T[:, :, None]
    scaled = mixture * lax.rsqrt(jnp.mean(mixture * mixture, axis=2, keepdims=True) + 1e-05)
    return scaled.reshape(scaled.shape[0], -1).astype(jnp.bfloat16)


def combine_states(earlier, latter):
    decay_first, state_first = earlier
    decay_second, state_second = latter
    return (decay_first * decay_second, decay_second[:, None, None] * state_first + state_second)


def pass_states(local_state, total_decay):
    identity = (jnp.ones_like(total_decay), jnp.zeros_like(local_state))
    prefix = entering_2((total_decay, local_state), "seq", combine_states, identity)
    return prefix[1]


def fold_keys(query_heads, key_rows, values):
    row_count, head_count, head_width = query_heads.shape
    scale = 1.0 / math.sqrt(head_width)
    initial = (
        jnp.full((head_count, row_count), -jnp.inf, jnp.float32),
        jnp.zeros((head_count, row_count), jnp.float32),
        jnp.zeros((head_count, row_count, head_width), jnp.float32),
    )
    key_piece = lax.all_gather(key_rows, "seq", axis=0, tiled=True)
    value_piece = lax.all_gather(values, "seq", axis=0, tiled=True)
    piece_rows = key_piece.shape[0]
    block_rows = math.gcd(piece_rows, 1024)

    def one_step(block_index, carry_state):
        run_max, run_sum, accumulated = carry_state
        key_block = lax.dynamic_slice_in_dim(
            key_piece, block_index * block_rows, block_rows, 0
        ).reshape(block_rows, head_count, head_width)
        value_block = lax.dynamic_slice_in_dim(
            value_piece, block_index * block_rows, block_rows, 0
        ).reshape(block_rows, head_count, head_width)
        scores = (
            jnp.einsum("qhd,khd->hqk", query_heads, key_block, preferred_element_type=jnp.float32)
            * scale
        )
        new_max = jnp.maximum(run_max, jnp.max(scores, axis=2))
        shrink = jnp.exp(run_max - new_max)
        raised = jnp.exp(scores - new_max[:, :, None])
        run_sum = run_sum * shrink + jnp.sum(raised, axis=2)
        accumulated = accumulated * shrink[:, :, None] + jnp.einsum(
            "hqk,khd->hqd",
            raised.astype(jnp.bfloat16),
            value_block,
            preferred_element_type=jnp.float32,
        )
        return (new_max, run_sum, accumulated)

    run_max, run_sum, accumulated = lax.fori_loop(0, piece_rows // block_rows, one_step, initial)
    attended = accumulated / run_sum[:, :, None]
    return (
        attended.transpose(1, 0, 2).reshape(row_count, head_count * head_width).astype(jnp.bfloat16)
    )


def slot_rank(owners_here, owner_count, group_rows):
    row_count = owners_here.shape[0]
    one_hot = (owners_here[:, None] == jnp.arange(owner_count, dtype=jnp.int32)[None, :]).astype(
        jnp.bfloat16
    )
    later_rows = lax.broadcasted_iota(jnp.int32, (row_count, row_count), 0)
    earlier_cols = lax.broadcasted_iota(jnp.int32, (row_count, row_count), 1)
    before = (
        (earlier_cols < later_rows) & (later_rows // group_rows == earlier_cols // group_rows)
    ).astype(jnp.bfloat16)
    counted = jnp.dot(before, one_hot, preferred_element_type=jnp.float32)
    return jnp.sum(counted * one_hot.astype(jnp.float32), axis=1)


def per_device(
    tokens,
    queries,
    key_rows,
    values,
    ssm_input,
    write_proj,
    read_proj,
    log_decay,
    attn_project,
    ssm_project,
    gauss_project,
    tile_owner,
):
    row_count = queries.shape[0]
    head_count = queries.shape[1] // HDIM
    query_heads = queries.reshape(row_count, head_count, HDIM)
    attended = fold_keys(query_heads, key_rows, values)
    cumulative, inner_part, local_state, total_decay = chain_pieces(
        ssm_input, write_proj, read_proj, log_decay
    )
    entering = pass_states(local_state, total_decay)
    ssm_mix = chain_output(cumulative, inner_part, entering, read_proj)
    owner_count = lax.axis_size("head")
    own_index = lax.axis_index("head")
    sub_rows = row_count // owner_count
    capacity = sub_rows // 2
    width_out = gauss_project.shape[1]
    slot_count = owner_count * capacity
    slot_ids = jnp.arange(slot_count, dtype=jnp.float32)
    update = lax.psum_scatter(
        (
            jnp.dot(attended, attn_project, preferred_element_type=jnp.float32)
            + jnp.dot(ssm_mix, ssm_project, preferred_element_type=jnp.float32)
        ).astype(jnp.bfloat16),
        "head",
        scatter_dimension=0,
        tiled=True,
    ).astype(jnp.float32)
    own_tokens = lax.dynamic_slice_in_dim(tokens, own_index * sub_rows, sub_rows, 0)
    block_out = (own_tokens.astype(jnp.float32) + update).astype(jnp.bfloat16)
    gaussians = jnp.dot(block_out, gauss_project, preferred_element_type=jnp.float32).astype(
        jnp.bfloat16
    )
    owners_here = lax.dynamic_slice_in_dim(tile_owner, own_index * sub_rows, sub_rows, 0)
    slot_value = owners_here.astype(jnp.float32) * capacity + slot_rank(
        owners_here, owner_count, sub_rows
    )
    selector = (slot_ids[:, None] == slot_value[None, :]).astype(jnp.bfloat16)
    packed = jnp.dot(selector, gaussians, preferred_element_type=jnp.float32).astype(jnp.bfloat16)
    packed = packed.reshape(owner_count, capacity, width_out)
    received = lax.all_to_all(packed, "head", split_axis=0, concat_axis=0, tiled=True)
    tile_rows = received.reshape(1, 1, owner_count, capacity, width_out)
    return (block_out, tile_rows)


def solution(mesh):
    in_specs = (
        P("seq", None),
        P("seq", "head"),
        P("seq", "head"),
        P("seq", "head"),
        P("seq", "head"),
        P("seq", None),
        P("seq", None),
        P("head", "seq"),
        P("head", None),
        P("head", None),
        P(),
        P("seq"),
    )
    out_specs = (P(("seq", "head"), None), P("seq", "head", None, None, None))
    return jax.shard_map(
        per_device, mesh=mesh, in_specs=in_specs, out_specs=out_specs, check_vma=False
    )
```

profile of v0, /device:TPU:1, one launch (start us, length us, event | category | flops | bytes accessed | tf_op | source)
XLA Modules:
  0.0 632.4 jit_solution(15385614962645540333)
XLA Ops:
  7.2 1.4 reduce-window.6
  9.1 1.1 copy.44
  10.2 1.7 fusion.16
  12.0 1.7 copy.41
  13.8 1.7 copy.43
  16.4 1.3 dynamic-slice
  18.4 161.7 %all-reduce = bf16[512]{0:T(512)(128)(2,1)S(1)} all-reduce(bf16[512]{0:T(512)(128)(2,1)S(1)} %dynamic-update-slice), channel_id=2, replica_groups=mesh['seq'=64,'head'=4] {'seq'}, use_global_device_ids=true, to_apply=%add | all-reduce | flops 512 | bytes 2048
  182.3 82.8 %while.33 = (s32[]{:T(128)}, f32[8,128,64]{2,1,0:T(8,128)S(1)}, s32[]{:T(128)}, bf16[64,8]{1,0:T(8,128)(2,1)S(1)}, bf16[64,8,128,64]{2,3,1,0:T(8,128)(2,1)}, /*index=5*/s32[]{:T(128)}, s32[]{:T(128)}) while((s32[]{:T(128)}, f32[8,128,64]{2,1,0:T(8,128)S(1)}, s32[]{:T(128)}, bf16[64,8]{1,0:T(8,128)(2,1)S(1)}, ...), condition=%wide.region_7.8_spmd.clone, body=%wide.region_6.7_spmd.clone.sunk | while | flops 327692 | bytes 1179833 | solution.py:31
  265.4 2.3 multiply_reduce_fusion
  267.7 41.6 %all-gather.6.cloned.1.call-done = bf16[16384,256]{0,1:T(8,128)(2,1)} async-done(((bf16[256,256]{0,1:T(8,128)(2,1)}), bf16[16384,256]{0,1:T(8,128)(2,1)}) %all-gather.6.cloned.1.call-update) | async-done | bytes 8388624 | tf_op jit(solution)/shard_map/all_gather | solution.py:88
  309.3 148.9 %all-gather.8.cloned.1.call-done = bf16[16384,256]{0,1:T(8,128)(2,1)} async-done(((bf16[256,256]{0,1:T(8,128)(2,1)}), bf16[16384,256]{0,1:T(8,128)(2,1)}) %all-gather.8.cloned.1.call-update) | async-done | bytes 8388624 | tf_op jit(solution)/shard_map/all_gather | solution.py:89
  458.2 133.3 %while.32 = (s32[]{:T(128)}, f32[4,256]{1,0:T(4,128)S(1)}, f32[4,256]{1,0:T(4,128)S(1)}, f32[4,256,64]{1,2,0:T(8,128)S(1)}, bf16[16384,256]{0,1:T(8,128)(2,1)}, ...) while((s32[]{:T(128)}, f32[4,256]{1,0:T(4,128)S(1)}, ...), condition=%wide.region_3.0_spmd.clone, body=%wide.region_0.0_spmd.clone.sunk | while | flops 277025792 | bytes 33226948 | solution.py:117
  458.2 1.3 constant_dynamic-slice_fusion.5
  459.5 2.7 bitcast_reduce_fusion.2
  462.2 3.0 fusion.66
  466.5 1.3 constant_dynamic-slice_fusion.5
  467.8 2.7 bitcast_reduce_fusion.2
  470.5 3.0 fusion.66
  474.9 1.3 constant_dynamic-slice_fusion.5
  476.1 2.7 bitcast_reduce_fusion.2
  478.8 3.0 fusion.66
  483.2 1.3 constant_dynamic-slice_fusion.5
  484.5 2.7 bitcast_reduce_fusion.2
  487.2 3.0 fusion.66
  491.5 1.3 constant_dynamic-slice_fusion.5
  492.8 2.7 bitcast_reduce_fusion.2
  495.5 3.0 fusion.66
  499.9 1.3 constant_dynamic-slice_fusion.5
  501.1 2.7 bitcast_reduce_fusion.2
  503.8 3.0 fusion.66
  508.2 1.3 constant_dynamic-slice_fusion.5
  509.5 2.7 bitcast_reduce_fusion.2
  512.2 3.0 fusion.66
  516.5 1.3 constant_dynamic-slice_fusion.5
  517.8 2.7 bitcast_reduce_fusion.2
  520.5 3.0 fusion.66
  524.8 1.3 constant_dynamic-slice_fusion.5
  526.1 2.7 bitcast_reduce_fusion.2
  528.8 3.0 fusion.66
  533.2 1.3 constant_dynamic-slice_fusion.5
  534.4 2.7 bitcast_reduce_fusion.2
  537.1 3.0 fusion.66
  541.5 1.3 constant_dynamic-slice_fusion.5
  542.8 2.7 bitcast_reduce_fusion.2
  545.5 3.0 fusion.66
  549.8 1.3 constant_dynamic-slice_fusion.5
  551.1 2.7 bitcast_reduce_fusion.2
  553.8 3.0 fusion.66
  558.2 1.3 constant_dynamic-slice_fusion.5
  559.4 2.7 bitcast_reduce_fusion.2
  562.1 3.0 fusion.66
  566.5 1.3 constant_dynamic-slice_fusion.5
  567.8 2.7 bitcast_reduce_fusion.2
  570.5 3.0 fusion.66
  574.8 1.3 constant_dynamic-slice_fusion.5
  576.1 2.7 bitcast_reduce_fusion.2
  578.8 3.0 fusion.66
  583.1 1.3 constant_dynamic-slice_fusion.5
  584.4 2.7 bitcast_reduce_fusion.2
  587.1 3.0 fusion.66
  592.6 1.7 fusion.41
  594.3 1.1 fusion.13
  595.9 20.9 %reduce-scatter.2.cloned.1.call-done = bf16[64,1024]{1,0:T(8,128)(2,1)} async-done(((bf16[256,1024]{1,0:T(8,128)(2,1)}), bf16[64,1024]{1,0:T(8,128)(2,1)}) %reduce-scatter.2.cloned.1.call-update) | async-done | bytes 131088 | tf_op jit(solution)/shard_map/reduce_scatter | solution.py:168
  618.4 6.8 %all_to_all.5 = bf16[4,32,768]{2,1,0:T(8,128)(2,1)S(1)} all-to-all(bf16[4,32,768]{2,1,0:T(8,128)(2,1)S(1)} %bitcast.92), channel_id=1, replica_groups=mesh['seq'=64,'head'=4] {'head'}, dimensions={0} | all-to-all | bytes 393216 | tf_op jit(solution)/shard_map/all_to_all | solution.py:189
  (400 shorter events, 108.8 us)
Async XLA Ops:
  7.2 610.6 %copy-start = (bf16[1024,768]{1,0:T(8,128)(2,1)S(1)}, bf16[1024,768]{1,0:T(8,128)(2,1)}, u32[]{:S(2)}) copy-start(bf16[1024,768]{1,0:T(8,128)(2,1)} %param.26) | copy-start | bytes 4718596
  7.2 175.1 %all-gather.10.cloned.1.call-start = ((), (), s32[]{:S(2)}) async-start(), calls=%async_computation.5 | async-start | bytes 8519680 | tf_op jit(solution)/shard_map/all_gather | solution.py:14
  12.0 297.3 %all-gather.6.cloned.1.call-start = ((), (), s32[]{:S(2)}) async-start(), calls=%async_computation.2 | async-start | bytes 8519680 | tf_op jit(solution)/shard_map/all_gather | solution.py:88
  13.7 444.4 %all-gather.8.cloned.1.call-start = ((), (), s32[]{:S(2)}) async-start(), calls=%async_computation.3 | async-start | bytes 8519680 | tf_op jit(solution)/shard_map/all_gather | solution.py:89
  15.5 601.3 %reduce-scatter.2.cloned.1.call-start = ((), (), s32[]{:S(2)}) async-start(), calls=%async_computation.4 | async-start | bytes 655360 | tf_op jit(solution)/shard_map/reduce_scatter | solution.py:168
  182.3 82.8 %copy-start.4 = (bf16[256,128]{1,0:T(8,128)(2,1)S(1)}, bf16[256,128]{1,0:T(8,128)(2,1)}, u32[]{:S(2)}) copy-start(bf16[256,128]{1,0:T(8,128)(2,1)} %param.22) | copy-start | bytes 196612
  458.2 136.1 %copy-start.2 = (bf16[256,1024]{1,0:T(8,128)(2,1)S(1)}, bf16[256,1024]{1,0:T(8,128)(2,1)}, u32[]{:S(2)}) copy-start(bf16[256,1024]{1,0:T(8,128)(2,1)} %param.24) | copy-start | bytes 1572868
  462.2 3.4 copy-start.1
  470.5 3.4 copy-start.1
  478.8 3.4 copy-start.1
  487.2 3.4 copy-start.1
  495.5 3.4 copy-start.1
  503.8 3.4 copy-start.1
  512.2 3.4 copy-start.1
  520.5 3.4 copy-start.1
  528.8 3.4 copy-start.1
  537.1 3.4 copy-start.1
  545.5 3.4 copy-start.1
  553.8 3.4 copy-start.1
  562.1 3.4 copy-start.1
  570.5 3.4 copy-start.1
  578.8 3.4 copy-start.1
  587.1 3.4 copy-start.1
  591.5 4.0 copy-start.5
  617.8 8.1 %copy-start.3 = (bf16[64,1024]{1,0:T(8,128)(2,1)}, bf16[64,1024]{1,0:T(8,128)(2,1)S(1)}, u32[]{:S(2)}) copy-start(bf16[64,1024]{1,0:T(8,128)(2,1)S(1)} %add_convert_fusion) | copy-start | bytes 393220
Sparse Core Ops, SparseCore 0:
  12.2 148.4 all-gather.9
  164.8 144.4 all-gather.5
  312.7 145.3 all-gather.7
  595.6 21.1 reduce-scatter.1
where the time goes:
time: 634 us; the launch traced here: 632 us
  waiting for transfers between devices  211 us (33%)
  blocking collectives  168 us (26%)
  local copies, waits for them, and re-layouts  105 us (17%)
  matrix products  66 us (10%)
  other arithmetic  63.3 us (10%)
  between operations  14.5 us (2%)
    unnamed x1, blocking collectives  162 us
    all_gather x1, waiting for transfers between devices, fold_keys(): value_piece = lax.all_gather(values, 'seq', axis=0, tiled=True)  149 us
    dynamic_slice x128, local copies, waits for them, and re-layouts, hop(): part[k].astype(own.dtype)  70.3 us
    reduce_sum x16, other arithmetic, one_step(): run_sum = run_sum * shrink + jnp.sum(raised, axis=2)  48.5 us
    dot_general x16, matrix products, one_step(): jnp.einsum('qhd,khd->hqk', query_heads, key_block, preferred_element_type...  43.1 us
    all_gather x1, waiting for transfers between devices, fold_keys(): key_piece = lax.all_gather(key_rows, 'seq', axis=0, tiled=True)  41.6 us
    reduce_scatter x1, waiting for transfers between devices, per_device(): lax.psum_scatter((jnp.dot(attended, attn_project, preferred_element_type=...  20.9 us
    dynamic_slice x16, local copies, waits for them, and re-layouts, one_step(): lax.dynamic_slice_in_dim(value_piece, block_index * block_rows, block_row...  20.5 us
  transfers between devices with their start and end apart: 4, of which 3 were waited for; matrix products, arithmetic and copies ran while one was open for 14% of the time, Pallas kernels for 0%

commit v1 on v0

--- a/solution.py
+++ b/solution.py
@@ -6,29 +6,6 @@
 from jax.sharding import PartitionSpec as P
 
 HDIM = 64
-
-
-def entering_2(array, axis, combine, identity):
-    devices, mine = (lax.axis_size(axis), lax.axis_index(axis))
-    everything = jax.tree.map(
-        lambda part, kind: lax.all_gather(part.astype(kind), axis),
-        array,
-        (jnp.bfloat16, jnp.bfloat16),
-    )
-    start = jax.tree.map(
-        lambda part, zero: jnp.broadcast_to(jnp.asarray(zero, part.dtype), part.shape),
-        array,
-        identity,
-    )
-
-    def hop(k, before):
-        reached = k < mine
-        new = combine(
-            before, jax.tree.map(lambda part, own: part[k].astype(own.dtype), everything, array)
-        )
-        return jax.tree.map(lambda a, b: jnp.where(reached, a, b), new, before)
-
-    return lax.fori_loop(0, devices, hop, start)
 
 
 def chain_pieces(ssm_input, write_proj, read_proj, log_decay):
@@ -65,16 +42,29 @@
     return scaled.reshape(scaled.shape[0], -1).astype(jnp.bfloat16)
 
 
-def combine_states(earlier, latter):
-    decay_first, state_first = earlier
-    decay_second, state_second = latter
-    return (decay_first * decay_second, decay_second[:, None, None] * state_first + state_second)
-
-
 def pass_states(local_state, total_decay):
-    identity = (jnp.ones_like(total_decay), jnp.zeros_like(local_state))
-    prefix = entering_2((total_decay, local_state), "seq", combine_states, identity)
-    return prefix[1]
+    axis = "seq"
+    devices = lax.axis_size(axis)
+    mine = lax.axis_index(axis)
+
+    def shifted(tree, distance):
+        pairs = [(j, j + distance) for j in range(devices - distance)]
+        return jax.tree.map(lambda part: lax.ppermute(part, axis, pairs), tree)
+
+    decay, state = shifted((total_decay, local_state), 1)
+    first = mine >= 1
+    decay = jnp.where(first, decay, jnp.ones_like(decay))
+    state = jnp.where(first, state, jnp.zeros_like(state))
+    distance = 1
+    while distance < devices:
+        earlier_decay, earlier_state = shifted((decay, state), distance)
+        reached = mine >= distance
+        new_decay = earlier_decay * decay
+        new_state = decay[:, None, None] * earlier_state + state
+        decay = jnp.where(reached, new_decay, decay)
+        state = jnp.where(reached, new_state, state)
+        distance *= 2
+    return state
 
 
 def fold_keys(query_heads, key_rows, values):

time: 634 us -> 428 us (0.68)
  blocking collectives: 168 us -> 6.76 us
  starting transfers between devices: 0.16 us -> 91.1 us
  local copies, waits for them, and re-layouts: 105 us -> 26.3 us
  other arithmetic: 63.3 us -> 15.4 us
  matrix products: 66 us -> 31.9 us
  waiting for transfers between devices: 211 us -> 240 us
    unnamed x1 -> x0, blocking collectives: 162 us -> none
    ppermute x0 -> x13, starting transfers between devices: none -> 90.9 us  [shifted(): return jax.tree.map(lambda part: lax.ppermute(part, axis, pairs), tree)]
    dynamic_slice x128 -> x0, local copies, waits for them, and re-layouts: 70.3 us -> none  [hop(): part[k].astype(own.dtype)]
    reduce_sum x16, other arithmetic: 48.5 us -> 11.2 us  [one_step(): run_sum = run_sum * shrink + jnp.sum(raised, axis=2)]
    dot_general x16, matrix products: 43.1 us -> 12.4 us  [one_step(): jnp.einsum('qhd,khd->hqk', query_heads, key_block, preferred_element_type...]
    all_gather x1, waiting for transfers between devices: 41.6 us -> 59.6 us  [fold_keys(): key_piece = lax.all_gather(key_rows, 'seq', axis=0, tiled=True)]
    ppermute x0 -> x13, waiting for transfers between devices: none -> 10.3 us  [shifted(): return jax.tree.map(lambda part: lax.ppermute(part, axis, pairs), tree)]
    select_n x64 -> x12, other arithmetic: 8.99 us -> 1.16 us  [the longest x5 0.64 us: pass_states(): decay = jnp.where(reached, new_decay, decay)]
  transfers between devices with their start and end apart: 4 -> 16, of which waited for: 3 -> 10; matrix products, arithmetic and copies ran while one was open for 14% -> 2% of each run, Pallas kernels for 0% -> 0%
where the time goes in v1:
time: 428 us; the launch traced here: 427 us
  waiting for transfers between devices  240 us (56%)
  starting transfers between devices  91.1 us (21%)
  matrix products  31.9 us (7%)
  local copies, waits for them, and re-layouts  26.3 us (6%)
  other arithmetic  15.4 us (4%)
  between operations  14.1 us (3%)
  blocking collectives  6.76 us (2%)
    all_gather x1, waiting for transfers between devices, fold_keys(): value_piece = lax.all_gather(values, 'seq', axis=0, tiled=True)  149 us
    ppermute x13, starting transfers between devices, shifted(): return jax.tree.map(lambda part: lax.ppermute(part, axis, pairs), tree)  90.9 us
    all_gather x1, waiting for transfers between devices, fold_keys(): key_piece = lax.all_gather(key_rows, 'seq', axis=0, tiled=True)  59.6 us
    reduce_scatter x1, waiting for transfers between devices, per_device(): lax.psum_scatter((jnp.dot(attended, attn_project, preferred_element_type=...  20.9 us
    dynamic_slice x16, local copies, waits for them, and re-layouts, one_step(): lax.dynamic_slice_in_dim(value_piece, block_index * block_rows, block_row...  20.5 us
    dot_general x16, matrix products, one_step(): jnp.einsum('hqk,khd->hqd', raised.astype(jnp.bfloat16), value_block, pref...  13.6 us
    dot_general x16, matrix products, one_step(): jnp.einsum('qhd,khd->hqk', query_heads, key_block, preferred_element_type...  12.4 us
    reduce_sum x16, other arithmetic, one_step(): run_sum = run_sum * shrink + jnp.sum(raised, axis=2)  11.2 us
  transfers between devices with their start and end apart: 16, of which 10 were waited for; matrix products, arithmetic and copies ran while one was open for 2% of the time, Pallas kernels for 0%

profile of v1, /device:TPU:1, one launch (start us, length us, event | category | flops | bytes accessed | tf_op | source)
XLA Modules:
  0.0 426.7 jit_solution(14737537672849875051)
XLA Ops:
  7.2 1.8 copy.30
  9.1 1.7 copy.32
  10.8 1.3 reduce-window.6
  12.3 1.1 copy.33
  13.7 1.1 convolution_bitcast_fusion.2
  14.8 4.5 %collective-permute-start.6 = (f32[8,128,64]{1,2,0:T(8,128)S(1)}, f32[8,128,64]{1,2,0:T(8,128)S(1)}, u32[]{:S(2)}, u32[]{:S(2)}) collective-permute-start(f32[8,128,64]{1,2,0:T(8,128)S(1)} %convolution_bitcast_fusion.2), channel_id=1, source_target_pairs={{0,4},{4,8},{8,12},{12,16},{16,20},{20,24},{24,28},{28,32},{32,36}... | collective-permute-start | bytes 786440 | tf_op jit(solution)/shard_map/ppermute | solution.py:52
  19.3 4.9 %collective-permute-done.6 = f32[8,128,64]{1,2,0:T(8,128)S(1)} collective-permute-done((f32[8,128,64]{1,2,0:T(8,128)S(1)}, f32[8,128,64]{1,2,0:T(8,128)S(1)}, u32[]{:S(2)}, u32[]{:S(2)}) %collective-permute-start.6) | collective-permute-done | bytes 262176 | tf_op jit(solution)/shard_map/ppermute | solution.py:52
  24.3 4.1 collective-permute-start.7
  28.4 3.5 collective-permute-start
  32.0 1.3 collective-permute-done
  33.4 6.7 %collective-permute-start.8 = (f32[8,128,64]{1,2,0:T(8,128)S(1)}, f32[8,128,64]{1,2,0:T(8,128)S(1)}, u32[]{:S(2)}, u32[]{:S(2)}) collective-permute-start(f32[8,128,64]{1,2,0:T(8,128)S(1)} %add_select_fusion.5), channel_id=1, source_target_pairs={{0,8},{4,12},{8,16},{12,20},{16,24},{20,28},{24,32},{28,36},{32,40... | collective-permute-start | bytes 786440 | tf_op jit(solution)/shard_map/ppermute | solution.py:52
  40.1 4.1 collective-permute-start.1
  45.0 16.6 %collective-permute-start.9 = (f32[8,128,64]{1,2,0:T(8,128)S(1)}, f32[8,128,64]{1,2,0:T(8,128)S(1)}, u32[]{:S(2)}, u32[]{:S(2)}) collective-permute-start(f32[8,128,64]{1,2,0:T(8,128)S(1)} %add_select_fusion.4), channel_id=1, source_target_pairs={{0,16},{4,20},{8,24},{12,28},{16,32},{20,36},{24,40},{28,44},{32,4... | collective-permute-start | bytes 786440 | tf_op jit(solution)/shard_map/ppermute | solution.py:52
  61.7 3.3 collective-permute-start.2
  65.8 19.3 %collective-permute-start.10 = (f32[8,128,64]{1,2,0:T(8,128)S(1)}, f32[8,128,64]{1,2,0:T(8,128)S(1)}, u32[]{:S(2)}, u32[]{:S(2)}) collective-permute-start(f32[8,128,64]{1,2,0:T(8,128)S(1)} %add_select_fusion.3), channel_id=1, source_target_pairs={{0,32},{4,36},{8,40},{12,44},{16,48},{20,52},{24,56},{28,60},{32,6... | collective-permute-start | bytes 786440 | tf_op jit(solution)/shard_map/ppermute | solution.py:52
  85.3 4.2 collective-permute-start.3
  90.3 12.4 %collective-permute-start.11 = (f32[8,128,64]{1,2,0:T(8,128)S(1)}, f32[8,128,64]{1,2,0:T(8,128)S(1)}, u32[]{:S(2)}, u32[]{:S(2)}) collective-permute-start(f32[8,128,64]{1,2,0:T(8,128)S(1)} %add_select_fusion.2), channel_id=1, source_target_pairs={{0,64},{4,68},{8,72},{12,76},{16,80},{20,84},{24,88},{28,92},{32,9... | collective-permute-start | bytes 786440 | tf_op jit(solution)/shard_map/ppermute | solution.py:52
  102.8 5.8 %collective-permute-start.4 = (f32[8]{0:T(128)S(1)}, f32[8]{0:T(128)S(1)}, u32[]{:S(2)}, u32[]{:S(2)}) collective-permute-start(f32[8]{0:T(128)S(1)} %broadcast_select_fusion.4), channel_id=1, source_target_pairs={{0,32},{4,36},{8,40},{12,44},{16,48},{20,52},{24,56},{28,60},{32,6... | collective-permute-start | bytes 104 | tf_op jit(solution)/shard_map/ppermute | solution.py:52
  109.5 5.0 %collective-permute-start.12 = (f32[8,128,64]{1,2,0:T(8,128)S(1)}, f32[8,128,64]{1,2,0:T(8,128)S(1)}, u32[]{:S(2)}, u32[]{:S(2)}) collective-permute-start(f32[8,128,64]{1,2,0:T(8,128)S(1)} %add_select_fusion.1), channel_id=1, source_target_pairs={{0,128},{4,132},{8,136},{12,140},{16,144},{20,148},{24,152},{28,15... | collective-permute-start | bytes 786440 | tf_op jit(solution)/shard_map/ppermute | solution.py:52
  115.3 1.3 collective-permute-start.5
  116.6 1.2 collective-permute-done.5
  118.8 1.7 fusion.41
  120.5 59.6 %all-gather.3.cloned.1.call-done = bf16[16384,256]{0,1:T(8,128)(2,1)} async-done(((bf16[256,256]{0,1:T(8,128)(2,1)}), bf16[16384,256]{0,1:T(8,128)(2,1)}) %all-gather.3.cloned.1.call-update) | async-done | bytes 8388624 | tf_op jit(solution)/shard_map/all_gather | solution.py:78
  180.1 149.4 %all-gather.5.cloned.1.call-done = bf16[16384,256]{0,1:T(8,128)(2,1)} async-done(((bf16[256,256]{0,1:T(8,128)(2,1)}), bf16[16384,256]{0,1:T(8,128)(2,1)}) %all-gather.5.cloned.1.call-update) | async-done | bytes 8388624 | tf_op jit(solution)/shard_map/all_gather | solution.py:79
  329.6 59.0 %while.18 = (s32[]{:T(128)}, f32[4,256]{1,0:T(4,128)S(1)}, f32[4,256]{1,0:T(4,128)S(1)}, f32[4,256,64]{1,2,0:T(8,128)S(1)}, bf16[16384,256]{0,1:T(8,128)(2,1)}, ...) while((s32[]{:T(128)}, f32[4,256]{1,0:T(4,128)S(1)}, ...), condition=%wide.region_3.0_spmd.clone, body=%wide.region_0.0_spmd.clone.sunk | while | flops 277025792 | bytes 16449715 | solution.py:107
  329.6 1.3 constant_dynamic-slice_fusion.3
  330.9 0.8 bitcast_reduce_fusion.2
  332.4 0.9 fusion.67
  333.3 1.3 constant_dynamic-slice_fusion.3
  334.6 0.8 bitcast_reduce_fusion.2
  336.1 0.8 fusion.67
  337.0 1.3 constant_dynamic-slice_fusion.3
  339.8 0.9 fusion.67
  340.7 1.3 constant_dynamic-slice_fusion.3
  343.5 0.9 fusion.67
  344.4 1.3 constant_dynamic-slice_fusion.3
  347.2 0.9 fusion.67
  348.0 1.3 constant_dynamic-slice_fusion.3
  349.3 0.8 bitcast_reduce_fusion.2
  350.8 0.8 fusion.67
  351.7 1.3 constant_dynamic-slice_fusion.3
  354.5 0.9 fusion.67
  355.4 1.3 constant_dynamic-slice_fusion.3
  358.2 0.9 fusion.67
  359.1 1.3 constant_dynamic-slice_fusion.3
  361.9 0.9 fusion.67
  362.8 1.3 constant_dynamic-slice_fusion.3
  365.6 0.8 fusion.67
  366.5 1.3 constant_dynamic-slice_fusion.3
  369.3 0.9 fusion.67
  370.1 1.3 constant_dynamic-slice_fusion.3
  372.9 0.9 fusion.67
  373.8 1.3 constant_dynamic-slice_fusion.3
  376.6 0.9 fusion.67
  377.5 1.3 constant_dynamic-slice_fusion.3
  380.3 0.8 fusion.67
  381.2 1.3 constant_dynamic-slice_fusion.3
  384.0 0.9 fusion.67
  384.9 1.3 constant_dynamic-slice_fusion.3
  387.7 0.9 fusion.67
  388.6 1.1 fusion.12
  390.2 20.9 %reduce-scatter.2.cloned.1.call-done = bf16[64,1024]{1,0:T(8,128)(2,1)} async-done(((bf16[256,1024]{1,0:T(8,128)(2,1)}), bf16[64,1024]{1,0:T(8,128)(2,1)}) %reduce-scatter.2.cloned.1.call-update) | async-done | bytes 131088 | tf_op jit(solution)/shard_map/reduce_scatter | solution.py:158
  411.0 1.0 add_convert_fusion
  412.7 6.8 %all_to_all.5 = bf16[4,32,768]{2,1,0:T(8,128)(2,1)S(1)} all-to-all(bf16[4,32,768]{2,1,0:T(8,128)(2,1)S(1)} %bitcast.82), channel_id=1, replica_groups=mesh['seq'=64,'head'=4] {'head'}, dimensions={0} | all-to-all | bytes 393216 | tf_op jit(solution)/shard_map/all_to_all | solution.py:179
  (146 shorter events, 29.5 us)
Async XLA Ops:
  7.2 404.9 %copy-start = (bf16[1024,768]{1,0:T(8,128)(2,1)S(1)}, bf16[1024,768]{1,0:T(8,128)(2,1)}, u32[]{:S(2)}) copy-start(bf16[1024,768]{1,0:T(8,128)(2,1)} %param.24) | copy-start | bytes 4718596
  7.2 77.9 %copy-start.3 = (bf16[256,128]{1,0:T(8,128)(2,1)S(1)}, bf16[256,128]{1,0:T(8,128)(2,1)}, u32[]{:S(2)}) copy-start(bf16[256,128]{1,0:T(8,128)(2,1)} %param.19) | copy-start | bytes 196612
  7.2 77.9 %copy-start.4 = (bf16[256,128]{1,0:T(8,128)(2,1)S(1)}, bf16[256,128]{1,0:T(8,128)(2,1)}, u32[]{:S(2)}) copy-start(bf16[256,128]{1,0:T(8,128)(2,1)} %param.20) | copy-start | bytes 196612
  7.2 172.9 %all-gather.3.cloned.1.call-start = ((), (), s32[]{:S(2)}) async-start(), calls=%async_computation.2 | async-start | bytes 8519680 | tf_op jit(solution)/shard_map/all_gather | solution.py:78
  9.0 320.5 %all-gather.5.cloned.1.call-start = ((), (), s32[]{:S(2)}) async-start(), calls=%async_computation.3 | async-start | bytes 8519680 | tf_op jit(solution)/shard_map/all_gather | solution.py:79
  10.8 400.3 %reduce-scatter.2.cloned.1.call-start = ((), (), s32[]{:S(2)}) async-start(), calls=%async_computation.4 | async-start | bytes 655360 | tf_op jit(solution)/shard_map/reduce_scatter | solution.py:158
  14.8 100.4 %copy-start.5 = (bf16[256,256]{1,0:T(8,128)(2,1)S(1)}, bf16[256,256]{1,0:T(8,128)(2,1)}, u32[]{:S(2)}) copy-start(bf16[256,256]{1,0:T(8,128)(2,1)} %param.15) | copy-start | bytes 393220
  14.8 9.5 %collective-permute-start.6 = (f32[8,128,64]{1,2,0:T(8,128)S(1)}, f32[8,128,64]{1,2,0:T(8,128)S(1)}, u32[]{:S(2)}, u32[]{:S(2)}) collective-permute-start(f32[8,128,64]{1,2,0:T(8,128)S(1)} %convolution_bitcast_fusion.2), channel_id=1, source_target_pairs={{0,4},{4,8},{8,12},{12,16},{16,20},{20,24},{24,28},{28,32},{32,36}... | collective-permute-start | bytes 786440 | tf_op jit(solution)/shard_map/ppermute | solution.py:52
  24.3 9.0 %collective-permute-start.7 = (f32[8,128,64]{1,2,0:T(8,128)S(1)}, f32[8,128,64]{1,2,0:T(8,128)S(1)}, u32[]{:S(2)}, u32[]{:S(2)}) collective-permute-start(f32[8,128,64]{1,2,0:T(8,128)S(1)} %broadcast_select_fusion), channel_id=1, source_target_pairs={{0,4},{4,8},{8,12},{12,16},{16,20},{20,24},{24,28},{28,32},{32,36}... | collective-permute-start | bytes 786440 | tf_op jit(solution)/shard_map/ppermute | solution.py:52
  28.4 4.9 %collective-permute-start = (f32[8]{0:T(128)S(1)}, f32[8]{0:T(128)S(1)}, u32[]{:S(2)}, u32[]{:S(2)}) collective-permute-start(f32[8]{0:T(128)S(1)} %exp.27), channel_id=1, source_target_pairs={{0,4},{4,8},{8,12},{12,16},{16,20},{20,24},{24,28},{28,32},{32,36}... | collective-permute-start | bytes 104 | tf_op jit(solution)/shard_map/ppermute | solution.py:52
  33.4 11.5 %collective-permute-start.8 = (f32[8,128,64]{1,2,0:T(8,128)S(1)}, f32[8,128,64]{1,2,0:T(8,128)S(1)}, u32[]{:S(2)}, u32[]{:S(2)}) collective-permute-start(f32[8,128,64]{1,2,0:T(8,128)S(1)} %add_select_fusion.5), channel_id=1, source_target_pairs={{0,8},{4,12},{8,16},{12,20},{16,24},{20,28},{24,32},{28,36},{32,40... | collective-permute-start | bytes 786440 | tf_op jit(solution)/shard_map/ppermute | solution.py:52
  40.1 4.8 %collective-permute-start.1 = (f32[8]{0:T(128)S(1)}, f32[8]{0:T(128)S(1)}, u32[]{:S(2)}, u32[]{:S(2)}) collective-permute-start(f32[8]{0:T(128)S(1)} %broadcast_select_fusion.2), channel_id=1, source_target_pairs={{0,4},{4,8},{8,12},{12,16},{16,20},{20,24},{24,28},{28,32},{32,36}... | collective-permute-start | bytes 104 | tf_op jit(solution)/shard_map/ppermute | solution.py:52
  45.0 20.7 %collective-permute-start.9 = (f32[8,128,64]{1,2,0:T(8,128)S(1)}, f32[8,128,64]{1,2,0:T(8,128)S(1)}, u32[]{:S(2)}, u32[]{:S(2)}) collective-permute-start(f32[8,128,64]{1,2,0:T(8,128)S(1)} %add_select_fusion.4), channel_id=1, source_target_pairs={{0,16},{4,20},{8,24},{12,28},{16,32},{20,36},{24,40},{28,44},{32,4... | collective-permute-start | bytes 786440 | tf_op jit(solution)/shard_map/ppermute | solution.py:52
  61.7 4.0 collective-permute-start.2
  65.8 24.4 %collective-permute-start.10 = (f32[8,128,64]{1,2,0:T(8,128)S(1)}, f32[8,128,64]{1,2,0:T(8,128)S(1)}, u32[]{:S(2)}, u32[]{:S(2)}) collective-permute-start(f32[8,128,64]{1,2,0:T(8,128)S(1)} %add_select_fusion.3), channel_id=1, source_target_pairs={{0,32},{4,36},{8,40},{12,44},{16,48},{20,52},{24,56},{28,60},{32,6... | collective-permute-start | bytes 786440 | tf_op jit(solution)/shard_map/ppermute | solution.py:52
  85.3 4.9 %collective-permute-start.3 = (f32[8]{0:T(128)S(1)}, f32[8]{0:T(128)S(1)}, u32[]{:S(2)}, u32[]{:S(2)}) collective-permute-start(f32[8]{0:T(128)S(1)} %broadcast_select_fusion.3), channel_id=1, source_target_pairs={{0,16},{4,20},{8,24},{12,28},{16,32},{20,36},{24,40},{28,44},{32,4... | collective-permute-start | bytes 104 | tf_op jit(solution)/shard_map/ppermute | solution.py:52
  90.3 19.1 %collective-permute-start.11 = (f32[8,128,64]{1,2,0:T(8,128)S(1)}, f32[8,128,64]{1,2,0:T(8,128)S(1)}, u32[]{:S(2)}, u32[]{:S(2)}) collective-permute-start(f32[8,128,64]{1,2,0:T(8,128)S(1)} %add_select_fusion.2), channel_id=1, source_target_pairs={{0,64},{4,68},{8,72},{12,76},{16,80},{20,84},{24,88},{28,92},{32,9... | collective-permute-start | bytes 786440 | tf_op jit(solution)/shard_map/ppermute | solution.py:52
  102.8 6.6 %collective-permute-start.4 = (f32[8]{0:T(128)S(1)}, f32[8]{0:T(128)S(1)}, u32[]{:S(2)}, u32[]{:S(2)}) collective-permute-start(f32[8]{0:T(128)S(1)} %broadcast_select_fusion.4), channel_id=1, source_target_pairs={{0,32},{4,36},{8,40},{12,44},{16,48},{20,52},{24,56},{28,60},{32,6... | collective-permute-start | bytes 104 | tf_op jit(solution)/shard_map/ppermute | solution.py:52
  109.4 5.8 %copy-start.6 = (f32[8]{0:T(128)}, f32[8]{0:T(128)S(1)}, u32[]{:S(2)}) copy-start(f32[8]{0:T(128)S(1)} %broadcast_select_fusion.5) | copy-start | bytes 100
  109.5 9.0 %collective-permute-start.12 = (f32[8,128,64]{1,2,0:T(8,128)S(1)}, f32[8,128,64]{1,2,0:T(8,128)S(1)}, u32[]{:S(2)}, u32[]{:S(2)}) collective-permute-start(f32[8,128,64]{1,2,0:T(8,128)S(1)} %add_select_fusion.1), channel_id=1, source_target_pairs={{0,128},{4,132},{8,136},{12,140},{16,144},{20,148},{24,152},{28,15... | collective-permute-start | bytes 786440 | tf_op jit(solution)/shard_map/ppermute | solution.py:52
  115.3 2.5 collective-permute-start.5
  329.6 59.0 %copy-start.1 = (bf16[256,1024]{1,0:T(8,128)(2,1)S(1)}, bf16[256,1024]{1,0:T(8,128)(2,1)}, u32[]{:S(2)}) copy-start(bf16[256,1024]{1,0:T(8,128)(2,1)} %param.22) | copy-start | bytes 1572868
  329.6 60.2 %copy-start.7 = (s32[256]{0:T(256)S(1)}, s32[256]{0:T(256)}, u32[]{:S(2)}) copy-start(s32[256]{0:T(256)} %param.25) | copy-start | bytes 3076
  412.1 8.1 %copy-start.2 = (bf16[64,1024]{1,0:T(8,128)(2,1)}, bf16[64,1024]{1,0:T(8,128)(2,1)S(1)}, u32[]{:S(2)}) copy-start(bf16[64,1024]{1,0:T(8,128)(2,1)S(1)} %add_convert_fusion) | copy-start | bytes 393220
Sparse Core Ops, SparseCore 0:
  12.0 168.0 all-gather.2
  184.2 145.3 all-gather.4
  389.9 21.1 reduce-scatter.1

commit v2 on v1

--- a/solution.py
+++ b/solution.py
@@ -3,7 +3,7 @@
 import jax
 import jax.numpy as jnp
 from jax import lax
-from jax.sharding import PartitionSpec as P
+from jax.sharding import Mesh, PartitionSpec as P
 
 HDIM = 64
 
@@ -43,7 +43,7 @@
 
 
 def pass_states(local_state, total_decay):
-    axis = "seq"
+    axis = ("sa", "sb")
     devices = lax.axis_size(axis)
     mine = lax.axis_index(axis)
 
@@ -75,8 +75,8 @@
         jnp.zeros((head_count, row_count), jnp.float32),
         jnp.zeros((head_count, row_count, head_width), jnp.float32),
     )
-    key_piece = lax.all_gather(key_rows, "seq", axis=0, tiled=True)
-    value_piece = lax.all_gather(values, "seq", axis=0, tiled=True)
+    key_piece = lax.all_gather(key_rows, "sa", axis=0, tiled=True)
+    value_piece = lax.all_gather(values, "sa", axis=0, tiled=True)
     piece_rows = key_piece.shape[0]
     block_rows = math.gcd(piece_rows, 1024)
 
@@ -141,8 +141,18 @@
 ):
     row_count = queries.shape[0]
     head_count = queries.shape[1] // HDIM
-    query_heads = queries.reshape(row_count, head_count, HDIM)
-    attended = fold_keys(query_heads, key_rows, values)
+
+    def spread(part):
+        split = part.reshape(row_count, head_count, HDIM)
+        return lax.all_to_all(split, "sb", split_axis=1, concat_axis=0, tiled=True)
+
+    query_heads = spread(queries)
+    group_keys = spread(key_rows).reshape(-1, HDIM)
+    group_values = spread(values).reshape(-1, HDIM)
+    attended_one = fold_keys(query_heads, group_keys, group_values)
+    attended = lax.all_to_all(
+        attended_one.reshape(-1, 1, HDIM), "sb", split_axis=0, concat_axis=1, tiled=True
+    ).reshape(row_count, head_count * HDIM)
     cumulative, inner_part, local_state, total_decay = chain_pieces(
         ssm_input, write_proj, read_proj, log_decay
     )
@@ -182,21 +192,27 @@
 
 
 def solution(mesh):
+    seq_count = mesh.shape["seq"]
+    inner = math.gcd(seq_count, mesh.shape["head"])
+    split_mesh = Mesh(
+        mesh.devices.reshape(seq_count // inner, inner, mesh.shape["head"]), ("sa", "sb", "head")
+    )
+    seq = ("sa", "sb")
     in_specs = (
-        P("seq", None),
-        P("seq", "head"),
-        P("seq", "head"),
-        P("seq", "head"),
-        P("seq", "head"),
-        P("seq", None),
-        P("seq", None),
-        P("head", "seq"),
+        P(seq, None),
+        P(seq, "head"),
+        P(seq, "head"),
+        P(seq, "head"),
+        P(seq, "head"),
+        P(seq, None),
+        P(seq, None),
+        P("head", seq),
         P("head", None),
         P("head", None),
         P(),
-        P("seq"),
-    )
-    out_specs = (P(("seq", "head"), None), P("seq", "head", None, None, None))
+        P(seq),
+    )
+    out_specs = (P(("sa", "sb", "head"), None), P(seq, "head", None, None, None))
     return jax.shard_map(
-        per_device, mesh=mesh, in_specs=in_specs, out_specs=out_specs, check_vma=False
-    )
+        per_device, mesh=split_mesh, in_specs=in_specs, out_specs=out_specs, check_vma=False
+    )

time: 428 us -> 331 us (0.77)
  waiting for transfers between devices: 240 us -> 123 us
  matrix products: 31.9 us -> 63.5 us
  local copies, waits for them, and re-layouts: 26.3 us -> 9.19 us
  blocking collectives: 6.76 us -> 17.7 us
  starting transfers between devices: 91.1 us -> 84.2 us
    all_gather x2, waiting for transfers between devices: 209 us -> 84.6 us  [the longest x1 84.6 us: fold_keys(): value_piece = lax.all_gather(values, 'sa', axis=0, tiled=True)]
    dynamic_slice x16 -> x0, local copies, waits for them, and re-layouts: 20.5 us -> none  [one_step(): lax.dynamic_slice_in_dim(value_piece, block_index * block_rows, block_row...]
    ppermute x13, starting transfers between devices: 90.9 us -> 72 us  [shifted(): return jax.tree.map(lambda part: lax.ppermute(part, axis, pairs), tree)]
    dot_general x16, matrix products: 13.6 us -> 28.6 us  [one_step(): jnp.einsum('hqk,khd->hqd', raised.astype(jnp.bfloat16), value_block, pref...]
    dot_general x16, matrix products: 12.4 us -> 26.3 us  [one_step(): jnp.einsum('qhd,khd->hqk', query_heads, key_block, preferred_element_type...]
    all_to_all x0 -> x3, starting transfers between devices: none -> 12.2 us  [the longest x2 7.99 us: spread(): return lax.all_to_all(split, 'sb', split_axis=1, concat_axis=0, tiled=True)]
    all_to_all x0 -> x1, blocking collectives: none -> 11 us  [spread(): return lax.all_to_all(split, 'sb', split_axis=1, concat_axis=0, tiled=True)]
  transfers between devices with their start and end apart: 16 -> 19, of which waited for: 10 -> 10; matrix products, arithmetic and copies ran while one was open for 2% -> 4% of each run, Pallas kernels for 0% -> 0%
where the time goes in v2:
time: 331 us; the launch traced here: 329 us
  waiting for transfers between devices  123 us (37%)
  starting transfers between devices  84.2 us (25%)
  matrix products  63.5 us (19%)
  blocking collectives  17.7 us (5%)
  other arithmetic  16.7 us (5%)
  between operations  14.2 us (4%)
  local copies, waits for them, and re-layouts  9.19 us (3%)
    all_gather x1, waiting for transfers between devices, fold_keys(): value_piece = lax.all_gather(values, 'sa', axis=0, tiled=True)  84.6 us
    ppermute x13, starting transfers between devices, shifted(): return jax.tree.map(lambda part: lax.ppermute(part, axis, pairs), tree)  72 us
    dot_general x16, matrix products, one_step(): jnp.einsum('hqk,khd->hqd', raised.astype(jnp.bfloat16), value_block, pref...  28.6 us
    dot_general x16, matrix products, one_step(): jnp.einsum('qhd,khd->hqk', query_heads, key_block, preferred_element_type...  26.3 us
    reduce_scatter x1, waiting for transfers between devices, per_device(): lax.psum_scatter((jnp.dot(attended, attn_project, preferred_element_type=...  21.5 us
    ppermute x13, waiting for transfers between devices, shifted(): return jax.tree.map(lambda part: lax.ppermute(part, axis, pairs), tree)  13.8 us
    reduce_sum x16, other arithmetic, one_step(): run_sum = run_sum * shrink + jnp.sum(raised, axis=2)  11.7 us
    all_to_all x1, blocking collectives, spread(): return lax.all_to_all(split, 'sb', split_axis=1, concat_axis=0, tiled=True)  11 us
  transfers between devices with their start and end apart: 19, of which 10 were waited for; matrix products, arithmetic and copies ran while one was open for 4% of the time, Pallas kernels for 0%

profile of v2, /device:TPU:1, one launch (start us, length us, event | category | flops | bytes accessed | tf_op | source)
XLA Modules:
  0.0 329.5 jit_solution(5763158095060913970)
XLA Ops:
  7.2 1.1 copy.50
  8.4 11.0 %all_to_all.68 = bf16[256,4,64]{0,2,1:T(8,128)(2,1)S(1)} all-to-all(bf16[256,4,64]{0,2,1:T(8,128)(2,1)S(1)} %bitcast.112), channel_id=1, replica_groups=mesh['sa'=16,'sb'=4,'head'=4] {'sb'}, dimensions={1} | all-to-all | bytes 262144 | tf_op jit(solution)/shard_map/all_to_all | solution.py:147
  20.2 1.3 reduce-window.6
  24.1 3.0 collective-permute-start.6
  27.9 4.7 %all-to-all-start.2 = ((bf16[256,4,64]{0,2,1:T(8,128)(2,1)}), bf16[256,4,64]{0,2,1:T(8,128)(2,1)S(1)}, u32[]{:S(2)}, u32[]{:S(2)}) async-start(bf16[256,4,64]{0,2,1:T(8,128)(2,1)} %bitcast.6), calls=%async_computation.2 | async-start | bytes 262144 | tf_op jit(solution)/shard_map/all_to_all | solution.py:147
  32.7 3.5 %collective-permute-start.7 = (f32[8,128,64]{1,2,0:T(8,128)S(1)}, f32[8,128,64]{1,2,0:T(8,128)S(1)}, u32[]{:S(2)}, u32[]{:S(2)}) collective-permute-start(f32[8,128,64]{1,2,0:T(8,128)S(1)} %broadcast_select_fusion.2), channel_id=1, source_target_pairs={{0,4},{4,8},{8,12},{12,16},{16,20},{20,24},{24,28},{28,32},{32,36}... | collective-permute-start | bytes 786440 | tf_op jit(solution)/shard_map/ppermute | solution.py:52
  36.2 3.1 collective-permute-start
  40.1 2.5 collective-permute-done
  42.7 6.3 %collective-permute-start.8 = (f32[8,128,64]{1,2,0:T(8,128)S(1)}, f32[8,128,64]{1,2,0:T(8,128)S(1)}, u32[]{:S(2)}, u32[]{:S(2)}) collective-permute-start(f32[8,128,64]{1,2,0:T(8,128)S(1)} %add_select_fusion.5), channel_id=1, source_target_pairs={{0,8},{4,12},{8,16},{12,20},{16,24},{20,28},{24,32},{28,36},{32,40... | collective-permute-start | bytes 786440 | tf_op jit(solution)/shard_map/ppermute | solution.py:52
  48.9 3.0 collective-permute-start.1
  51.9 3.4 %collective-permute-done.1 = f32[8]{0:T(128)S(1)} collective-permute-done((f32[8]{0:T(128)S(1)}, f32[8]{0:T(128)S(1)}, u32[]{:S(2)}, u32[]{:S(2)}) %collective-permute-start.1) | collective-permute-done | bytes 64 | tf_op jit(solution)/shard_map/ppermute | solution.py:52
  55.4 11.9 %collective-permute-start.9 = (f32[8,128,64]{1,2,0:T(8,128)S(1)}, f32[8,128,64]{1,2,0:T(8,128)S(1)}, u32[]{:S(2)}, u32[]{:S(2)}) collective-permute-start(f32[8,128,64]{1,2,0:T(8,128)S(1)} %add_select_fusion.4), channel_id=1, source_target_pairs={{0,16},{4,20},{8,24},{12,28},{16,32},{20,36},{24,40},{28,44},{32,4... | collective-permute-start | bytes 786440 | tf_op jit(solution)/shard_map/ppermute | solution.py:52
  68.1 3.3 %all-to-all-start.1 = ((bf16[256,4,64]{0,2,1:T(8,128)(2,1)}), bf16[256,4,64]{0,2,1:T(8,128)(2,1)S(1)}, u32[]{:S(2)}, u32[]{:S(2)}) async-start(bf16[256,4,64]{0,2,1:T(8,128)(2,1)} %bitcast.3), calls=%async_computation.1 | async-start | bytes 262144 | tf_op jit(solution)/shard_map/all_to_all | solution.py:147
  71.5 4.2 %collective-permute-start.2 = (f32[8]{0:T(128)S(1)}, f32[8]{0:T(128)S(1)}, u32[]{:S(2)}, u32[]{:S(2)}) collective-permute-start(f32[8]{0:T(128)S(1)} %broadcast_select_fusion.3), channel_id=1, source_target_pairs={{0,8},{4,12},{8,16},{12,20},{16,24},{20,28},{24,32},{28,36},{32,40... | collective-permute-start | bytes 104 | tf_op jit(solution)/shard_map/ppermute | solution.py:52
  75.7 3.6 %collective-permute-done.2 = f32[8]{0:T(128)S(1)} collective-permute-done((f32[8]{0:T(128)S(1)}, f32[8]{0:T(128)S(1)}, u32[]{:S(2)}, u32[]{:S(2)}) %collective-permute-start.2) | collective-permute-done | bytes 64 | tf_op jit(solution)/shard_map/ppermute | solution.py:52
  79.4 8.4 %collective-permute-start.10 = (f32[8,128,64]{1,2,0:T(8,128)S(1)}, f32[8,128,64]{1,2,0:T(8,128)S(1)}, u32[]{:S(2)}, u32[]{:S(2)}) collective-permute-start(f32[8,128,64]{1,2,0:T(8,128)S(1)} %add_select_fusion.3), channel_id=1, source_target_pairs={{0,32},{4,36},{8,40},{12,44},{16,48},{20,52},{24,56},{28,60},{32,6... | collective-permute-start | bytes 786440 | tf_op jit(solution)/shard_map/ppermute | solution.py:52
  88.0 6.6 %collective-permute-start.3 = (f32[8]{0:T(128)S(1)}, f32[8]{0:T(128)S(1)}, u32[]{:S(2)}, u32[]{:S(2)}) collective-permute-start(f32[8]{0:T(128)S(1)} %broadcast_select_fusion.5), channel_id=1, source_target_pairs={{0,16},{4,20},{8,24},{12,28},{16,32},{20,36},{24,40},{28,44},{32,4... | collective-permute-start | bytes 104 | tf_op jit(solution)/shard_map/ppermute | solution.py:52
  95.4 2.2 collective-permute-done.10
  97.7 9.0 %collective-permute-start.11 = (f32[8,128,64]{1,2,0:T(8,128)S(1)}, f32[8,128,64]{1,2,0:T(8,128)S(1)}, u32[]{:S(2)}, u32[]{:S(2)}) collective-permute-start(f32[8,128,64]{1,2,0:T(8,128)S(1)} %add_select_fusion.2), channel_id=1, source_target_pairs={{0,64},{4,68},{8,72},{12,76},{16,80},{20,84},{24,88},{28,92},{32,9... | collective-permute-start | bytes 786440 | tf_op jit(solution)/shard_map/ppermute | solution.py:52
  107.3 6.1 %collective-permute-start.4 = (f32[8]{0:T(128)S(1)}, f32[8]{0:T(128)S(1)}, u32[]{:S(2)}, u32[]{:S(2)}) collective-permute-start(f32[8]{0:T(128)S(1)} %broadcast_select_fusion.6), channel_id=1, source_target_pairs={{0,32},{4,36},{8,40},{12,44},{16,48},{20,52},{24,56},{28,60},{32,6... | collective-permute-start | bytes 104 | tf_op jit(solution)/shard_map/ppermute | solution.py:52
  114.6 5.7 %collective-permute-start.12 = (f32[8,128,64]{1,2,0:T(8,128)S(1)}, f32[8,128,64]{1,2,0:T(8,128)S(1)}, u32[]{:S(2)}, u32[]{:S(2)}) collective-permute-start(f32[8,128,64]{1,2,0:T(8,128)S(1)} %add_select_fusion.1), channel_id=1, source_target_pairs={{0,128},{4,132},{8,136},{12,140},{16,144},{20,148},{24,152},{28,15... | collective-permute-start | bytes 786440 | tf_op jit(solution)/shard_map/ppermute | solution.py:52
  120.3 1.5 convolution_bitcast_fusion.1
  121.8 1.3 collective-permute-start.5
  123.9 1.1 multiply_reduce_fusion.1
  125.1 84.6 %all-gather.5.cloned.1.call-done = bf16[16384,64]{0,1:T(8,128)(2,1)} async-done(((bf16[1024,64]{0,1:T(8,128)(2,1)}), bf16[16384,64]{0,1:T(8,128)(2,1)}) %all-gather.5.cloned.1.call-update) | async-done | bytes 2097168 | tf_op jit(solution)/shard_map/all_gather | solution.py:79
  209.7 68.0 %while.18 = (s32[]{:T(128)}, f32[1,1024]{1,0:T(1,128)S(1)}, f32[1,1024]{1,0:T(1,128)S(1)}, f32[1,1024,64]{1,2,0:T(8,128)S(1)}, bf16[16384,64]{0,1:T(8,128)(2,1)}...) while((s32[]{:T(128)}, f32[1,1024]{1,0:T(1,128)S(1)}, ...), condition=%wide.region_3.0_spmd.clone, body=%wide.region_0.0_spmd.clone.sunk | while | flops 277025792 | bytes 13566135 | solution.py:107
  209.7 1.6 multiply_reduce_fusion.3
  212.1 1.8 fusion.71
  213.9 1.6 multiply_reduce_fusion.3
  216.4 1.8 fusion.71
  218.2 1.6 multiply_reduce_fusion.3
  220.6 1.8 fusion.71
  222.5 1.6 multiply_reduce_fusion.3
  224.9 1.8 fusion.71
  226.7 1.6 multiply_reduce_fusion.3
  229.1 1.8 fusion.71
  231.0 1.6 multiply_reduce_fusion.3
  233.4 1.8 fusion.71
  235.2 1.6 multiply_reduce_fusion.3
  237.6 1.8 fusion.71
  239.5 1.6 multiply_reduce_fusion.3
  241.9 1.8 fusion.71
  243.7 1.6 multiply_reduce_fusion.3
  246.1 1.8 fusion.71
  248.0 1.6 multiply_reduce_fusion.3
  250.4 1.8 fusion.71
  252.2 1.6 multiply_reduce_fusion.3
  254.6 1.8 fusion.71
  256.5 1.6 multiply_reduce_fusion.3
  258.9 1.8 fusion.71
  260.7 1.6 multiply_reduce_fusion.3
  263.1 1.8 fusion.71
  265.0 1.6 multiply_reduce_fusion.3
  267.4 1.8 fusion.71
  269.2 1.6 multiply_reduce_fusion.3
  271.7 1.8 fusion.71
  273.5 1.6 multiply_reduce_fusion.3
  275.9 1.8 fusion.71
  280.0 4.2 %all-to-all-start.3 = ((bf16[4,2,8192]{2,1,0:T(2,128)(2,1)}), bf16[4,2,8192]{2,1,0:T(2,128)(2,1)S(1)}, u32[]{:S(2)}, u32[]{:S(2)}) async-start(bf16[4,2,8192]{2,1,0:T(2,128)(2,1)} %reshape.168), calls=%async_computation.3 | async-start | bytes 262144 | tf_op jit(solution)/shard_map/all_to_all | solution.py:153
  284.2 1.7 fusion.50
  285.9 3.1 all-to-all-done.3
  289.8 2.2 fusion.20
  292.4 21.5 %reduce-scatter.2.cloned.1.call-done = bf16[64,1024]{1,0:T(8,128)(2,1)} async-done(((bf16[256,1024]{1,0:T(8,128)(2,1)}), bf16[64,1024]{1,0:T(8,128)(2,1)}) %reduce-scatter.2.cloned.1.call-update) | async-done | bytes 131088 | tf_op jit(solution)/shard_map/reduce_scatter | solution.py:168
  315.5 6.7 %all_to_all.69 = bf16[4,32,768]{2,1,0:T(8,128)(2,1)S(1)} all-to-all(bf16[4,32,768]{2,1,0:T(8,128)(2,1)S(1)} %bitcast.101), channel_id=1, replica_groups=mesh['sa'=16,'sb'=4,'head'=4] {'head'}, dimensions={0} | all-to-all | bytes 393216 | tf_op jit(solution)/shard_map/all_to_all | solution.py:189
  (152 shorter events, 27.8 us)
Async XLA Ops:
  7.2 307.7 %copy-start = (bf16[1024,768]{1,0:T(8,128)(2,1)S(1)}, bf16[1024,768]{1,0:T(8,128)(2,1)}, u32[]{:S(2)}) copy-start(bf16[1024,768]{1,0:T(8,128)(2,1)} %param.24) | copy-start | bytes 4718596
  7.2 20.0 %copy-start.4 = (bf16[256,256]{1,0:T(8,128)(2,1)S(1)}, bf16[256,256]{1,0:T(8,128)(2,1)}, u32[]{:S(2)}) copy-start(bf16[256,256]{1,0:T(8,128)(2,1)} %param.17) | copy-start | bytes 393220
  7.2 117.9 %all-gather.3.cloned.1.call-start = ((), (), s32[]{:S(2)}) async-start(), calls=%async_computation.6 | async-start | bytes 2228224 | tf_op jit(solution)/shard_map/all_gather | solution.py:78
  22.7 44.6 %copy-start.5 = (bf16[256,256]{1,0:T(8,128)(2,1)S(1)}, bf16[256,256]{1,0:T(8,128)(2,1)}, u32[]{:S(2)}) copy-start(bf16[256,256]{1,0:T(8,128)(2,1)} %param.15) | copy-start | bytes 393220
  24.1 8.5 %collective-permute-start.6 = (f32[8,128,64]{1,2,0:T(8,128)S(1)}, f32[8,128,64]{1,2,0:T(8,128)S(1)}, u32[]{:S(2)}, u32[]{:S(2)}) collective-permute-start(f32[8,128,64]{1,2,0:T(8,128)S(1)} %convolution_bitcast_fusion.2), channel_id=1, source_target_pairs={{0,4},{4,8},{8,12},{12,16},{16,20},{20,24},{24,28},{28,32},{32,36}... | collective-permute-start | bytes 786440 | tf_op jit(solution)/shard_map/ppermute | solution.py:52
  27.9 11.3 %all-to-all-start.2 = ((bf16[256,4,64]{0,2,1:T(8,128)(2,1)}), bf16[256,4,64]{0,2,1:T(8,128)(2,1)S(1)}, u32[]{:S(2)}, u32[]{:S(2)}) async-start(bf16[256,4,64]{0,2,1:T(8,128)(2,1)} %bitcast.6), calls=%async_computation.2 | async-start | bytes 262144 | tf_op jit(solution)/shard_map/all_to_all | solution.py:147
  32.6 55.2 %copy-start.2 = (bf16[256,128]{1,0:T(8,128)(2,1)S(1)}, bf16[256,128]{1,0:T(8,128)(2,1)}, u32[]{:S(2)}) copy-start(bf16[256,128]{1,0:T(8,128)(2,1)} %param.19) | copy-start | bytes 196612
  32.6 55.2 %copy-start.3 = (bf16[256,128]{1,0:T(8,128)(2,1)S(1)}, bf16[256,128]{1,0:T(8,128)(2,1)}, u32[]{:S(2)}) copy-start(bf16[256,128]{1,0:T(8,128)(2,1)} %param.20) | copy-start | bytes 196612
  32.6 177.1 %all-gather.5.cloned.1.call-start = ((), (), s32[]{:S(2)}) async-start(), calls=%async_computation.7 | async-start | bytes 2228224 | tf_op jit(solution)/shard_map/all_gather | solution.py:79
  32.7 9.9 %collective-permute-start.7 = (f32[8,128,64]{1,2,0:T(8,128)S(1)}, f32[8,128,64]{1,2,0:T(8,128)S(1)}, u32[]{:S(2)}, u32[]{:S(2)}) collective-permute-start(f32[8,128,64]{1,2,0:T(8,128)S(1)} %broadcast_select_fusion.2), channel_id=1, source_target_pairs={{0,4},{4,8},{8,12},{12,16},{16,20},{20,24},{24,28},{28,32},{32,36}... | collective-permute-start | bytes 786440 | tf_op jit(solution)/shard_map/ppermute | solution.py:52
  36.2 6.4 %collective-permute-start = (f32[8]{0:T(128)S(1)}, f32[8]{0:T(128)S(1)}, u32[]{:S(2)}, u32[]{:S(2)}) collective-permute-start(f32[8]{0:T(128)S(1)} %exp.29), channel_id=1, source_target_pairs={{0,4},{4,8},{8,12},{12,16},{16,20},{20,24},{24,28},{28,32},{32,36}... | collective-permute-start | bytes 104 | tf_op jit(solution)/shard_map/ppermute | solution.py:52
  42.7 12.7 %collective-permute-start.8 = (f32[8,128,64]{1,2,0:T(8,128)S(1)}, f32[8,128,64]{1,2,0:T(8,128)S(1)}, u32[]{:S(2)}, u32[]{:S(2)}) collective-permute-start(f32[8,128,64]{1,2,0:T(8,128)S(1)} %add_select_fusion.5), channel_id=1, source_target_pairs={{0,8},{4,12},{8,16},{12,20},{16,24},{20,28},{24,32},{28,36},{32,40... | collective-permute-start | bytes 786440 | tf_op jit(solution)/shard_map/ppermute | solution.py:52
  48.9 6.4 %collective-permute-start.1 = (f32[8]{0:T(128)S(1)}, f32[8]{0:T(128)S(1)}, u32[]{:S(2)}, u32[]{:S(2)}) collective-permute-start(f32[8]{0:T(128)S(1)} %broadcast_select_fusion.4), channel_id=1, source_target_pairs={{0,4},{4,8},{8,12},{12,16},{16,20},{20,24},{24,28},{28,32},{32,36}... | collective-permute-start | bytes 104 | tf_op jit(solution)/shard_map/ppermute | solution.py:52
  55.4 23.9 %collective-permute-start.9 = (f32[8,128,64]{1,2,0:T(8,128)S(1)}, f32[8,128,64]{1,2,0:T(8,128)S(1)}, u32[]{:S(2)}, u32[]{:S(2)}) collective-permute-start(f32[8,128,64]{1,2,0:T(8,128)S(1)} %add_select_fusion.4), channel_id=1, source_target_pairs={{0,16},{4,20},{8,24},{12,28},{16,32},{20,36},{24,40},{28,44},{32,4... | collective-permute-start | bytes 786440 | tf_op jit(solution)/shard_map/ppermute | solution.py:52
  68.1 55.7 %all-to-all-start.1 = ((bf16[256,4,64]{0,2,1:T(8,128)(2,1)}), bf16[256,4,64]{0,2,1:T(8,128)(2,1)S(1)}, u32[]{:S(2)}, u32[]{:S(2)}) async-start(bf16[256,4,64]{0,2,1:T(8,128)(2,1)} %bitcast.3), calls=%async_computation.1 | async-start | bytes 262144 | tf_op jit(solution)/shard_map/all_to_all | solution.py:147
  71.5 7.8 %collective-permute-start.2 = (f32[8]{0:T(128)S(1)}, f32[8]{0:T(128)S(1)}, u32[]{:S(2)}, u32[]{:S(2)}) collective-permute-start(f32[8]{0:T(128)S(1)} %broadcast_select_fusion.3), channel_id=1, source_target_pairs={{0,8},{4,12},{8,16},{12,20},{16,24},{20,28},{24,32},{28,36},{32,40... | collective-permute-start | bytes 104 | tf_op jit(solution)/shard_map/ppermute | solution.py:52
  79.4 18.1 %collective-permute-start.10 = (f32[8,128,64]{1,2,0:T(8,128)S(1)}, f32[8,128,64]{1,2,0:T(8,128)S(1)}, u32[]{:S(2)}, u32[]{:S(2)}) collective-permute-start(f32[8,128,64]{1,2,0:T(8,128)S(1)} %add_select_fusion.3), channel_id=1, source_target_pairs={{0,32},{4,36},{8,40},{12,44},{16,48},{20,52},{24,56},{28,60},{32,6... | collective-permute-start | bytes 786440 | tf_op jit(solution)/shard_map/ppermute | solution.py:52
  88.0 7.3 %collective-permute-start.3 = (f32[8]{0:T(128)S(1)}, f32[8]{0:T(128)S(1)}, u32[]{:S(2)}, u32[]{:S(2)}) collective-permute-start(f32[8]{0:T(128)S(1)} %broadcast_select_fusion.5), channel_id=1, source_target_pairs={{0,16},{4,20},{8,24},{12,28},{16,32},{20,36},{24,40},{28,44},{32,4... | collective-permute-start | bytes 104 | tf_op jit(solution)/shard_map/ppermute | solution.py:52
  97.7 16.4 %collective-permute-start.11 = (f32[8,128,64]{1,2,0:T(8,128)S(1)}, f32[8,128,64]{1,2,0:T(8,128)S(1)}, u32[]{:S(2)}, u32[]{:S(2)}) collective-permute-start(f32[8,128,64]{1,2,0:T(8,128)S(1)} %add_select_fusion.2), channel_id=1, source_target_pairs={{0,64},{4,68},{8,72},{12,76},{16,80},{20,84},{24,88},{28,92},{32,9... | collective-permute-start | bytes 786440 | tf_op jit(solution)/shard_map/ppermute | solution.py:52
  107.3 6.8 %collective-permute-start.4 = (f32[8]{0:T(128)S(1)}, f32[8]{0:T(128)S(1)}, u32[]{:S(2)}, u32[]{:S(2)}) collective-permute-start(f32[8]{0:T(128)S(1)} %broadcast_select_fusion.6), channel_id=1, source_target_pairs={{0,32},{4,36},{8,40},{12,44},{16,48},{20,52},{24,56},{28,60},{32,6... | collective-permute-start | bytes 104 | tf_op jit(solution)/shard_map/ppermute | solution.py:52
  114.1 0.5 copy-start.6
  114.6 9.2 %collective-permute-start.12 = (f32[8,128,64]{1,2,0:T(8,128)S(1)}, f32[8,128,64]{1,2,0:T(8,128)S(1)}, u32[]{:S(2)}, u32[]{:S(2)}) collective-permute-start(f32[8,128,64]{1,2,0:T(8,128)S(1)} %add_select_fusion.1), channel_id=1, source_target_pairs={{0,128},{4,132},{8,136},{12,140},{16,144},{20,148},{24,152},{28,15... | collective-permute-start | bytes 786440 | tf_op jit(solution)/shard_map/ppermute | solution.py:52
  120.3 1.5 copy-start.7
  121.8 2.0 collective-permute-start.5
  280.0 9.0 %all-to-all-start.3 = ((bf16[4,2,8192]{2,1,0:T(2,128)(2,1)}), bf16[4,2,8192]{2,1,0:T(2,128)(2,1)S(1)}, u32[]{:S(2)}, u32[]{:S(2)}) async-start(bf16[4,2,8192]{2,1,0:T(2,128)(2,1)} %reshape.168), calls=%async_computation.3 | async-start | bytes 262144 | tf_op jit(solution)/shard_map/all_to_all | solution.py:153
  284.2 29.7 %reduce-scatter.2.cloned.1.call-start = ((), (), s32[]{:S(2)}) async-start(), calls=%async_computation.8 | async-start | bytes 655360 | tf_op jit(solution)/shard_map/reduce_scatter | solution.py:168
  289.3 2.6 copy-start.8
  314.9 8.0 %copy-start.1 = (bf16[64,1024]{1,0:T(8,128)(2,1)}, bf16[64,1024]{1,0:T(8,128)(2,1)S(1)}, u32[]{:S(2)}) copy-start(bf16[64,1024]{1,0:T(8,128)(2,1)S(1)} %add_convert_fusion) | copy-start | bytes 393220
Sparse Core Ops, SparseCore 0:
  20.3 95.4 all-gather.2
  119.3 90.3 all-gather.4
  292.1 21.7 reduce-scatter.1

commit v3 on v2

--- a/solution.py
+++ b/solution.py
@@ -75,8 +75,8 @@
         jnp.zeros((head_count, row_count), jnp.float32),
         jnp.zeros((head_count, row_count, head_width), jnp.float32),
     )
-    key_piece = lax.all_gather(key_rows, "sa", axis=0, tiled=True)
-    value_piece = lax.all_gather(values, "sa", axis=0, tiled=True)
+    key_piece = key_rows
+    value_piece = values
     piece_rows = key_piece.shape[0]
     block_rows = math.gcd(piece_rows, 1024)
 
@@ -142,13 +142,21 @@
     row_count = queries.shape[0]
     head_count = queries.shape[1] // HDIM
 
-    def spread(part):
-        split = part.reshape(row_count, head_count, HDIM)
-        return lax.all_to_all(split, "sb", split_axis=1, concat_axis=0, tiled=True)
-
-    query_heads = spread(queries)
-    group_keys = spread(key_rows).reshape(-1, HDIM)
-    group_values = spread(values).reshape(-1, HDIM)
+    stacked = jnp.stack([queries, key_rows, values]).reshape(3, row_count, head_count, HDIM)
+    spread = lax.all_to_all(stacked, "sb", split_axis=2, concat_axis=1, tiled=True)
+    query_heads = spread[0]
+    group_rows = spread.shape[1]
+    peers = lax.axis_size("sa")
+    pair = spread[1:].reshape(2, group_rows, HDIM)
+    gathered = lax.all_to_all(
+        jnp.broadcast_to(pair[None], (peers, 2, group_rows, HDIM)),
+        "sa",
+        split_axis=0,
+        concat_axis=0,
+        tiled=True,
+    )
+    group_keys = gathered[:, 0].reshape(peers * group_rows, HDIM)
+    group_values = gathered[:, 1].reshape(peers * group_rows, HDIM)
     attended_one = fold_keys(query_heads, group_keys, group_values)
     attended = lax.all_to_all(
         attended_one.reshape(-1, 1, HDIM), "sb", split_axis=0, concat_axis=1, tiled=True

time: 331 us -> 439 us (1.33)
  other arithmetic: 16.7 us -> 52.9 us
  matrix products: 63.5 us -> 93.9 us
  local copies, waits for them, and re-layouts: 9.19 us -> 30 us
  starting transfers between devices: 84.2 us -> 95.4 us
  blocking collectives: 17.7 us -> 23.8 us
    ppermute x13, waiting for transfers between devices: 13.8 us -> 100 us  [shifted(): return jax.tree.map(lambda part: lax.ppermute(part, axis, pairs), tree)]
    all_gather x2 -> x0, waiting for transfers between devices: 84.6 us -> none  [the longest x1 84.6 us: fold_keys(): value_piece = lax.all_gather(values, 'sa', axis=0, tiled=True)]
    reduce_sum x16, other arithmetic: 11.7 us -> 49.1 us  [one_step(): run_sum = run_sum * shrink + jnp.sum(raised, axis=2)]
    dot_general x16, matrix products: 26.3 us -> 57.5 us  [one_step(): jnp.einsum('qhd,khd->hqk', query_heads, key_block, preferred_element_type...]
    ppermute x13, starting transfers between devices: 72 us -> 81.1 us  [shifted(): return jax.tree.map(lambda part: lax.ppermute(part, axis, pairs), tree)]
    unnamed x28 -> x24, local copies, waits for them, and re-layouts: 7.58 us -> 14.9 us
    all_to_all x1, blocking collectives: 11 us -> 17.1 us  [per_device(): lax.all_to_all(stacked, 'sb', split_axis=2, concat_axis=1, tiled=True)]
    while x16 -> x48, local copies, waits for them, and re-layouts: 0.04 us -> 5.54 us
  transfers between devices with their start and end apart: 19 -> 16, of which waited for: 10 -> 10; matrix products, arithmetic and copies ran while one was open for 4% -> 1% of each run, Pallas kernels for 0% -> 0%
where the time goes in v3:
time: 439 us; the launch traced here: 437 us
  waiting for transfers between devices  126 us (29%)
  starting transfers between devices  95.4 us (22%)
  matrix products  93.9 us (21%)
  other arithmetic  52.9 us (12%)
  local copies, waits for them, and re-layouts  30 us (7%)
  blocking collectives  23.8 us (5%)
  between operations  14.5 us (3%)
    ppermute x13, waiting for transfers between devices, shifted(): return jax.tree.map(lambda part: lax.ppermute(part, axis, pairs), tree)  100 us
    ppermute x13, starting transfers between devices, shifted(): return jax.tree.map(lambda part: lax.ppermute(part, axis, pairs), tree)  81.1 us
    dot_general x16, matrix products, one_step(): jnp.einsum('qhd,khd->hqk', query_heads, key_block, preferred_element_type...  57.5 us
    reduce_sum x16, other arithmetic, one_step(): run_sum = run_sum * shrink + jnp.sum(raised, axis=2)  49.1 us
    dot_general x16, matrix products, one_step(): jnp.einsum('hqk,khd->hqd', raised.astype(jnp.bfloat16), value_block, pref...  29.4 us
    reduce_scatter x1, waiting for transfers between devices, per_device(): lax.psum_scatter((jnp.dot(attended, attn_project, preferred_element_type=...  22.3 us
    all_to_all x1, blocking collectives, per_device(): lax.all_to_all(stacked, 'sb', split_axis=2, concat_axis=1, tiled=True)  17.1 us
    unnamed x24, local copies, waits for them, and re-layouts  14.9 us
  transfers between devices with their start and end apart: 16, of which 10 were waited for; matrix products, arithmetic and copies ran while one was open for 1% of the time, Pallas kernels for 0%

profile of v3, /device:TPU:1, one launch (start us, length us, event | category | flops | bytes accessed | tf_op | source)
XLA Modules:
  0.0 436.7 jit_solution(7667147901140543649)
XLA Ops:
  10.4 17.1 %all_to_all.40 = bf16[3,256,4,64]{1,3,0,2:T(8,128)(2,1)S(1)} all-to-all(bf16[3,256,4,64]{1,3,0,2:T(8,128)(2,1)S(1)} %copy.49), channel_id=1, replica_groups=mesh['sa'=16,'sb'=4,'head'=4] {'sb'}, dimensions={2} | all-to-all | bytes 786432 | tf_op jit(solution)/shard_map/all_to_all | solution.py:146
  27.9 2.5 broadcast_in_dim.34
  30.5 10.9 %all-to-all-start.1 = ((bf16[16,2,1024,64]{2,3,1,0:T(8,128)(2,1)}), bf16[16,2,1024,64]{2,3,1,0:T(8,128)(2,1)}, u32[]{:S(2)}, u32[]{:S(2)}) async-start(bf16[16,2,1024,64]{2,3,1,0:T(8,128)(2,1)} %broadcast_in_dim.34), calls=%async_computation.1 | async-start | bytes 8388608 | tf_op jit(solution)/shard_map/all_to_all | solution.py:151
  44.2 93.2 %collective-permute-done.6 = f32[8,128,64]{1,2,0:T(8,128)S(1)} collective-permute-done((f32[8,128,64]{1,2,0:T(8,128)S(1)}, f32[8,128,64]{1,2,0:T(8,128)S(1)}, u32[]{:S(2)}, u32[]{:S(2)}) %collective-permute-start.6) | collective-permute-done | bytes 262176 | tf_op jit(solution)/shard_map/ppermute | solution.py:52
  137.5 4.3 collective-permute-start.7
  141.7 2.9 collective-permute-start
  145.5 5.8 %collective-permute-start.8 = (f32[8,128,64]{1,2,0:T(8,128)S(1)}, f32[8,128,64]{1,2,0:T(8,128)S(1)}, u32[]{:S(2)}, u32[]{:S(2)}) collective-permute-start(f32[8,128,64]{1,2,0:T(8,128)S(1)} %add_select_fusion.5), channel_id=1, source_target_pairs={{0,8},{4,12},{8,16},{12,20},{16,24},{20,28},{24,32},{28,36},{32,40... | collective-permute-start | bytes 786440 | tf_op jit(solution)/shard_map/ppermute | solution.py:52
  151.3 2.8 collective-permute-start.1
  154.9 13.6 %collective-permute-start.9 = (f32[8,128,64]{1,2,0:T(8,128)S(1)}, f32[8,128,64]{1,2,0:T(8,128)S(1)}, u32[]{:S(2)}, u32[]{:S(2)}) collective-permute-start(f32[8,128,64]{1,2,0:T(8,128)S(1)} %add_select_fusion.4), channel_id=1, source_target_pairs={{0,16},{4,20},{8,24},{12,28},{16,32},{20,36},{24,40},{28,44},{32,4... | collective-permute-start | bytes 786440 | tf_op jit(solution)/shard_map/ppermute | solution.py:52
  168.5 10.2 %collective-permute-start.2 = (f32[8]{0:T(128)S(1)}, f32[8]{0:T(128)S(1)}, u32[]{:S(2)}, u32[]{:S(2)}) collective-permute-start(f32[8]{0:T(128)S(1)} %broadcast_select_fusion.3), channel_id=1, source_target_pairs={{0,8},{4,12},{8,16},{12,20},{16,24},{20,28},{24,32},{28,36},{32,40... | collective-permute-start | bytes 104 | tf_op jit(solution)/shard_map/ppermute | solution.py:52
  179.5 17.3 %collective-permute-start.10 = (f32[8,128,64]{1,2,0:T(8,128)S(1)}, f32[8,128,64]{1,2,0:T(8,128)S(1)}, u32[]{:S(2)}, u32[]{:S(2)}) collective-permute-start(f32[8,128,64]{1,2,0:T(8,128)S(1)} %add_select_fusion.3), channel_id=1, source_target_pairs={{0,32},{4,36},{8,40},{12,44},{16,48},{20,52},{24,56},{28,60},{32,6... | collective-permute-start | bytes 786440 | tf_op jit(solution)/shard_map/ppermute | solution.py:52
  199.1 2.9 collective-permute-done.10
  202.1 10.2 %collective-permute-start.11 = (f32[8,128,64]{1,2,0:T(8,128)S(1)}, f32[8,128,64]{1,2,0:T(8,128)S(1)}, u32[]{:S(2)}, u32[]{:S(2)}) collective-permute-start(f32[8,128,64]{1,2,0:T(8,128)S(1)} %add_select_fusion.2), channel_id=1, source_target_pairs={{0,64},{4,68},{8,72},{12,76},{16,80},{20,84},{24,88},{28,92},{32,9... | collective-permute-start | bytes 786440 | tf_op jit(solution)/shard_map/ppermute | solution.py:52
  212.3 4.9 %collective-permute-start.4 = (f32[8]{0:T(128)S(1)}, f32[8]{0:T(128)S(1)}, u32[]{:S(2)}, u32[]{:S(2)}) collective-permute-start(f32[8]{0:T(128)S(1)} %broadcast_select_fusion.6), channel_id=1, source_target_pairs={{0,32},{4,36},{8,40},{12,44},{16,48},{20,52},{24,56},{28,60},{32,6... | collective-permute-start | bytes 104 | tf_op jit(solution)/shard_map/ppermute | solution.py:52
  218.0 5.3 %collective-permute-start.12 = (f32[8,128,64]{1,2,0:T(8,128)S(1)}, f32[8,128,64]{1,2,0:T(8,128)}, u32[]{:S(2)}, u32[]{:S(2)}) collective-permute-start(f32[8,128,64]{1,2,0:T(8,128)S(1)} %add_select_fusion.1), channel_id=1, source_target_pairs={{0,128},{4,132},{8,136},{12,140},{16,144},{20,148},{24,152},{28,15... | collective-permute-start | bytes 786440 | tf_op jit(solution)/shard_map/ppermute | solution.py:52
  227.6 5.0 %fusion.49 = (bf16[16,1,1024,64]{2,3,1,0:T(8,128)(2,1)}, bf16[16,1,1024,64]{2,3,1,0:T(8,128)(2,1)}) fusion(bf16[16,2,1024,64]{2,3,1,0:T(8,128)(2,1)} %all-to-all-done.1), kind=kLoop, calls=%fused_computation.92 | loop fusion | bytes 8388608 | tf_op jit(solution)/shard_map/slice | solution.py:159
  232.6 4.8 %copy.60 = bf16[16,1,1024,64]{3,2,0,1:T(8,128)(2,1)} copy(bf16[16,1,1024,64]{2,3,1,0:T(8,128)(2,1)} %get-tuple-element.181) | data formatting | bytes 4194304
  237.4 4.8 %copy.61 = bf16[16,1,1024,64]{3,2,0,1:T(8,128)(2,1)} copy(bf16[16,1,1024,64]{2,3,1,0:T(8,128)(2,1)} %get-tuple-element.180) | data formatting | bytes 4194304
  242.2 142.7 %while.18 = (s32[]{:T(128)}, f32[1,1024]{1,0:T(1,128)S(1)}, f32[1,1024]{1,0:T(1,128)S(1)}, f32[1,1024,64]{1,2,0:T(8,128)S(1)}, bf16[16384,64]{1,0:T(8,128)(2,1)}...) while((s32[]{:T(128)}, f32[1,1024]{1,0:T(1,128)S(1)}, ...), condition=%wide.region_3.0_spmd.clone, body=%wide.region_0.0_spmd.clone.sunk | while | flops 277025792 | bytes 30605512 | solution.py:107
  242.2 3.6 multiply_reduce_fusion.3
  245.8 3.1 fusion.70
  249.2 1.8 fusion.72
  251.1 3.6 multiply_reduce_fusion.3
  254.7 3.1 fusion.70
  258.1 1.8 fusion.72
  260.0 3.6 multiply_reduce_fusion.3
  263.6 3.1 fusion.70
  267.0 1.8 fusion.72
  268.9 3.6 multiply_reduce_fusion.3
  272.5 3.1 fusion.70
  277.8 3.6 multiply_reduce_fusion.3
  281.4 3.1 fusion.70
  286.7 3.6 multiply_reduce_fusion.3
  290.4 3.1 fusion.70
  293.8 1.8 fusion.72
  295.7 3.6 multiply_reduce_fusion.3
  299.3 3.1 fusion.70
  302.7 1.8 fusion.72
  304.6 3.6 multiply_reduce_fusion.3
  308.2 3.1 fusion.70
  313.5 3.6 multiply_reduce_fusion.3
  317.1 3.1 fusion.70
  322.4 3.6 multiply_reduce_fusion.3
  326.0 3.1 fusion.70
  329.5 1.8 fusion.72
  331.3 3.6 multiply_reduce_fusion.3
  334.9 3.1 fusion.70
  338.4 1.8 fusion.72
  340.3 3.6 multiply_reduce_fusion.3
  343.9 3.1 fusion.70
  349.2 3.6 multiply_reduce_fusion.3
  352.8 3.1 fusion.70
  358.1 3.6 multiply_reduce_fusion.3
  361.7 3.1 fusion.70
  365.1 1.8 fusion.72
  367.0 3.6 multiply_reduce_fusion.3
  370.6 3.1 fusion.70
  375.9 3.6 multiply_reduce_fusion.3
  379.5 3.1 fusion.70
  387.2 3.3 all-to-all-start.2
  392.2 3.0 all-to-all-done.2
  396.0 2.2 fusion.20
  398.6 22.3 %reduce-scatter.2.cloned.1.call-done = bf16[64,1024]{1,0:T(8,128)(2,1)} async-done(((bf16[256,1024]{1,0:T(8,128)(2,1)}), bf16[64,1024]{1,0:T(8,128)(2,1)}) %reduce-scatter.2.cloned.1.call-update) | async-done | bytes 131088 | tf_op jit(solution)/shard_map/reduce_scatter | solution.py:176
  422.5 6.7 %all_to_all.41 = bf16[4,32,768]{2,1,0:T(8,128)(2,1)S(1)} all-to-all(bf16[4,32,768]{2,1,0:T(8,128)(2,1)S(1)} %bitcast.92), channel_id=1, replica_groups=mesh['sa'=16,'sb'=4,'head'=4] {'head'}, dimensions={0} | all-to-all | bytes 393216 | tf_op jit(solution)/shard_map/all_to_all | solution.py:197
  (179 shorter events, 44.3 us)
Async XLA Ops:
  7.2 414.7 %copy-start = (bf16[1024,768]{1,0:T(8,128)(2,1)S(1)}, bf16[1024,768]{1,0:T(8,128)(2,1)}, u32[]{:S(2)}) copy-start(bf16[1024,768]{1,0:T(8,128)(2,1)} %param.24) | copy-start | bytes 4718596
  30.5 10.9 %copy-start.6 = (f32[8,256]{1,0:T(8,128)S(1)}, f32[8,256]{1,0:T(8,128)}, u32[]{:S(2)}) copy-start(f32[8,256]{1,0:T(8,128)} %param.21) | copy-start | bytes 24580
  30.5 11.7 %copy-start.3 = (bf16[256,512]{1,0:T(8,128)(2,1)S(1)}, bf16[256,512]{1,0:T(8,128)(2,1)}, u32[]{:S(2)}) copy-start(bf16[256,512]{1,0:T(8,128)(2,1)} %param.18) | copy-start | bytes 786436
  30.5 12.2 %copy-start.4 = (bf16[256,128]{1,0:T(8,128)(2,1)S(1)}, bf16[256,128]{1,0:T(8,128)(2,1)}, u32[]{:S(2)}) copy-start(bf16[256,128]{1,0:T(8,128)(2,1)} %param.19) | copy-start | bytes 196612
  30.5 166.4 %copy-start.5 = (bf16[256,128]{1,0:T(8,128)(2,1)S(1)}, bf16[256,128]{1,0:T(8,128)(2,1)}, u32[]{:S(2)}) copy-start(bf16[256,128]{1,0:T(8,128)(2,1)} %param.20) | copy-start | bytes 196612
  30.5 197.1 %all-to-all-start.1 = ((bf16[16,2,1024,64]{2,3,1,0:T(8,128)(2,1)}), bf16[16,2,1024,64]{2,3,1,0:T(8,128)(2,1)}, u32[]{:S(2)}, u32[]{:S(2)}) async-start(bf16[16,2,1024,64]{2,3,1,0:T(8,128)(2,1)} %broadcast_in_dim.34), calls=%async_computation.1 | async-start | bytes 8388608 | tf_op jit(solution)/shard_map/all_to_all | solution.py:151
  42.9 94.6 %collective-permute-start.6 = (f32[8,128,64]{1,2,0:T(8,128)S(1)}, f32[8,128,64]{1,2,0:T(8,128)S(1)}, u32[]{:S(2)}, u32[]{:S(2)}) collective-permute-start(f32[8,128,64]{1,2,0:T(8,128)S(1)} %convolution_bitcast_fusion.2), channel_id=1, source_target_pairs={{0,4},{4,8},{8,12},{12,16},{16,20},{20,24},{24,28},{28,32},{32,36}... | collective-permute-start | bytes 786440 | tf_op jit(solution)/shard_map/ppermute | solution.py:52
  137.5 7.9 %collective-permute-start.7 = (f32[8,128,64]{1,2,0:T(8,128)S(1)}, f32[8,128,64]{1,2,0:T(8,128)S(1)}, u32[]{:S(2)}, u32[]{:S(2)}) collective-permute-start(f32[8,128,64]{1,2,0:T(8,128)S(1)} %broadcast_select_fusion.2), channel_id=1, source_target_pairs={{0,4},{4,8},{8,12},{12,16},{16,20},{20,24},{24,28},{28,32},{32,36}... | collective-permute-start | bytes 786440 | tf_op jit(solution)/shard_map/ppermute | solution.py:52
  141.7 3.6 collective-permute-start
  145.5 9.4 %collective-permute-start.8 = (f32[8,128,64]{1,2,0:T(8,128)S(1)}, f32[8,128,64]{1,2,0:T(8,128)S(1)}, u32[]{:S(2)}, u32[]{:S(2)}) collective-permute-start(f32[8,128,64]{1,2,0:T(8,128)S(1)} %add_select_fusion.5), channel_id=1, source_target_pairs={{0,8},{4,12},{8,16},{12,20},{16,24},{20,28},{24,32},{28,36},{32,40... | collective-permute-start | bytes 786440 | tf_op jit(solution)/shard_map/ppermute | solution.py:52
  151.3 3.5 collective-permute-start.1
  154.9 24.5 %collective-permute-start.9 = (f32[8,128,64]{1,2,0:T(8,128)S(1)}, f32[8,128,64]{1,2,0:T(8,128)S(1)}, u32[]{:S(2)}, u32[]{:S(2)}) collective-permute-start(f32[8,128,64]{1,2,0:T(8,128)S(1)} %add_select_fusion.4), channel_id=1, source_target_pairs={{0,16},{4,20},{8,24},{12,28},{16,32},{20,36},{24,40},{28,44},{32,4... | collective-permute-start | bytes 786440 | tf_op jit(solution)/shard_map/ppermute | solution.py:52
  168.5 10.9 %collective-permute-start.2 = (f32[8]{0:T(128)S(1)}, f32[8]{0:T(128)S(1)}, u32[]{:S(2)}, u32[]{:S(2)}) collective-permute-start(f32[8]{0:T(128)S(1)} %broadcast_select_fusion.3), channel_id=1, source_target_pairs={{0,8},{4,12},{8,16},{12,20},{16,24},{20,28},{24,32},{28,36},{32,40... | collective-permute-start | bytes 104 | tf_op jit(solution)/shard_map/ppermute | solution.py:52
  179.5 22.5 %collective-permute-start.10 = (f32[8,128,64]{1,2,0:T(8,128)S(1)}, f32[8,128,64]{1,2,0:T(8,128)S(1)}, u32[]{:S(2)}, u32[]{:S(2)}) collective-permute-start(f32[8,128,64]{1,2,0:T(8,128)S(1)} %add_select_fusion.3), channel_id=1, source_target_pairs={{0,32},{4,36},{8,40},{12,44},{16,48},{20,52},{24,56},{28,60},{32,6... | collective-permute-start | bytes 786440 | tf_op jit(solution)/shard_map/ppermute | solution.py:52
  197.1 2.0 collective-permute-start.3
  202.1 15.8 %collective-permute-start.11 = (f32[8,128,64]{1,2,0:T(8,128)S(1)}, f32[8,128,64]{1,2,0:T(8,128)S(1)}, u32[]{:S(2)}, u32[]{:S(2)}) collective-permute-start(f32[8,128,64]{1,2,0:T(8,128)S(1)} %add_select_fusion.2), channel_id=1, source_target_pairs={{0,64},{4,68},{8,72},{12,76},{16,80},{20,84},{24,88},{28,92},{32,9... | collective-permute-start | bytes 786440 | tf_op jit(solution)/shard_map/ppermute | solution.py:52
  212.3 5.6 %collective-permute-start.4 = (f32[8]{0:T(128)S(1)}, f32[8]{0:T(128)S(1)}, u32[]{:S(2)}, u32[]{:S(2)}) collective-permute-start(f32[8]{0:T(128)S(1)} %broadcast_select_fusion.6), channel_id=1, source_target_pairs={{0,32},{4,36},{8,40},{12,44},{16,48},{20,52},{24,56},{28,60},{32,6... | collective-permute-start | bytes 104 | tf_op jit(solution)/shard_map/ppermute | solution.py:52
  218.0 8.2 %collective-permute-start.12 = (f32[8,128,64]{1,2,0:T(8,128)S(1)}, f32[8,128,64]{1,2,0:T(8,128)}, u32[]{:S(2)}, u32[]{:S(2)}) collective-permute-start(f32[8,128,64]{1,2,0:T(8,128)S(1)} %add_select_fusion.1), channel_id=1, source_target_pairs={{0,128},{4,132},{8,136},{12,140},{16,144},{20,148},{24,152},{28,15... | collective-permute-start | bytes 786440 | tf_op jit(solution)/shard_map/ppermute | solution.py:52
  224.0 2.0 collective-permute-start.5
  245.8 3.4 copy-start.1
  254.7 3.4 copy-start.1
  263.6 3.4 copy-start.1
  272.5 3.4 copy-start.1
  281.4 3.4 copy-start.1
  290.3 3.4 copy-start.1
  299.3 3.4 copy-start.1
  308.2 3.4 copy-start.1
  317.1 3.4 copy-start.1
  326.0 3.4 copy-start.1
  334.9 3.4 copy-start.1
  343.8 3.4 copy-start.1
  352.8 3.4 copy-start.1
  361.7 3.4 copy-start.1
  370.6 3.4 copy-start.1
  379.5 3.4 copy-start.1
  384.9 13.3 %copy-start.7 = (s32[256]{0:T(256)S(1)}, s32[256]{0:T(256)}, u32[]{:S(2)}) copy-start(s32[256]{0:T(256)} %param.25) | copy-start | bytes 3076
  387.2 8.1 %all-to-all-start.2 = ((bf16[4,2,8192]{2,1,0:T(2,128)(2,1)}), bf16[4,2,8192]{2,1,0:T(2,128)(2,1)S(1)}, u32[]{:S(2)}, u32[]{:S(2)}) async-start(bf16[4,2,8192]{2,1,0:T(2,128)(2,1)} %reshape.158), calls=%async_computation.2 | async-start | bytes 262144 | tf_op jit(solution)/shard_map/all_to_all | solution.py:161
  390.5 30.3 %reduce-scatter.2.cloned.1.call-start = ((), (), s32[]{:S(2)}) async-start(), calls=%async_computation.5 | async-start | bytes 655360 | tf_op jit(solution)/shard_map/reduce_scatter | solution.py:176
  421.8 8.0 %copy-start.2 = (bf16[64,1024]{1,0:T(8,128)(2,1)}, bf16[64,1024]{1,0:T(8,128)(2,1)S(1)}, u32[]{:S(2)}) copy-start(bf16[64,1024]{1,0:T(8,128)(2,1)S(1)} %add_convert_fusion) | copy-start | bytes 393220
Sparse Core Ops, SparseCore 0:
  398.3 22.5 reduce-scatter.1

commit v4 on v2

--- a/solution.py
+++ b/solution.py
@@ -75,8 +75,8 @@
         jnp.zeros((head_count, row_count), jnp.float32),
         jnp.zeros((head_count, row_count, head_width), jnp.float32),
     )
-    key_piece = lax.all_gather(key_rows, "sa", axis=0, tiled=True)
-    value_piece = lax.all_gather(values, "sa", axis=0, tiled=True)
+    key_piece = key_rows
+    value_piece = values
     piece_rows = key_piece.shape[0]
     block_rows = math.gcd(piece_rows, 1024)
 
@@ -147,8 +147,10 @@
         return lax.all_to_all(split, "sb", split_axis=1, concat_axis=0, tiled=True)
 
     query_heads = spread(queries)
-    group_keys = spread(key_rows).reshape(-1, HDIM)
-    group_values = spread(values).reshape(-1, HDIM)
+    pair = jnp.stack([spread(key_rows), spread(values)]).reshape(2, -1, HDIM)
+    gathered = lax.all_gather(pair, "sa", axis=1, tiled=True)
+    group_keys = gathered[0]
+    group_values = gathered[1]
     attended_one = fold_keys(query_heads, group_keys, group_values)
     attended = lax.all_to_all(
         attended_one.reshape(-1, 1, HDIM), "sb", split_axis=0, concat_axis=1, tiled=True

time: 331 us -> 279 us (0.84)
  waiting for transfers between devices: 123 us -> 65.2 us
  starting transfers between devices: 84.2 us -> 101 us
  blocking collectives: 17.7 us -> 6.71 us
  local copies, waits for them, and re-layouts: 9.19 us -> 12.8 us
    all_gather x2 -> x1, waiting for transfers between devices: 84.6 us -> 25.7 us  [per_device(): gathered = lax.all_gather(pair, 'sa', axis=1, tiled=True)]
    all_to_all x2 -> x3, starting transfers between devices: 7.99 us -> 20.8 us  [spread(): return lax.all_to_all(split, 'sb', split_axis=1, concat_axis=0, tiled=True)]
    all_to_all x1 -> x0, blocking collectives: 11 us -> none  [spread(): return lax.all_to_all(split, 'sb', split_axis=1, concat_axis=0, tiled=True)]
    all_to_all x2 -> x3, waiting for transfers between devices: 0.01 us -> 7.69 us  [spread(): return lax.all_to_all(split, 'sb', split_axis=1, concat_axis=0, tiled=True)]
    ppermute x13, waiting for transfers between devices: 13.8 us -> 8.84 us  [shifted(): return jax.tree.map(lambda part: lax.ppermute(part, axis, pairs), tree)]
    ppermute x13, starting transfers between devices: 72 us -> 76.6 us  [shifted(): return jax.tree.map(lambda part: lax.ppermute(part, axis, pairs), tree)]
    squeeze x0 -> x1, local copies, waits for them, and re-layouts: none -> 4.55 us  [per_device(): group_values = gathered[1]]
    unnamed x28 -> x24, local copies, waits for them, and re-layouts: 7.58 us -> 6.47 us
  transfers between devices with their start and end apart: 19 -> 19, of which waited for: 10 -> 12; matrix products, arithmetic and copies ran while one was open for 4% -> 3% of each run, Pallas kernels for 0% -> 0%
where the time goes in v4:
time: 279 us; the launch traced here: 278 us
  starting transfers between devices  101 us (36%)
  waiting for transfers between devices  65.2 us (23%)
  matrix products  61 us (22%)
  other arithmetic  16.1 us (6%)
  between operations  14.5 us (5%)
  local copies, waits for them, and re-layouts  12.8 us (5%)
  blocking collectives  6.71 us (2%)
    ppermute x13, starting transfers between devices, shifted(): return jax.tree.map(lambda part: lax.ppermute(part, axis, pairs), tree)  76.6 us
    dot_general x16, matrix products, one_step(): jnp.einsum('hqk,khd->hqd', raised.astype(jnp.bfloat16), value_block, pref...  28.6 us
    dot_general x16, matrix products, one_step(): jnp.einsum('qhd,khd->hqk', query_heads, key_block, preferred_element_type...  26.3 us
    all_gather x1, waiting for transfers between devices, per_device(): gathered = lax.all_gather(pair, 'sa', axis=1, tiled=True)  25.7 us
    all_to_all x3, starting transfers between devices, spread(): return lax.all_to_all(split, 'sb', split_axis=1, concat_axis=0, tiled=True)  20.8 us
    reduce_scatter x1, waiting for transfers between devices, per_device(): lax.psum_scatter((jnp.dot(attended, attn_project, preferred_element_type=...  19.9 us
    reduce_sum x16, other arithmetic, one_step(): run_sum = run_sum * shrink + jnp.sum(raised, axis=2)  11.7 us
    ppermute x13, waiting for transfers between devices, shifted(): return jax.tree.map(lambda part: lax.ppermute(part, axis, pairs), tree)  8.84 us
  transfers between devices with their start and end apart: 19, of which 12 were waited for; matrix products, arithmetic and copies ran while one was open for 3% of the time, Pallas kernels for 0%

profile of v4, /device:TPU:1, one launch (start us, length us, event | category | flops | bytes accessed | tf_op | source)
XLA Modules:
  0.0 277.9 jit_solution(17351323056841911900)
XLA Ops:
  7.2 1.8 copy.50
  9.0 6.4 %all-to-all-start = ((bf16[256,4,64]{0,2,1:T(8,128)(2,1)}), bf16[256,4,64]{0,2,1:T(8,128)(2,1)S(1)}, u32[]{:S(2)}, u32[]{:S(2)}) async-start(bf16[256,4,64]{0,2,1:T(8,128)(2,1)} %bitcast), calls=%async_computation | async-start | bytes 262144 | tf_op jit(solution)/shard_map/all_to_all | solution.py:147
  15.4 1.7 copy.52
  17.1 3.1 %all-to-all-done = bf16[256,4,64]{0,2,1:T(8,128)(2,1)S(1)} async-done(((bf16[256,4,64]{0,2,1:T(8,128)(2,1)}), bf16[256,4,64]{0,2,1:T(8,128)(2,1)S(1)}, u32[]{:S(2)}, u32[]{:S(2)}) %all-to-all-start) | async-done | bytes 131104 | tf_op jit(solution)/shard_map/all_to_all | solution.py:147
  20.2 3.5 %all-to-all-start.1 = ((bf16[256,4,64]{0,2,1:T(8,128)(2,1)}), bf16[256,4,64]{0,2,1:T(8,128)(2,1)S(1)}, u32[]{:S(2)}, u32[]{:S(2)}) async-start(bf16[256,4,64]{0,2,1:T(8,128)(2,1)} %bitcast.3), calls=%async_computation.1 | async-start | bytes 262144 | tf_op jit(solution)/shard_map/all_to_all | solution.py:147
  23.9 4.6 %all-to-all-done.1 = bf16[256,4,64]{0,2,1:T(8,128)(2,1)S(1)} async-done(((bf16[256,4,64]{0,2,1:T(8,128)(2,1)}), bf16[256,4,64]{0,2,1:T(8,128)(2,1)S(1)}, u32[]{:S(2)}, u32[]{:S(2)}) %all-to-all-start.1) | async-done | bytes 131104 | tf_op jit(solution)/shard_map/all_to_all | solution.py:147
  31.0 2.9 %collective-permute-start.6 = (f32[8,128,64]{1,2,0:T(8,128)S(1)}, f32[8,128,64]{1,2,0:T(8,128)S(1)}, u32[]{:S(2)}, u32[]{:S(2)}) collective-permute-start(f32[8,128,64]{1,2,0:T(8,128)S(1)} %convolution_bitcast_fusion.2), channel_id=1, source_target_pairs={{0,4},{4,8},{8,12},{12,16},{16,20},{20,24},{24,28},{28,32},{32,36}... | collective-permute-start | bytes 786440 | tf_op jit(solution)/shard_map/ppermute | solution.py:52
  33.9 3.3 %collective-permute-done.6 = f32[8,128,64]{1,2,0:T(8,128)S(1)} collective-permute-done((f32[8,128,64]{1,2,0:T(8,128)S(1)}, f32[8,128,64]{1,2,0:T(8,128)S(1)}, u32[]{:S(2)}, u32[]{:S(2)}) %collective-permute-start.6) | collective-permute-done | bytes 262176 | tf_op jit(solution)/shard_map/ppermute | solution.py:52
  37.2 3.8 %collective-permute-start.7 = (f32[8,128,64]{1,2,0:T(8,128)S(1)}, f32[8,128,64]{1,2,0:T(8,128)S(1)}, u32[]{:S(2)}, u32[]{:S(2)}) collective-permute-start(f32[8,128,64]{1,2,0:T(8,128)S(1)} %broadcast_select_fusion.2), channel_id=1, source_target_pairs={{0,4},{4,8},{8,12},{12,16},{16,20},{20,24},{24,28},{28,32},{32,36}... | collective-permute-start | bytes 786440 | tf_op jit(solution)/shard_map/ppermute | solution.py:52
  41.0 1.9 collective-permute-start
  42.9 1.4 collective-permute-done
  44.4 6.7 %collective-permute-start.8 = (f32[8,128,64]{1,2,0:T(8,128)S(1)}, f32[8,128,64]{1,2,0:T(8,128)S(1)}, u32[]{:S(2)}, u32[]{:S(2)}) collective-permute-start(f32[8,128,64]{1,2,0:T(8,128)S(1)} %add_select_fusion.5), channel_id=1, source_target_pairs={{0,8},{4,12},{8,16},{12,20},{16,24},{20,28},{24,32},{28,36},{32,40... | collective-permute-start | bytes 786440 | tf_op jit(solution)/shard_map/ppermute | solution.py:52
  51.1 3.9 %collective-permute-start.1 = (f32[8]{0:T(128)S(1)}, f32[8]{0:T(128)S(1)}, u32[]{:S(2)}, u32[]{:S(2)}) collective-permute-start(f32[8]{0:T(128)S(1)} %broadcast_select_fusion.4), channel_id=1, source_target_pairs={{0,4},{4,8},{8,12},{12,16},{16,20},{20,24},{24,28},{28,32},{32,36}... | collective-permute-start | bytes 104 | tf_op jit(solution)/shard_map/ppermute | solution.py:52
  55.9 11.1 %collective-permute-start.9 = (f32[8,128,64]{1,2,0:T(8,128)S(1)}, f32[8,128,64]{1,2,0:T(8,128)S(1)}, u32[]{:S(2)}, u32[]{:S(2)}) collective-permute-start(f32[8,128,64]{1,2,0:T(8,128)S(1)} %add_select_fusion.4), channel_id=1, source_target_pairs={{0,16},{4,20},{8,24},{12,28},{16,32},{20,36},{24,40},{28,44},{32,4... | collective-permute-start | bytes 786440 | tf_op jit(solution)/shard_map/ppermute | solution.py:52
  67.7 10.8 %all-to-all-start.2 = ((bf16[256,4,64]{0,2,1:T(8,128)(2,1)}), bf16[256,4,64]{0,2,1:T(8,128)(2,1)S(1)}, u32[]{:S(2)}, u32[]{:S(2)}) async-start(bf16[256,4,64]{0,2,1:T(8,128)(2,1)} %bitcast.7), calls=%async_computation.2 | async-start | bytes 262144 | tf_op jit(solution)/shard_map/all_to_all | solution.py:147
  78.6 4.3 %collective-permute-start.2 = (f32[8]{0:T(128)S(1)}, f32[8]{0:T(128)S(1)}, u32[]{:S(2)}, u32[]{:S(2)}) collective-permute-start(f32[8]{0:T(128)S(1)} %broadcast_select_fusion.3), channel_id=1, source_target_pairs={{0,8},{4,12},{8,16},{12,20},{16,24},{20,28},{24,32},{28,36},{32,40... | collective-permute-start | bytes 104 | tf_op jit(solution)/shard_map/ppermute | solution.py:52
  83.7 15.9 %collective-permute-start.10 = (f32[8,128,64]{1,2,0:T(8,128)S(1)}, f32[8,128,64]{1,2,0:T(8,128)S(1)}, u32[]{:S(2)}, u32[]{:S(2)}) collective-permute-start(f32[8,128,64]{1,2,0:T(8,128)S(1)} %add_select_fusion.3), channel_id=1, source_target_pairs={{0,32},{4,36},{8,40},{12,44},{16,48},{20,52},{24,56},{28,60},{32,6... | collective-permute-start | bytes 786440 | tf_op jit(solution)/shard_map/ppermute | solution.py:52
  99.7 3.8 %collective-permute-start.3 = (f32[8]{0:T(128)S(1)}, f32[8]{0:T(128)S(1)}, u32[]{:S(2)}, u32[]{:S(2)}) collective-permute-start(f32[8]{0:T(128)S(1)} %broadcast_select_fusion.5), channel_id=1, source_target_pairs={{0,16},{4,20},{8,24},{12,28},{16,32},{20,36},{24,40},{28,44},{32,4... | collective-permute-start | bytes 104 | tf_op jit(solution)/shard_map/ppermute | solution.py:52
  104.4 9.7 %collective-permute-start.11 = (f32[8,128,64]{1,2,0:T(8,128)S(1)}, f32[8,128,64]{1,2,0:T(8,128)S(1)}, u32[]{:S(2)}, u32[]{:S(2)}) collective-permute-start(f32[8,128,64]{1,2,0:T(8,128)S(1)} %add_select_fusion.2), channel_id=1, source_target_pairs={{0,64},{4,68},{8,72},{12,76},{16,80},{20,84},{24,88},{28,92},{32,9... | collective-permute-start | bytes 786440 | tf_op jit(solution)/shard_map/ppermute | solution.py:52
  114.1 4.8 %collective-permute-start.4 = (f32[8]{0:T(128)S(1)}, f32[8]{0:T(128)S(1)}, u32[]{:S(2)}, u32[]{:S(2)}) collective-permute-start(f32[8]{0:T(128)S(1)} %broadcast_select_fusion.6), channel_id=1, source_target_pairs={{0,32},{4,36},{8,40},{12,44},{16,48},{20,52},{24,56},{28,60},{32,6... | collective-permute-start | bytes 104 | tf_op jit(solution)/shard_map/ppermute | solution.py:52
  119.7 6.6 %collective-permute-start.12 = (f32[8,128,64]{1,2,0:T(8,128)S(1)}, f32[8,128,64]{1,2,0:T(8,128)S(1)}, u32[]{:S(2)}, u32[]{:S(2)}) collective-permute-start(f32[8,128,64]{1,2,0:T(8,128)S(1)} %add_select_fusion.1), channel_id=1, source_target_pairs={{0,128},{4,132},{8,136},{12,140},{16,144},{20,148},{24,152},{28,15... | collective-permute-start | bytes 786440 | tf_op jit(solution)/shard_map/ppermute | solution.py:52
  127.0 1.3 collective-permute-start.5
  128.3 1.3 collective-permute-done.5
  130.1 25.7 %all-gather.3.cloned.1.call-done = bf16[2,16384,1,64]{1,3,2,0:T(8,128)(2,1)} async-done(((bf16[2,1024,1,64]{1,3,2,0:T(8,128)(2,1)}), bf16[2,16384,1,64]{1,3,2,0:T(8,128)(2,1)}) %all-gather.3.cloned.1.call-update) | async-done | bytes 4194320 | tf_op jit(solution)/shard_map/all_gather | solution.py:151
  155.8 4.6 %slice_bitcast_fusion = (bf16[16384,64]{0,1:T(8,128)(2,1)}, bf16[16384,64]{0,1:T(8,128)(2,1)}) fusion(bf16[2,16384,1,64]{1,3,2,0:T(8,128)(2,1)} %all-gather.3.cloned.1.call-done), kind=kLoop, calls=%fused_computation.21 | loop fusion | bytes 8388608 | tf_op jit(solution)/shard_map/squeeze | solution.py:153
  160.3 68.0 %while.18 = (s32[]{:T(128)}, f32[1,1024]{1,0:T(1,128)S(1)}, f32[1,1024]{1,0:T(1,128)S(1)}, f32[1,1024,64]{1,2,0:T(8,128)S(1)}, bf16[16384,64]{0,1:T(8,128)(2,1)}...) while((s32[]{:T(128)}, f32[1,1024]{1,0:T(1,128)S(1)}, ...), condition=%wide.region_3.0_spmd.clone, body=%wide.region_0.0_spmd.clone.sunk | while | flops 277025792 | bytes 13566135 | solution.py:107
  160.3 1.6 multiply_reduce_fusion.3
  162.7 1.8 fusion.71
  164.6 1.6 multiply_reduce_fusion.3
  167.0 1.8 fusion.71
  168.8 1.6 multiply_reduce_fusion.3
  171.2 1.8 fusion.71
  173.1 1.6 multiply_reduce_fusion.3
  175.5 1.8 fusion.71
  177.3 1.6 multiply_reduce_fusion.3
  179.7 1.8 fusion.71
  181.6 1.6 multiply_reduce_fusion.3
  184.0 1.8 fusion.71
  185.8 1.6 multiply_reduce_fusion.3
  188.2 1.8 fusion.71
  190.1 1.6 multiply_reduce_fusion.3
  192.5 1.8 fusion.71
  194.3 1.6 multiply_reduce_fusion.3
  196.7 1.8 fusion.71
  198.6 1.6 multiply_reduce_fusion.3
  201.0 1.8 fusion.71
  202.8 1.6 multiply_reduce_fusion.3
  205.3 1.8 fusion.71
  207.1 1.6 multiply_reduce_fusion.3
  209.5 1.8 fusion.71
  211.3 1.6 multiply_reduce_fusion.3
  213.8 1.8 fusion.71
  215.6 1.6 multiply_reduce_fusion.3
  218.0 1.8 fusion.71
  219.8 1.6 multiply_reduce_fusion.3
  222.3 1.8 fusion.71
  224.1 1.6 multiply_reduce_fusion.3
  226.5 1.8 fusion.71
  230.6 3.3 %all-to-all-start.3 = ((bf16[4,2,8192]{2,1,0:T(2,128)(2,1)}), bf16[4,2,8192]{2,1,0:T(2,128)(2,1)S(1)}, u32[]{:S(2)}, u32[]{:S(2)}) async-start(bf16[4,2,8192]{2,1,0:T(2,128)(2,1)} %reshape.169), calls=%async_computation.3 | async-start | bytes 262144 | tf_op jit(solution)/shard_map/all_to_all | solution.py:155
  234.0 1.7 fusion.50
  235.7 3.0 %all-to-all-done.3 = bf16[4,2,8192]{2,1,0:T(2,128)(2,1)S(1)} async-done(((bf16[4,2,8192]{2,1,0:T(2,128)(2,1)}), bf16[4,2,8192]{2,1,0:T(2,128)(2,1)S(1)}, u32[]{:S(2)}, u32[]{:S(2)}) %all-to-all-start.3) | async-done | bytes 131104 | tf_op jit(solution)/shard_map/all_to_all | solution.py:155
  239.5 2.2 fusion.20
  242.1 19.9 %reduce-scatter.2.cloned.1.call-done = bf16[64,1024]{1,0:T(8,128)(2,1)} async-done(((bf16[256,1024]{1,0:T(8,128)(2,1)}), bf16[64,1024]{1,0:T(8,128)(2,1)}) %reduce-scatter.2.cloned.1.call-update) | async-done | bytes 131088 | tf_op jit(solution)/shard_map/reduce_scatter | solution.py:170
  263.6 6.7 %all_to_all.68 = bf16[4,32,768]{2,1,0:T(8,128)(2,1)S(1)} all-to-all(bf16[4,32,768]{2,1,0:T(8,128)(2,1)S(1)} %bitcast.99), channel_id=1, replica_groups=mesh['sa'=16,'sb'=4,'head'=4] {'head'}, dimensions={0} | all-to-all | bytes 393216 | tf_op jit(solution)/shard_map/all_to_all | solution.py:191
  (150 shorter events, 26.0 us)
Async XLA Ops:
  7.2 255.8 %copy-start = (bf16[1024,768]{1,0:T(8,128)(2,1)S(1)}, bf16[1024,768]{1,0:T(8,128)(2,1)}, u32[]{:S(2)}) copy-start(bf16[1024,768]{1,0:T(8,128)(2,1)} %param.24) | copy-start | bytes 4718596
  7.2 22.3 %copy-start.6 = (f32[8,256]{1,0:T(8,128)S(1)}, f32[8,256]{1,0:T(8,128)}, u32[]{:S(2)}) copy-start(f32[8,256]{1,0:T(8,128)} %param.21) | copy-start | bytes 24580
  7.2 23.0 %copy-start.2 = (bf16[256,512]{1,0:T(8,128)(2,1)S(1)}, bf16[256,512]{1,0:T(8,128)(2,1)}, u32[]{:S(2)}) copy-start(bf16[256,512]{1,0:T(8,128)(2,1)} %param.18) | copy-start | bytes 786436
  7.2 23.5 %copy-start.3 = (bf16[256,128]{1,0:T(8,128)(2,1)S(1)}, bf16[256,128]{1,0:T(8,128)(2,1)}, u32[]{:S(2)}) copy-start(bf16[256,128]{1,0:T(8,128)(2,1)} %param.19) | copy-start | bytes 196612
  9.0 11.2 %all-to-all-start = ((bf16[256,4,64]{0,2,1:T(8,128)(2,1)}), bf16[256,4,64]{0,2,1:T(8,128)(2,1)S(1)}, u32[]{:S(2)}, u32[]{:S(2)}) async-start(bf16[256,4,64]{0,2,1:T(8,128)(2,1)} %bitcast), calls=%async_computation | async-start | bytes 262144 | tf_op jit(solution)/shard_map/all_to_all | solution.py:147
  20.2 8.3 %all-to-all-start.1 = ((bf16[256,4,64]{0,2,1:T(8,128)(2,1)}), bf16[256,4,64]{0,2,1:T(8,128)(2,1)S(1)}, u32[]{:S(2)}, u32[]{:S(2)}) async-start(bf16[256,4,64]{0,2,1:T(8,128)(2,1)} %bitcast.3), calls=%async_computation.1 | async-start | bytes 262144 | tf_op jit(solution)/shard_map/all_to_all | solution.py:147
  23.7 132.0 %all-gather.3.cloned.1.call-start = ((), (), s32[]{:S(2)}) async-start(), calls=%async_computation.7 | async-start | bytes 4456448 | tf_op jit(solution)/shard_map/all_gather | solution.py:151
  28.7 38.3 %copy-start.5 = (bf16[256,256]{1,0:T(8,128)(2,1)S(1)}, bf16[256,256]{1,0:T(8,128)(2,1)}, u32[]{:S(2)}) copy-start(bf16[256,256]{1,0:T(8,128)(2,1)} %param.15) | copy-start | bytes 393220
  30.4 69.2 %copy-start.4 = (bf16[256,128]{1,0:T(8,128)(2,1)S(1)}, bf16[256,128]{1,0:T(8,128)(2,1)}, u32[]{:S(2)}) copy-start(bf16[256,128]{1,0:T(8,128)(2,1)} %param.20) | copy-start | bytes 196612
  31.0 6.2 %collective-permute-start.6 = (f32[8,128,64]{1,2,0:T(8,128)S(1)}, f32[8,128,64]{1,2,0:T(8,128)S(1)}, u32[]{:S(2)}, u32[]{:S(2)}) collective-permute-start(f32[8,128,64]{1,2,0:T(8,128)S(1)} %convolution_bitcast_fusion.2), channel_id=1, source_target_pairs={{0,4},{4,8},{8,12},{12,16},{16,20},{20,24},{24,28},{28,32},{32,36}... | collective-permute-start | bytes 786440 | tf_op jit(solution)/shard_map/ppermute | solution.py:52
  37.2 7.2 %collective-permute-start.7 = (f32[8,128,64]{1,2,0:T(8,128)S(1)}, f32[8,128,64]{1,2,0:T(8,128)S(1)}, u32[]{:S(2)}, u32[]{:S(2)}) collective-permute-start(f32[8,128,64]{1,2,0:T(8,128)S(1)} %broadcast_select_fusion.2), channel_id=1, source_target_pairs={{0,4},{4,8},{8,12},{12,16},{16,20},{20,24},{24,28},{28,32},{32,36}... | collective-permute-start | bytes 786440 | tf_op jit(solution)/shard_map/ppermute | solution.py:52
  41.0 3.3 %collective-permute-start = (f32[8]{0:T(128)S(1)}, f32[8]{0:T(128)S(1)}, u32[]{:S(2)}, u32[]{:S(2)}) collective-permute-start(f32[8]{0:T(128)S(1)} %exp.29), channel_id=1, source_target_pairs={{0,4},{4,8},{8,12},{12,16},{16,20},{20,24},{24,28},{28,32},{32,36}... | collective-permute-start | bytes 104 | tf_op jit(solution)/shard_map/ppermute | solution.py:52
  44.4 11.3 %collective-permute-start.8 = (f32[8,128,64]{1,2,0:T(8,128)S(1)}, f32[8,128,64]{1,2,0:T(8,128)S(1)}, u32[]{:S(2)}, u32[]{:S(2)}) collective-permute-start(f32[8,128,64]{1,2,0:T(8,128)S(1)} %add_select_fusion.5), channel_id=1, source_target_pairs={{0,8},{4,12},{8,16},{12,20},{16,24},{20,28},{24,32},{28,36},{32,40... | collective-permute-start | bytes 786440 | tf_op jit(solution)/shard_map/ppermute | solution.py:52
  51.1 4.6 %collective-permute-start.1 = (f32[8]{0:T(128)S(1)}, f32[8]{0:T(128)S(1)}, u32[]{:S(2)}, u32[]{:S(2)}) collective-permute-start(f32[8]{0:T(128)S(1)} %broadcast_select_fusion.4), channel_id=1, source_target_pairs={{0,4},{4,8},{8,12},{12,16},{16,20},{20,24},{24,28},{28,32},{32,36}... | collective-permute-start | bytes 104 | tf_op jit(solution)/shard_map/ppermute | solution.py:52
  55.9 27.7 %collective-permute-start.9 = (f32[8,128,64]{1,2,0:T(8,128)S(1)}, f32[8,128,64]{1,2,0:T(8,128)S(1)}, u32[]{:S(2)}, u32[]{:S(2)}) collective-permute-start(f32[8,128,64]{1,2,0:T(8,128)S(1)} %add_select_fusion.4), channel_id=1, source_target_pairs={{0,16},{4,20},{8,24},{12,28},{16,32},{20,36},{24,40},{28,44},{32,4... | collective-permute-start | bytes 786440 | tf_op jit(solution)/shard_map/ppermute | solution.py:52
  67.7 61.9 %all-to-all-start.2 = ((bf16[256,4,64]{0,2,1:T(8,128)(2,1)}), bf16[256,4,64]{0,2,1:T(8,128)(2,1)S(1)}, u32[]{:S(2)}, u32[]{:S(2)}) async-start(bf16[256,4,64]{0,2,1:T(8,128)(2,1)} %bitcast.7), calls=%async_computation.2 | async-start | bytes 262144 | tf_op jit(solution)/shard_map/all_to_all | solution.py:147
  78.6 5.0 %collective-permute-start.2 = (f32[8]{0:T(128)S(1)}, f32[8]{0:T(128)S(1)}, u32[]{:S(2)}, u32[]{:S(2)}) collective-permute-start(f32[8]{0:T(128)S(1)} %broadcast_select_fusion.3), channel_id=1, source_target_pairs={{0,8},{4,12},{8,16},{12,20},{16,24},{20,28},{24,32},{28,36},{32,40... | collective-permute-start | bytes 104 | tf_op jit(solution)/shard_map/ppermute | solution.py:52
  83.7 20.6 %collective-permute-start.10 = (f32[8,128,64]{1,2,0:T(8,128)S(1)}, f32[8,128,64]{1,2,0:T(8,128)S(1)}, u32[]{:S(2)}, u32[]{:S(2)}) collective-permute-start(f32[8,128,64]{1,2,0:T(8,128)S(1)} %add_select_fusion.3), channel_id=1, source_target_pairs={{0,32},{4,36},{8,40},{12,44},{16,48},{20,52},{24,56},{28,60},{32,6... | collective-permute-start | bytes 786440 | tf_op jit(solution)/shard_map/ppermute | solution.py:52
  99.7 4.6 %collective-permute-start.3 = (f32[8]{0:T(128)S(1)}, f32[8]{0:T(128)S(1)}, u32[]{:S(2)}, u32[]{:S(2)}) collective-permute-start(f32[8]{0:T(128)S(1)} %broadcast_select_fusion.5), channel_id=1, source_target_pairs={{0,16},{4,20},{8,24},{12,28},{16,32},{20,36},{24,40},{28,44},{32,4... | collective-permute-start | bytes 104 | tf_op jit(solution)/shard_map/ppermute | solution.py:52
  104.4 15.2 %collective-permute-start.11 = (f32[8,128,64]{1,2,0:T(8,128)S(1)}, f32[8,128,64]{1,2,0:T(8,128)S(1)}, u32[]{:S(2)}, u32[]{:S(2)}) collective-permute-start(f32[8,128,64]{1,2,0:T(8,128)S(1)} %add_select_fusion.2), channel_id=1, source_target_pairs={{0,64},{4,68},{8,72},{12,76},{16,80},{20,84},{24,88},{28,92},{32,9... | collective-permute-start | bytes 786440 | tf_op jit(solution)/shard_map/ppermute | solution.py:52
  114.1 5.5 %collective-permute-start.4 = (f32[8]{0:T(128)S(1)}, f32[8]{0:T(128)S(1)}, u32[]{:S(2)}, u32[]{:S(2)}) collective-permute-start(f32[8]{0:T(128)S(1)} %broadcast_select_fusion.6), channel_id=1, source_target_pairs={{0,32},{4,36},{8,40},{12,44},{16,48},{20,52},{24,56},{28,60},{32,6... | collective-permute-start | bytes 104 | tf_op jit(solution)/shard_map/ppermute | solution.py:52
  119.7 10.0 %collective-permute-start.12 = (f32[8,128,64]{1,2,0:T(8,128)S(1)}, f32[8,128,64]{1,2,0:T(8,128)S(1)}, u32[]{:S(2)}, u32[]{:S(2)}) collective-permute-start(f32[8,128,64]{1,2,0:T(8,128)S(1)} %add_select_fusion.1), channel_id=1, source_target_pairs={{0,128},{4,132},{8,136},{12,140},{16,144},{20,148},{24,152},{28,15... | collective-permute-start | bytes 786440 | tf_op jit(solution)/shard_map/ppermute | solution.py:52
  127.0 2.6 collective-permute-start.5
  230.6 8.1 %all-to-all-start.3 = ((bf16[4,2,8192]{2,1,0:T(2,128)(2,1)}), bf16[4,2,8192]{2,1,0:T(2,128)(2,1)S(1)}, u32[]{:S(2)}, u32[]{:S(2)}) async-start(bf16[4,2,8192]{2,1,0:T(2,128)(2,1)} %reshape.169), calls=%async_computation.3 | async-start | bytes 262144 | tf_op jit(solution)/shard_map/all_to_all | solution.py:155
  234.0 28.0 %reduce-scatter.2.cloned.1.call-start = ((), (), s32[]{:S(2)}) async-start(), calls=%async_computation.6 | async-start | bytes 655360 | tf_op jit(solution)/shard_map/reduce_scatter | solution.py:170
  239.0 2.6 copy-start.7
  263.0 8.0 %copy-start.1 = (bf16[64,1024]{1,0:T(8,128)(2,1)}, bf16[64,1024]{1,0:T(8,128)(2,1)S(1)}, u32[]{:S(2)}) copy-start(bf16[64,1024]{1,0:T(8,128)(2,1)S(1)} %add_convert_fusion) | copy-start | bytes 393220
Sparse Core Ops, SparseCore 0:
  29.6 126.1 all-gather.2
  241.8 20.1 reduce-scatter.1

commit v5 on v4

--- a/solution.py
+++ b/solution.py
@@ -43,7 +43,7 @@
 
 
 def pass_states(local_state, total_decay):
-    axis = ("sa", "sb")
+    axis = ("sb", "sa")
     devices = lax.axis_size(axis)
     mine = lax.axis_index(axis)
 
@@ -195,11 +195,11 @@
 
 def solution(mesh):
     seq_count = mesh.shape["seq"]
-    inner = math.gcd(seq_count, mesh.shape["head"])
+    outer = math.gcd(seq_count, mesh.shape["head"])
     split_mesh = Mesh(
-        mesh.devices.reshape(seq_count // inner, inner, mesh.shape["head"]), ("sa", "sb", "head")
-    )
-    seq = ("sa", "sb")
+        mesh.devices.reshape(outer, seq_count // outer, mesh.shape["head"]), ("sb", "sa", "head")
+    )
+    seq = ("sb", "sa")
     in_specs = (
         P(seq, None),
         P(seq, "head"),
@@ -214,7 +214,7 @@
         P(),
         P(seq),
     )
-    out_specs = (P(("sa", "sb", "head"), None), P(seq, "head", None, None, None))
+    out_specs = (P(("sb", "sa", "head"), None), P(seq, "head", None, None, None))
     return jax.shard_map(
         per_device, mesh=split_mesh, in_specs=in_specs, out_specs=out_specs, check_vma=False
     )

time: 279 us -> 271 us (0.971)
  waiting for transfers between devices: 65.2 us -> 45.7 us
  starting transfers between devices: 101 us -> 112 us
    all_gather x1, waiting for transfers between devices: 25.7 us -> 6.9 us  [per_device(): gathered = lax.all_gather(pair, 'sa', axis=1, tiled=True)]
    all_to_all x1, starting transfers between devices: 3.33 us -> 10.1 us  [per_device(): lax.all_to_all(attended_one.reshape(-1, 1, HDIM), 'sb', split_axis=0, con...]
    ppermute x13, starting transfers between devices: 76.6 us -> 82.8 us  [shifted(): return jax.tree.map(lambda part: lax.ppermute(part, axis, pairs), tree)]
where the time goes in v5:
time: 271 us; the launch traced here: 270 us
  starting transfers between devices  112 us (41%)
  matrix products  61 us (23%)
  waiting for transfers between devices  45.7 us (17%)
  other arithmetic  16.1 us (6%)
  between operations  14.5 us (5%)
  local copies, waits for them, and re-layouts  12.8 us (5%)
  blocking collectives  6.74 us (2%)
    ppermute x13, starting transfers between devices, shifted(): return jax.tree.map(lambda part: lax.ppermute(part, axis, pairs), tree)  82.8 us
    dot_general x16, matrix products, one_step(): jnp.einsum('hqk,khd->hqd', raised.astype(jnp.bfloat16), value_block, pref...  28.6 us
    dot_general x16, matrix products, one_step(): jnp.einsum('qhd,khd->hqk', query_heads, key_block, preferred_element_type...  26.3 us
    reduce_scatter x1, waiting for transfers between devices, per_device(): lax.psum_scatter((jnp.dot(attended, attn_project, preferred_element_type=...  20.4 us
    all_to_all x3, starting transfers between devices, spread(): return lax.all_to_all(split, 'sb', split_axis=1, concat_axis=0, tiled=True)  19.1 us
    reduce_sum x16, other arithmetic, one_step(): run_sum = run_sum * shrink + jnp.sum(raised, axis=2)  11.7 us
    all_to_all x1, starting transfers between devices, per_device(): lax.all_to_all(attended_one.reshape(-1, 1, HDIM), 'sb', split_axis=0, con...  10.1 us
    all_to_all x3, waiting for transfers between devices, spread(): return lax.all_to_all(split, 'sb', split_axis=1, concat_axis=0, tiled=True)  7.72 us
  transfers between devices with their start and end apart: 19, of which 12 were waited for; matrix products, arithmetic and copies ran while one was open for 3% of the time, Pallas kernels for 0%

profile of v5, /device:TPU:1, one launch (start us, length us, event | category | flops | bytes accessed | tf_op | source)
XLA Modules:
  0.0 269.6 jit_solution(17372271821420800139)
XLA Ops:
  7.2 1.8 copy.50
  9.0 4.8 %all-to-all-start = ((bf16[256,4,64]{0,2,1:T(8,128)(2,1)}), bf16[256,4,64]{0,2,1:T(8,128)(2,1)S(1)}, u32[]{:S(2)}, u32[]{:S(2)}) async-start(bf16[256,4,64]{0,2,1:T(8,128)(2,1)} %bitcast), calls=%async_computation | async-start | bytes 262144 | tf_op jit(solution)/shard_map/all_to_all | solution.py:147
  13.8 1.7 copy.52
  15.5 3.2 %all-to-all-done = bf16[256,4,64]{0,2,1:T(8,128)(2,1)S(1)} async-done(((bf16[256,4,64]{0,2,1:T(8,128)(2,1)}), bf16[256,4,64]{0,2,1:T(8,128)(2,1)S(1)}, u32[]{:S(2)}, u32[]{:S(2)}) %all-to-all-start) | async-done | bytes 131104 | tf_op jit(solution)/shard_map/all_to_all | solution.py:147
  18.7 3.3 %all-to-all-start.1 = ((bf16[256,4,64]{0,2,1:T(8,128)(2,1)}), bf16[256,4,64]{0,2,1:T(8,128)(2,1)S(1)}, u32[]{:S(2)}, u32[]{:S(2)}) async-start(bf16[256,4,64]{0,2,1:T(8,128)(2,1)} %bitcast.3), calls=%async_computation.1 | async-start | bytes 262144 | tf_op jit(solution)/shard_map/all_to_all | solution.py:147
  22.2 4.6 %all-to-all-done.1 = bf16[256,4,64]{0,2,1:T(8,128)(2,1)S(1)} async-done(((bf16[256,4,64]{0,2,1:T(8,128)(2,1)}), bf16[256,4,64]{0,2,1:T(8,128)(2,1)S(1)}, u32[]{:S(2)}, u32[]{:S(2)}) %all-to-all-start.1) | async-done | bytes 131104 | tf_op jit(solution)/shard_map/all_to_all | solution.py:147
  29.3 3.6 %collective-permute-start.6 = (f32[8,128,64]{1,2,0:T(8,128)S(1)}, f32[8,128,64]{1,2,0:T(8,128)S(1)}, u32[]{:S(2)}, u32[]{:S(2)}) collective-permute-start(f32[8,128,64]{1,2,0:T(8,128)S(1)} %convolution_bitcast_fusion.2), channel_id=1, source_target_pairs={{0,4},{4,8},{8,12},{12,16},{16,20},{20,24},{24,28},{28,32},{32,36}... | collective-permute-start | bytes 786440 | tf_op jit(solution)/shard_map/ppermute | solution.py:52
  32.8 3.3 %collective-permute-done.6 = f32[8,128,64]{1,2,0:T(8,128)S(1)} collective-permute-done((f32[8,128,64]{1,2,0:T(8,128)S(1)}, f32[8,128,64]{1,2,0:T(8,128)S(1)}, u32[]{:S(2)}, u32[]{:S(2)}) %collective-permute-start.6) | collective-permute-done | bytes 262176 | tf_op jit(solution)/shard_map/ppermute | solution.py:52
  36.1 3.8 %collective-permute-start.7 = (f32[8,128,64]{1,2,0:T(8,128)S(1)}, f32[8,128,64]{1,2,0:T(8,128)S(1)}, u32[]{:S(2)}, u32[]{:S(2)}) collective-permute-start(f32[8,128,64]{1,2,0:T(8,128)S(1)} %broadcast_select_fusion.2), channel_id=1, source_target_pairs={{0,4},{4,8},{8,12},{12,16},{16,20},{20,24},{24,28},{28,32},{32,36}... | collective-permute-start | bytes 786440 | tf_op jit(solution)/shard_map/ppermute | solution.py:52
  40.0 3.5 %collective-permute-start = (f32[8]{0:T(128)S(1)}, f32[8]{0:T(128)S(1)}, u32[]{:S(2)}, u32[]{:S(2)}) collective-permute-start(f32[8]{0:T(128)S(1)} %exp.29), channel_id=1, source_target_pairs={{0,4},{4,8},{8,12},{12,16},{16,20},{20,24},{24,28},{28,32},{32,36}... | collective-permute-start | bytes 104 | tf_op jit(solution)/shard_map/ppermute | solution.py:52
  44.3 7.3 %collective-permute-start.8 = (f32[8,128,64]{1,2,0:T(8,128)S(1)}, f32[8,128,64]{1,2,0:T(8,128)S(1)}, u32[]{:S(2)}, u32[]{:S(2)}) collective-permute-start(f32[8,128,64]{1,2,0:T(8,128)S(1)} %add_select_fusion.5), channel_id=1, source_target_pairs={{0,8},{4,12},{8,16},{12,20},{16,24},{20,28},{24,32},{28,36},{32,40... | collective-permute-start | bytes 786440 | tf_op jit(solution)/shard_map/ppermute | solution.py:52
  51.7 4.0 %collective-permute-start.1 = (f32[8]{0:T(128)S(1)}, f32[8]{0:T(128)S(1)}, u32[]{:S(2)}, u32[]{:S(2)}) collective-permute-start(f32[8]{0:T(128)S(1)} %broadcast_select_fusion.4), channel_id=1, source_target_pairs={{0,4},{4,8},{8,12},{12,16},{16,20},{20,24},{24,28},{28,32},{32,36}... | collective-permute-start | bytes 104 | tf_op jit(solution)/shard_map/ppermute | solution.py:52
  56.5 17.3 %collective-permute-start.9 = (f32[8,128,64]{1,2,0:T(8,128)S(1)}, f32[8,128,64]{1,2,0:T(8,128)S(1)}, u32[]{:S(2)}, u32[]{:S(2)}) collective-permute-start(f32[8,128,64]{1,2,0:T(8,128)S(1)} %add_select_fusion.4), channel_id=1, source_target_pairs={{0,16},{4,20},{8,24},{12,28},{16,32},{20,36},{24,40},{28,44},{32,4... | collective-permute-start | bytes 786440 | tf_op jit(solution)/shard_map/ppermute | solution.py:52
  74.6 10.9 %all-to-all-start.2 = ((bf16[256,4,64]{0,2,1:T(8,128)(2,1)}), bf16[256,4,64]{0,2,1:T(8,128)(2,1)S(1)}, u32[]{:S(2)}, u32[]{:S(2)}) async-start(bf16[256,4,64]{0,2,1:T(8,128)(2,1)} %bitcast.7), calls=%async_computation.2 | async-start | bytes 262144 | tf_op jit(solution)/shard_map/all_to_all | solution.py:147
  85.5 1.3 collective-permute-start.2
  87.6 5.5 %collective-permute-start.10 = (f32[8,128,64]{1,2,0:T(8,128)S(1)}, f32[8,128,64]{1,2,0:T(8,128)S(1)}, u32[]{:S(2)}, u32[]{:S(2)}) collective-permute-start(f32[8,128,64]{1,2,0:T(8,128)S(1)} %add_select_fusion.3), channel_id=1, source_target_pairs={{0,32},{4,36},{8,40},{12,44},{16,48},{20,52},{24,56},{28,60},{32,6... | collective-permute-start | bytes 786440 | tf_op jit(solution)/shard_map/ppermute | solution.py:52
  93.4 10.8 %collective-permute-start.3 = (f32[8]{0:T(128)S(1)}, f32[8]{0:T(128)S(1)}, u32[]{:S(2)}, u32[]{:S(2)}) collective-permute-start(f32[8]{0:T(128)S(1)} %broadcast_select_fusion.5), channel_id=1, source_target_pairs={{0,16},{4,20},{8,24},{12,28},{16,32},{20,36},{24,40},{28,44},{32,4... | collective-permute-start | bytes 104 | tf_op jit(solution)/shard_map/ppermute | solution.py:52
  105.0 9.2 %collective-permute-start.11 = (f32[8,128,64]{1,2,0:T(8,128)S(1)}, f32[8,128,64]{1,2,0:T(8,128)S(1)}, u32[]{:S(2)}, u32[]{:S(2)}) collective-permute-start(f32[8,128,64]{1,2,0:T(8,128)S(1)} %add_select_fusion.2), channel_id=1, source_target_pairs={{0,64},{4,68},{8,72},{12,76},{16,80},{20,84},{24,88},{28,92},{32,9... | collective-permute-start | bytes 786440 | tf_op jit(solution)/shard_map/ppermute | solution.py:52
  114.2 5.1 %collective-permute-start.4 = (f32[8]{0:T(128)S(1)}, f32[8]{0:T(128)S(1)}, u32[]{:S(2)}, u32[]{:S(2)}) collective-permute-start(f32[8]{0:T(128)S(1)} %broadcast_select_fusion.6), channel_id=1, source_target_pairs={{0,32},{4,36},{8,40},{12,44},{16,48},{20,52},{24,56},{28,60},{32,6... | collective-permute-start | bytes 104 | tf_op jit(solution)/shard_map/ppermute | solution.py:52
  120.1 7.1 %collective-permute-start.12 = (f32[8,128,64]{1,2,0:T(8,128)S(1)}, f32[8,128,64]{1,2,0:T(8,128)S(1)}, u32[]{:S(2)}, u32[]{:S(2)}) collective-permute-start(f32[8,128,64]{1,2,0:T(8,128)S(1)} %add_select_fusion.1), channel_id=1, source_target_pairs={{0,128},{4,132},{8,136},{12,140},{16,144},{20,148},{24,152},{28,15... | collective-permute-start | bytes 786440 | tf_op jit(solution)/shard_map/ppermute | solution.py:52
  127.9 4.3 %collective-permute-start.5 = (f32[8]{0:T(128)S(1)}, f32[8]{0:T(128)S(1)}, u32[]{:S(2)}, u32[]{:S(2)}) collective-permute-start(f32[8]{0:T(128)S(1)} %broadcast_select_fusion.7), channel_id=1, source_target_pairs={{0,64},{4,68},{8,72},{12,76},{16,80},{20,84},{24,88},{28,92},{32,9... | collective-permute-start | bytes 104 | tf_op jit(solution)/shard_map/ppermute | solution.py:52
  133.3 6.9 %all-gather.3.cloned.1.call-done = bf16[2,16384,1,64]{1,3,2,0:T(8,128)(2,1)} async-done(((bf16[2,1024,1,64]{1,3,2,0:T(8,128)(2,1)}), bf16[2,16384,1,64]{1,3,2,0:T(8,128)(2,1)}) %all-gather.3.cloned.1.call-update) | async-done | bytes 4194320 | tf_op jit(solution)/shard_map/all_gather | solution.py:151
  140.2 4.6 %slice_bitcast_fusion = (bf16[16384,64]{0,1:T(8,128)(2,1)}, bf16[16384,64]{0,1:T(8,128)(2,1)}) fusion(bf16[2,16384,1,64]{1,3,2,0:T(8,128)(2,1)} %all-gather.3.cloned.1.call-done), kind=kLoop, calls=%fused_computation.21 | loop fusion | bytes 8388608 | tf_op jit(solution)/shard_map/squeeze | solution.py:153
  144.7 68.0 %while.18 = (s32[]{:T(128)}, f32[1,1024]{1,0:T(1,128)S(1)}, f32[1,1024]{1,0:T(1,128)S(1)}, f32[1,1024,64]{1,2,0:T(8,128)S(1)}, bf16[16384,64]{0,1:T(8,128)(2,1)}...) while((s32[]{:T(128)}, f32[1,1024]{1,0:T(1,128)S(1)}, ...), condition=%wide.region_3.0_spmd.clone, body=%wide.region_0.0_spmd.clone.sunk | while | flops 277025792 | bytes 13566135 | solution.py:107
  144.7 1.6 multiply_reduce_fusion.3
  147.1 1.8 fusion.71
  149.0 1.6 multiply_reduce_fusion.3
  151.4 1.8 fusion.71
  153.2 1.6 multiply_reduce_fusion.3
  155.6 1.8 fusion.71
  157.5 1.6 multiply_reduce_fusion.3
  159.9 1.8 fusion.71
  161.7 1.6 multiply_reduce_fusion.3
  164.2 1.8 fusion.71
  166.0 1.6 multiply_reduce_fusion.3
  168.4 1.8 fusion.71
  170.2 1.6 multiply_reduce_fusion.3
  172.7 1.8 fusion.71
  174.5 1.6 multiply_reduce_fusion.3
  176.9 1.8 fusion.71
  178.7 1.6 multiply_reduce_fusion.3
  181.2 1.8 fusion.71
  183.0 1.6 multiply_reduce_fusion.3
  185.4 1.8 fusion.71
  187.2 1.6 multiply_reduce_fusion.3
  189.7 1.8 fusion.71
  191.5 1.6 multiply_reduce_fusion.3
  193.9 1.8 fusion.71
  195.7 1.6 multiply_reduce_fusion.3
  198.2 1.8 fusion.71
  200.0 1.6 multiply_reduce_fusion.3
  202.4 1.8 fusion.71
  204.3 1.6 multiply_reduce_fusion.3
  206.7 1.8 fusion.71
  208.5 1.6 multiply_reduce_fusion.3
  210.9 1.8 fusion.71
  214.1 0.9 reshape.169
  215.1 10.1 %all-to-all-start.3 = ((bf16[4,2,8192]{2,1,0:T(2,128)(2,1)}), bf16[4,2,8192]{2,1,0:T(2,128)(2,1)S(1)}, u32[]{:S(2)}, u32[]{:S(2)}) async-start(bf16[4,2,8192]{2,1,0:T(2,128)(2,1)} %reshape.169), calls=%async_computation.3 | async-start | bytes 262144 | tf_op jit(solution)/shard_map/all_to_all | solution.py:155
  225.1 1.7 fusion.50
  226.8 3.1 %all-to-all-done.3 = bf16[4,2,8192]{2,1,0:T(2,128)(2,1)S(1)} async-done(((bf16[4,2,8192]{2,1,0:T(2,128)(2,1)}), bf16[4,2,8192]{2,1,0:T(2,128)(2,1)S(1)}, u32[]{:S(2)}, u32[]{:S(2)}) %all-to-all-start.3) | async-done | bytes 131104 | tf_op jit(solution)/shard_map/all_to_all | solution.py:155
  230.7 2.2 fusion.20
  233.3 20.4 %reduce-scatter.2.cloned.1.call-done = bf16[64,1024]{1,0:T(8,128)(2,1)} async-done(((bf16[256,1024]{1,0:T(8,128)(2,1)}), bf16[64,1024]{1,0:T(8,128)(2,1)}) %reduce-scatter.2.cloned.1.call-update) | async-done | bytes 131088 | tf_op jit(solution)/shard_map/reduce_scatter | solution.py:170
  253.7 1.0 add_convert_fusion
  255.4 6.7 %all_to_all.68 = bf16[4,32,768]{2,1,0:T(8,128)(2,1)S(1)} all-to-all(bf16[4,32,768]{2,1,0:T(8,128)(2,1)S(1)} %bitcast.99), channel_id=1, replica_groups=mesh['sb'=4,'sa'=16,'head'=4] {'head'}, dimensions={0} | all-to-all | bytes 393216 | tf_op jit(solution)/shard_map/all_to_all | solution.py:191
  (150 shorter events, 25.5 us)
Async XLA Ops:
  7.2 247.6 %copy-start = (bf16[1024,768]{1,0:T(8,128)(2,1)S(1)}, bf16[1024,768]{1,0:T(8,128)(2,1)}, u32[]{:S(2)}) copy-start(bf16[1024,768]{1,0:T(8,128)(2,1)} %param.24) | copy-start | bytes 4718596
  7.2 20.6 %copy-start.6 = (f32[8,256]{1,0:T(8,128)S(1)}, f32[8,256]{1,0:T(8,128)}, u32[]{:S(2)}) copy-start(f32[8,256]{1,0:T(8,128)} %param.21) | copy-start | bytes 24580
  7.2 21.3 %copy-start.2 = (bf16[256,512]{1,0:T(8,128)(2,1)S(1)}, bf16[256,512]{1,0:T(8,128)(2,1)}, u32[]{:S(2)}) copy-start(bf16[256,512]{1,0:T(8,128)(2,1)} %param.18) | copy-start | bytes 786436
  7.2 21.8 %copy-start.3 = (bf16[256,128]{1,0:T(8,128)(2,1)S(1)}, bf16[256,128]{1,0:T(8,128)(2,1)}, u32[]{:S(2)}) copy-start(bf16[256,128]{1,0:T(8,128)(2,1)} %param.19) | copy-start | bytes 196612
  9.0 9.7 %all-to-all-start = ((bf16[256,4,64]{0,2,1:T(8,128)(2,1)}), bf16[256,4,64]{0,2,1:T(8,128)(2,1)S(1)}, u32[]{:S(2)}, u32[]{:S(2)}) async-start(bf16[256,4,64]{0,2,1:T(8,128)(2,1)} %bitcast), calls=%async_computation | async-start | bytes 262144 | tf_op jit(solution)/shard_map/all_to_all | solution.py:147
  18.7 8.1 %all-to-all-start.1 = ((bf16[256,4,64]{0,2,1:T(8,128)(2,1)}), bf16[256,4,64]{0,2,1:T(8,128)(2,1)S(1)}, u32[]{:S(2)}, u32[]{:S(2)}) async-start(bf16[256,4,64]{0,2,1:T(8,128)(2,1)} %bitcast.3), calls=%async_computation.1 | async-start | bytes 262144 | tf_op jit(solution)/shard_map/all_to_all | solution.py:147
  22.0 118.2 %all-gather.3.cloned.1.call-start = ((), (), s32[]{:S(2)}) async-start(), calls=%async_computation.7 | async-start | bytes 4456448 | tf_op jit(solution)/shard_map/all_gather | solution.py:151
  27.0 46.9 %copy-start.5 = (bf16[256,256]{1,0:T(8,128)(2,1)S(1)}, bf16[256,256]{1,0:T(8,128)(2,1)}, u32[]{:S(2)}) copy-start(bf16[256,256]{1,0:T(8,128)(2,1)} %param.15) | copy-start | bytes 393220
  28.7 64.5 %copy-start.4 = (bf16[256,128]{1,0:T(8,128)(2,1)S(1)}, bf16[256,128]{1,0:T(8,128)(2,1)}, u32[]{:S(2)}) copy-start(bf16[256,128]{1,0:T(8,128)(2,1)} %param.20) | copy-start | bytes 196612
  29.3 6.8 %collective-permute-start.6 = (f32[8,128,64]{1,2,0:T(8,128)S(1)}, f32[8,128,64]{1,2,0:T(8,128)S(1)}, u32[]{:S(2)}, u32[]{:S(2)}) collective-permute-start(f32[8,128,64]{1,2,0:T(8,128)S(1)} %convolution_bitcast_fusion.2), channel_id=1, source_target_pairs={{0,4},{4,8},{8,12},{12,16},{16,20},{20,24},{24,28},{28,32},{32,36}... | collective-permute-start | bytes 786440 | tf_op jit(solution)/shard_map/ppermute | solution.py:52
  36.1 8.1 %collective-permute-start.7 = (f32[8,128,64]{1,2,0:T(8,128)S(1)}, f32[8,128,64]{1,2,0:T(8,128)S(1)}, u32[]{:S(2)}, u32[]{:S(2)}) collective-permute-start(f32[8,128,64]{1,2,0:T(8,128)S(1)} %broadcast_select_fusion.2), channel_id=1, source_target_pairs={{0,4},{4,8},{8,12},{12,16},{16,20},{20,24},{24,28},{28,32},{32,36}... | collective-permute-start | bytes 786440 | tf_op jit(solution)/shard_map/ppermute | solution.py:52
  40.0 4.2 %collective-permute-start = (f32[8]{0:T(128)S(1)}, f32[8]{0:T(128)S(1)}, u32[]{:S(2)}, u32[]{:S(2)}) collective-permute-start(f32[8]{0:T(128)S(1)} %exp.29), channel_id=1, source_target_pairs={{0,4},{4,8},{8,12},{12,16},{16,20},{20,24},{24,28},{28,32},{32,36}... | collective-permute-start | bytes 104 | tf_op jit(solution)/shard_map/ppermute | solution.py:52
  44.3 12.1 %collective-permute-start.8 = (f32[8,128,64]{1,2,0:T(8,128)S(1)}, f32[8,128,64]{1,2,0:T(8,128)S(1)}, u32[]{:S(2)}, u32[]{:S(2)}) collective-permute-start(f32[8,128,64]{1,2,0:T(8,128)S(1)} %add_select_fusion.5), channel_id=1, source_target_pairs={{0,8},{4,12},{8,16},{12,20},{16,24},{20,28},{24,32},{28,36},{32,40... | collective-permute-start | bytes 786440 | tf_op jit(solution)/shard_map/ppermute | solution.py:52
  51.7 4.7 %collective-permute-start.1 = (f32[8]{0:T(128)S(1)}, f32[8]{0:T(128)S(1)}, u32[]{:S(2)}, u32[]{:S(2)}) collective-permute-start(f32[8]{0:T(128)S(1)} %broadcast_select_fusion.4), channel_id=1, source_target_pairs={{0,4},{4,8},{8,12},{12,16},{16,20},{20,24},{24,28},{28,32},{32,36}... | collective-permute-start | bytes 104 | tf_op jit(solution)/shard_map/ppermute | solution.py:52
  56.5 31.0 %collective-permute-start.9 = (f32[8,128,64]{1,2,0:T(8,128)S(1)}, f32[8,128,64]{1,2,0:T(8,128)S(1)}, u32[]{:S(2)}, u32[]{:S(2)}) collective-permute-start(f32[8,128,64]{1,2,0:T(8,128)S(1)} %add_select_fusion.4), channel_id=1, source_target_pairs={{0,16},{4,20},{8,24},{12,28},{16,32},{20,36},{24,40},{28,44},{32,4... | collective-permute-start | bytes 786440 | tf_op jit(solution)/shard_map/ppermute | solution.py:52
  74.6 58.2 %all-to-all-start.2 = ((bf16[256,4,64]{0,2,1:T(8,128)(2,1)}), bf16[256,4,64]{0,2,1:T(8,128)(2,1)S(1)}, u32[]{:S(2)}, u32[]{:S(2)}) async-start(bf16[256,4,64]{0,2,1:T(8,128)(2,1)} %bitcast.7), calls=%async_computation.2 | async-start | bytes 262144 | tf_op jit(solution)/shard_map/all_to_all | solution.py:147
  85.5 2.0 collective-permute-start.2
  87.6 17.2 %collective-permute-start.10 = (f32[8,128,64]{1,2,0:T(8,128)S(1)}, f32[8,128,64]{1,2,0:T(8,128)S(1)}, u32[]{:S(2)}, u32[]{:S(2)}) collective-permute-start(f32[8,128,64]{1,2,0:T(8,128)S(1)} %add_select_fusion.3), channel_id=1, source_target_pairs={{0,32},{4,36},{8,40},{12,44},{16,48},{20,52},{24,56},{28,60},{32,6... | collective-permute-start | bytes 786440 | tf_op jit(solution)/shard_map/ppermute | solution.py:52
  93.4 11.5 %collective-permute-start.3 = (f32[8]{0:T(128)S(1)}, f32[8]{0:T(128)S(1)}, u32[]{:S(2)}, u32[]{:S(2)}) collective-permute-start(f32[8]{0:T(128)S(1)} %broadcast_select_fusion.5), channel_id=1, source_target_pairs={{0,16},{4,20},{8,24},{12,28},{16,32},{20,36},{24,40},{28,44},{32,4... | collective-permute-start | bytes 104 | tf_op jit(solution)/shard_map/ppermute | solution.py:52
  105.0 15.0 %collective-permute-start.11 = (f32[8,128,64]{1,2,0:T(8,128)S(1)}, f32[8,128,64]{1,2,0:T(8,128)S(1)}, u32[]{:S(2)}, u32[]{:S(2)}) collective-permute-start(f32[8,128,64]{1,2,0:T(8,128)S(1)} %add_select_fusion.2), channel_id=1, source_target_pairs={{0,64},{4,68},{8,72},{12,76},{16,80},{20,84},{24,88},{28,92},{32,9... | collective-permute-start | bytes 786440 | tf_op jit(solution)/shard_map/ppermute | solution.py:52
  114.2 5.8 %collective-permute-start.4 = (f32[8]{0:T(128)S(1)}, f32[8]{0:T(128)S(1)}, u32[]{:S(2)}, u32[]{:S(2)}) collective-permute-start(f32[8]{0:T(128)S(1)} %broadcast_select_fusion.6), channel_id=1, source_target_pairs={{0,32},{4,36},{8,40},{12,44},{16,48},{20,52},{24,56},{28,60},{32,6... | collective-permute-start | bytes 104 | tf_op jit(solution)/shard_map/ppermute | solution.py:52
  120.1 12.8 %collective-permute-start.12 = (f32[8,128,64]{1,2,0:T(8,128)S(1)}, f32[8,128,64]{1,2,0:T(8,128)S(1)}, u32[]{:S(2)}, u32[]{:S(2)}) collective-permute-start(f32[8,128,64]{1,2,0:T(8,128)S(1)} %add_select_fusion.1), channel_id=1, source_target_pairs={{0,128},{4,132},{8,136},{12,140},{16,144},{20,148},{24,152},{28,15... | collective-permute-start | bytes 786440 | tf_op jit(solution)/shard_map/ppermute | solution.py:52
  127.9 5.0 %collective-permute-start.5 = (f32[8]{0:T(128)S(1)}, f32[8]{0:T(128)S(1)}, u32[]{:S(2)}, u32[]{:S(2)}) collective-permute-start(f32[8]{0:T(128)S(1)} %broadcast_select_fusion.7), channel_id=1, source_target_pairs={{0,64},{4,68},{8,72},{12,76},{16,80},{20,84},{24,88},{28,92},{32,9... | collective-permute-start | bytes 104 | tf_op jit(solution)/shard_map/ppermute | solution.py:52
  215.1 14.9 %all-to-all-start.3 = ((bf16[4,2,8192]{2,1,0:T(2,128)(2,1)}), bf16[4,2,8192]{2,1,0:T(2,128)(2,1)S(1)}, u32[]{:S(2)}, u32[]{:S(2)}) async-start(bf16[4,2,8192]{2,1,0:T(2,128)(2,1)} %reshape.169), calls=%async_computation.3 | async-start | bytes 262144 | tf_op jit(solution)/shard_map/all_to_all | solution.py:155
  225.1 28.6 %reduce-scatter.2.cloned.1.call-start = ((), (), s32[]{:S(2)}) async-start(), calls=%async_computation.6 | async-start | bytes 655360 | tf_op jit(solution)/shard_map/reduce_scatter | solution.py:170
  230.3 2.6 copy-start.7
  254.7 8.0 %copy-start.1 = (bf16[64,1024]{1,0:T(8,128)(2,1)}, bf16[64,1024]{1,0:T(8,128)(2,1)S(1)}, u32[]{:S(2)}) copy-start(bf16[64,1024]{1,0:T(8,128)(2,1)S(1)} %add_convert_fusion) | copy-start | bytes 393220
Sparse Core Ops, SparseCore 0:
  27.9 112.2 all-gather.2
  233.0 20.6 reduce-scatter.1

commit v6 on v5

--- a/solution.py
+++ b/solution.py
@@ -3,6 +3,8 @@
 import jax
 import jax.numpy as jnp
 from jax import lax
+from jax.experimental import pallas as pl
+from jax.experimental.pallas import tpu as pltpu
 from jax.sharding import Mesh, PartitionSpec as P
 
 HDIM = 64
@@ -67,48 +69,55 @@
     return state
 
 
-def fold_keys(query_heads, key_rows, values):
-    row_count, head_count, head_width = query_heads.shape
-    scale = 1.0 / math.sqrt(head_width)
-    initial = (
-        jnp.full((head_count, row_count), -jnp.inf, jnp.float32),
-        jnp.zeros((head_count, row_count), jnp.float32),
-        jnp.zeros((head_count, row_count, head_width), jnp.float32),
-    )
-    key_piece = key_rows
-    value_piece = values
-    piece_rows = key_piece.shape[0]
-    block_rows = math.gcd(piece_rows, 1024)
-
-    def one_step(block_index, carry_state):
-        run_max, run_sum, accumulated = carry_state
-        key_block = lax.dynamic_slice_in_dim(
-            key_piece, block_index * block_rows, block_rows, 0
-        ).reshape(block_rows, head_count, head_width)
-        value_block = lax.dynamic_slice_in_dim(
-            value_piece, block_index * block_rows, block_rows, 0
-        ).reshape(block_rows, head_count, head_width)
-        scores = (
-            jnp.einsum("qhd,khd->hqk", query_heads, key_block, preferred_element_type=jnp.float32)
-            * scale
+def flash_one_head(query_rows, pair, key_block=1024):
+    row_count, width = query_rows.shape
+    key_count = pair.shape[1]
+    steps = key_count // key_block
+    scale = 1.0 / math.sqrt(width)
+
+    def kernel(q_ref, k_ref, v_ref, o_ref, top_ref, sum_ref, acc_ref):
+        step = pl.program_id(0)
+
+        @pl.when(step == 0)
+        def _():
+            top_ref[...] = jnp.full(top_ref.shape, -jnp.inf, jnp.float32)
+            sum_ref[...] = jnp.zeros(sum_ref.shape, jnp.float32)
+            acc_ref[...] = jnp.zeros(acc_ref.shape, jnp.float32)
+
+        scores = lax.dot_general(
+            q_ref[...], k_ref[...], (((1,), (1,)), ((), ())), preferred_element_type=jnp.float32
+        ) * scale
+        old_top = top_ref[...]
+        new_top = jnp.maximum(old_top, jnp.max(scores, axis=1, keepdims=True))
+        shrink = jnp.exp(old_top - new_top)
+        raised = jnp.exp(scores - new_top)
+        sum_ref[...] = sum_ref[...] * shrink + jnp.sum(raised, axis=1, keepdims=True)
+        acc_ref[...] = acc_ref[...] * shrink + jnp.dot(
+            raised.astype(jnp.bfloat16), v_ref[...], preferred_element_type=jnp.float32
         )
-        new_max = jnp.maximum(run_max, jnp.max(scores, axis=2))
-        shrink = jnp.exp(run_max - new_max)
-        raised = jnp.exp(scores - new_max[:, :, None])
-        run_sum = run_sum * shrink + jnp.sum(raised, axis=2)
-        accumulated = accumulated * shrink[:, :, None] + jnp.einsum(
-            "hqk,khd->hqd",
-            raised.astype(jnp.bfloat16),
-            value_block,
-            preferred_element_type=jnp.float32,
-        )
-        return (new_max, run_sum, accumulated)
-
-    run_max, run_sum, accumulated = lax.fori_loop(0, piece_rows // block_rows, one_step, initial)
-    attended = accumulated / run_sum[:, :, None]
-    return (
-        attended.transpose(1, 0, 2).reshape(row_count, head_count * head_width).astype(jnp.bfloat16)
-    )
+        top_ref[...] = new_top
+
+        @pl.when(step == steps - 1)
+        def _():
+            o_ref[...] = (acc_ref[...] / sum_ref[...]).astype(o_ref.dtype)
+
+    return pl.pallas_call(
+        kernel,
+        out_shape=jax.ShapeDtypeStruct((row_count, width), jnp.bfloat16),
+        grid=(steps,),
+        in_specs=[
+            pl.BlockSpec((row_count, width), lambda j: (0, 0)),
+            pl.BlockSpec((None, key_block, width), lambda j: (0, j, 0)),
+            pl.BlockSpec((None, key_block, width), lambda j: (1, j, 0)),
+        ],
+        out_specs=pl.BlockSpec((row_count, width), lambda j: (0, 0)),
+        scratch_shapes=[
+            pltpu.VMEM((row_count, 1), jnp.float32),
+            pltpu.VMEM((row_count, 1), jnp.float32),
+            pltpu.VMEM((row_count, width), jnp.float32),
+        ],
+        compiler_params=pltpu.CompilerParams(dimension_semantics=("arbitrary",)),
+    )(query_rows, pair, pair)
 
 
 def slot_rank(owners_here, owner_count, group_rows):
@@ -149,9 +158,7 @@
     query_heads = spread(queries)
     pair = jnp.stack([spread(key_rows), spread(values)]).reshape(2, -1, HDIM)
     gathered = lax.all_gather(pair, "sa", axis=1, tiled=True)
-    group_keys = gathered[0]
-    group_values = gathered[1]
-    attended_one = fold_keys(query_heads, group_keys, group_values)
+    attended_one = flash_one_head(query_heads.reshape(-1, HDIM), gathered)
     attended = lax.all_to_all(
         attended_one.reshape(-1, 1, HDIM), "sb", split_axis=0, concat_axis=1, tiled=True
     ).reshape(row_count, head_count * HDIM)

time: 271 us -> 282 us (1.041)
  matrix products: 61 us -> 6.05 us
  Pallas kernels: 0 us -> 44.3 us
  waiting for transfers between devices: 45.7 us -> 86.8 us
  other arithmetic: 16.1 us -> 5.18 us
  starting transfers between devices: 112 us -> 108 us
  local copies, waits for them, and re-layouts: 12.8 us -> 8.85 us
    dot_general x32 -> x0, matrix products: 54.9 us -> none  [the longest x16 28.6 us: one_step(): jnp.einsum('hqk,khd->hqd', raised.astype(jnp.bfloat16), value_block, pref...]
    pallas_call x0 -> x1, Pallas kernels: none -> 44.3 us  [flash_one_head(): pl.pallas_call(kernel, out_shape=jax.ShapeDtypeStruct((row_count, width),...]
    all_gather x1, waiting for transfers between devices: 6.9 us -> 46.1 us  [per_device(): gathered = lax.all_gather(pair, 'sa', axis=1, tiled=True)]
    reduce_sum x16 -> x0, other arithmetic: 11.7 us -> none  [one_step(): run_sum = run_sum * shrink + jnp.sum(raised, axis=2)]
    squeeze x1 -> x0, local copies, waits for them, and re-layouts: 4.55 us -> none  [per_device(): group_values = gathered[1]]
    unnamed x24 -> x23, local copies, waits for them, and re-layouts: 6.47 us -> 6.29 us
where the time goes in v6:
time: 282 us; the launch traced here: 281 us
  starting transfers between devices  108 us (38%)
  waiting for transfers between devices  86.8 us (31%)
  Pallas kernels  44.3 us (16%)
  between operations  14.4 us (5%)
  local copies, waits for them, and re-layouts  8.85 us (3%)
  blocking collectives  6.73 us (2%)
  matrix products  6.05 us (2%)
  other arithmetic  5.18 us (2%)
    ppermute x13, starting transfers between devices, shifted(): return jax.tree.map(lambda part: lax.ppermute(part, axis, pairs), tree)  81.2 us
    all_gather x1, waiting for transfers between devices, per_device(): gathered = lax.all_gather(pair, 'sa', axis=1, tiled=True)  46.1 us
    pallas_call x1, Pallas kernels, flash_one_head(): pl.pallas_call(kernel, out_shape=jax.ShapeDtypeStruct((row_count, width),...  44.3 us
    reduce_scatter x1, waiting for transfers between devices, per_device(): lax.psum_scatter((jnp.dot(attended, attn_project, preferred_element_type=...  19.8 us
    all_to_all x3, starting transfers between devices, spread(): return lax.all_to_all(split, 'sb', split_axis=1, concat_axis=0, tiled=True)  19.2 us
    ppermute x13, waiting for transfers between devices, shifted(): return jax.tree.map(lambda part: lax.ppermute(part, axis, pairs), tree)  10.1 us
    all_to_all x1, starting transfers between devices, per_device(): lax.all_to_all(attended_one.reshape(-1, 1, HDIM), 'sb', split_axis=0, con...  8.03 us
    all_to_all x3, waiting for transfers between devices, spread(): return lax.all_to_all(split, 'sb', split_axis=1, concat_axis=0, tiled=True)  7.73 us
  transfers between devices with their start and end apart: 19, of which 12 were waited for; matrix products, arithmetic and copies ran while one was open for 3% of the time, Pallas kernels for 0%

profile of v6, /device:TPU:1, one launch (start us, length us, event | category | flops | bytes accessed | tf_op | source)
XLA Modules:
  0.0 280.8 jit_solution(9972751014775099537)
XLA Ops:
  7.2 1.8 copy.49
  9.0 4.8 %all-to-all-start.1 = ((bf16[256,4,64]{0,2,1:T(8,128)(2,1)}), bf16[256,4,64]{0,2,1:T(8,128)(2,1)S(1)}, u32[]{:S(2)}, u32[]{:S(2)}) async-start(bf16[256,4,64]{0,2,1:T(8,128)(2,1)} %bitcast.4), calls=%async_computation.1 | async-start | bytes 262144 | tf_op jit(solution)/shard_map/all_to_all | solution.py:156
  13.8 1.7 copy.51
  15.5 3.2 %all-to-all-done.1 = bf16[256,4,64]{0,2,1:T(8,128)(2,1)S(1)} async-done(((bf16[256,4,64]{0,2,1:T(8,128)(2,1)}), bf16[256,4,64]{0,2,1:T(8,128)(2,1)S(1)}, u32[]{:S(2)}, u32[]{:S(2)}) %all-to-all-start.1) | async-done | bytes 131104 | tf_op jit(solution)/shard_map/all_to_all | solution.py:156
  18.7 3.3 %all-to-all-start.2 = ((bf16[256,4,64]{0,2,1:T(8,128)(2,1)}), bf16[256,4,64]{0,2,1:T(8,128)(2,1)S(1)}, u32[]{:S(2)}, u32[]{:S(2)}) async-start(bf16[256,4,64]{0,2,1:T(8,128)(2,1)} %bitcast.8), calls=%async_computation.2 | async-start | bytes 262144 | tf_op jit(solution)/shard_map/all_to_all | solution.py:156
  22.0 0.2 copy.50
  22.2 4.6 %all-to-all-done.2 = bf16[256,4,64]{0,2,1:T(8,128)(2,1)S(1)} async-done(((bf16[256,4,64]{0,2,1:T(8,128)(2,1)}), bf16[256,4,64]{0,2,1:T(8,128)(2,1)S(1)}, u32[]{:S(2)}, u32[]{:S(2)}) %all-to-all-start.2) | async-done | bytes 131104 | tf_op jit(solution)/shard_map/all_to_all | solution.py:156
  26.8 0.2 copy.52
  27.0 0.9 pad_maximum_fusion
  27.9 0.6 reduce-window.6
  28.5 0.2 slice_reduce_fusion
  28.7 0.1 copy.56
  29.0 0.2 slice_reduce_fusion.1
  29.1 0.1 exponential_bitcast_fusion.1
  29.2 0.2 convolution_bitcast_fusion.2
  29.5 3.6 %collective-permute-start.6 = (f32[8,128,64]{1,2,0:T(8,128)S(1)}, f32[8,128,64]{1,2,0:T(8,128)S(1)}, u32[]{:S(2)}, u32[]{:S(2)}) collective-permute-start(f32[8,128,64]{1,2,0:T(8,128)S(1)} %convolution_bitcast_fusion.2), channel_id=1, source_target_pairs={{0,4},{4,8},{8,12},{12,16},{16,20},{20,24},{24,28},{28,32},{32,36}... | collective-permute-start | bytes 786440 | tf_op jit(solution)/shard_map/ppermute | solution.py:54
  33.0 3.3 %collective-permute-done.6 = f32[8,128,64]{1,2,0:T(8,128)S(1)} collective-permute-done((f32[8,128,64]{1,2,0:T(8,128)S(1)}, f32[8,128,64]{1,2,0:T(8,128)S(1)}, u32[]{:S(2)}, u32[]{:S(2)}) %collective-permute-start.6) | collective-permute-done | bytes 262176 | tf_op jit(solution)/shard_map/ppermute | solution.py:54
  36.3 3.8 %collective-permute-start.7 = (f32[8,128,64]{1,2,0:T(8,128)S(1)}, f32[8,128,64]{1,2,0:T(8,128)S(1)}, u32[]{:S(2)}, u32[]{:S(2)}) collective-permute-start(f32[8,128,64]{1,2,0:T(8,128)S(1)} %broadcast_select_fusion), channel_id=1, source_target_pairs={{0,4},{4,8},{8,12},{12,16},{16,20},{20,24},{24,28},{28,32},{32,36}... | collective-permute-start | bytes 786440 | tf_op jit(solution)/shard_map/ppermute | solution.py:54
  40.2 3.5 %collective-permute-start = (f32[8]{0:T(128)S(1)}, f32[8]{0:T(128)S(1)}, u32[]{:S(2)}, u32[]{:S(2)}) collective-permute-start(f32[8]{0:T(128)S(1)} %exp.13), channel_id=1, source_target_pairs={{0,4},{4,8},{8,12},{12,16},{16,20},{20,24},{24,28},{28,32},{32,36}... | collective-permute-start | bytes 104 | tf_op jit(solution)/shard_map/ppermute | solution.py:54
  43.7 0.7 collective-permute-done
  44.4 0.1 add_select_fusion.5
  44.5 7.3 %collective-permute-start.8 = (f32[8,128,64]{1,2,0:T(8,128)S(1)}, f32[8,128,64]{1,2,0:T(8,128)S(1)}, u32[]{:S(2)}, u32[]{:S(2)}) collective-permute-start(f32[8,128,64]{1,2,0:T(8,128)S(1)} %add_select_fusion.5), channel_id=1, source_target_pairs={{0,8},{4,12},{8,16},{12,20},{16,24},{20,28},{24,32},{28,36},{32,40... | collective-permute-start | bytes 786440 | tf_op jit(solution)/shard_map/ppermute | solution.py:54
  51.9 5.2 %collective-permute-start.1 = (f32[8]{0:T(128)S(1)}, f32[8]{0:T(128)S(1)}, u32[]{:S(2)}, u32[]{:S(2)}) collective-permute-start(f32[8]{0:T(128)S(1)} %broadcast_select_fusion.2), channel_id=1, source_target_pairs={{0,4},{4,8},{8,12},{12,16},{16,20},{20,24},{24,28},{28,32},{32,36}... | collective-permute-start | bytes 104 | tf_op jit(solution)/shard_map/ppermute | solution.py:54
  57.1 0.9 collective-permute-done.1
  57.9 0.1 add_select_fusion.4
  58.0 20.4 %collective-permute-start.9 = (f32[8,128,64]{1,2,0:T(8,128)S(1)}, f32[8,128,64]{1,2,0:T(8,128)S(1)}, u32[]{:S(2)}, u32[]{:S(2)}) collective-permute-start(f32[8,128,64]{1,2,0:T(8,128)S(1)} %add_select_fusion.4), channel_id=1, source_target_pairs={{0,16},{4,20},{8,24},{12,28},{16,32},{20,36},{24,40},{28,44},{32,4... | collective-permute-start | bytes 786440 | tf_op jit(solution)/shard_map/ppermute | solution.py:54
  78.5 0.8 copy.47
  79.3 11.1 %all-to-all-start = ((bf16[256,4,64]{0,2,1:T(8,128)(2,1)}), bf16[256,4,64]{0,2,1:T(8,128)(2,1)S(1)}, u32[]{:S(2)}, u32[]{:S(2)}) async-start(bf16[256,4,64]{0,2,1:T(8,128)(2,1)} %bitcast), calls=%async_computation | async-start | bytes 262144 | tf_op jit(solution)/shard_map/all_to_all | solution.py:156
  90.3 1.3 collective-permute-start.2
  91.6 0.7 collective-permute-done.2
  92.3 0.1 add_select_fusion.3
  92.4 5.5 %collective-permute-start.10 = (f32[8,128,64]{1,2,0:T(8,128)S(1)}, f32[8,128,64]{1,2,0:T(8,128)S(1)}, u32[]{:S(2)}, u32[]{:S(2)}) collective-permute-start(f32[8,128,64]{1,2,0:T(8,128)S(1)} %add_select_fusion.3), channel_id=1, source_target_pairs={{0,32},{4,36},{8,40},{12,44},{16,48},{20,52},{24,56},{28,60},{32,6... | collective-permute-start | bytes 786440 | tf_op jit(solution)/shard_map/ppermute | solution.py:54
  97.9 0.2 fusion.28
  98.1 12.6 %collective-permute-start.3 = (f32[8]{0:T(128)S(1)}, f32[8]{0:T(128)S(1)}, u32[]{:S(2)}, u32[]{:S(2)}) collective-permute-start(f32[8]{0:T(128)S(1)} %broadcast_select_fusion.3), channel_id=1, source_target_pairs={{0,16},{4,20},{8,24},{12,28},{16,32},{20,36},{24,40},{28,44},{32,4... | collective-permute-start | bytes 104 | tf_op jit(solution)/shard_map/ppermute | solution.py:54
  110.7 0.7 collective-permute-done.3
  111.4 0.1 add_select_fusion.2
  111.6 8.3 %collective-permute-start.11 = (f32[8,128,64]{1,2,0:T(8,128)S(1)}, f32[8,128,64]{1,2,0:T(8,128)S(1)}, u32[]{:S(2)}, u32[]{:S(2)}) collective-permute-start(f32[8,128,64]{1,2,0:T(8,128)S(1)} %add_select_fusion.2), channel_id=1, source_target_pairs={{0,64},{4,68},{8,72},{12,76},{16,80},{20,84},{24,88},{28,92},{32,9... | collective-permute-start | bytes 786440 | tf_op jit(solution)/shard_map/ppermute | solution.py:54
  119.9 3.6 %collective-permute-start.4 = (f32[8]{0:T(128)S(1)}, f32[8]{0:T(128)S(1)}, u32[]{:S(2)}, u32[]{:S(2)}) collective-permute-start(f32[8]{0:T(128)S(1)} %broadcast_select_fusion.4), channel_id=1, source_target_pairs={{0,32},{4,36},{8,40},{12,44},{16,48},{20,52},{24,56},{28,60},{32,6... | collective-permute-start | bytes 104 | tf_op jit(solution)/shard_map/ppermute | solution.py:54
  123.4 0.7 collective-permute-done.4
  124.1 0.1 add_select_fusion.1
  124.2 4.8 %collective-permute-start.12 = (f32[8,128,64]{1,2,0:T(8,128)S(1)}, f32[8,128,64]{1,2,0:T(8,128)S(1)}, u32[]{:S(2)}, u32[]{:S(2)}) collective-permute-start(f32[8,128,64]{1,2,0:T(8,128)S(1)} %add_select_fusion.1), channel_id=1, source_target_pairs={{0,128},{4,132},{8,136},{12,140},{16,144},{20,148},{24,152},{28,15... | collective-permute-start | bytes 786440 | tf_op jit(solution)/shard_map/ppermute | solution.py:54
  129.0 0.7 convolution_bitcast_fusion.1
  129.7 1.3 collective-permute-start.5
  131.0 3.1 %collective-permute-done.5 = f32[8]{0:T(128)S(1)} collective-permute-done((f32[8]{0:T(128)S(1)}, f32[8]{0:T(128)S(1)}, u32[]{:S(2)}, u32[]{:S(2)}) %collective-permute-start.5) | collective-permute-done | bytes 64 | tf_op jit(solution)/shard_map/ppermute | solution.py:54
  134.1 0.9 copy.48
  135.0 0.3 multiply_reduce_fusion
  135.4 46.1 %all-gather.3.cloned.1.call-done = bf16[2,16384,1,64]{3,1,0,2:T(8,128)(2,1)} async-done(((bf16[2,1024,1,64]{3,1,0,2:T(8,128)(2,1)}), bf16[2,16384,1,64]{3,1,0,2:T(8,128)(2,1)}) %all-gather.3.cloned.1.call-update) | async-done | bytes 4194320 | tf_op jit(solution)/shard_map/all_gather | solution.py:160
  181.4 44.3 %shard_map.131 = bf16[1024,64]{1,0:T(8,128)(2,1)} custom-call(bf16[1024,64]{1,0:T(8,128)(2,1)} %bitcast.63, bf16[2,16384,64]{2,1,0:T(8,128)(2,1)} %bitcast.60, bf16[2,16384,64]{2,1,0:T(8,128)(2,1)} %bitcast.61), custom_call_target="tpu_custom_call" | custom-call | tf_op jit(solution)/shard_map/pallas_call | solution.py:104
  225.7 0.5 broadcast.86
  226.3 1.8 reduce.4
  228.0 0.9 reshape.117
  228.9 8.0 %all-to-all-start.3 = ((bf16[4,2,8192]{2,1,0:T(2,128)(2,1)}), bf16[4,2,8192]{2,1,0:T(2,128)(2,1)S(1)}, u32[]{:S(2)}, u32[]{:S(2)}) async-start(bf16[4,2,8192]{2,1,0:T(2,128)(2,1)} %reshape.117), calls=%async_computation.3 | async-start | bytes 262144 | tf_op jit(solution)/shard_map/all_to_all | solution.py:162
  236.9 1.7 fusion.29
  238.6 3.1 %all-to-all-done.3 = bf16[4,2,8192]{2,1,0:T(2,128)(2,1)S(1)} async-done(((bf16[4,2,8192]{2,1,0:T(2,128)(2,1)}), bf16[4,2,8192]{2,1,0:T(2,128)(2,1)S(1)}, u32[]{:S(2)}, u32[]{:S(2)}) %all-to-all-start.3) | async-done | bytes 131104 | tf_op jit(solution)/shard_map/all_to_all | solution.py:162
  241.8 0.3 reshape.118
  242.1 0.3 copy.54
  242.5 2.2 fusion
  244.8 0.2 fusion.3
  245.0 0.1 multiply_add_fusion
  245.1 19.8 %reduce-scatter.2.cloned.1.call-done = bf16[64,1024]{1,0:T(8,128)(2,1)} async-done(((bf16[256,1024]{1,0:T(8,128)(2,1)}), bf16[64,1024]{1,0:T(8,128)(2,1)}) %reduce-scatter.2.cloned.1.call-update) | async-done | bytes 131088 | tf_op jit(solution)/shard_map/reduce_scatter | solution.py:177
  264.9 1.0 add_convert_fusion
  265.9 0.6 convolution_convert_fusion
  266.6 6.7 %all_to_all.65 = bf16[4,32,768]{2,1,0:T(8,128)(2,1)S(1)} all-to-all(bf16[4,32,768]{2,1,0:T(8,128)(2,1)S(1)} %bitcast.69), channel_id=1, replica_groups=mesh['sb'=4,'sa'=16,'head'=4] {'head'}, dimensions={0} | all-to-all | bytes 393216 | tf_op jit(solution)/shard_map/all_to_all | solution.py:198
  273.3 0.7 copy.59
  (46 shorter events, 0.6 us)
Async XLA Ops:
  7.2 258.8 %copy-start = (bf16[1024,768]{1,0:T(8,128)(2,1)S(1)}, bf16[1024,768]{1,0:T(8,128)(2,1)}, u32[]{:S(2)}) copy-start(bf16[1024,768]{1,0:T(8,128)(2,1)} %param.22) | copy-start | bytes 4718596
  7.2 20.8 %copy-start.6 = (f32[8,256]{1,0:T(8,128)S(1)}, f32[8,256]{1,0:T(8,128)}, u32[]{:S(2)}) copy-start(f32[8,256]{1,0:T(8,128)} %param.19) | copy-start | bytes 24580
  7.2 21.5 %copy-start.2 = (bf16[256,512]{1,0:T(8,128)(2,1)S(1)}, bf16[256,512]{1,0:T(8,128)(2,1)}, u32[]{:S(2)}) copy-start(bf16[256,512]{1,0:T(8,128)(2,1)} %param.16) | copy-start | bytes 786436
  7.2 22.0 %copy-start.3 = (bf16[256,128]{1,0:T(8,128)(2,1)S(1)}, bf16[256,128]{1,0:T(8,128)(2,1)}, u32[]{:S(2)}) copy-start(bf16[256,128]{1,0:T(8,128)(2,1)} %param.17) | copy-start | bytes 196612
  9.0 9.7 %all-to-all-start.1 = ((bf16[256,4,64]{0,2,1:T(8,128)(2,1)}), bf16[256,4,64]{0,2,1:T(8,128)(2,1)S(1)}, u32[]{:S(2)}, u32[]{:S(2)}) async-start(bf16[256,4,64]{0,2,1:T(8,128)(2,1)} %bitcast.4), calls=%async_computation.1 | async-start | bytes 262144 | tf_op jit(solution)/shard_map/all_to_all | solution.py:156
  18.7 8.1 %all-to-all-start.2 = ((bf16[256,4,64]{0,2,1:T(8,128)(2,1)}), bf16[256,4,64]{0,2,1:T(8,128)(2,1)S(1)}, u32[]{:S(2)}, u32[]{:S(2)}) async-start(bf16[256,4,64]{0,2,1:T(8,128)(2,1)} %bitcast.8), calls=%async_computation.2 | async-start | bytes 262144 | tf_op jit(solution)/shard_map/all_to_all | solution.py:156
  22.0 159.4 %all-gather.3.cloned.1.call-start = ((), (), s32[]{:S(2)}) async-start(), calls=%async_computation.7 | async-start | bytes 8912896 | tf_op jit(solution)/shard_map/all_gather | solution.py:160
  27.9 50.6 %copy-start.5 = (bf16[256,256]{1,0:T(8,128)(2,1)S(1)}, bf16[256,256]{1,0:T(8,128)(2,1)}, u32[]{:S(2)}) copy-start(bf16[256,256]{1,0:T(8,128)(2,1)} %param.13) | copy-start | bytes 393220
  28.9 69.0 %copy-start.4 = (bf16[256,128]{1,0:T(8,128)(2,1)S(1)}, bf16[256,128]{1,0:T(8,128)(2,1)}, u32[]{:S(2)}) copy-start(bf16[256,128]{1,0:T(8,128)(2,1)} %param.18) | copy-start | bytes 196612
  29.5 6.9 %collective-permute-start.6 = (f32[8,128,64]{1,2,0:T(8,128)S(1)}, f32[8,128,64]{1,2,0:T(8,128)S(1)}, u32[]{:S(2)}, u32[]{:S(2)}) collective-permute-start(f32[8,128,64]{1,2,0:T(8,128)S(1)} %convolution_bitcast_fusion.2), channel_id=1, source_target_pairs={{0,4},{4,8},{8,12},{12,16},{16,20},{20,24},{24,28},{28,32},{32,36}... | collective-permute-start | bytes 786440 | tf_op jit(solution)/shard_map/ppermute | solution.py:54
  36.3 8.1 %collective-permute-start.7 = (f32[8,128,64]{1,2,0:T(8,128)S(1)}, f32[8,128,64]{1,2,0:T(8,128)S(1)}, u32[]{:S(2)}, u32[]{:S(2)}) collective-permute-start(f32[8,128,64]{1,2,0:T(8,128)S(1)} %broadcast_select_fusion), channel_id=1, source_target_pairs={{0,4},{4,8},{8,12},{12,16},{16,20},{20,24},{24,28},{28,32},{32,36}... | collective-permute-start | bytes 786440 | tf_op jit(solution)/shard_map/ppermute | solution.py:54
  40.2 4.2 %collective-permute-start = (f32[8]{0:T(128)S(1)}, f32[8]{0:T(128)S(1)}, u32[]{:S(2)}, u32[]{:S(2)}) collective-permute-start(f32[8]{0:T(128)S(1)} %exp.13), channel_id=1, source_target_pairs={{0,4},{4,8},{8,12},{12,16},{16,20},{20,24},{24,28},{28,32},{32,36}... | collective-permute-start | bytes 104 | tf_op jit(solution)/shard_map/ppermute | solution.py:54
  44.5 13.4 %collective-permute-start.8 = (f32[8,128,64]{1,2,0:T(8,128)S(1)}, f32[8,128,64]{1,2,0:T(8,128)S(1)}, u32[]{:S(2)}, u32[]{:S(2)}) collective-permute-start(f32[8,128,64]{1,2,0:T(8,128)S(1)} %add_select_fusion.5), channel_id=1, source_target_pairs={{0,8},{4,12},{8,16},{12,20},{16,24},{20,28},{24,32},{28,36},{32,40... | collective-permute-start | bytes 786440 | tf_op jit(solution)/shard_map/ppermute | solution.py:54
  51.9 6.1 %collective-permute-start.1 = (f32[8]{0:T(128)S(1)}, f32[8]{0:T(128)S(1)}, u32[]{:S(2)}, u32[]{:S(2)}) collective-permute-start(f32[8]{0:T(128)S(1)} %broadcast_select_fusion.2), channel_id=1, source_target_pairs={{0,4},{4,8},{8,12},{12,16},{16,20},{20,24},{24,28},{28,32},{32,36}... | collective-permute-start | bytes 104 | tf_op jit(solution)/shard_map/ppermute | solution.py:54
  58.0 34.3 %collective-permute-start.9 = (f32[8,128,64]{1,2,0:T(8,128)S(1)}, f32[8,128,64]{1,2,0:T(8,128)S(1)}, u32[]{:S(2)}, u32[]{:S(2)}) collective-permute-start(f32[8,128,64]{1,2,0:T(8,128)S(1)} %add_select_fusion.4), channel_id=1, source_target_pairs={{0,16},{4,20},{8,24},{12,28},{16,32},{20,36},{24,40},{28,44},{32,4... | collective-permute-start | bytes 786440 | tf_op jit(solution)/shard_map/ppermute | solution.py:54
  79.3 54.9 %all-to-all-start = ((bf16[256,4,64]{0,2,1:T(8,128)(2,1)}), bf16[256,4,64]{0,2,1:T(8,128)(2,1)S(1)}, u32[]{:S(2)}, u32[]{:S(2)}) async-start(bf16[256,4,64]{0,2,1:T(8,128)(2,1)} %bitcast), calls=%async_computation | async-start | bytes 262144 | tf_op jit(solution)/shard_map/all_to_all | solution.py:156
  90.3 2.0 collective-permute-start.2
  92.4 19.0 %collective-permute-start.10 = (f32[8,128,64]{1,2,0:T(8,128)S(1)}, f32[8,128,64]{1,2,0:T(8,128)S(1)}, u32[]{:S(2)}, u32[]{:S(2)}) collective-permute-start(f32[8,128,64]{1,2,0:T(8,128)S(1)} %add_select_fusion.3), channel_id=1, source_target_pairs={{0,32},{4,36},{8,40},{12,44},{16,48},{20,52},{24,56},{28,60},{32,6... | collective-permute-start | bytes 786440 | tf_op jit(solution)/shard_map/ppermute | solution.py:54
  98.1 13.3 %collective-permute-start.3 = (f32[8]{0:T(128)S(1)}, f32[8]{0:T(128)S(1)}, u32[]{:S(2)}, u32[]{:S(2)}) collective-permute-start(f32[8]{0:T(128)S(1)} %broadcast_select_fusion.3), channel_id=1, source_target_pairs={{0,16},{4,20},{8,24},{12,28},{16,32},{20,36},{24,40},{28,44},{32,4... | collective-permute-start | bytes 104 | tf_op jit(solution)/shard_map/ppermute | solution.py:54
  111.6 12.6 %collective-permute-start.11 = (f32[8,128,64]{1,2,0:T(8,128)S(1)}, f32[8,128,64]{1,2,0:T(8,128)S(1)}, u32[]{:S(2)}, u32[]{:S(2)}) collective-permute-start(f32[8,128,64]{1,2,0:T(8,128)S(1)} %add_select_fusion.2), channel_id=1, source_target_pairs={{0,64},{4,68},{8,72},{12,76},{16,80},{20,84},{24,88},{28,92},{32,9... | collective-permute-start | bytes 786440 | tf_op jit(solution)/shard_map/ppermute | solution.py:54
  119.9 4.3 %collective-permute-start.4 = (f32[8]{0:T(128)S(1)}, f32[8]{0:T(128)S(1)}, u32[]{:S(2)}, u32[]{:S(2)}) collective-permute-start(f32[8]{0:T(128)S(1)} %broadcast_select_fusion.4), channel_id=1, source_target_pairs={{0,32},{4,36},{8,40},{12,44},{16,48},{20,52},{24,56},{28,60},{32,6... | collective-permute-start | bytes 104 | tf_op jit(solution)/shard_map/ppermute | solution.py:54
  124.2 10.8 %collective-permute-start.12 = (f32[8,128,64]{1,2,0:T(8,128)S(1)}, f32[8,128,64]{1,2,0:T(8,128)S(1)}, u32[]{:S(2)}, u32[]{:S(2)}) collective-permute-start(f32[8,128,64]{1,2,0:T(8,128)S(1)} %add_select_fusion.1), channel_id=1, source_target_pairs={{0,128},{4,132},{8,136},{12,140},{16,144},{20,148},{24,152},{28,15... | collective-permute-start | bytes 786440 | tf_op jit(solution)/shard_map/ppermute | solution.py:54
  129.7 4.4 %collective-permute-start.5 = (f32[8]{0:T(128)S(1)}, f32[8]{0:T(128)S(1)}, u32[]{:S(2)}, u32[]{:S(2)}) collective-permute-start(f32[8]{0:T(128)S(1)} %broadcast_select_fusion.5), channel_id=1, source_target_pairs={{0,64},{4,68},{8,72},{12,76},{16,80},{20,84},{24,88},{28,92},{32,9... | collective-permute-start | bytes 104 | tf_op jit(solution)/shard_map/ppermute | solution.py:54
  228.9 12.9 %all-to-all-start.3 = ((bf16[4,2,8192]{2,1,0:T(2,128)(2,1)}), bf16[4,2,8192]{2,1,0:T(2,128)(2,1)S(1)}, u32[]{:S(2)}, u32[]{:S(2)}) async-start(bf16[4,2,8192]{2,1,0:T(2,128)(2,1)} %reshape.117), calls=%async_computation.3 | async-start | bytes 262144 | tf_op jit(solution)/shard_map/all_to_all | solution.py:162
  236.9 28.0 %reduce-scatter.2.cloned.1.call-start = ((), (), s32[]{:S(2)}) async-start(), calls=%async_computation.6 | async-start | bytes 655360 | tf_op jit(solution)/shard_map/reduce_scatter | solution.py:177
  242.1 2.6 copy-start.7
  265.9 8.0 %copy-start.1 = (bf16[64,1024]{1,0:T(8,128)(2,1)}, bf16[64,1024]{1,0:T(8,128)(2,1)S(1)}, u32[]{:S(2)}) copy-start(bf16[64,1024]{1,0:T(8,128)(2,1)S(1)} %add_convert_fusion) | copy-start | bytes 393220
Sparse Core Ops, SparseCore 0:
  28.1 153.3 all-gather.2
  244.8 20.0 reduce-scatter.1

commit v7 on v6

--- a/solution.py
+++ b/solution.py
@@ -69,9 +69,9 @@
     return state
 
 
-def flash_one_head(query_rows, pair, key_block=1024):
+def flash_one_head(query_rows, pair_t, key_block=4096):
     row_count, width = query_rows.shape
-    key_count = pair.shape[1]
+    key_count = pair_t.shape[2]
     steps = key_count // key_block
     scale = 1.0 / math.sqrt(width)
 
@@ -84,16 +84,17 @@
             sum_ref[...] = jnp.zeros(sum_ref.shape, jnp.float32)
             acc_ref[...] = jnp.zeros(acc_ref.shape, jnp.float32)
 
-        scores = lax.dot_general(
-            q_ref[...], k_ref[...], (((1,), (1,)), ((), ())), preferred_element_type=jnp.float32
-        ) * scale
+        scores = jnp.dot(q_ref[...], k_ref[...], preferred_element_type=jnp.float32) * scale
         old_top = top_ref[...]
         new_top = jnp.maximum(old_top, jnp.max(scores, axis=1, keepdims=True))
         shrink = jnp.exp(old_top - new_top)
         raised = jnp.exp(scores - new_top)
         sum_ref[...] = sum_ref[...] * shrink + jnp.sum(raised, axis=1, keepdims=True)
-        acc_ref[...] = acc_ref[...] * shrink + jnp.dot(
-            raised.astype(jnp.bfloat16), v_ref[...], preferred_element_type=jnp.float32
+        acc_ref[...] = acc_ref[...] * shrink + lax.dot_general(
+            raised.astype(jnp.bfloat16),
+            v_ref[...],
+            (((1,), (1,)), ((), ())),
+            preferred_element_type=jnp.float32,
         )
         top_ref[...] = new_top
 
@@ -107,8 +108,8 @@
         grid=(steps,),
         in_specs=[
             pl.BlockSpec((row_count, width), lambda j: (0, 0)),
-            pl.BlockSpec((None, key_block, width), lambda j: (0, j, 0)),
-            pl.BlockSpec((None, key_block, width), lambda j: (1, j, 0)),
+            pl.BlockSpec((None, width, key_block), lambda j: (0, 0, j)),
+            pl.BlockSpec((None, width, key_block), lambda j: (1, 0, j)),
         ],
         out_specs=pl.BlockSpec((row_count, width), lambda j: (0, 0)),
         scratch_shapes=[
@@ -117,7 +118,7 @@
             pltpu.VMEM((row_count, width), jnp.float32),
         ],
         compiler_params=pltpu.CompilerParams(dimension_semantics=("arbitrary",)),
-    )(query_rows, pair, pair)
+    )(query_rows, pair_t, pair_t)
 
 
 def slot_rank(owners_here, owner_count, group_rows):
@@ -156,8 +157,10 @@
         return lax.all_to_all(split, "sb", split_axis=1, concat_axis=0, tiled=True)
 
     query_heads = spread(queries)
-    pair = jnp.stack([spread(key_rows), spread(values)]).reshape(2, -1, HDIM)
-    gathered = lax.all_gather(pair, "sa", axis=1, tiled=True)
+    pair_t = jnp.stack(
+        [spread(key_rows).reshape(-1, HDIM).T, spread(values).reshape(-1, HDIM).T]
+    )
+    gathered = lax.all_gather(pair_t, "sa", axis=2, tiled=True)
     attended_one = flash_one_head(query_heads.reshape(-1, HDIM), gathered)
     attended = lax.all_to_all(
         attended_one.reshape(-1, 1, HDIM), "sb", split_axis=0, concat_axis=1, tiled=True

time: 282 us -> 231 us (0.82)
  waiting for transfers between devices: 86.8 us -> 44.9 us
  Pallas kernels: 44.3 us -> 32.1 us
  starting transfers between devices: 108 us -> 112 us
    all_gather x1, waiting for transfers between devices: 46.1 us -> 6.19 us  [per_device(): gathered = lax.all_gather(pair_t, 'sa', axis=2, tiled=True)]
    pallas_call x1, Pallas kernels: 44.3 us -> 32.1 us  [flash_one_head(): pl.pallas_call(kernel, out_shape=jax.ShapeDtypeStruct((row_count, width),...]
    unnamed x23 -> x25, local copies, waits for them, and re-layouts: 6.29 us -> 6.32 us
  transfers between devices with their start and end apart: 19 -> 19, of which waited for: 12 -> 12; matrix products, arithmetic and copies ran while one was open for 3% -> 4% of each run, Pallas kernels for 0% -> 0%
where the time goes in v7:
time: 231 us; the launch traced here: 230 us
  starting transfers between devices  112 us (48%)
  waiting for transfers between devices  44.9 us (19%)
  Pallas kernels  32.1 us (14%)
  between operations  14.5 us (6%)
  local copies, waits for them, and re-layouts  8.73 us (4%)
  blocking collectives  6.74 us (3%)
  matrix products  6.06 us (3%)
  other arithmetic  4.98 us (2%)
    ppermute x13, starting transfers between devices, shifted(): return jax.tree.map(lambda part: lax.ppermute(part, axis, pairs), tree)  82.5 us
    pallas_call x1, Pallas kernels, flash_one_head(): pl.pallas_call(kernel, out_shape=jax.ShapeDtypeStruct((row_count, width),...  32.1 us
    reduce_scatter x1, waiting for transfers between devices, per_device(): lax.psum_scatter((jnp.dot(attended, attn_project, preferred_element_type=...  20.2 us
    all_to_all x3, starting transfers between devices, spread(): return lax.all_to_all(split, 'sb', split_axis=1, concat_axis=0, tiled=True)  19.1 us
    all_to_all x1, starting transfers between devices, per_device(): lax.all_to_all(attended_one.reshape(-1, 1, HDIM), 'sb', split_axis=0, con...  10.3 us
    all_to_all x3, waiting for transfers between devices, spread(): return lax.all_to_all(split, 'sb', split_axis=1, concat_axis=0, tiled=True)  7.77 us
    ppermute x13, waiting for transfers between devices, shifted(): return jax.tree.map(lambda part: lax.ppermute(part, axis, pairs), tree)  7.51 us
    all_to_all x1, blocking collectives, per_device(): lax.all_to_all(packed, 'head', split_axis=0, concat_axis=0, tiled=True)  6.74 us
  transfers between devices with their start and end apart: 19, of which 12 were waited for; matrix products, arithmetic and copies ran while one was open for 4% of the time, Pallas kernels for 0%

profile of v7, /device:TPU:1, one launch (start us, length us, event | category | flops | bytes accessed | tf_op | source)
XLA Modules:
  0.0 229.9 jit_solution(15263894694895761649)
XLA Ops:
  7.2 1.8 copy.49
  9.0 4.8 %all-to-all-start.1 = ((bf16[256,4,64]{0,2,1:T(8,128)(2,1)}), bf16[256,4,64]{0,2,1:T(8,128)(2,1)S(1)}, u32[]{:S(2)}, u32[]{:S(2)}) async-start(bf16[256,4,64]{0,2,1:T(8,128)(2,1)} %bitcast.4), calls=%async_computation.1 | async-start | bytes 262144 | tf_op jit(solution)/shard_map/all_to_all | solution.py:157
  13.8 1.7 copy.51
  15.5 3.2 %all-to-all-done.1 = bf16[256,4,64]{0,2,1:T(8,128)(2,1)S(1)} async-done(((bf16[256,4,64]{0,2,1:T(8,128)(2,1)}), bf16[256,4,64]{0,2,1:T(8,128)(2,1)S(1)}, u32[]{:S(2)}, u32[]{:S(2)}) %all-to-all-start.1) | async-done | bytes 131104 | tf_op jit(solution)/shard_map/all_to_all | solution.py:157
  18.7 3.3 %all-to-all-start.2 = ((bf16[256,4,64]{0,2,1:T(8,128)(2,1)}), bf16[256,4,64]{0,2,1:T(8,128)(2,1)S(1)}, u32[]{:S(2)}, u32[]{:S(2)}) async-start(bf16[256,4,64]{0,2,1:T(8,128)(2,1)} %bitcast.9), calls=%async_computation.2 | async-start | bytes 262144 | tf_op jit(solution)/shard_map/all_to_all | solution.py:157
  22.0 0.1 copy.50
  22.2 4.6 %all-to-all-done.2 = bf16[256,4,64]{0,2,1:T(8,128)(2,1)S(1)} async-done(((bf16[256,4,64]{0,2,1:T(8,128)(2,1)}), bf16[256,4,64]{0,2,1:T(8,128)(2,1)S(1)}, u32[]{:S(2)}, u32[]{:S(2)}) %all-to-all-start.2) | async-done | bytes 131104 | tf_op jit(solution)/shard_map/all_to_all | solution.py:157
  26.8 0.1 copy.52
  26.9 0.7 pad_maximum_fusion
  27.7 0.6 reduce-window.6
  28.3 0.2 slice_reduce_fusion
  28.5 0.1 copy.56
  28.7 0.2 slice_reduce_fusion.1
  28.9 0.1 exponential_bitcast_fusion.1
  29.0 0.2 convolution_bitcast_fusion.2
  29.2 3.6 %collective-permute-start.6 = (f32[8,128,64]{1,2,0:T(8,128)S(1)}, f32[8,128,64]{1,2,0:T(8,128)S(1)}, u32[]{:S(2)}, u32[]{:S(2)}) collective-permute-start(f32[8,128,64]{1,2,0:T(8,128)S(1)} %convolution_bitcast_fusion.2), channel_id=1, source_target_pairs={{0,4},{4,8},{8,12},{12,16},{16,20},{20,24},{24,28},{28,32},{32,36}... | collective-permute-start | bytes 786440 | tf_op jit(solution)/shard_map/ppermute | solution.py:54
  32.8 3.3 %collective-permute-done.6 = f32[8,128,64]{1,2,0:T(8,128)S(1)} collective-permute-done((f32[8,128,64]{1,2,0:T(8,128)S(1)}, f32[8,128,64]{1,2,0:T(8,128)S(1)}, u32[]{:S(2)}, u32[]{:S(2)}) %collective-permute-start.6) | collective-permute-done | bytes 262176 | tf_op jit(solution)/shard_map/ppermute | solution.py:54
  36.1 3.8 %collective-permute-start.7 = (f32[8,128,64]{1,2,0:T(8,128)S(1)}, f32[8,128,64]{1,2,0:T(8,128)S(1)}, u32[]{:S(2)}, u32[]{:S(2)}) collective-permute-start(f32[8,128,64]{1,2,0:T(8,128)S(1)} %broadcast_select_fusion), channel_id=1, source_target_pairs={{0,4},{4,8},{8,12},{12,16},{16,20},{20,24},{24,28},{28,32},{32,36}... | collective-permute-start | bytes 786440 | tf_op jit(solution)/shard_map/ppermute | solution.py:54
  39.9 3.5 %collective-permute-start = (f32[8]{0:T(128)S(1)}, f32[8]{0:T(128)S(1)}, u32[]{:S(2)}, u32[]{:S(2)}) collective-permute-start(f32[8]{0:T(128)S(1)} %exp.13), channel_id=1, source_target_pairs={{0,4},{4,8},{8,12},{12,16},{16,20},{20,24},{24,28},{28,32},{32,36}... | collective-permute-start | bytes 104 | tf_op jit(solution)/shard_map/ppermute | solution.py:54
  43.5 0.7 collective-permute-done
  44.2 0.1 add_select_fusion.5
  44.3 7.3 %collective-permute-start.8 = (f32[8,128,64]{1,2,0:T(8,128)S(1)}, f32[8,128,64]{1,2,0:T(8,128)S(1)}, u32[]{:S(2)}, u32[]{:S(2)}) collective-permute-start(f32[8,128,64]{1,2,0:T(8,128)S(1)} %add_select_fusion.5), channel_id=1, source_target_pairs={{0,8},{4,12},{8,16},{12,20},{16,24},{20,28},{24,32},{28,36},{32,40... | collective-permute-start | bytes 786440 | tf_op jit(solution)/shard_map/ppermute | solution.py:54
  51.6 4.0 %collective-permute-start.1 = (f32[8]{0:T(128)S(1)}, f32[8]{0:T(128)S(1)}, u32[]{:S(2)}, u32[]{:S(2)}) collective-permute-start(f32[8]{0:T(128)S(1)} %broadcast_select_fusion.2), channel_id=1, source_target_pairs={{0,4},{4,8},{8,12},{12,16},{16,20},{20,24},{24,28},{28,32},{32,36}... | collective-permute-start | bytes 104 | tf_op jit(solution)/shard_map/ppermute | solution.py:54
  55.7 0.7 collective-permute-done.1
  56.4 0.1 add_select_fusion.4
  56.5 17.4 %collective-permute-start.9 = (f32[8,128,64]{1,2,0:T(8,128)S(1)}, f32[8,128,64]{1,2,0:T(8,128)S(1)}, u32[]{:S(2)}, u32[]{:S(2)}) collective-permute-start(f32[8,128,64]{1,2,0:T(8,128)S(1)} %add_select_fusion.4), channel_id=1, source_target_pairs={{0,16},{4,20},{8,24},{12,28},{16,32},{20,36},{24,40},{28,44},{32,4... | collective-permute-start | bytes 786440 | tf_op jit(solution)/shard_map/ppermute | solution.py:54
  73.9 0.8 copy.47
  74.7 11.0 %all-to-all-start = ((bf16[256,4,64]{0,2,1:T(8,128)(2,1)}), bf16[256,4,64]{0,2,1:T(8,128)(2,1)S(1)}, u32[]{:S(2)}, u32[]{:S(2)}) async-start(bf16[256,4,64]{0,2,1:T(8,128)(2,1)} %bitcast), calls=%async_computation | async-start | bytes 262144 | tf_op jit(solution)/shard_map/all_to_all | solution.py:157
  85.7 1.3 collective-permute-start.2
  86.9 0.7 collective-permute-done.2
  87.7 0.1 add_select_fusion.3
  87.8 5.3 %collective-permute-start.10 = (f32[8,128,64]{1,2,0:T(8,128)S(1)}, f32[8,128,64]{1,2,0:T(8,128)S(1)}, u32[]{:S(2)}, u32[]{:S(2)}) collective-permute-start(f32[8,128,64]{1,2,0:T(8,128)S(1)} %add_select_fusion.3), channel_id=1, source_target_pairs={{0,32},{4,36},{8,40},{12,44},{16,48},{20,52},{24,56},{28,60},{32,6... | collective-permute-start | bytes 786440 | tf_op jit(solution)/shard_map/ppermute | solution.py:54
  93.1 0.2 fusion.28
  93.3 10.7 %collective-permute-start.3 = (f32[8]{0:T(128)S(1)}, f32[8]{0:T(128)S(1)}, u32[]{:S(2)}, u32[]{:S(2)}) collective-permute-start(f32[8]{0:T(128)S(1)} %broadcast_select_fusion.3), channel_id=1, source_target_pairs={{0,16},{4,20},{8,24},{12,28},{16,32},{20,36},{24,40},{28,44},{32,4... | collective-permute-start | bytes 104 | tf_op jit(solution)/shard_map/ppermute | solution.py:54
  104.0 0.7 collective-permute-done.3
  104.7 0.1 add_select_fusion.2
  104.8 9.4 %collective-permute-start.11 = (f32[8,128,64]{1,2,0:T(8,128)S(1)}, f32[8,128,64]{1,2,0:T(8,128)S(1)}, u32[]{:S(2)}, u32[]{:S(2)}) collective-permute-start(f32[8,128,64]{1,2,0:T(8,128)S(1)} %add_select_fusion.2), channel_id=1, source_target_pairs={{0,64},{4,68},{8,72},{12,76},{16,80},{20,84},{24,88},{28,92},{32,9... | collective-permute-start | bytes 786440 | tf_op jit(solution)/shard_map/ppermute | solution.py:54
  114.3 5.1 %collective-permute-start.4 = (f32[8]{0:T(128)S(1)}, f32[8]{0:T(128)S(1)}, u32[]{:S(2)}, u32[]{:S(2)}) collective-permute-start(f32[8]{0:T(128)S(1)} %broadcast_select_fusion.4), channel_id=1, source_target_pairs={{0,32},{4,36},{8,40},{12,44},{16,48},{20,52},{24,56},{28,60},{32,6... | collective-permute-start | bytes 104 | tf_op jit(solution)/shard_map/ppermute | solution.py:54
  119.4 0.7 collective-permute-done.4
  120.1 0.1 add_select_fusion.1
  120.2 6.8 %collective-permute-start.12 = (f32[8,128,64]{1,2,0:T(8,128)S(1)}, f32[8,128,64]{1,2,0:T(8,128)S(1)}, u32[]{:S(2)}, u32[]{:S(2)}) collective-permute-start(f32[8,128,64]{1,2,0:T(8,128)S(1)} %add_select_fusion.1), channel_id=1, source_target_pairs={{0,128},{4,132},{8,136},{12,140},{16,144},{20,148},{24,152},{28,15... | collective-permute-start | bytes 786440 | tf_op jit(solution)/shard_map/ppermute | solution.py:54
  127.0 0.7 convolution_bitcast_fusion.1
  127.7 4.3 %collective-permute-start.5 = (f32[8]{0:T(128)S(1)}, f32[8]{0:T(128)S(1)}, u32[]{:S(2)}, u32[]{:S(2)}) collective-permute-start(f32[8]{0:T(128)S(1)} %broadcast_select_fusion.5), channel_id=1, source_target_pairs={{0,64},{4,68},{8,72},{12,76},{16,80},{20,84},{24,88},{28,92},{32,9... | collective-permute-start | bytes 104 | tf_op jit(solution)/shard_map/ppermute | solution.py:54
  131.9 0.7 collective-permute-done.5
  132.6 0.8 copy.48
  133.5 0.3 multiply_reduce_fusion
  133.9 6.2 %all-gather.2.cloned.1.call-done.k_ref.v_ref = bf16[2,64,16384]{2,1,0:T(8,128)(2,1)} async-done(((bf16[2,64,1024]{2,1,0:T(8,128)(2,1)}), bf16[2,64,16384]{2,1,0:T(8,128)(2,1)}) %all-gather.2.cloned.1.call-update) | async-done | bytes 4194320 | tf_op jit(solution)/shard_map/all_gather | solution.py:163
  140.0 32.1 %shard_map.131 = bf16[1024,64]{1,0:T(8,128)(2,1)} custom-call(bf16[1024,64]{1,0:T(8,128)(2,1)} %bitcast.77, bf16[2,64,16384]{2,1,0:T(8,128)(2,1)} %all-gather.2.cloned.1.call-done.k_ref.v_ref, bf16[2,64,16384]{2,1,0:T(8,128)(2,1)} %all-gather.2.cloned.1.call-done.k_ref.v_ref), custom_call_target="tpu_custom_call" | custom-call | tf_op jit(solution)/shard_map/pallas_call | solution.py:105
  172.2 0.5 broadcast.86
  172.7 1.8 reduce.4
  174.4 0.9 reshape.120
  175.3 10.3 %all-to-all-start.3 = ((bf16[4,2,8192]{2,1,0:T(2,128)(2,1)}), bf16[4,2,8192]{2,1,0:T(2,128)(2,1)S(1)}, u32[]{:S(2)}, u32[]{:S(2)}) async-start(bf16[4,2,8192]{2,1,0:T(2,128)(2,1)} %reshape.120), calls=%async_computation.3 | async-start | bytes 262144 | tf_op jit(solution)/shard_map/all_to_all | solution.py:165
  185.6 1.7 fusion.29
  187.3 3.1 %all-to-all-done.3 = bf16[4,2,8192]{2,1,0:T(2,128)(2,1)S(1)} async-done(((bf16[4,2,8192]{2,1,0:T(2,128)(2,1)}), bf16[4,2,8192]{2,1,0:T(2,128)(2,1)S(1)}, u32[]{:S(2)}, u32[]{:S(2)}) %all-to-all-start.3) | async-done | bytes 131104 | tf_op jit(solution)/shard_map/all_to_all | solution.py:165
  190.4 0.3 reshape.121
  190.7 0.3 copy.54
  191.2 2.2 fusion
  193.5 0.2 fusion.3
  193.7 0.1 multiply_add_fusion
  193.8 20.2 %reduce-scatter.2.cloned.1.call-done = bf16[64,1024]{1,0:T(8,128)(2,1)} async-done(((bf16[256,1024]{1,0:T(8,128)(2,1)}), bf16[64,1024]{1,0:T(8,128)(2,1)}) %reduce-scatter.2.cloned.1.call-update) | async-done | bytes 131088 | tf_op jit(solution)/shard_map/reduce_scatter | solution.py:180
  214.0 1.0 add_convert_fusion
  215.0 0.6 convolution_convert_fusion
  215.7 6.7 %all_to_all.65 = bf16[4,32,768]{2,1,0:T(8,128)(2,1)S(1)} all-to-all(bf16[4,32,768]{2,1,0:T(8,128)(2,1)S(1)} %bitcast.80), channel_id=1, replica_groups=mesh['sb'=4,'sa'=16,'head'=4] {'head'}, dimensions={0} | all-to-all | bytes 393216 | tf_op jit(solution)/shard_map/all_to_all | solution.py:201
  222.4 0.7 copy.61
  (48 shorter events, 0.6 us)
Async XLA Ops:
  7.2 207.9 %copy-start = (bf16[1024,768]{1,0:T(8,128)(2,1)S(1)}, bf16[1024,768]{1,0:T(8,128)(2,1)}, u32[]{:S(2)}) copy-start(bf16[1024,768]{1,0:T(8,128)(2,1)} %param.22) | copy-start | bytes 4718596
  7.2 20.5 %copy-start.6 = (f32[8,256]{1,0:T(8,128)S(1)}, f32[8,256]{1,0:T(8,128)}, u32[]{:S(2)}) copy-start(f32[8,256]{1,0:T(8,128)} %param.19) | copy-start | bytes 24580
  7.2 21.3 %copy-start.2 = (bf16[256,512]{1,0:T(8,128)(2,1)S(1)}, bf16[256,512]{1,0:T(8,128)(2,1)}, u32[]{:S(2)}) copy-start(bf16[256,512]{1,0:T(8,128)(2,1)} %param.16) | copy-start | bytes 786436
  7.2 21.8 %copy-start.3 = (bf16[256,128]{1,0:T(8,128)(2,1)S(1)}, bf16[256,128]{1,0:T(8,128)(2,1)}, u32[]{:S(2)}) copy-start(bf16[256,128]{1,0:T(8,128)(2,1)} %param.17) | copy-start | bytes 196612
  9.0 9.7 %all-to-all-start.1 = ((bf16[256,4,64]{0,2,1:T(8,128)(2,1)}), bf16[256,4,64]{0,2,1:T(8,128)(2,1)S(1)}, u32[]{:S(2)}, u32[]{:S(2)}) async-start(bf16[256,4,64]{0,2,1:T(8,128)(2,1)} %bitcast.4), calls=%async_computation.1 | async-start | bytes 262144 | tf_op jit(solution)/shard_map/all_to_all | solution.py:157
  18.7 8.1 %all-to-all-start.2 = ((bf16[256,4,64]{0,2,1:T(8,128)(2,1)}), bf16[256,4,64]{0,2,1:T(8,128)(2,1)S(1)}, u32[]{:S(2)}, u32[]{:S(2)}) async-start(bf16[256,4,64]{0,2,1:T(8,128)(2,1)} %bitcast.9), calls=%async_computation.2 | async-start | bytes 262144 | tf_op jit(solution)/shard_map/all_to_all | solution.py:157
  22.0 118.0 %all-gather.2.cloned.1.call-start = ((), (), s32[]{:S(2)}) async-start(), calls=%async_computation.6 | async-start | bytes 4456448 | tf_op jit(solution)/shard_map/all_gather | solution.py:163
  26.9 47.0 %copy-start.5 = (bf16[256,256]{1,0:T(8,128)(2,1)S(1)}, bf16[256,256]{1,0:T(8,128)(2,1)}, u32[]{:S(2)}) copy-start(bf16[256,256]{1,0:T(8,128)(2,1)} %param.13) | copy-start | bytes 393220
  28.6 64.4 %copy-start.4 = (bf16[256,128]{1,0:T(8,128)(2,1)S(1)}, bf16[256,128]{1,0:T(8,128)(2,1)}, u32[]{:S(2)}) copy-start(bf16[256,128]{1,0:T(8,128)(2,1)} %param.18) | copy-start | bytes 196612
  29.2 6.8 %collective-permute-start.6 = (f32[8,128,64]{1,2,0:T(8,128)S(1)}, f32[8,128,64]{1,2,0:T(8,128)S(1)}, u32[]{:S(2)}, u32[]{:S(2)}) collective-permute-start(f32[8,128,64]{1,2,0:T(8,128)S(1)} %convolution_bitcast_fusion.2), channel_id=1, source_target_pairs={{0,4},{4,8},{8,12},{12,16},{16,20},{20,24},{24,28},{28,32},{32,36}... | collective-permute-start | bytes 786440 | tf_op jit(solution)/shard_map/ppermute | solution.py:54
  36.1 8.1 %collective-permute-start.7 = (f32[8,128,64]{1,2,0:T(8,128)S(1)}, f32[8,128,64]{1,2,0:T(8,128)S(1)}, u32[]{:S(2)}, u32[]{:S(2)}) collective-permute-start(f32[8,128,64]{1,2,0:T(8,128)S(1)} %broadcast_select_fusion), channel_id=1, source_target_pairs={{0,4},{4,8},{8,12},{12,16},{16,20},{20,24},{24,28},{28,32},{32,36}... | collective-permute-start | bytes 786440 | tf_op jit(solution)/shard_map/ppermute | solution.py:54
  39.9 4.2 %collective-permute-start = (f32[8]{0:T(128)S(1)}, f32[8]{0:T(128)S(1)}, u32[]{:S(2)}, u32[]{:S(2)}) collective-permute-start(f32[8]{0:T(128)S(1)} %exp.13), channel_id=1, source_target_pairs={{0,4},{4,8},{8,12},{12,16},{16,20},{20,24},{24,28},{28,32},{32,36}... | collective-permute-start | bytes 104 | tf_op jit(solution)/shard_map/ppermute | solution.py:54
  44.3 12.1 %collective-permute-start.8 = (f32[8,128,64]{1,2,0:T(8,128)S(1)}, f32[8,128,64]{1,2,0:T(8,128)S(1)}, u32[]{:S(2)}, u32[]{:S(2)}) collective-permute-start(f32[8,128,64]{1,2,0:T(8,128)S(1)} %add_select_fusion.5), channel_id=1, source_target_pairs={{0,8},{4,12},{8,16},{12,20},{16,24},{20,28},{24,32},{28,36},{32,40... | collective-permute-start | bytes 786440 | tf_op jit(solution)/shard_map/ppermute | solution.py:54
  51.6 4.7 %collective-permute-start.1 = (f32[8]{0:T(128)S(1)}, f32[8]{0:T(128)S(1)}, u32[]{:S(2)}, u32[]{:S(2)}) collective-permute-start(f32[8]{0:T(128)S(1)} %broadcast_select_fusion.2), channel_id=1, source_target_pairs={{0,4},{4,8},{8,12},{12,16},{16,20},{20,24},{24,28},{28,32},{32,36}... | collective-permute-start | bytes 104 | tf_op jit(solution)/shard_map/ppermute | solution.py:54
  56.5 31.2 %collective-permute-start.9 = (f32[8,128,64]{1,2,0:T(8,128)S(1)}, f32[8,128,64]{1,2,0:T(8,128)S(1)}, u32[]{:S(2)}, u32[]{:S(2)}) collective-permute-start(f32[8,128,64]{1,2,0:T(8,128)S(1)} %add_select_fusion.4), channel_id=1, source_target_pairs={{0,16},{4,20},{8,24},{12,28},{16,32},{20,36},{24,40},{28,44},{32,4... | collective-permute-start | bytes 786440 | tf_op jit(solution)/shard_map/ppermute | solution.py:54
  74.7 58.0 %all-to-all-start = ((bf16[256,4,64]{0,2,1:T(8,128)(2,1)}), bf16[256,4,64]{0,2,1:T(8,128)(2,1)S(1)}, u32[]{:S(2)}, u32[]{:S(2)}) async-start(bf16[256,4,64]{0,2,1:T(8,128)(2,1)} %bitcast), calls=%async_computation | async-start | bytes 262144 | tf_op jit(solution)/shard_map/all_to_all | solution.py:157
  85.7 2.0 collective-permute-start.2
  87.8 17.0 %collective-permute-start.10 = (f32[8,128,64]{1,2,0:T(8,128)S(1)}, f32[8,128,64]{1,2,0:T(8,128)S(1)}, u32[]{:S(2)}, u32[]{:S(2)}) collective-permute-start(f32[8,128,64]{1,2,0:T(8,128)S(1)} %add_select_fusion.3), channel_id=1, source_target_pairs={{0,32},{4,36},{8,40},{12,44},{16,48},{20,52},{24,56},{28,60},{32,6... | collective-permute-start | bytes 786440 | tf_op jit(solution)/shard_map/ppermute | solution.py:54
  93.3 11.4 %collective-permute-start.3 = (f32[8]{0:T(128)S(1)}, f32[8]{0:T(128)S(1)}, u32[]{:S(2)}, u32[]{:S(2)}) collective-permute-start(f32[8]{0:T(128)S(1)} %broadcast_select_fusion.3), channel_id=1, source_target_pairs={{0,16},{4,20},{8,24},{12,28},{16,32},{20,36},{24,40},{28,44},{32,4... | collective-permute-start | bytes 104 | tf_op jit(solution)/shard_map/ppermute | solution.py:54
  104.8 15.3 %collective-permute-start.11 = (f32[8,128,64]{1,2,0:T(8,128)S(1)}, f32[8,128,64]{1,2,0:T(8,128)S(1)}, u32[]{:S(2)}, u32[]{:S(2)}) collective-permute-start(f32[8,128,64]{1,2,0:T(8,128)S(1)} %add_select_fusion.2), channel_id=1, source_target_pairs={{0,64},{4,68},{8,72},{12,76},{16,80},{20,84},{24,88},{28,92},{32,9... | collective-permute-start | bytes 786440 | tf_op jit(solution)/shard_map/ppermute | solution.py:54
  114.3 5.8 %collective-permute-start.4 = (f32[8]{0:T(128)S(1)}, f32[8]{0:T(128)S(1)}, u32[]{:S(2)}, u32[]{:S(2)}) collective-permute-start(f32[8]{0:T(128)S(1)} %broadcast_select_fusion.4), channel_id=1, source_target_pairs={{0,32},{4,36},{8,40},{12,44},{16,48},{20,52},{24,56},{28,60},{32,6... | collective-permute-start | bytes 104 | tf_op jit(solution)/shard_map/ppermute | solution.py:54
  120.2 13.3 %collective-permute-start.12 = (f32[8,128,64]{1,2,0:T(8,128)S(1)}, f32[8,128,64]{1,2,0:T(8,128)S(1)}, u32[]{:S(2)}, u32[]{:S(2)}) collective-permute-start(f32[8,128,64]{1,2,0:T(8,128)S(1)} %add_select_fusion.1), channel_id=1, source_target_pairs={{0,128},{4,132},{8,136},{12,140},{16,144},{20,148},{24,152},{28,15... | collective-permute-start | bytes 786440 | tf_op jit(solution)/shard_map/ppermute | solution.py:54
  127.7 5.0 %collective-permute-start.5 = (f32[8]{0:T(128)S(1)}, f32[8]{0:T(128)S(1)}, u32[]{:S(2)}, u32[]{:S(2)}) collective-permute-start(f32[8]{0:T(128)S(1)} %broadcast_select_fusion.5), channel_id=1, source_target_pairs={{0,64},{4,68},{8,72},{12,76},{16,80},{20,84},{24,88},{28,92},{32,9... | collective-permute-start | bytes 104 | tf_op jit(solution)/shard_map/ppermute | solution.py:54
  175.3 15.1 %all-to-all-start.3 = ((bf16[4,2,8192]{2,1,0:T(2,128)(2,1)}), bf16[4,2,8192]{2,1,0:T(2,128)(2,1)S(1)}, u32[]{:S(2)}, u32[]{:S(2)}) async-start(bf16[4,2,8192]{2,1,0:T(2,128)(2,1)} %reshape.120), calls=%async_computation.3 | async-start | bytes 262144 | tf_op jit(solution)/shard_map/all_to_all | solution.py:165
  185.6 28.4 %reduce-scatter.2.cloned.1.call-start = ((), (), s32[]{:S(2)}) async-start(), calls=%async_computation.7 | async-start | bytes 655360 | tf_op jit(solution)/shard_map/reduce_scatter | solution.py:180
  190.7 2.6 %copy-start.7 = (s32[256]{0:T(256)S(1)}, s32[256]{0:T(256)}, u32[]{:S(2)}) copy-start(s32[256]{0:T(256)} %param.23) | copy-start | bytes 3076
  215.0 8.1 %copy-start.1 = (bf16[64,1024]{1,0:T(8,128)(2,1)}, bf16[64,1024]{1,0:T(8,128)(2,1)S(1)}, u32[]{:S(2)}) copy-start(bf16[64,1024]{1,0:T(8,128)(2,1)S(1)} %add_convert_fusion) | copy-start | bytes 393220
Sparse Core Ops, SparseCore 0:
  27.8 112.1 all-gather.1
  193.5 20.4 reduce-scatter.1

commit v8 on v7

--- a/solution.py
+++ b/solution.py
@@ -48,25 +48,32 @@
     axis = ("sb", "sa")
     devices = lax.axis_size(axis)
     mine = lax.axis_index(axis)
-
-    def shifted(tree, distance):
+    head_count, state_rows, width = local_state.shape
+    decay_rows = jnp.broadcast_to(total_decay[:, None, None], (head_count, 8, width))
+    packed = jnp.concatenate([local_state, decay_rows], axis=1)
+
+    def shifted(part, distance):
         pairs = [(j, j + distance) for j in range(devices - distance)]
-        return jax.tree.map(lambda part: lax.ppermute(part, axis, pairs), tree)
-
-    decay, state = shifted((total_decay, local_state), 1)
-    first = mine >= 1
-    decay = jnp.where(first, decay, jnp.ones_like(decay))
-    state = jnp.where(first, state, jnp.zeros_like(state))
+        return lax.ppermute(part, axis, pairs)
+
+    identity = jnp.concatenate(
+        [jnp.zeros_like(local_state), jnp.ones_like(decay_rows)], axis=1
+    )
+    packed = jnp.where(mine >= 1, shifted(packed, 1), identity)
     distance = 1
     while distance < devices:
-        earlier_decay, earlier_state = shifted((decay, state), distance)
-        reached = mine >= distance
-        new_decay = earlier_decay * decay
-        new_state = decay[:, None, None] * earlier_state + state
-        decay = jnp.where(reached, new_decay, decay)
-        state = jnp.where(reached, new_state, state)
+        earlier = shifted(packed, distance)
+        decay = packed[:, state_rows:state_rows + 1, :1]
+        combined = jnp.concatenate(
+            [
+                decay * earlier[:, :state_rows] + packed[:, :state_rows],
+                earlier[:, state_rows:] * packed[:, state_rows:],
+            ],
+            axis=1,
+        )
+        packed = jnp.where(mine >= distance, combined, packed)
         distance *= 2
-    return state
+    return packed[:, :state_rows]
 
 
 def flash_one_head(query_rows, pair_t, key_block=4096):

time: 231 us -> 268 us (1.16)
  waiting for transfers between devices: 44.9 us -> 88.5 us
  starting transfers between devices: 112 us -> 101 us
  local copies, waits for them, and re-layouts: 8.73 us -> 11.5 us
    ppermute x13 -> x7, waiting for transfers between devices: 7.51 us -> 62.9 us  [shifted(): return lax.ppermute(part, axis, pairs)]
    all_to_all x3, starting transfers between devices: 19.1 us -> 12.2 us  [spread(): return lax.all_to_all(split, 'sb', split_axis=1, concat_axis=0, tiled=True)]
    all_gather x1, waiting for transfers between devices: 6.19 us -> 0.02 us  [per_device(): gathered = lax.all_gather(pair_t, 'sa', axis=2, tiled=True)]
    all_to_all x1, starting transfers between devices: 10.3 us -> 4.98 us  [per_device(): lax.all_to_all(attended_one.reshape(-1, 1, HDIM), 'sb', split_axis=0, con...]
    all_to_all x3, waiting for transfers between devices: 7.77 us -> 4.88 us  [spread(): return lax.all_to_all(split, 'sb', split_axis=1, concat_axis=0, tiled=True)]
    reduce_scatter x1, waiting for transfers between devices: 20.2 us -> 17.5 us  [per_device(): lax.psum_scatter((jnp.dot(attended, attn_project, preferred_element_type=...]
    unnamed x25 -> x19, local copies, waits for them, and re-layouts: 6.32 us -> 8.18 us
    ppermute x13 -> x7, starting transfers between devices: 82.5 us -> 83.9 us  [shifted(): return lax.ppermute(part, axis, pairs)]
  transfers between devices with their start and end apart: 19 -> 13, of which waited for: 12 -> 11; matrix products, arithmetic and copies ran while one was open for 4% -> 5% of each run, Pallas kernels for 0% -> 0%
where the time goes in v8:
time: 268 us; the launch traced here: 267 us
  starting transfers between devices  101 us (38%)
  waiting for transfers between devices  88.5 us (33%)
  Pallas kernels  32.1 us (12%)
  between operations  14.5 us (5%)
  local copies, waits for them, and re-layouts  11.5 us (4%)
  blocking collectives  6.75 us (3%)
  other arithmetic  6.31 us (2%)
  matrix products  6.02 us (2%)
    ppermute x7, starting transfers between devices, shifted(): return lax.ppermute(part, axis, pairs)  83.9 us
    ppermute x7, waiting for transfers between devices, shifted(): return lax.ppermute(part, axis, pairs)  62.9 us
    pallas_call x1, Pallas kernels, flash_one_head(): pl.pallas_call(kernel, out_shape=jax.ShapeDtypeStruct((row_count, width),...  32.1 us
    reduce_scatter x1, waiting for transfers between devices, per_device(): lax.psum_scatter((jnp.dot(attended, attn_project, preferred_element_type=...  17.5 us
    all_to_all x3, starting transfers between devices, spread(): return lax.all_to_all(split, 'sb', split_axis=1, concat_axis=0, tiled=True)  12.2 us
    unnamed x19, local copies, waits for them, and re-layouts  8.18 us
    all_to_all x1, blocking collectives, per_device(): lax.all_to_all(packed, 'head', split_axis=0, concat_axis=0, tiled=True)  6.75 us
  transfers between devices with their start and end apart: 13, of which 11 were waited for; matrix products, arithmetic and copies ran while one was open for 5% of the time, Pallas kernels for 0%

profile of v8, /device:TPU:1, one launch (start us, length us, event | category | flops | bytes accessed | tf_op | source)
XLA Modules:
  0.0 266.8 jit_solution(13815371877375761549)
XLA Ops:
  7.2 1.8 copy.49
  9.0 4.8 %all-to-all-start.1 = ((bf16[256,4,64]{0,2,1:T(8,128)(2,1)}), bf16[256,4,64]{0,2,1:T(8,128)(2,1)S(1)}, u32[]{:S(2)}, u32[]{:S(2)}) async-start(bf16[256,4,64]{0,2,1:T(8,128)(2,1)} %bitcast.4), calls=%async_computation.1 | async-start | bytes 262144 | tf_op jit(solution)/shard_map/all_to_all | solution.py:164
  13.8 1.2 reduce-window.6
  15.1 0.2 slice_reduce_fusion
  15.3 1.7 copy.51
  17.0 0.2 slice_reduce_fusion.7
  17.2 1.4 all-to-all-done.1
  18.7 3.3 %all-to-all-start.2 = ((bf16[256,4,64]{0,2,1:T(8,128)(2,1)}), bf16[256,4,64]{0,2,1:T(8,128)(2,1)S(1)}, u32[]{:S(2)}, u32[]{:S(2)}) async-start(bf16[256,4,64]{0,2,1:T(8,128)(2,1)} %bitcast.9), calls=%async_computation.2 | async-start | bytes 262144 | tf_op jit(solution)/shard_map/all_to_all | solution.py:164
  22.1 1.1 copy.56
  23.2 0.1 copy.50
  23.3 3.4 %all-to-all-done.2 = bf16[256,4,64]{0,2,1:T(8,128)(2,1)S(1)} async-done(((bf16[256,4,64]{0,2,1:T(8,128)(2,1)}), bf16[256,4,64]{0,2,1:T(8,128)(2,1)S(1)}, u32[]{:S(2)}, u32[]{:S(2)}) %all-to-all-start.2) | async-done | bytes 131104 | tf_op jit(solution)/shard_map/all_to_all | solution.py:164
  26.8 0.1 copy.52
  26.9 0.7 pad_maximum_fusion.2
  27.7 0.2 convolution_bitcast_fusion.2
  27.9 0.1 broadcast_in_dim.18
  28.0 3.6 %collective-permute-start = (f32[8,136,64]{1,2,0:T(8,128)S(1)}, f32[8,136,64]{1,2,0:T(8,128)S(1)}, u32[]{:S(2)}, u32[]{:S(2)}) collective-permute-start(f32[8,136,64]{1,2,0:T(8,128)S(1)} %pad_maximum_fusion), channel_id=1, source_target_pairs={{0,4},{4,8},{8,12},{12,16},{16,20},{20,24},{24,28},{28,32},{32,36}... | collective-permute-start | bytes 835592 | tf_op jit(solution)/shard_map/ppermute | solution.py:57
  31.7 8.0 %collective-permute-done = f32[8,136,64]{1,2,0:T(8,128)S(1)} collective-permute-done((f32[8,136,64]{1,2,0:T(8,128)S(1)}, f32[8,136,64]{1,2,0:T(8,128)S(1)}, u32[]{:S(2)}, u32[]{:S(2)}) %collective-permute-start) | collective-permute-done | bytes 278560 | tf_op jit(solution)/shard_map/ppermute | solution.py:57
  39.7 4.1 %collective-permute-start.1 = (f32[8,136,64]{1,2,0:T(8,128)S(1)}, f32[8,136,64]{1,2,0:T(8,128)S(1)}, u32[]{:S(2)}, u32[]{:S(2)}) collective-permute-start(f32[8,136,64]{1,2,0:T(8,128)S(1)} %broadcast_select_fusion), channel_id=1, source_target_pairs={{0,4},{4,8},{8,12},{12,16},{16,20},{20,24},{24,28},{28,32},{32,36}... | collective-permute-start | bytes 835592 | tf_op jit(solution)/shard_map/ppermute | solution.py:57
  43.8 0.1 slice_reduce_fusion.6
  43.9 11.5 %collective-permute-done.1 = f32[8,136,64]{1,2,0:T(8,128)S(1)} collective-permute-done((f32[8,136,64]{1,2,0:T(8,128)S(1)}, f32[8,136,64]{1,2,0:T(8,128)S(1)}, u32[]{:S(2)}, u32[]{:S(2)}) %collective-permute-start.1) | collective-permute-done | bytes 278560 | tf_op jit(solution)/shard_map/ppermute | solution.py:57
  55.5 0.1 slice_add_fusion.4
  55.7 6.8 %collective-permute-start.2 = (f32[8,136,64]{1,2,0:T(8,128)S(1)}, f32[8,136,64]{1,2,0:T(8,128)S(1)}, u32[]{:S(2)}, u32[]{:S(2)}) collective-permute-start(f32[8,136,64]{1,2,0:T(8,128)S(1)} %maximum_select_fusion), channel_id=1, source_target_pairs={{0,8},{4,12},{8,16},{12,20},{16,24},{20,28},{24,32},{28,36},{32,40... | collective-permute-start | bytes 835592 | tf_op jit(solution)/shard_map/ppermute | solution.py:57
  62.5 0.1 slice_reduce_fusion.5
  62.7 17.7 %collective-permute-done.2 = f32[8,136,64]{1,2,0:T(8,128)S(1)} collective-permute-done((f32[8,136,64]{1,2,0:T(8,128)S(1)}, f32[8,136,64]{1,2,0:T(8,128)S(1)}, u32[]{:S(2)}, u32[]{:S(2)}) %collective-permute-start.2) | collective-permute-done | bytes 278560 | tf_op jit(solution)/shard_map/ppermute | solution.py:57
  80.4 0.1 slice_add_fusion.3
  80.6 8.8 %collective-permute-start.3 = (f32[8,136,64]{1,2,0:T(8,128)S(1)}, f32[8,136,64]{1,2,0:T(8,128)S(1)}, u32[]{:S(2)}, u32[]{:S(2)}) collective-permute-start(f32[8,136,64]{1,2,0:T(8,128)S(1)} %maximum_select_fusion.1), channel_id=1, source_target_pairs={{0,16},{4,20},{8,24},{12,28},{16,32},{20,36},{24,40},{28,44},{32,4... | collective-permute-start | bytes 835592 | tf_op jit(solution)/shard_map/ppermute | solution.py:57
  89.4 0.1 slice_reduce_fusion.4
  89.5 8.8 %collective-permute-done.3 = f32[8,136,64]{1,2,0:T(8,128)S(1)} collective-permute-done((f32[8,136,64]{1,2,0:T(8,128)S(1)}, f32[8,136,64]{1,2,0:T(8,128)S(1)}, u32[]{:S(2)}, u32[]{:S(2)}) %collective-permute-start.3) | collective-permute-done | bytes 278560 | tf_op jit(solution)/shard_map/ppermute | solution.py:57
  98.3 0.1 slice_add_fusion.2
  98.5 34.1 %collective-permute-start.4 = (f32[8,136,64]{1,2,0:T(8,128)S(1)}, f32[8,136,64]{1,2,0:T(8,128)S(1)}, u32[]{:S(2)}, u32[]{:S(2)}) collective-permute-start(f32[8,136,64]{1,2,0:T(8,128)S(1)} %maximum_select_fusion.2), channel_id=1, source_target_pairs={{0,32},{4,36},{8,40},{12,44},{16,48},{20,52},{24,56},{28,60},{32,6... | collective-permute-start | bytes 835592 | tf_op jit(solution)/shard_map/ppermute | solution.py:57
  132.6 0.1 slice_reduce_fusion.3
  132.7 5.9 %collective-permute-done.4 = f32[8,136,64]{1,2,0:T(8,128)S(1)} collective-permute-done((f32[8,136,64]{1,2,0:T(8,128)S(1)}, f32[8,136,64]{1,2,0:T(8,128)S(1)}, u32[]{:S(2)}, u32[]{:S(2)}) %collective-permute-start.4) | collective-permute-done | bytes 278560 | tf_op jit(solution)/shard_map/ppermute | solution.py:57
  138.7 0.1 slice_add_fusion.1
  138.9 18.9 %collective-permute-start.5 = (f32[8,136,64]{1,2,0:T(8,128)S(1)}, f32[8,136,64]{1,2,0:T(8,128)S(1)}, u32[]{:S(2)}, u32[]{:S(2)}) collective-permute-start(f32[8,136,64]{1,2,0:T(8,128)S(1)} %maximum_select_fusion.3), channel_id=1, source_target_pairs={{0,64},{4,68},{8,72},{12,76},{16,80},{20,84},{24,88},{28,92},{32,9... | collective-permute-start | bytes 835592 | tf_op jit(solution)/shard_map/ppermute | solution.py:57
  157.8 1.7 copy.47
  159.5 4.1 %all-to-all-start = ((bf16[256,4,64]{0,2,1:T(8,128)(2,1)}), bf16[256,4,64]{0,2,1:T(8,128)(2,1)S(1)}, u32[]{:S(2)}, u32[]{:S(2)}) async-start(bf16[256,4,64]{0,2,1:T(8,128)(2,1)} %bitcast), calls=%async_computation | async-start | bytes 262144 | tf_op jit(solution)/shard_map/all_to_all | solution.py:164
  163.6 0.1 slice_reduce_fusion.2
  163.7 4.0 %collective-permute-done.5 = f32[8,136,64]{1,2,0:T(8,128)S(1)} collective-permute-done((f32[8,136,64]{1,2,0:T(8,128)S(1)}, f32[8,136,64]{1,2,0:T(8,128)S(1)}, u32[]{:S(2)}, u32[]{:S(2)}) %collective-permute-start.5) | collective-permute-done | bytes 278560 | tf_op jit(solution)/shard_map/ppermute | solution.py:57
  167.8 0.1 slice_add_fusion
  168.0 7.6 %collective-permute-start.6 = (f32[8,136,64]{1,2,0:T(8,128)S(1)}, f32[8,136,64]{1,2,0:T(8,128)S(1)}, u32[]{:S(2)}, u32[]{:S(2)}) collective-permute-start(f32[8,136,64]{1,2,0:T(8,128)S(1)} %maximum_select_fusion.4), channel_id=1, source_target_pairs={{0,128},{4,132},{8,136},{12,140},{16,144},{20,148},{24,152},{28,15... | collective-permute-start | bytes 835592 | tf_op jit(solution)/shard_map/ppermute | solution.py:57
  175.6 0.2 fusion.30
  175.8 0.8 copy.48
  176.6 0.1 slice_reduce_fusion.1
  176.8 7.0 %collective-permute-done.6 = f32[8,136,64]{1,2,0:T(8,128)S(1)} collective-permute-done((f32[8,136,64]{1,2,0:T(8,128)S(1)}, f32[8,136,64]{1,2,0:T(8,128)S(1)}, u32[]{:S(2)}, u32[]{:S(2)}) %collective-permute-start.6) | collective-permute-done | bytes 278560 | tf_op jit(solution)/shard_map/ppermute | solution.py:57
  183.8 0.1 fusion.11
  183.9 0.2 fusion.1
  184.2 0.7 multiply_reduce_fusion
  185.0 32.1 %shard_map.131 = bf16[1024,64]{1,0:T(8,128)(2,1)} custom-call(bf16[1024,64]{1,0:T(8,128)(2,1)} %bitcast.75, bf16[2,64,16384]{2,1,0:T(8,128)(2,1)} %all-gather.2.cloned.1.call-done.k_ref.v_ref, bf16[2,64,16384]{2,1,0:T(8,128)(2,1)} %all-gather.2.cloned.1.call-done.k_ref.v_ref), custom_call_target="tpu_custom_call" | custom-call | tf_op jit(solution)/shard_map/pallas_call | solution.py:112
  217.1 0.5 broadcast.82
  217.6 1.8 reduce.16
  219.4 0.9 reshape.125
  220.3 5.0 %all-to-all-start.3 = ((bf16[4,2,8192]{2,1,0:T(2,128)(2,1)}), bf16[4,2,8192]{2,1,0:T(2,128)(2,1)S(1)}, u32[]{:S(2)}, u32[]{:S(2)}) async-start(bf16[4,2,8192]{2,1,0:T(2,128)(2,1)} %reshape.125), calls=%async_computation.3 | async-start | bytes 262144 | tf_op jit(solution)/shard_map/all_to_all | solution.py:172
  225.3 1.7 fusion.31
  227.0 3.1 %all-to-all-done.3 = bf16[4,2,8192]{2,1,0:T(2,128)(2,1)S(1)} async-done(((bf16[4,2,8192]{2,1,0:T(2,128)(2,1)}), bf16[4,2,8192]{2,1,0:T(2,128)(2,1)S(1)}, u32[]{:S(2)}, u32[]{:S(2)}) %all-to-all-start.3) | async-done | bytes 131104 | tf_op jit(solution)/shard_map/all_to_all | solution.py:172
  230.1 0.3 reshape.126
  230.4 0.3 copy.54
  230.9 2.2 fusion
  233.1 0.2 fusion.3
  233.4 0.1 multiply_add_fusion
  233.4 17.5 %reduce-scatter.2.cloned.1.call-done = bf16[64,1024]{1,0:T(8,128)(2,1)} async-done(((bf16[256,1024]{1,0:T(8,128)(2,1)}), bf16[64,1024]{1,0:T(8,128)(2,1)}) %reduce-scatter.2.cloned.1.call-update) | async-done | bytes 131088 | tf_op jit(solution)/shard_map/reduce_scatter | solution.py:187
  250.9 1.0 add_convert_fusion
  252.0 0.6 convolution_convert_fusion
  252.6 6.8 %all_to_all.65 = bf16[4,32,768]{2,1,0:T(8,128)(2,1)S(1)} all-to-all(bf16[4,32,768]{2,1,0:T(8,128)(2,1)S(1)} %bitcast.78), channel_id=1, replica_groups=mesh['sb'=4,'sa'=16,'head'=4] {'head'}, dimensions={0} | all-to-all | bytes 393216 | tf_op jit(solution)/shard_map/all_to_all | solution.py:208
  259.3 0.7 copy.61
  (46 shorter events, 1.3 us)
Async XLA Ops:
  7.2 244.8 %copy-start = (bf16[1024,768]{1,0:T(8,128)(2,1)S(1)}, bf16[1024,768]{1,0:T(8,128)(2,1)}, u32[]{:S(2)}) copy-start(bf16[1024,768]{1,0:T(8,128)(2,1)} %param.22) | copy-start | bytes 4718596
  7.2 20.5 %copy-start.2 = (bf16[256,128]{1,0:T(8,128)(2,1)S(1)}, bf16[256,128]{1,0:T(8,128)(2,1)}, u32[]{:S(2)}) copy-start(bf16[256,128]{1,0:T(8,128)(2,1)} %param.17) | copy-start | bytes 196612
  9.0 9.7 %all-to-all-start.1 = ((bf16[256,4,64]{0,2,1:T(8,128)(2,1)}), bf16[256,4,64]{0,2,1:T(8,128)(2,1)S(1)}, u32[]{:S(2)}, u32[]{:S(2)}) async-start(bf16[256,4,64]{0,2,1:T(8,128)(2,1)} %bitcast.4), calls=%async_computation.1 | async-start | bytes 262144 | tf_op jit(solution)/shard_map/all_to_all | solution.py:164
  18.7 8.1 %all-to-all-start.2 = ((bf16[256,4,64]{0,2,1:T(8,128)(2,1)}), bf16[256,4,64]{0,2,1:T(8,128)(2,1)S(1)}, u32[]{:S(2)}, u32[]{:S(2)}) async-start(bf16[256,4,64]{0,2,1:T(8,128)(2,1)} %bitcast.9), calls=%async_computation.2 | async-start | bytes 262144 | tf_op jit(solution)/shard_map/all_to_all | solution.py:164
  22.0 163.0 %all-gather.2.cloned.1.call-start = ((), (), s32[]{:S(2)}) async-start(), calls=%async_computation.6 | async-start | bytes 4456448 | tf_op jit(solution)/shard_map/all_gather | solution.py:170
  28.0 11.6 %collective-permute-start = (f32[8,136,64]{1,2,0:T(8,128)S(1)}, f32[8,136,64]{1,2,0:T(8,128)S(1)}, u32[]{:S(2)}, u32[]{:S(2)}) collective-permute-start(f32[8,136,64]{1,2,0:T(8,128)S(1)} %pad_maximum_fusion), channel_id=1, source_target_pairs={{0,4},{4,8},{8,12},{12,16},{16,20},{20,24},{24,28},{28,32},{32,36}... | collective-permute-start | bytes 835592 | tf_op jit(solution)/shard_map/ppermute | solution.py:57
  39.7 15.8 %collective-permute-start.1 = (f32[8,136,64]{1,2,0:T(8,128)S(1)}, f32[8,136,64]{1,2,0:T(8,128)S(1)}, u32[]{:S(2)}, u32[]{:S(2)}) collective-permute-start(f32[8,136,64]{1,2,0:T(8,128)S(1)} %broadcast_select_fusion), channel_id=1, source_target_pairs={{0,4},{4,8},{8,12},{12,16},{16,20},{20,24},{24,28},{28,32},{32,36}... | collective-permute-start | bytes 835592 | tf_op jit(solution)/shard_map/ppermute | solution.py:57
  55.7 24.6 %collective-permute-start.2 = (f32[8,136,64]{1,2,0:T(8,128)S(1)}, f32[8,136,64]{1,2,0:T(8,128)S(1)}, u32[]{:S(2)}, u32[]{:S(2)}) collective-permute-start(f32[8,136,64]{1,2,0:T(8,128)S(1)} %maximum_select_fusion), channel_id=1, source_target_pairs={{0,8},{4,12},{8,16},{12,20},{16,24},{20,28},{24,32},{28,36},{32,40... | collective-permute-start | bytes 835592 | tf_op jit(solution)/shard_map/ppermute | solution.py:57
  80.6 17.7 %collective-permute-start.3 = (f32[8,136,64]{1,2,0:T(8,128)S(1)}, f32[8,136,64]{1,2,0:T(8,128)S(1)}, u32[]{:S(2)}, u32[]{:S(2)}) collective-permute-start(f32[8,136,64]{1,2,0:T(8,128)S(1)} %maximum_select_fusion.1), channel_id=1, source_target_pairs={{0,16},{4,20},{8,24},{12,28},{16,32},{20,36},{24,40},{28,44},{32,4... | collective-permute-start | bytes 835592 | tf_op jit(solution)/shard_map/ppermute | solution.py:57
  98.5 40.2 %collective-permute-start.4 = (f32[8,136,64]{1,2,0:T(8,128)S(1)}, f32[8,136,64]{1,2,0:T(8,128)S(1)}, u32[]{:S(2)}, u32[]{:S(2)}) collective-permute-start(f32[8,136,64]{1,2,0:T(8,128)S(1)} %maximum_select_fusion.2), channel_id=1, source_target_pairs={{0,32},{4,36},{8,40},{12,44},{16,48},{20,52},{24,56},{28,60},{32,6... | collective-permute-start | bytes 835592 | tf_op jit(solution)/shard_map/ppermute | solution.py:57
  138.9 36.7 %copy-start.3 = (bf16[256,128]{1,0:T(8,128)(2,1)S(1)}, bf16[256,128]{1,0:T(8,128)(2,1)}, u32[]{:S(2)}) copy-start(bf16[256,128]{1,0:T(8,128)(2,1)} %param.18) | copy-start | bytes 196612
  138.9 28.9 %collective-permute-start.5 = (f32[8,136,64]{1,2,0:T(8,128)S(1)}, f32[8,136,64]{1,2,0:T(8,128)S(1)}, u32[]{:S(2)}, u32[]{:S(2)}) collective-permute-start(f32[8,136,64]{1,2,0:T(8,128)S(1)} %maximum_select_fusion.3), channel_id=1, source_target_pairs={{0,64},{4,68},{8,72},{12,76},{16,80},{20,84},{24,88},{28,92},{32,9... | collective-permute-start | bytes 835592 | tf_op jit(solution)/shard_map/ppermute | solution.py:57
  159.5 16.3 %all-to-all-start = ((bf16[256,4,64]{0,2,1:T(8,128)(2,1)}), bf16[256,4,64]{0,2,1:T(8,128)(2,1)S(1)}, u32[]{:S(2)}, u32[]{:S(2)}) async-start(bf16[256,4,64]{0,2,1:T(8,128)(2,1)} %bitcast), calls=%async_computation | async-start | bytes 262144 | tf_op jit(solution)/shard_map/all_to_all | solution.py:164
  168.0 15.8 %collective-permute-start.6 = (f32[8,136,64]{1,2,0:T(8,128)S(1)}, f32[8,136,64]{1,2,0:T(8,128)S(1)}, u32[]{:S(2)}, u32[]{:S(2)}) collective-permute-start(f32[8,136,64]{1,2,0:T(8,128)S(1)} %maximum_select_fusion.4), channel_id=1, source_target_pairs={{0,128},{4,132},{8,136},{12,140},{16,144},{20,148},{24,152},{28,15... | collective-permute-start | bytes 835592 | tf_op jit(solution)/shard_map/ppermute | solution.py:57
  220.3 9.8 %all-to-all-start.3 = ((bf16[4,2,8192]{2,1,0:T(2,128)(2,1)}), bf16[4,2,8192]{2,1,0:T(2,128)(2,1)S(1)}, u32[]{:S(2)}, u32[]{:S(2)}) async-start(bf16[4,2,8192]{2,1,0:T(2,128)(2,1)} %reshape.125), calls=%async_computation.3 | async-start | bytes 262144 | tf_op jit(solution)/shard_map/all_to_all | solution.py:172
  225.3 25.7 %reduce-scatter.2.cloned.1.call-start = ((), (), s32[]{:S(2)}) async-start(), calls=%async_computation.7 | async-start | bytes 655360 | tf_op jit(solution)/shard_map/reduce_scatter | solution.py:187
  230.4 2.6 copy-start.4
  251.9 8.1 %copy-start.1 = (bf16[64,1024]{1,0:T(8,128)(2,1)}, bf16[64,1024]{1,0:T(8,128)(2,1)S(1)}, u32[]{:S(2)}) copy-start(bf16[64,1024]{1,0:T(8,128)(2,1)S(1)} %add_convert_fusion) | copy-start | bytes 393220
Sparse Core Ops, SparseCore 0:
  27.8 115.8 all-gather.1
  233.2 17.7 reduce-scatter.1

commit v9 on v7

--- a/solution.py
+++ b/solution.py
@@ -69,8 +69,8 @@
     return state
 
 
-def flash_one_head(query_rows, pair_t, key_block=4096):
-    row_count, width = query_rows.shape
+def flash_one_head_t(query_t, pair_t, key_block=4096):
+    width, row_count = query_t.shape
     key_count = pair_t.shape[2]
     steps = key_count // key_block
     scale = 1.0 / math.sqrt(width)
@@ -84,17 +84,16 @@
             sum_ref[...] = jnp.zeros(sum_ref.shape, jnp.float32)
             acc_ref[...] = jnp.zeros(acc_ref.shape, jnp.float32)
 
-        scores = jnp.dot(q_ref[...], k_ref[...], preferred_element_type=jnp.float32) * scale
+        scores = lax.dot_general(
+            k_ref[...], q_ref[...], (((0,), (0,)), ((), ())), preferred_element_type=jnp.float32
+        ) * scale
         old_top = top_ref[...]
-        new_top = jnp.maximum(old_top, jnp.max(scores, axis=1, keepdims=True))
+        new_top = jnp.maximum(old_top, jnp.max(scores, axis=0, keepdims=True))
         shrink = jnp.exp(old_top - new_top)
         raised = jnp.exp(scores - new_top)
-        sum_ref[...] = sum_ref[...] * shrink + jnp.sum(raised, axis=1, keepdims=True)
-        acc_ref[...] = acc_ref[...] * shrink + lax.dot_general(
-            raised.astype(jnp.bfloat16),
-            v_ref[...],
-            (((1,), (1,)), ((), ())),
-            preferred_element_type=jnp.float32,
+        sum_ref[...] = sum_ref[...] * shrink + jnp.sum(raised, axis=0, keepdims=True)
+        acc_ref[...] = acc_ref[...] * shrink + jnp.dot(
+            v_ref[...], raised.astype(jnp.bfloat16), preferred_element_type=jnp.float32
         )
         top_ref[...] = new_top
 
@@ -104,21 +103,21 @@
 
     return pl.pallas_call(
         kernel,
-        out_shape=jax.ShapeDtypeStruct((row_count, width), jnp.bfloat16),
+        out_shape=jax.ShapeDtypeStruct((width, row_count), jnp.bfloat16),
         grid=(steps,),
         in_specs=[
-            pl.BlockSpec((row_count, width), lambda j: (0, 0)),
+            pl.BlockSpec((width, row_count), lambda j: (0, 0)),
             pl.BlockSpec((None, width, key_block), lambda j: (0, 0, j)),
             pl.BlockSpec((None, width, key_block), lambda j: (1, 0, j)),
         ],
-        out_specs=pl.BlockSpec((row_count, width), lambda j: (0, 0)),
+        out_specs=pl.BlockSpec((width, row_count), lambda j: (0, 0)),
         scratch_shapes=[
-            pltpu.VMEM((row_count, 1), jnp.float32),
-            pltpu.VMEM((row_count, 1), jnp.float32),
-            pltpu.VMEM((row_count, width), jnp.float32),
+            pltpu.VMEM((1, row_count), jnp.float32),
+            pltpu.VMEM((1, row_count), jnp.float32),
+            pltpu.VMEM((width, row_count), jnp.float32),
         ],
         compiler_params=pltpu.CompilerParams(dimension_semantics=("arbitrary",)),
-    )(query_rows, pair_t, pair_t)
+    )(query_t, pair_t, pair_t)
 
 
 def slot_rank(owners_here, owner_count, group_rows):
@@ -161,7 +160,7 @@
         [spread(key_rows).reshape(-1, HDIM).T, spread(values).reshape(-1, HDIM).T]
     )
     gathered = lax.all_gather(pair_t, "sa", axis=2, tiled=True)
-    attended_one = flash_one_head(query_heads.reshape(-1, HDIM), gathered)
+    attended_one = flash_one_head_t(query_heads.reshape(-1, HDIM).T, gathered).T
     attended = lax.all_to_all(
         attended_one.reshape(-1, 1, HDIM), "sb", split_axis=0, concat_axis=1, tiled=True
     ).reshape(row_count, head_count * HDIM)
@@ -177,15 +176,18 @@
     width_out = gauss_project.shape[1]
     slot_count = owner_count * capacity
     slot_ids = jnp.arange(slot_count, dtype=jnp.float32)
-    update = lax.psum_scatter(
-        (
-            jnp.dot(attended, attn_project, preferred_element_type=jnp.float32)
-            + jnp.dot(ssm_mix, ssm_project, preferred_element_type=jnp.float32)
-        ).astype(jnp.bfloat16),
+    partial = (
+        jnp.dot(attended, attn_project, preferred_element_type=jnp.float32)
+        + jnp.dot(ssm_mix, ssm_project, preferred_element_type=jnp.float32)
+    ).astype(jnp.bfloat16)
+    pieces = lax.all_to_all(
+        partial.reshape(owner_count, sub_rows, partial.shape[1]),
         "head",
-        scatter_dimension=0,
+        split_axis=0,
+        concat_axis=0,
         tiled=True,
-    ).astype(jnp.float32)
+    )
+    update = jnp.sum(pieces.astype(jnp.float32), axis=0)
     own_tokens = lax.dynamic_slice_in_dim(tokens, own_index * sub_rows, sub_rows, 0)
     block_out = (own_tokens.astype(jnp.float32) + update).astype(jnp.bfloat16)
     gaussians = jnp.dot(block_out, gauss_project, preferred_element_type=jnp.float32).astype(

time: 231 us -> 224 us (0.970)
  waiting for transfers between devices: 44.9 us -> 38.6 us
  Pallas kernels: 32.1 us -> 29.4 us
    reduce_scatter x1 -> x0, waiting for transfers between devices: 20.2 us -> none  [per_device(): lax.psum_scatter((jnp.dot(attended, attn_project, preferred_element_type=...]
    all_to_all x0 -> x1, starting transfers between devices: none -> 7.82 us  [per_device(): lax.all_to_all(partial.reshape(owner_count, sub_rows, partial.shape[1]),...]
    all_to_all x0 -> x1, waiting for transfers between devices: none -> 7.46 us  [per_device(): lax.all_to_all(partial.reshape(owner_count, sub_rows, partial.shape[1]),...]
    ppermute x13, starting transfers between devices: 82.5 us -> 75.2 us  [shifted(): return jax.tree.map(lambda part: lax.ppermute(part, axis, pairs), tree)]
    ppermute x13, waiting for transfers between devices: 7.51 us -> 11.4 us  [shifted(): return jax.tree.map(lambda part: lax.ppermute(part, axis, pairs), tree)]
    pallas_call x1, Pallas kernels: 32.1 us -> 29.4 us  [flash_one_head_t(): pl.pallas_call(kernel, out_shape=jax.ShapeDtypeStruct((width, row_count),...]
    all_gather x1, waiting for transfers between devices: 6.19 us -> 8.78 us  [per_device(): gathered = lax.all_gather(pair_t, 'sa', axis=2, tiled=True)]
    unnamed x25 -> x27, local copies, waits for them, and re-layouts: 6.32 us -> 7.17 us
where the time goes in v9:
time: 224 us; the launch traced here: 222 us
  starting transfers between devices  112 us (50%)
  waiting for transfers between devices  38.6 us (17%)
  Pallas kernels  29.4 us (13%)
  between operations  14.4 us (6%)
  local copies, waits for them, and re-layouts  8.83 us (4%)
  blocking collectives  7.9 us (4%)
  matrix products  6.05 us (3%)
  other arithmetic  4.82 us (2%)
    ppermute x13, starting transfers between devices, shifted(): return jax.tree.map(lambda part: lax.ppermute(part, axis, pairs), tree)  75.2 us
    pallas_call x1, Pallas kernels, flash_one_head_t(): pl.pallas_call(kernel, out_shape=jax.ShapeDtypeStruct((width, row_count),...  29.4 us
    all_to_all x3, starting transfers between devices, spread(): return lax.all_to_all(split, 'sb', split_axis=1, concat_axis=0, tiled=True)  20.1 us
    ppermute x13, waiting for transfers between devices, shifted(): return jax.tree.map(lambda part: lax.ppermute(part, axis, pairs), tree)  11.4 us
    all_to_all x1, starting transfers between devices, per_device(): lax.all_to_all(attended_one.reshape(-1, 1, HDIM), 'sb', split_axis=0, con...  9.32 us
    all_gather x1, waiting for transfers between devices, per_device(): gathered = lax.all_gather(pair_t, 'sa', axis=2, tiled=True)  8.78 us
    all_to_all x1, blocking collectives, per_device(): lax.all_to_all(packed, 'head', split_axis=0, concat_axis=0, tiled=True)  7.9 us
    all_to_all x1, starting transfers between devices, per_device(): lax.all_to_all(partial.reshape(owner_count, sub_rows, partial.shape[1]),...  7.82 us
  transfers between devices with their start and end apart: 19, of which 12 were waited for; matrix products, arithmetic and copies ran while one was open for 4% of the time, Pallas kernels for 0%

profile of v9, /device:TPU:1, one launch (start us, length us, event | category | flops | bytes accessed | tf_op | source)
XLA Modules:
  0.0 222.5 jit_solution(13084127194017919221)
XLA Ops:
  7.2 1.8 copy.49
  9.0 4.8 %all-to-all-start.1 = ((bf16[256,4,64]{0,2,1:T(8,128)(2,1)}), bf16[256,4,64]{0,2,1:T(8,128)(2,1)S(1)}, u32[]{:S(2)}, u32[]{:S(2)}) async-start(bf16[256,4,64]{0,2,1:T(8,128)(2,1)} %bitcast.4), calls=%async_computation.1 | async-start | bytes 262144 | tf_op jit(solution)/shard_map/all_to_all | solution.py:156
  13.8 1.7 copy.51
  15.5 3.2 %all-to-all-done.1 = bf16[256,4,64]{0,2,1:T(8,128)(2,1)S(1)} async-done(((bf16[256,4,64]{0,2,1:T(8,128)(2,1)}), bf16[256,4,64]{0,2,1:T(8,128)(2,1)S(1)}, u32[]{:S(2)}, u32[]{:S(2)}) %all-to-all-start.1) | async-done | bytes 131104 | tf_op jit(solution)/shard_map/all_to_all | solution.py:156
  18.7 3.3 %all-to-all-start.2 = ((bf16[256,4,64]{0,2,1:T(8,128)(2,1)}), bf16[256,4,64]{0,2,1:T(8,128)(2,1)S(1)}, u32[]{:S(2)}, u32[]{:S(2)}) async-start(bf16[256,4,64]{0,2,1:T(8,128)(2,1)} %bitcast.9), calls=%async_computation.2 | async-start | bytes 262144 | tf_op jit(solution)/shard_map/all_to_all | solution.py:156
  22.0 0.1 copy.50
  22.2 4.6 %all-to-all-done.2 = bf16[256,4,64]{0,2,1:T(8,128)(2,1)S(1)} async-done(((bf16[256,4,64]{0,2,1:T(8,128)(2,1)}), bf16[256,4,64]{0,2,1:T(8,128)(2,1)S(1)}, u32[]{:S(2)}, u32[]{:S(2)}) %all-to-all-start.2) | async-done | bytes 131104 | tf_op jit(solution)/shard_map/all_to_all | solution.py:156
  26.8 0.1 copy.52
  26.9 0.7 pad_maximum_fusion
  27.7 0.6 reduce-window.6
  28.3 0.2 slice_reduce_fusion
  28.5 0.1 copy.56
  28.7 0.2 slice_reduce_fusion.1
  29.0 0.2 convolution_bitcast_fusion.2
  29.2 3.6 %collective-permute-start.6 = (f32[8,128,64]{1,2,0:T(8,128)S(1)}, f32[8,128,64]{1,2,0:T(8,128)S(1)}, u32[]{:S(2)}, u32[]{:S(2)}) collective-permute-start(f32[8,128,64]{1,2,0:T(8,128)S(1)} %convolution_bitcast_fusion.2), channel_id=1, source_target_pairs={{0,4},{4,8},{8,12},{12,16},{16,20},{20,24},{24,28},{28,32},{32,36}... | collective-permute-start | bytes 786440 | tf_op jit(solution)/shard_map/ppermute | solution.py:54
  32.8 3.3 %collective-permute-done.6 = f32[8,128,64]{1,2,0:T(8,128)S(1)} collective-permute-done((f32[8,128,64]{1,2,0:T(8,128)S(1)}, f32[8,128,64]{1,2,0:T(8,128)S(1)}, u32[]{:S(2)}, u32[]{:S(2)}) %collective-permute-start.6) | collective-permute-done | bytes 262176 | tf_op jit(solution)/shard_map/ppermute | solution.py:54
  36.1 3.8 %collective-permute-start.7 = (f32[8,128,64]{1,2,0:T(8,128)S(1)}, f32[8,128,64]{1,2,0:T(8,128)S(1)}, u32[]{:S(2)}, u32[]{:S(2)}) collective-permute-start(f32[8,128,64]{1,2,0:T(8,128)S(1)} %broadcast_select_fusion), channel_id=1, source_target_pairs={{0,4},{4,8},{8,12},{12,16},{16,20},{20,24},{24,28},{28,32},{32,36}... | collective-permute-start | bytes 786440 | tf_op jit(solution)/shard_map/ppermute | solution.py:54
  39.9 3.5 %collective-permute-start = (f32[8]{0:T(128)S(1)}, f32[8]{0:T(128)S(1)}, u32[]{:S(2)}, u32[]{:S(2)}) collective-permute-start(f32[8]{0:T(128)S(1)} %exp.13), channel_id=1, source_target_pairs={{0,4},{4,8},{8,12},{12,16},{16,20},{20,24},{24,28},{28,32},{32,36}... | collective-permute-start | bytes 104 | tf_op jit(solution)/shard_map/ppermute | solution.py:54
  43.4 0.7 collective-permute-done
  44.2 0.1 add_select_fusion.5
  44.3 7.3 %collective-permute-start.8 = (f32[8,128,64]{1,2,0:T(8,128)S(1)}, f32[8,128,64]{1,2,0:T(8,128)S(1)}, u32[]{:S(2)}, u32[]{:S(2)}) collective-permute-start(f32[8,128,64]{1,2,0:T(8,128)S(1)} %add_select_fusion.5), channel_id=1, source_target_pairs={{0,8},{4,12},{8,16},{12,20},{16,24},{20,28},{24,32},{28,36},{32,40... | collective-permute-start | bytes 786440 | tf_op jit(solution)/shard_map/ppermute | solution.py:54
  51.6 0.8 copy.47
  52.4 12.0 %all-to-all-start = ((bf16[256,4,64]{0,2,1:T(8,128)(2,1)}), bf16[256,4,64]{0,2,1:T(8,128)(2,1)S(1)}, u32[]{:S(2)}, u32[]{:S(2)}) async-start(bf16[256,4,64]{0,2,1:T(8,128)(2,1)} %bitcast), calls=%async_computation | async-start | bytes 262144 | tf_op jit(solution)/shard_map/all_to_all | solution.py:156
  64.3 1.3 collective-permute-start.1
  65.6 0.7 collective-permute-done.1
  66.3 0.1 add_select_fusion.4
  66.4 7.6 %collective-permute-start.9 = (f32[8,128,64]{1,2,0:T(8,128)S(1)}, f32[8,128,64]{1,2,0:T(8,128)S(1)}, u32[]{:S(2)}, u32[]{:S(2)}) collective-permute-start(f32[8,128,64]{1,2,0:T(8,128)S(1)} %add_select_fusion.4), channel_id=1, source_target_pairs={{0,16},{4,20},{8,24},{12,28},{16,32},{20,36},{24,40},{28,44},{32,4... | collective-permute-start | bytes 786440 | tf_op jit(solution)/shard_map/ppermute | solution.py:54
  74.1 0.2 fusion.28
  74.3 2.5 %collective-permute-start.2 = (f32[8]{0:T(128)S(1)}, f32[8]{0:T(128)S(1)}, u32[]{:S(2)}, u32[]{:S(2)}) collective-permute-start(f32[8]{0:T(128)S(1)} %broadcast_select_fusion.1), channel_id=1, source_target_pairs={{0,8},{4,12},{8,16},{12,20},{16,24},{20,28},{24,32},{28,36},{32,40... | collective-permute-start | bytes 104 | tf_op jit(solution)/shard_map/ppermute | solution.py:54
  76.8 3.6 %collective-permute-done.2 = f32[8]{0:T(128)S(1)} collective-permute-done((f32[8]{0:T(128)S(1)}, f32[8]{0:T(128)S(1)}, u32[]{:S(2)}, u32[]{:S(2)}) %collective-permute-start.2) | collective-permute-done | bytes 64 | tf_op jit(solution)/shard_map/ppermute | solution.py:54
  80.4 0.1 add_select_fusion.3
  80.5 9.6 %collective-permute-start.10 = (f32[8,128,64]{1,2,0:T(8,128)S(1)}, f32[8,128,64]{1,2,0:T(8,128)S(1)}, u32[]{:S(2)}, u32[]{:S(2)}) collective-permute-start(f32[8,128,64]{1,2,0:T(8,128)S(1)} %add_select_fusion.3), channel_id=1, source_target_pairs={{0,32},{4,36},{8,40},{12,44},{16,48},{20,52},{24,56},{28,60},{32,6... | collective-permute-start | bytes 786440 | tf_op jit(solution)/shard_map/ppermute | solution.py:54
  90.2 11.5 %collective-permute-start.3 = (f32[8]{0:T(128)S(1)}, f32[8]{0:T(128)S(1)}, u32[]{:S(2)}, u32[]{:S(2)}) collective-permute-start(f32[8]{0:T(128)S(1)} %broadcast_select_fusion.3), channel_id=1, source_target_pairs={{0,16},{4,20},{8,24},{12,28},{16,32},{20,36},{24,40},{28,44},{32,4... | collective-permute-start | bytes 104 | tf_op jit(solution)/shard_map/ppermute | solution.py:54
  101.7 0.7 collective-permute-done.3
  102.5 12.4 %collective-permute-start.11 = (f32[8,128,64]{1,2,0:T(8,128)S(1)}, f32[8,128,64]{1,2,0:T(8,128)S(1)}, u32[]{:S(2)}, u32[]{:S(2)}) collective-permute-start(f32[8,128,64]{1,2,0:T(8,128)S(1)} %add_select_fusion.2), channel_id=1, source_target_pairs={{0,64},{4,68},{8,72},{12,76},{16,80},{20,84},{24,88},{28,92},{32,9... | collective-permute-start | bytes 786440 | tf_op jit(solution)/shard_map/ppermute | solution.py:54
  114.9 0.7 convolution_bitcast_fusion.1
  115.6 5.5 %collective-permute-start.4 = (f32[8]{0:T(128)S(1)}, f32[8]{0:T(128)S(1)}, u32[]{:S(2)}, u32[]{:S(2)}) collective-permute-start(f32[8]{0:T(128)S(1)} %broadcast_select_fusion.4), channel_id=1, source_target_pairs={{0,32},{4,36},{8,40},{12,44},{16,48},{20,52},{24,56},{28,60},{32,6... | collective-permute-start | bytes 104 | tf_op jit(solution)/shard_map/ppermute | solution.py:54
  121.1 0.7 collective-permute-done.4
  121.8 0.1 add_select_fusion.1
  122.0 4.8 %collective-permute-start.12 = (f32[8,128,64]{1,2,0:T(8,128)S(1)}, f32[8,128,64]{1,2,0:T(8,128)S(1)}, u32[]{:S(2)}, u32[]{:S(2)}) collective-permute-start(f32[8,128,64]{1,2,0:T(8,128)S(1)} %add_select_fusion.1), channel_id=1, source_target_pairs={{0,128},{4,132},{8,136},{12,140},{16,144},{20,148},{24,152},{28,15... | collective-permute-start | bytes 786440 | tf_op jit(solution)/shard_map/ppermute | solution.py:54
  126.8 1.6 collective-permute-start.5
  128.4 1.7 collective-permute-done.5
  130.1 0.1 copy.48
  130.2 0.7 copy.57
  130.9 0.3 multiply_reduce_fusion
  131.3 8.8 %all-gather.2.cloned.1.call-done.k_ref.v_ref = bf16[2,64,16384]{2,1,0:T(8,128)(2,1)} async-done(((bf16[2,64,1024]{2,1,0:T(8,128)(2,1)}), bf16[2,64,16384]{2,1,0:T(8,128)(2,1)}) %all-gather.2.cloned.1.call-update) | async-done | bytes 4194320 | tf_op jit(solution)/shard_map/all_gather | solution.py:162
  140.1 29.4 %shard_map.131 = bf16[64,1024]{1,0:T(8,128)(2,1)} custom-call(bf16[64,1024]{1,0:T(8,128)(2,1)} %bitcast.89, bf16[2,64,16384]{2,1,0:T(8,128)(2,1)} %all-gather.2.cloned.1.call-done.k_ref.v_ref, bf16[2,64,16384]{2,1,0:T(8,128)(2,1)} %all-gather.2.cloned.1.call-done.k_ref.v_ref), custom_call_target="tpu_custom_call" | custom-call | tf_op jit(solution)/shard_map/pallas_call | solution.py:104
  169.5 0.5 broadcast.86
  170.0 1.6 reduce.4
  171.6 0.2 copy.60
  171.7 0.9 reshape.124
  172.6 9.3 %all-to-all-start.3 = ((bf16[4,2,8192]{2,1,0:T(2,128)(2,1)}), bf16[4,2,8192]{2,1,0:T(2,128)(2,1)S(1)}, u32[]{:S(2)}, u32[]{:S(2)}) async-start(bf16[4,2,8192]{2,1,0:T(2,128)(2,1)} %reshape.124), calls=%async_computation.3 | async-start | bytes 262144 | tf_op jit(solution)/shard_map/all_to_all | solution.py:164
  182.0 1.7 fusion.29
  183.7 3.1 %all-to-all-done.3 = bf16[4,2,8192]{2,1,0:T(2,128)(2,1)S(1)} async-done(((bf16[4,2,8192]{2,1,0:T(2,128)(2,1)}), bf16[4,2,8192]{2,1,0:T(2,128)(2,1)S(1)}, u32[]{:S(2)}, u32[]{:S(2)}) %all-to-all-start.3) | async-done | bytes 131104 | tf_op jit(solution)/shard_map/all_to_all | solution.py:164
  186.8 0.3 reshape.125
  187.1 0.3 copy.54
  187.6 2.2 fusion
  189.7 7.8 %all-to-all-start.4 = ((bf16[4,64,1024]{2,1,0:T(8,128)(2,1)}), bf16[4,64,1024]{2,1,0:T(8,128)(2,1)S(1)}, u32[]{:S(2)}, u32[]{:S(2)}) async-start(bf16[4,64,1024]{2,1,0:T(8,128)(2,1)} %bitcast.29), calls=%async_computation.4 | async-start | bytes 1048576 | tf_op jit(solution)/shard_map/all_to_all | solution.py:183
  197.6 0.2 fusion.3
  197.9 7.5 %all-to-all-done.4 = bf16[4,64,1024]{2,1,0:T(8,128)(2,1)S(1)} async-done(((bf16[4,64,1024]{2,1,0:T(8,128)(2,1)}), bf16[4,64,1024]{2,1,0:T(8,128)(2,1)S(1)}, u32[]{:S(2)}, u32[]{:S(2)}) %all-to-all-start.4) | async-done | bytes 524320 | tf_op jit(solution)/shard_map/all_to_all | solution.py:183
  205.5 0.9 add_convert_fusion
  206.4 0.6 convolution_convert_fusion
  207.1 7.9 %all_to_all.70 = bf16[4,32,768]{2,1,0:T(8,128)(2,1)S(1)} all-to-all(bf16[4,32,768]{2,1,0:T(8,128)(2,1)S(1)} %bitcast.87), channel_id=1, replica_groups=mesh['sb'=4,'sa'=16,'head'=4] {'head'}, dimensions={0} | all-to-all | bytes 393216 | tf_op jit(solution)/shard_map/all_to_all | solution.py:203
  215.0 0.7 copy.62
  (50 shorter events, 0.9 us)
Async XLA Ops:
  7.2 199.3 %copy-start = (bf16[1024,768]{1,0:T(8,128)(2,1)S(1)}, bf16[1024,768]{1,0:T(8,128)(2,1)}, u32[]{:S(2)}) copy-start(bf16[1024,768]{1,0:T(8,128)(2,1)} %param.22) | copy-start | bytes 4718596
  7.2 20.5 %copy-start.6 = (f32[8,256]{1,0:T(8,128)S(1)}, f32[8,256]{1,0:T(8,128)}, u32[]{:S(2)}) copy-start(f32[8,256]{1,0:T(8,128)} %param.19) | copy-start | bytes 24580
  7.2 21.3 %copy-start.2 = (bf16[256,512]{1,0:T(8,128)(2,1)S(1)}, bf16[256,512]{1,0:T(8,128)(2,1)}, u32[]{:S(2)}) copy-start(bf16[256,512]{1,0:T(8,128)(2,1)} %param.16) | copy-start | bytes 786436
  7.2 21.8 %copy-start.3 = (bf16[256,128]{1,0:T(8,128)(2,1)S(1)}, bf16[256,128]{1,0:T(8,128)(2,1)}, u32[]{:S(2)}) copy-start(bf16[256,128]{1,0:T(8,128)(2,1)} %param.17) | copy-start | bytes 196612
  9.0 9.7 %all-to-all-start.1 = ((bf16[256,4,64]{0,2,1:T(8,128)(2,1)}), bf16[256,4,64]{0,2,1:T(8,128)(2,1)S(1)}, u32[]{:S(2)}, u32[]{:S(2)}) async-start(bf16[256,4,64]{0,2,1:T(8,128)(2,1)} %bitcast.4), calls=%async_computation.1 | async-start | bytes 262144 | tf_op jit(solution)/shard_map/all_to_all | solution.py:156
  18.7 8.1 %all-to-all-start.2 = ((bf16[256,4,64]{0,2,1:T(8,128)(2,1)}), bf16[256,4,64]{0,2,1:T(8,128)(2,1)S(1)}, u32[]{:S(2)}, u32[]{:S(2)}) async-start(bf16[256,4,64]{0,2,1:T(8,128)(2,1)} %bitcast.9), calls=%async_computation.2 | async-start | bytes 262144 | tf_op jit(solution)/shard_map/all_to_all | solution.py:156
  22.0 118.1 %all-gather.2.cloned.1.call-start = ((), (), s32[]{:S(2)}) async-start(), calls=%async_computation.6 | async-start | bytes 4456448 | tf_op jit(solution)/shard_map/all_gather | solution.py:162
  22.2 29.4 %copy-start.5 = (bf16[256,256]{1,0:T(8,128)(2,1)S(1)}, bf16[256,256]{1,0:T(8,128)(2,1)}, u32[]{:S(2)}) copy-start(bf16[256,256]{1,0:T(8,128)(2,1)} %param.13) | copy-start | bytes 393220
  27.6 46.4 %copy-start.4 = (bf16[256,128]{1,0:T(8,128)(2,1)S(1)}, bf16[256,128]{1,0:T(8,128)(2,1)}, u32[]{:S(2)}) copy-start(bf16[256,128]{1,0:T(8,128)(2,1)} %param.18) | copy-start | bytes 196612
  29.2 6.8 %collective-permute-start.6 = (f32[8,128,64]{1,2,0:T(8,128)S(1)}, f32[8,128,64]{1,2,0:T(8,128)S(1)}, u32[]{:S(2)}, u32[]{:S(2)}) collective-permute-start(f32[8,128,64]{1,2,0:T(8,128)S(1)} %convolution_bitcast_fusion.2), channel_id=1, source_target_pairs={{0,4},{4,8},{8,12},{12,16},{16,20},{20,24},{24,28},{28,32},{32,36}... | collective-permute-start | bytes 786440 | tf_op jit(solution)/shard_map/ppermute | solution.py:54
  36.1 8.1 %collective-permute-start.7 = (f32[8,128,64]{1,2,0:T(8,128)S(1)}, f32[8,128,64]{1,2,0:T(8,128)S(1)}, u32[]{:S(2)}, u32[]{:S(2)}) collective-permute-start(f32[8,128,64]{1,2,0:T(8,128)S(1)} %broadcast_select_fusion), channel_id=1, source_target_pairs={{0,4},{4,8},{8,12},{12,16},{16,20},{20,24},{24,28},{28,32},{32,36}... | collective-permute-start | bytes 786440 | tf_op jit(solution)/shard_map/ppermute | solution.py:54
  39.9 4.2 %collective-permute-start = (f32[8]{0:T(128)S(1)}, f32[8]{0:T(128)S(1)}, u32[]{:S(2)}, u32[]{:S(2)}) collective-permute-start(f32[8]{0:T(128)S(1)} %exp.13), channel_id=1, source_target_pairs={{0,4},{4,8},{8,12},{12,16},{16,20},{20,24},{24,28},{28,32},{32,36}... | collective-permute-start | bytes 104 | tf_op jit(solution)/shard_map/ppermute | solution.py:54
  44.3 22.1 %collective-permute-start.8 = (f32[8,128,64]{1,2,0:T(8,128)S(1)}, f32[8,128,64]{1,2,0:T(8,128)S(1)}, u32[]{:S(2)}, u32[]{:S(2)}) collective-permute-start(f32[8,128,64]{1,2,0:T(8,128)S(1)} %add_select_fusion.5), channel_id=1, source_target_pairs={{0,8},{4,12},{8,16},{12,20},{16,24},{20,28},{24,32},{28,36},{32,40... | collective-permute-start | bytes 786440 | tf_op jit(solution)/shard_map/ppermute | solution.py:54
  52.4 77.7 %all-to-all-start = ((bf16[256,4,64]{0,2,1:T(8,128)(2,1)}), bf16[256,4,64]{0,2,1:T(8,128)(2,1)S(1)}, u32[]{:S(2)}, u32[]{:S(2)}) async-start(bf16[256,4,64]{0,2,1:T(8,128)(2,1)} %bitcast), calls=%async_computation | async-start | bytes 262144 | tf_op jit(solution)/shard_map/all_to_all | solution.py:156
  64.3 2.0 collective-permute-start.1
  66.4 14.0 %collective-permute-start.9 = (f32[8,128,64]{1,2,0:T(8,128)S(1)}, f32[8,128,64]{1,2,0:T(8,128)S(1)}, u32[]{:S(2)}, u32[]{:S(2)}) collective-permute-start(f32[8,128,64]{1,2,0:T(8,128)S(1)} %add_select_fusion.4), channel_id=1, source_target_pairs={{0,16},{4,20},{8,24},{12,28},{16,32},{20,36},{24,40},{28,44},{32,4... | collective-permute-start | bytes 786440 | tf_op jit(solution)/shard_map/ppermute | solution.py:54
  74.3 6.1 %collective-permute-start.2 = (f32[8]{0:T(128)S(1)}, f32[8]{0:T(128)S(1)}, u32[]{:S(2)}, u32[]{:S(2)}) collective-permute-start(f32[8]{0:T(128)S(1)} %broadcast_select_fusion.1), channel_id=1, source_target_pairs={{0,8},{4,12},{8,16},{12,20},{16,24},{20,28},{24,32},{28,36},{32,40... | collective-permute-start | bytes 104 | tf_op jit(solution)/shard_map/ppermute | solution.py:54
  80.5 21.9 %collective-permute-start.10 = (f32[8,128,64]{1,2,0:T(8,128)S(1)}, f32[8,128,64]{1,2,0:T(8,128)S(1)}, u32[]{:S(2)}, u32[]{:S(2)}) collective-permute-start(f32[8,128,64]{1,2,0:T(8,128)S(1)} %add_select_fusion.3), channel_id=1, source_target_pairs={{0,32},{4,36},{8,40},{12,44},{16,48},{20,52},{24,56},{28,60},{32,6... | collective-permute-start | bytes 786440 | tf_op jit(solution)/shard_map/ppermute | solution.py:54
  90.2 12.2 %collective-permute-start.3 = (f32[8]{0:T(128)S(1)}, f32[8]{0:T(128)S(1)}, u32[]{:S(2)}, u32[]{:S(2)}) collective-permute-start(f32[8]{0:T(128)S(1)} %broadcast_select_fusion.3), channel_id=1, source_target_pairs={{0,16},{4,20},{8,24},{12,28},{16,32},{20,36},{24,40},{28,44},{32,4... | collective-permute-start | bytes 104 | tf_op jit(solution)/shard_map/ppermute | solution.py:54
  102.5 19.3 %collective-permute-start.11 = (f32[8,128,64]{1,2,0:T(8,128)S(1)}, f32[8,128,64]{1,2,0:T(8,128)S(1)}, u32[]{:S(2)}, u32[]{:S(2)}) collective-permute-start(f32[8,128,64]{1,2,0:T(8,128)S(1)} %add_select_fusion.2), channel_id=1, source_target_pairs={{0,64},{4,68},{8,72},{12,76},{16,80},{20,84},{24,88},{28,92},{32,9... | collective-permute-start | bytes 786440 | tf_op jit(solution)/shard_map/ppermute | solution.py:54
  115.6 6.3 %collective-permute-start.4 = (f32[8]{0:T(128)S(1)}, f32[8]{0:T(128)S(1)}, u32[]{:S(2)}, u32[]{:S(2)}) collective-permute-start(f32[8]{0:T(128)S(1)} %broadcast_select_fusion.4), channel_id=1, source_target_pairs={{0,32},{4,36},{8,40},{12,44},{16,48},{20,52},{24,56},{28,60},{32,6... | collective-permute-start | bytes 104 | tf_op jit(solution)/shard_map/ppermute | solution.py:54
  122.0 8.9 %collective-permute-start.12 = (f32[8,128,64]{1,2,0:T(8,128)S(1)}, f32[8,128,64]{1,2,0:T(8,128)S(1)}, u32[]{:S(2)}, u32[]{:S(2)}) collective-permute-start(f32[8,128,64]{1,2,0:T(8,128)S(1)} %add_select_fusion.1), channel_id=1, source_target_pairs={{0,128},{4,132},{8,136},{12,140},{16,144},{20,148},{24,152},{28,15... | collective-permute-start | bytes 786440 | tf_op jit(solution)/shard_map/ppermute | solution.py:54
  126.8 3.3 %collective-permute-start.5 = (f32[8]{0:T(128)S(1)}, f32[8]{0:T(128)S(1)}, u32[]{:S(2)}, u32[]{:S(2)}) collective-permute-start(f32[8]{0:T(128)S(1)} %broadcast_select_fusion.5), channel_id=1, source_target_pairs={{0,64},{4,68},{8,72},{12,76},{16,80},{20,84},{24,88},{28,92},{32,9... | collective-permute-start | bytes 104 | tf_op jit(solution)/shard_map/ppermute | solution.py:54
  172.6 14.2 %all-to-all-start.3 = ((bf16[4,2,8192]{2,1,0:T(2,128)(2,1)}), bf16[4,2,8192]{2,1,0:T(2,128)(2,1)S(1)}, u32[]{:S(2)}, u32[]{:S(2)}) async-start(bf16[4,2,8192]{2,1,0:T(2,128)(2,1)} %reshape.124), calls=%async_computation.3 | async-start | bytes 262144 | tf_op jit(solution)/shard_map/all_to_all | solution.py:164
  187.1 10.4 %copy-start.7 = (s32[256]{0:T(256)S(1)}, s32[256]{0:T(256)}, u32[]{:S(2)}) copy-start(s32[256]{0:T(256)} %param.23) | copy-start | bytes 3076
  189.7 15.7 %all-to-all-start.4 = ((bf16[4,64,1024]{2,1,0:T(8,128)(2,1)}), bf16[4,64,1024]{2,1,0:T(8,128)(2,1)S(1)}, u32[]{:S(2)}, u32[]{:S(2)}) async-start(bf16[4,64,1024]{2,1,0:T(8,128)(2,1)} %bitcast.29), calls=%async_computation.4 | async-start | bytes 1048576 | tf_op jit(solution)/shard_map/all_to_all | solution.py:183
  206.4 9.2 %copy-start.1 = (bf16[64,1024]{1,0:T(8,128)(2,1)}, bf16[64,1024]{1,0:T(8,128)(2,1)S(1)}, u32[]{:S(2)}) copy-start(bf16[64,1024]{1,0:T(8,128)(2,1)S(1)} %add_convert_fusion) | copy-start | bytes 393220
Sparse Core Ops, SparseCore 0:
  27.8 112.2 all-gather.1

commit v10 on v9

--- a/solution.py
+++ b/solution.py
@@ -45,7 +45,7 @@
 
 
 def pass_states(local_state, total_decay):
-    axis = ("sb", "sa")
+    axis = ("sb", "sy", "sz")
     devices = lax.axis_size(axis)
     mine = lax.axis_index(axis)
 
@@ -152,14 +152,13 @@
     head_count = queries.shape[1] // HDIM
 
     def spread(part):
-        split = part.reshape(row_count, head_count, HDIM)
-        return lax.all_to_all(split, "sb", split_axis=1, concat_axis=0, tiled=True)
+        split = part.reshape(part.shape[:-1] + (head_count, HDIM))
+        return lax.all_to_all(split, "sb", split_axis=split.ndim - 2, concat_axis=split.ndim - 3, tiled=True)
 
     query_heads = spread(queries)
-    pair_t = jnp.stack(
-        [spread(key_rows).reshape(-1, HDIM).T, spread(values).reshape(-1, HDIM).T]
-    )
-    gathered = lax.all_gather(pair_t, "sa", axis=2, tiled=True)
+    pair = spread(jnp.stack([key_rows, values]))
+    pair_t = pair.reshape(2, -1, HDIM).transpose(0, 2, 1)
+    gathered = lax.all_gather(pair_t, ("sy", "sz"), axis=2, tiled=True)
     attended_one = flash_one_head_t(query_heads.reshape(-1, HDIM).T, gathered).T
     attended = lax.all_to_all(
         attended_one.reshape(-1, 1, HDIM), "sb", split_axis=0, concat_axis=1, tiled=True
@@ -208,10 +207,12 @@
 def solution(mesh):
     seq_count = mesh.shape["seq"]
     outer = math.gcd(seq_count, mesh.shape["head"])
+    middle = math.gcd(seq_count // outer, 2)
     split_mesh = Mesh(
-        mesh.devices.reshape(outer, seq_count // outer, mesh.shape["head"]), ("sb", "sa", "head")
-    )
-    seq = ("sb", "sa")
+        mesh.devices.reshape(outer, middle, seq_count // outer // middle, mesh.shape["head"]),
+        ("sb", "sy", "sz", "head"),
+    )
+    seq = ("sb", "sy", "sz")
     in_specs = (
         P(seq, None),
         P(seq, "head"),
@@ -226,7 +227,7 @@
         P(),
         P(seq),
     )
-    out_specs = (P(("sb", "sa", "head"), None), P(seq, "head", None, None, None))
+    out_specs = (P(("sb", "sy", "sz", "head"), None), P(seq, "head", None, None, None))
     return jax.shard_map(
         per_device, mesh=split_mesh, in_specs=in_specs, out_specs=out_specs, check_vma=False
     )

time: 224 us -> 211 us (0.942)
  waiting for transfers between devices: 38.6 us -> 24.4 us
  blocking collectives: 7.9 us -> 18.2 us
  starting transfers between devices: 112 us -> 105 us
    all_to_all x0 -> x1, blocking collectives: none -> 10.3 us  [spread(): lax.all_to_all(split, 'sb', split_axis=split.ndim - 2, concat_axis=split....]
    all_gather x1, waiting for transfers between devices: 8.78 us -> 0.02 us  [per_device(): gathered = lax.all_gather(pair_t, ('sy', 'sz'), axis=2, tiled=True)]
    all_to_all x3 -> x1, starting transfers between devices: 20.1 us -> 12.2 us  [spread(): lax.all_to_all(split, 'sb', split_axis=split.ndim - 2, concat_axis=split....]
    all_to_all x3 -> x1, waiting for transfers between devices: 7.76 us -> 0.01 us  [spread(): lax.all_to_all(split, 'sb', split_axis=split.ndim - 2, concat_axis=split....]
    ppermute x13, waiting for transfers between devices: 11.4 us -> 13.8 us  [shifted(): return jax.tree.map(lambda part: lax.ppermute(part, axis, pairs), tree)]
    unnamed x27 -> x25, local copies, waits for them, and re-layouts: 7.17 us -> 5.8 us
  transfers between devices with their start and end apart: 19 -> 17, of which waited for: 12 -> 10; matrix products, arithmetic and copies ran while one was open for 4% -> 3% of each run, Pallas kernels for 0% -> 0%
where the time goes in v10:
time: 211 us; the launch traced here: 210 us
  starting transfers between devices  105 us (50%)
  Pallas kernels  29.4 us (14%)
  waiting for transfers between devices  24.4 us (12%)
  blocking collectives  18.2 us (9%)
  between operations  14.5 us (7%)
  local copies, waits for them, and re-layouts  8.35 us (4%)
  matrix products  6.05 us (3%)
  other arithmetic  4.12 us (2%)
    ppermute x13, starting transfers between devices, shifted(): return jax.tree.map(lambda part: lax.ppermute(part, axis, pairs), tree)  73.9 us
    pallas_call x1, Pallas kernels, flash_one_head_t(): pl.pallas_call(kernel, out_shape=jax.ShapeDtypeStruct((width, row_count),...  29.4 us
    ppermute x13, waiting for transfers between devices, shifted(): return jax.tree.map(lambda part: lax.ppermute(part, axis, pairs), tree)  13.8 us
    all_to_all x1, starting transfers between devices, spread(): lax.all_to_all(split, 'sb', split_axis=split.ndim - 2, concat_axis=split....  12.2 us
    all_to_all x1, starting transfers between devices, per_device(): lax.all_to_all(attended_one.reshape(-1, 1, HDIM), 'sb', split_axis=0, con...  10.4 us
    all_to_all x1, blocking collectives, spread(): lax.all_to_all(split, 'sb', split_axis=split.ndim - 2, concat_axis=split....  10.3 us
    all_to_all x1, starting transfers between devices, per_device(): lax.all_to_all(partial.reshape(owner_count, sub_rows, partial.shape[1]),...  8.31 us
    all_to_all x1, blocking collectives, per_device(): lax.all_to_all(packed, 'head', split_axis=0, concat_axis=0, tiled=True)  7.89 us
  transfers between devices with their start and end apart: 17, of which 10 were waited for; matrix products, arithmetic and copies ran while one was open for 3% of the time, Pallas kernels for 0%

profile of v10, /device:TPU:1, one launch (start us, length us, event | category | flops | bytes accessed | tf_op | source)
XLA Modules:
  0.0 209.9 jit_solution(11838337943034974632)
XLA Ops:
  7.3 1.1 copy.47
  8.4 1.0 copy.48
  9.5 10.3 %all_to_all.55 = bf16[2,256,4,64]{1,3,0,2:T(8,128)(2,1)S(1)} all-to-all(bf16[2,256,4,64]{1,3,0,2:T(8,128)(2,1)S(1)} %copy.49), channel_id=1, replica_groups=mesh['sb'=4,'sy'=2,'sz'=8,'head'=4] {'sb'}, dimensions={2} | all-to-all | bytes 524288 | tf_op jit(solution)/shard_map/all_to_all | solution.py:156
  19.8 0.2 copy.50
  20.0 0.9 reshape.103
  20.9 0.6 reduce-window.6
  21.5 0.2 slice_reduce_fusion
  21.7 0.1 copy.54
  21.9 0.2 slice_reduce_fusion.1
  22.1 0.1 exponential_bitcast_fusion.1
  22.2 0.2 convolution_bitcast_fusion.2
  22.4 3.6 %collective-permute-start.6 = (f32[8,128,64]{1,2,0:T(8,128)S(1)}, f32[8,128,64]{1,2,0:T(8,128)S(1)}, u32[]{:S(2)}, u32[]{:S(2)}) collective-permute-start(f32[8,128,64]{1,2,0:T(8,128)S(1)} %convolution_bitcast_fusion.2), channel_id=1, source_target_pairs={{0,4},{4,8},{8,12},{12,16},{16,20},{20,24},{24,28},{28,32},{32,36}... | collective-permute-start | bytes 786440 | tf_op jit(solution)/shard_map/ppermute | solution.py:54
  26.0 3.5 %collective-permute-done.6 = f32[8,128,64]{1,2,0:T(8,128)S(1)} collective-permute-done((f32[8,128,64]{1,2,0:T(8,128)S(1)}, f32[8,128,64]{1,2,0:T(8,128)S(1)}, u32[]{:S(2)}, u32[]{:S(2)}) %collective-permute-start.6) | collective-permute-done | bytes 262176 | tf_op jit(solution)/shard_map/ppermute | solution.py:54
  29.6 4.1 %collective-permute-start.7 = (f32[8,128,64]{1,2,0:T(8,128)S(1)}, f32[8,128,64]{1,2,0:T(8,128)S(1)}, u32[]{:S(2)}, u32[]{:S(2)}) collective-permute-start(f32[8,128,64]{1,2,0:T(8,128)S(1)} %broadcast_select_fusion), channel_id=1, source_target_pairs={{0,4},{4,8},{8,12},{12,16},{16,20},{20,24},{24,28},{28,32},{32,36}... | collective-permute-start | bytes 786440 | tf_op jit(solution)/shard_map/ppermute | solution.py:54
  33.7 3.5 %collective-permute-start = (f32[8]{0:T(128)S(1)}, f32[8]{0:T(128)S(1)}, u32[]{:S(2)}, u32[]{:S(2)}) collective-permute-start(f32[8]{0:T(128)S(1)} %exp.13), channel_id=1, source_target_pairs={{0,4},{4,8},{8,12},{12,16},{16,20},{20,24},{24,28},{28,32},{32,36}... | collective-permute-start | bytes 104 | tf_op jit(solution)/shard_map/ppermute | solution.py:54
  37.2 0.7 collective-permute-done
  37.9 0.1 add_select_fusion.5
  38.0 7.3 %collective-permute-start.8 = (f32[8,128,64]{1,2,0:T(8,128)S(1)}, f32[8,128,64]{1,2,0:T(8,128)S(1)}, u32[]{:S(2)}, u32[]{:S(2)}) collective-permute-start(f32[8,128,64]{1,2,0:T(8,128)S(1)} %add_select_fusion.5), channel_id=1, source_target_pairs={{0,8},{4,12},{8,16},{12,20},{16,24},{20,28},{24,32},{28,36},{32,40... | collective-permute-start | bytes 786440 | tf_op jit(solution)/shard_map/ppermute | solution.py:54
  45.4 0.8 copy.45
  46.2 12.2 %all-to-all-start = ((bf16[256,4,64]{0,2,1:T(8,128)(2,1)}), bf16[256,4,64]{0,2,1:T(8,128)(2,1)S(1)}, u32[]{:S(2)}, u32[]{:S(2)}) async-start(bf16[256,4,64]{0,2,1:T(8,128)(2,1)} %bitcast), calls=%async_computation | async-start | bytes 262144 | tf_op jit(solution)/shard_map/all_to_all | solution.py:156
  58.4 1.3 collective-permute-start.1
  59.7 0.7 collective-permute-done.1
  60.4 0.1 add_select_fusion.4
  60.5 6.6 %collective-permute-start.9 = (f32[8,128,64]{1,2,0:T(8,128)S(1)}, f32[8,128,64]{1,2,0:T(8,128)S(1)}, u32[]{:S(2)}, u32[]{:S(2)}) collective-permute-start(f32[8,128,64]{1,2,0:T(8,128)S(1)} %add_select_fusion.4), channel_id=1, source_target_pairs={{0,16},{4,20},{8,24},{12,28},{16,32},{20,36},{24,40},{28,44},{32,4... | collective-permute-start | bytes 786440 | tf_op jit(solution)/shard_map/ppermute | solution.py:54
  67.1 0.2 fusion.28
  67.3 4.0 %collective-permute-start.2 = (f32[8]{0:T(128)S(1)}, f32[8]{0:T(128)S(1)}, u32[]{:S(2)}, u32[]{:S(2)}) collective-permute-start(f32[8]{0:T(128)S(1)} %broadcast_select_fusion.1), channel_id=1, source_target_pairs={{0,8},{4,12},{8,16},{12,20},{16,24},{20,28},{24,32},{28,36},{32,40... | collective-permute-start | bytes 104 | tf_op jit(solution)/shard_map/ppermute | solution.py:54
  71.3 0.7 collective-permute-done.2
  72.0 0.1 add_select_fusion.3
  72.2 20.4 %collective-permute-start.10 = (f32[8,128,64]{1,2,0:T(8,128)S(1)}, f32[8,128,64]{1,2,0:T(8,128)S(1)}, u32[]{:S(2)}, u32[]{:S(2)}) collective-permute-start(f32[8,128,64]{1,2,0:T(8,128)S(1)} %add_select_fusion.3), channel_id=1, source_target_pairs={{0,32},{4,36},{8,40},{12,44},{16,48},{20,52},{24,56},{28,60},{32,6... | collective-permute-start | bytes 786440 | tf_op jit(solution)/shard_map/ppermute | solution.py:54
  92.6 5.1 %collective-permute-start.3 = (f32[8]{0:T(128)S(1)}, f32[8]{0:T(128)S(1)}, u32[]{:S(2)}, u32[]{:S(2)}) collective-permute-start(f32[8]{0:T(128)S(1)} %broadcast_select_fusion.3), channel_id=1, source_target_pairs={{0,16},{4,20},{8,24},{12,28},{16,32},{20,36},{24,40},{28,44},{32,4... | collective-permute-start | bytes 104 | tf_op jit(solution)/shard_map/ppermute | solution.py:54
  97.7 0.7 collective-permute-done.3
  98.4 4.7 %collective-permute-done.10 = f32[8,128,64]{1,2,0:T(8,128)S(1)} collective-permute-done((f32[8,128,64]{1,2,0:T(8,128)S(1)}, f32[8,128,64]{1,2,0:T(8,128)S(1)}, u32[]{:S(2)}, u32[]{:S(2)}) %collective-permute-start.10) | collective-permute-done | bytes 262176 | tf_op jit(solution)/shard_map/ppermute | solution.py:54
  103.1 0.1 add_select_fusion.2
  103.2 7.7 %collective-permute-start.11 = (f32[8,128,64]{1,2,0:T(8,128)S(1)}, f32[8,128,64]{1,2,0:T(8,128)S(1)}, u32[]{:S(2)}, u32[]{:S(2)}) collective-permute-start(f32[8,128,64]{1,2,0:T(8,128)S(1)} %add_select_fusion.2), channel_id=1, source_target_pairs={{0,64},{4,68},{8,72},{12,76},{16,80},{20,84},{24,88},{28,92},{32,9... | collective-permute-start | bytes 786440 | tf_op jit(solution)/shard_map/ppermute | solution.py:54
  111.0 0.7 convolution_bitcast_fusion.1
  111.6 5.0 %collective-permute-start.4 = (f32[8]{0:T(128)S(1)}, f32[8]{0:T(128)S(1)}, u32[]{:S(2)}, u32[]{:S(2)}) collective-permute-start(f32[8]{0:T(128)S(1)} %broadcast_select_fusion.4), channel_id=1, source_target_pairs={{0,32},{4,36},{8,40},{12,44},{16,48},{20,52},{24,56},{28,60},{32,6... | collective-permute-start | bytes 104 | tf_op jit(solution)/shard_map/ppermute | solution.py:54
  116.7 0.7 collective-permute-done.4
  117.4 0.1 add_select_fusion.1
  117.5 3.9 %collective-permute-start.12 = (f32[8,128,64]{1,2,0:T(8,128)S(1)}, f32[8,128,64]{1,2,0:T(8,128)S(1)}, u32[]{:S(2)}, u32[]{:S(2)}) collective-permute-start(f32[8,128,64]{1,2,0:T(8,128)S(1)} %add_select_fusion.1), channel_id=1, source_target_pairs={{0,128},{4,132},{8,136},{12,140},{16,144},{20,148},{24,152},{28,15... | collective-permute-start | bytes 786440 | tf_op jit(solution)/shard_map/ppermute | solution.py:54
  121.4 1.3 collective-permute-start.5
  122.7 2.0 collective-permute-done.5
  124.7 0.1 copy.46
  124.8 0.7 copy.55
  125.5 0.3 multiply_reduce_fusion
  125.9 29.4 %shard_map.131 = bf16[64,1024]{1,0:T(8,128)(2,1)} custom-call(bf16[64,1024]{1,0:T(8,128)(2,1)} %bitcast.73, bf16[2,64,16384]{2,1,0:T(8,128)(2,1)} %all-gather.2.cloned.1.call-done.k_ref.v_ref, bf16[2,64,16384]{2,1,0:T(8,128)(2,1)} %all-gather.2.cloned.1.call-done.k_ref.v_ref), custom_call_target="tpu_custom_call" | custom-call | tf_op jit(solution)/shard_map/pallas_call | solution.py:104
  155.3 0.5 broadcast.86
  155.8 1.6 reduce.4
  157.4 0.2 copy.56
  157.6 0.9 reshape.116
  158.5 10.4 %all-to-all-start.2 = ((bf16[4,2,8192]{2,1,0:T(2,128)(2,1)}), bf16[4,2,8192]{2,1,0:T(2,128)(2,1)S(1)}, u32[]{:S(2)}, u32[]{:S(2)}) async-start(bf16[4,2,8192]{2,1,0:T(2,128)(2,1)} %reshape.116), calls=%async_computation.2 | async-start | bytes 262144 | tf_op jit(solution)/shard_map/all_to_all | solution.py:163
  168.9 1.7 fusion.29
  170.6 3.1 %all-to-all-done.2 = bf16[4,2,8192]{2,1,0:T(2,128)(2,1)S(1)} async-done(((bf16[4,2,8192]{2,1,0:T(2,128)(2,1)}), bf16[4,2,8192]{2,1,0:T(2,128)(2,1)S(1)}, u32[]{:S(2)}, u32[]{:S(2)}) %all-to-all-start.2) | async-done | bytes 131104 | tf_op jit(solution)/shard_map/all_to_all | solution.py:163
  173.7 0.3 reshape.117
  174.1 0.3 copy.52
  174.5 2.2 %fusion = bf16[256,1024]{1,0:T(8,128)(2,1)} fusion(f32[256,1024]{1,0:T(8,128)S(1)} %fusion.29, bf16[256,256]{0,1:T(8,128)(2,1)S(1)} %bitcast.75, bf16[256,1024]{1,0:T(8,128)(2,1)} %param.20), kind=kOutput, calls=%fused_computation.2 | convolution fusion | flops 134742016 | bytes 2228224 | tf_op jit(solution)/shard_map/dot_general | solution.py:179
  176.7 8.3 %all-to-all-start.3 = ((bf16[4,64,1024]{2,1,0:T(8,128)(2,1)}), bf16[4,64,1024]{2,1,0:T(8,128)(2,1)S(1)}, u32[]{:S(2)}, u32[]{:S(2)}) async-start(bf16[4,64,1024]{2,1,0:T(8,128)(2,1)} %bitcast.24), calls=%async_computation.3 | async-start | bytes 1048576 | tf_op jit(solution)/shard_map/all_to_all | solution.py:182
  185.0 0.2 fusion.3
  185.3 0.1 multiply_add_fusion
  185.4 7.5 %all-to-all-done.3 = bf16[4,64,1024]{2,1,0:T(8,128)(2,1)S(1)} async-done(((bf16[4,64,1024]{2,1,0:T(8,128)(2,1)}), bf16[4,64,1024]{2,1,0:T(8,128)(2,1)S(1)}, u32[]{:S(2)}, u32[]{:S(2)}) %all-to-all-start.3) | async-done | bytes 524320 | tf_op jit(solution)/shard_map/all_to_all | solution.py:182
  192.8 0.1 convert_reduce_fusion
  192.9 0.9 add_convert_fusion
  193.9 0.6 convolution_convert_fusion
  194.5 7.9 %all_to_all.56 = bf16[4,32,768]{2,1,0:T(8,128)(2,1)S(1)} all-to-all(bf16[4,32,768]{2,1,0:T(8,128)(2,1)S(1)} %bitcast.71), channel_id=1, replica_groups=mesh['sb'=4,'sy'=2,'sz'=8,'head'=4] {'head'}, dimensions={0} | all-to-all | bytes 393216 | tf_op jit(solution)/shard_map/all_to_all | solution.py:202
  202.4 0.7 copy.58
  (46 shorter events, 0.6 us)
Async XLA Ops:
  7.2 186.7 %copy-start = (bf16[1024,768]{1,0:T(8,128)(2,1)S(1)}, bf16[1024,768]{1,0:T(8,128)(2,1)}, u32[]{:S(2)}) copy-start(bf16[1024,768]{1,0:T(8,128)(2,1)} %param.22) | copy-start | bytes 4718596
  7.2 13.7 %copy-start.6 = (f32[8,256]{1,0:T(8,128)S(1)}, f32[8,256]{1,0:T(8,128)}, u32[]{:S(2)}) copy-start(f32[8,256]{1,0:T(8,128)} %param.19) | copy-start | bytes 24580
  7.2 14.5 %copy-start.2 = (bf16[256,512]{1,0:T(8,128)(2,1)S(1)}, bf16[256,512]{1,0:T(8,128)(2,1)}, u32[]{:S(2)}) copy-start(bf16[256,512]{1,0:T(8,128)(2,1)} %param.16) | copy-start | bytes 786436
  7.2 15.0 %copy-start.3 = (bf16[256,128]{1,0:T(8,128)(2,1)S(1)}, bf16[256,128]{1,0:T(8,128)(2,1)}, u32[]{:S(2)}) copy-start(bf16[256,128]{1,0:T(8,128)(2,1)} %param.17) | copy-start | bytes 196612
  7.2 118.7 %all-gather.2.cloned.1.call-start = ((), (), s32[]{:S(2)}) async-start(), calls=%async_computation.5 | async-start | bytes 4456448 | tf_op jit(solution)/shard_map/all_gather | solution.py:161
  9.5 35.9 %copy-start.5 = (bf16[256,256]{1,0:T(8,128)(2,1)S(1)}, bf16[256,256]{1,0:T(8,128)(2,1)}, u32[]{:S(2)}) copy-start(bf16[256,256]{1,0:T(8,128)(2,1)} %param.13) | copy-start | bytes 393220
  20.9 46.2 %copy-start.4 = (bf16[256,128]{1,0:T(8,128)(2,1)S(1)}, bf16[256,128]{1,0:T(8,128)(2,1)}, u32[]{:S(2)}) copy-start(bf16[256,128]{1,0:T(8,128)(2,1)} %param.18) | copy-start | bytes 196612
  22.4 7.1 %collective-permute-start.6 = (f32[8,128,64]{1,2,0:T(8,128)S(1)}, f32[8,128,64]{1,2,0:T(8,128)S(1)}, u32[]{:S(2)}, u32[]{:S(2)}) collective-permute-start(f32[8,128,64]{1,2,0:T(8,128)S(1)} %convolution_bitcast_fusion.2), channel_id=1, source_target_pairs={{0,4},{4,8},{8,12},{12,16},{16,20},{20,24},{24,28},{28,32},{32,36}... | collective-permute-start | bytes 786440 | tf_op jit(solution)/shard_map/ppermute | solution.py:54
  29.6 8.4 %collective-permute-start.7 = (f32[8,128,64]{1,2,0:T(8,128)S(1)}, f32[8,128,64]{1,2,0:T(8,128)S(1)}, u32[]{:S(2)}, u32[]{:S(2)}) collective-permute-start(f32[8,128,64]{1,2,0:T(8,128)S(1)} %broadcast_select_fusion), channel_id=1, source_target_pairs={{0,4},{4,8},{8,12},{12,16},{16,20},{20,24},{24,28},{28,32},{32,36}... | collective-permute-start | bytes 786440 | tf_op jit(solution)/shard_map/ppermute | solution.py:54
  33.7 4.2 %collective-permute-start = (f32[8]{0:T(128)S(1)}, f32[8]{0:T(128)S(1)}, u32[]{:S(2)}, u32[]{:S(2)}) collective-permute-start(f32[8]{0:T(128)S(1)} %exp.13), channel_id=1, source_target_pairs={{0,4},{4,8},{8,12},{12,16},{16,20},{20,24},{24,28},{28,32},{32,36}... | collective-permute-start | bytes 104 | tf_op jit(solution)/shard_map/ppermute | solution.py:54
  38.0 22.4 %collective-permute-start.8 = (f32[8,128,64]{1,2,0:T(8,128)S(1)}, f32[8,128,64]{1,2,0:T(8,128)S(1)}, u32[]{:S(2)}, u32[]{:S(2)}) collective-permute-start(f32[8,128,64]{1,2,0:T(8,128)S(1)} %add_select_fusion.5), channel_id=1, source_target_pairs={{0,8},{4,12},{8,16},{12,20},{16,24},{20,28},{24,32},{28,36},{32,40... | collective-permute-start | bytes 786440 | tf_op jit(solution)/shard_map/ppermute | solution.py:54
  46.2 78.5 %all-to-all-start = ((bf16[256,4,64]{0,2,1:T(8,128)(2,1)}), bf16[256,4,64]{0,2,1:T(8,128)(2,1)S(1)}, u32[]{:S(2)}, u32[]{:S(2)}) async-start(bf16[256,4,64]{0,2,1:T(8,128)(2,1)} %bitcast), calls=%async_computation | async-start | bytes 262144 | tf_op jit(solution)/shard_map/all_to_all | solution.py:156
  58.4 2.0 collective-permute-start.1
  60.5 11.5 %collective-permute-start.9 = (f32[8,128,64]{1,2,0:T(8,128)S(1)}, f32[8,128,64]{1,2,0:T(8,128)S(1)}, u32[]{:S(2)}, u32[]{:S(2)}) collective-permute-start(f32[8,128,64]{1,2,0:T(8,128)S(1)} %add_select_fusion.4), channel_id=1, source_target_pairs={{0,16},{4,20},{8,24},{12,28},{16,32},{20,36},{24,40},{28,44},{32,4... | collective-permute-start | bytes 786440 | tf_op jit(solution)/shard_map/ppermute | solution.py:54
  67.3 4.7 %collective-permute-start.2 = (f32[8]{0:T(128)S(1)}, f32[8]{0:T(128)S(1)}, u32[]{:S(2)}, u32[]{:S(2)}) collective-permute-start(f32[8]{0:T(128)S(1)} %broadcast_select_fusion.1), channel_id=1, source_target_pairs={{0,8},{4,12},{8,16},{12,20},{16,24},{20,28},{24,32},{28,36},{32,40... | collective-permute-start | bytes 104 | tf_op jit(solution)/shard_map/ppermute | solution.py:54
  72.2 31.0 %collective-permute-start.10 = (f32[8,128,64]{1,2,0:T(8,128)S(1)}, f32[8,128,64]{1,2,0:T(8,128)S(1)}, u32[]{:S(2)}, u32[]{:S(2)}) collective-permute-start(f32[8,128,64]{1,2,0:T(8,128)S(1)} %add_select_fusion.3), channel_id=1, source_target_pairs={{0,32},{4,36},{8,40},{12,44},{16,48},{20,52},{24,56},{28,60},{32,6... | collective-permute-start | bytes 786440 | tf_op jit(solution)/shard_map/ppermute | solution.py:54
  92.6 5.8 %collective-permute-start.3 = (f32[8]{0:T(128)S(1)}, f32[8]{0:T(128)S(1)}, u32[]{:S(2)}, u32[]{:S(2)}) collective-permute-start(f32[8]{0:T(128)S(1)} %broadcast_select_fusion.3), channel_id=1, source_target_pairs={{0,16},{4,20},{8,24},{12,28},{16,32},{20,36},{24,40},{28,44},{32,4... | collective-permute-start | bytes 104 | tf_op jit(solution)/shard_map/ppermute | solution.py:54
  103.2 14.1 %collective-permute-start.11 = (f32[8,128,64]{1,2,0:T(8,128)S(1)}, f32[8,128,64]{1,2,0:T(8,128)S(1)}, u32[]{:S(2)}, u32[]{:S(2)}) collective-permute-start(f32[8,128,64]{1,2,0:T(8,128)S(1)} %add_select_fusion.2), channel_id=1, source_target_pairs={{0,64},{4,68},{8,72},{12,76},{16,80},{20,84},{24,88},{28,92},{32,9... | collective-permute-start | bytes 786440 | tf_op jit(solution)/shard_map/ppermute | solution.py:54
  111.6 5.7 %collective-permute-start.4 = (f32[8]{0:T(128)S(1)}, f32[8]{0:T(128)S(1)}, u32[]{:S(2)}, u32[]{:S(2)}) collective-permute-start(f32[8]{0:T(128)S(1)} %broadcast_select_fusion.4), channel_id=1, source_target_pairs={{0,32},{4,36},{8,40},{12,44},{16,48},{20,52},{24,56},{28,60},{32,6... | collective-permute-start | bytes 104 | tf_op jit(solution)/shard_map/ppermute | solution.py:54
  117.5 8.0 %collective-permute-start.12 = (f32[8,128,64]{1,2,0:T(8,128)S(1)}, f32[8,128,64]{1,2,0:T(8,128)S(1)}, u32[]{:S(2)}, u32[]{:S(2)}) collective-permute-start(f32[8,128,64]{1,2,0:T(8,128)S(1)} %add_select_fusion.1), channel_id=1, source_target_pairs={{0,128},{4,132},{8,136},{12,140},{16,144},{20,148},{24,152},{28,15... | collective-permute-start | bytes 786440 | tf_op jit(solution)/shard_map/ppermute | solution.py:54
  121.4 3.3 %collective-permute-start.5 = (f32[8]{0:T(128)S(1)}, f32[8]{0:T(128)S(1)}, u32[]{:S(2)}, u32[]{:S(2)}) collective-permute-start(f32[8]{0:T(128)S(1)} %broadcast_select_fusion.5), channel_id=1, source_target_pairs={{0,64},{4,68},{8,72},{12,76},{16,80},{20,84},{24,88},{28,92},{32,9... | collective-permute-start | bytes 104 | tf_op jit(solution)/shard_map/ppermute | solution.py:54
  158.5 15.2 %all-to-all-start.2 = ((bf16[4,2,8192]{2,1,0:T(2,128)(2,1)}), bf16[4,2,8192]{2,1,0:T(2,128)(2,1)S(1)}, u32[]{:S(2)}, u32[]{:S(2)}) async-start(bf16[4,2,8192]{2,1,0:T(2,128)(2,1)} %reshape.116), calls=%async_computation.2 | async-start | bytes 262144 | tf_op jit(solution)/shard_map/all_to_all | solution.py:163
  174.0 10.9 %copy-start.7 = (s32[256]{0:T(256)S(1)}, s32[256]{0:T(256)}, u32[]{:S(2)}) copy-start(s32[256]{0:T(256)} %param.23) | copy-start | bytes 3076
  176.7 16.2 %all-to-all-start.3 = ((bf16[4,64,1024]{2,1,0:T(8,128)(2,1)}), bf16[4,64,1024]{2,1,0:T(8,128)(2,1)S(1)}, u32[]{:S(2)}, u32[]{:S(2)}) async-start(bf16[4,64,1024]{2,1,0:T(8,128)(2,1)} %bitcast.24), calls=%async_computation.3 | async-start | bytes 1048576 | tf_op jit(solution)/shard_map/all_to_all | solution.py:182
  193.8 9.2 %copy-start.1 = (bf16[64,1024]{1,0:T(8,128)(2,1)}, bf16[64,1024]{1,0:T(8,128)(2,1)S(1)}, u32[]{:S(2)}) copy-start(bf16[64,1024]{1,0:T(8,128)(2,1)S(1)} %add_convert_fusion) | copy-start | bytes 393220
Sparse Core Ops, SparseCore 0:
  21.0 102.0 all-gather.1

commit v11 on v10

--- a/solution.py
+++ b/solution.py
@@ -159,10 +159,17 @@
     pair = spread(jnp.stack([key_rows, values]))
     pair_t = pair.reshape(2, -1, HDIM).transpose(0, 2, 1)
     gathered = lax.all_gather(pair_t, ("sy", "sz"), axis=2, tiled=True)
-    attended_one = flash_one_head_t(query_heads.reshape(-1, HDIM).T, gathered).T
-    attended = lax.all_to_all(
-        attended_one.reshape(-1, 1, HDIM), "sb", split_axis=0, concat_axis=1, tiled=True
-    ).reshape(row_count, head_count * HDIM)
+    peers = lax.axis_size("sb")
+    query_t = query_heads.reshape(peers, 2, row_count // 2, HDIM).transpose(1, 3, 0, 2)
+    halves = []
+    for half in range(2):
+        half_t = flash_one_head_t(query_t[half].reshape(HDIM, -1), gathered)
+        halves.append(
+            lax.all_to_all(
+                half_t.T.reshape(-1, 1, HDIM), "sb", split_axis=0, concat_axis=1, tiled=True
+            )
+        )
+    attended = jnp.concatenate(halves, axis=0).reshape(row_count, head_count * HDIM)
     cumulative, inner_part, local_state, total_decay = chain_pieces(
         ssm_input, write_proj, read_proj, log_decay
     )

time: 211 us -> 223 us (1.057)
  Pallas kernels: 29.4 us -> 34.6 us
  waiting for transfers between devices: 24.4 us -> 27.2 us
  other arithmetic: 4.12 us -> 6.58 us
    all_to_all x1, starting transfers between devices: 12.2 us -> 6.98 us  [spread(): lax.all_to_all(split, 'sb', split_axis=split.ndim - 2, concat_axis=split....]
    pallas_call x1 -> x2, Pallas kernels: 29.4 us -> 34.6 us  [flash_one_head_t(): pl.pallas_call(kernel, out_shape=jax.ShapeDtypeStruct((width, row_count),...]
    ppermute x13, waiting for transfers between devices: 13.8 us -> 17.3 us  [shifted(): return jax.tree.map(lambda part: lax.ppermute(part, axis, pairs), tree)]
    ppermute x13, starting transfers between devices: 73.9 us -> 76.7 us  [shifted(): return jax.tree.map(lambda part: lax.ppermute(part, axis, pairs), tree)]
    unnamed x25 -> x41, local copies, waits for them, and re-layouts: 5.8 us -> 7.53 us
    all_to_all x1 -> x2, starting transfers between devices: 10.4 us -> 10.5 us  [per_device(): lax.all_to_all(half_t.T.reshape(-1, 1, HDIM), 'sb', split_axis=0, concat_...]
  transfers between devices with their start and end apart: 17 -> 18, of which waited for: 10 -> 8; matrix products, arithmetic and copies ran while one was open for 3% -> 6% of each run, Pallas kernels for 0% -> 8%
where the time goes in v11:
time: 223 us; the launch traced here: 222 us
  starting transfers between devices  104 us (47%)
  Pallas kernels  34.6 us (16%)
  waiting for transfers between devices  27.2 us (12%)
  blocking collectives  18.2 us (8%)
  between operations  14.6 us (7%)
  local copies, waits for them, and re-layouts  10.3 us (5%)
  other arithmetic  6.58 us (3%)
  matrix products  5.9 us (3%)
    ppermute x13, starting transfers between devices, shifted(): return jax.tree.map(lambda part: lax.ppermute(part, axis, pairs), tree)  76.7 us
    pallas_call x2, Pallas kernels, flash_one_head_t(): pl.pallas_call(kernel, out_shape=jax.ShapeDtypeStruct((width, row_count),...  34.6 us
    ppermute x13, waiting for transfers between devices, shifted(): return jax.tree.map(lambda part: lax.ppermute(part, axis, pairs), tree)  17.3 us
    all_to_all x2, starting transfers between devices, per_device(): lax.all_to_all(half_t.T.reshape(-1, 1, HDIM), 'sb', split_axis=0, concat_...  10.5 us
    all_to_all x1, blocking collectives, spread(): lax.all_to_all(split, 'sb', split_axis=split.ndim - 2, concat_axis=split....  10.3 us
    all_to_all x1, starting transfers between devices, per_device(): lax.all_to_all(partial.reshape(owner_count, sub_rows, partial.shape[1]),...  10.1 us
    all_to_all x1, blocking collectives, per_device(): lax.all_to_all(packed, 'head', split_axis=0, concat_axis=0, tiled=True)  7.9 us
    unnamed x41, local copies, waits for them, and re-layouts  7.53 us
  transfers between devices with their start and end apart: 18, of which 8 were waited for; matrix products, arithmetic and copies ran while one was open for 6% of the time, Pallas kernels for 8%

profile of v11, /device:TPU:1, one launch (start us, length us, event | category | flops | bytes accessed | tf_op | source)
XLA Modules:
  0.0 221.6 jit_solution(15984171766482814129)
XLA Ops:
  7.3 1.1 copy.52
  8.4 1.0 copy.53
  9.5 10.3 %all_to_all.70 = bf16[2,256,4,64]{1,3,0,2:T(8,128)(2,1)S(1)} all-to-all(bf16[2,256,4,64]{1,3,0,2:T(8,128)(2,1)S(1)} %copy.54), channel_id=1, replica_groups=mesh['sb'=4,'sy'=2,'sz'=8,'head'=4] {'sb'}, dimensions={2} | all-to-all | bytes 524288 | tf_op jit(solution)/shard_map/all_to_all | solution.py:156
  19.8 0.2 copy.55
  20.0 0.9 reshape.107
  20.9 0.6 reduce-window.6
  21.5 0.2 slice_reduce_fusion
  21.7 0.1 copy.63
  21.9 0.2 slice_reduce_fusion.1
  22.2 0.2 convolution_bitcast_fusion.2
  22.4 3.6 %collective-permute-start.6 = (f32[8,128,64]{1,2,0:T(8,128)S(1)}, f32[8,128,64]{1,2,0:T(8,128)S(1)}, u32[]{:S(2)}, u32[]{:S(2)}) collective-permute-start(f32[8,128,64]{1,2,0:T(8,128)S(1)} %convolution_bitcast_fusion.2), channel_id=1, source_target_pairs={{0,4},{4,8},{8,12},{12,16},{16,20},{20,24},{24,28},{28,32},{32,36}... | collective-permute-start | bytes 786440 | tf_op jit(solution)/shard_map/ppermute | solution.py:54
  26.0 3.5 %collective-permute-done.6 = f32[8,128,64]{1,2,0:T(8,128)S(1)} collective-permute-done((f32[8,128,64]{1,2,0:T(8,128)S(1)}, f32[8,128,64]{1,2,0:T(8,128)S(1)}, u32[]{:S(2)}, u32[]{:S(2)}) %collective-permute-start.6) | collective-permute-done | bytes 262176 | tf_op jit(solution)/shard_map/ppermute | solution.py:54
  29.6 4.1 %collective-permute-start.7 = (f32[8,128,64]{1,2,0:T(8,128)S(1)}, f32[8,128,64]{1,2,0:T(8,128)S(1)}, u32[]{:S(2)}, u32[]{:S(2)}) collective-permute-start(f32[8,128,64]{1,2,0:T(8,128)S(1)} %broadcast_select_fusion), channel_id=1, source_target_pairs={{0,4},{4,8},{8,12},{12,16},{16,20},{20,24},{24,28},{28,32},{32,36}... | collective-permute-start | bytes 786440 | tf_op jit(solution)/shard_map/ppermute | solution.py:54
  33.7 3.5 %collective-permute-start = (f32[8]{0:T(128)S(1)}, f32[8]{0:T(128)S(1)}, u32[]{:S(2)}, u32[]{:S(2)}) collective-permute-start(f32[8]{0:T(128)S(1)} %exp.13), channel_id=1, source_target_pairs={{0,4},{4,8},{8,12},{12,16},{16,20},{20,24},{24,28},{28,32},{32,36}... | collective-permute-start | bytes 104 | tf_op jit(solution)/shard_map/ppermute | solution.py:54
  37.3 0.8 copy.50
  38.0 7.0 %all-to-all-start = ((bf16[256,4,64]{0,2,1:T(8,128)(2,1)}), bf16[256,4,64]{0,2,1:T(8,128)(2,1)S(1)}, u32[]{:S(2)}, u32[]{:S(2)}) async-start(bf16[256,4,64]{0,2,1:T(8,128)(2,1)} %bitcast), calls=%async_computation | async-start | bytes 262144 | tf_op jit(solution)/shard_map/all_to_all | solution.py:156
  45.1 3.7 %collective-permute-start.8 = (f32[8,128,64]{1,2,0:T(8,128)S(1)}, f32[8,128,64]{1,2,0:T(8,128)S(1)}, u32[]{:S(2)}, u32[]{:S(2)}) collective-permute-start(f32[8,128,64]{1,2,0:T(8,128)S(1)} %add_select_fusion.5), channel_id=1, source_target_pairs={{0,8},{4,12},{8,16},{12,20},{16,24},{20,28},{24,32},{28,36},{32,40... | collective-permute-start | bytes 786440 | tf_op jit(solution)/shard_map/ppermute | solution.py:54
  48.8 0.2 fusion.33
  49.0 1.9 collective-permute-start.1
  50.9 8.3 %collective-permute-done.1 = f32[8]{0:T(128)S(1)} collective-permute-done((f32[8]{0:T(128)S(1)}, f32[8]{0:T(128)S(1)}, u32[]{:S(2)}, u32[]{:S(2)}) %collective-permute-start.1) | collective-permute-done | bytes 64 | tf_op jit(solution)/shard_map/ppermute | solution.py:54
  59.4 10.1 %collective-permute-start.9 = (f32[8,128,64]{1,2,0:T(8,128)S(1)}, f32[8,128,64]{1,2,0:T(8,128)S(1)}, u32[]{:S(2)}, u32[]{:S(2)}) collective-permute-start(f32[8,128,64]{1,2,0:T(8,128)S(1)} %add_select_fusion.4), channel_id=1, source_target_pairs={{0,16},{4,20},{8,24},{12,28},{16,32},{20,36},{24,40},{28,44},{32,4... | collective-permute-start | bytes 786440 | tf_op jit(solution)/shard_map/ppermute | solution.py:54
  69.4 0.7 iota_compare_fusion
  70.1 4.4 %collective-permute-start.2 = (f32[8]{0:T(128)S(1)}, f32[8]{0:T(128)S(1)}, u32[]{:S(2)}, u32[]{:S(2)}) collective-permute-start(f32[8]{0:T(128)S(1)} %broadcast_select_fusion.1), channel_id=1, source_target_pairs={{0,8},{4,12},{8,16},{12,20},{16,24},{20,28},{24,32},{28,36},{32,40... | collective-permute-start | bytes 104 | tf_op jit(solution)/shard_map/ppermute | solution.py:54
  74.5 2.5 %collective-permute-done.2 = f32[8]{0:T(128)S(1)} collective-permute-done((f32[8]{0:T(128)S(1)}, f32[8]{0:T(128)S(1)}, u32[]{:S(2)}, u32[]{:S(2)}) %collective-permute-start.2) | collective-permute-done | bytes 64 | tf_op jit(solution)/shard_map/ppermute | solution.py:54
  77.1 0.4 copy-done.9
  77.5 9.4 %collective-permute-start.10 = (f32[8,128,64]{1,2,0:T(8,128)S(1)}, f32[8,128,64]{1,2,0:T(8,128)S(1)}, u32[]{:S(2)}, u32[]{:S(2)}) collective-permute-start(f32[8,128,64]{1,2,0:T(8,128)S(1)} %add_select_fusion.3), channel_id=1, source_target_pairs={{0,32},{4,36},{8,40},{12,44},{16,48},{20,52},{24,56},{28,60},{32,6... | collective-permute-start | bytes 786440 | tf_op jit(solution)/shard_map/ppermute | solution.py:54
  86.9 1.5 convolution_bitcast_fusion.1
  88.4 14.1 %collective-permute-start.3 = (f32[8]{0:T(128)S(1)}, f32[8]{0:T(128)S(1)}, u32[]{:S(2)}, u32[]{:S(2)}) collective-permute-start(f32[8]{0:T(128)S(1)} %copy-done.10), channel_id=1, source_target_pairs={{0,16},{4,20},{8,24},{12,28},{16,32},{20,36},{24,40},{28,44},{32,4... | collective-permute-start | bytes 104 | tf_op jit(solution)/shard_map/ppermute | solution.py:54
  102.5 0.7 collective-permute-done.3
  103.3 12.1 %collective-permute-start.11 = (f32[8,128,64]{1,2,0:T(8,128)S(1)}, f32[8,128,64]{1,2,0:T(8,128)S(1)}, u32[]{:S(2)}, u32[]{:S(2)}) collective-permute-start(f32[8,128,64]{1,2,0:T(8,128)S(1)} %add_select_fusion.2), channel_id=1, source_target_pairs={{0,64},{4,68},{8,72},{12,76},{16,80},{20,84},{24,88},{28,92},{32,9... | collective-permute-start | bytes 786440 | tf_op jit(solution)/shard_map/ppermute | solution.py:54
  115.4 0.6 iota_shift-right-logical_fusion
  116.0 3.9 %collective-permute-start.4 = (f32[8]{0:T(128)S(1)}, f32[8]{0:T(128)S(1)}, u32[]{:S(2)}, u32[]{:S(2)}) collective-permute-start(f32[8]{0:T(128)S(1)} %broadcast_select_fusion.4), channel_id=1, source_target_pairs={{0,32},{4,36},{8,40},{12,44},{16,48},{20,52},{24,56},{28,60},{32,6... | collective-permute-start | bytes 104 | tf_op jit(solution)/shard_map/ppermute | solution.py:54
  119.9 0.7 collective-permute-done.4
  120.6 4.0 %collective-permute-start.5 = (f32[8]{0:T(128)S(1)}, f32[8]{0:T(128)S(1)}, u32[]{:S(2)}, u32[]{:S(2)}) collective-permute-start(f32[8]{0:T(128)S(1)} %broadcast_select_fusion.5), channel_id=1, source_target_pairs={{0,64},{4,68},{8,72},{12,76},{16,80},{20,84},{24,88},{28,92},{32,9... | collective-permute-start | bytes 104 | tf_op jit(solution)/shard_map/ppermute | solution.py:54
  124.7 1.9 collective-permute-start.12
  126.7 0.2 fusion.32
  127.0 0.6 copy.69
  127.7 0.6 copy.68
  128.4 1.6 collective-permute-done.12
  129.9 0.3 multiply_reduce_fusion
  130.3 17.3 %shard_map.132 = bf16[64,512]{1,0:T(8,128)(2,1)} custom-call(bf16[64,512]{1,0:T(8,128)(2,1)} %bitcast.92, bf16[2,64,16384]{2,1,0:T(8,128)(2,1)} %all-gather.2.cloned.1.call-done.k_ref.v_ref, bf16[2,64,16384]{2,1,0:T(8,128)(2,1)} %all-gather.2.cloned.1.call-done.k_ref.v_ref), custom_call_target="tpu_custom_call" | custom-call | tf_op jit(solution)/shard_map/pallas_call | solution.py:104
  147.5 0.5 broadcast.86
  148.1 1.4 reduce.4
  149.5 0.1 copy.70
  149.6 0.8 reshape.120
  150.4 6.3 %all-to-all-start.3 = ((bf16[4,2,4096]{2,1,0:T(2,128)(2,1)}), bf16[4,2,4096]{2,1,0:T(2,128)(2,1)S(1)}, u32[]{:S(2)}, u32[]{:S(2)}) async-start(bf16[4,2,4096]{2,1,0:T(2,128)(2,1)} %reshape.120), calls=%async_computation.3 | async-start | bytes 131072 | tf_op jit(solution)/shard_map/all_to_all | solution.py:168
  156.7 17.3 %shard_map.131 = bf16[64,512]{1,0:T(8,128)(2,1)} custom-call(bf16[64,512]{1,0:T(8,128)(2,1)} %bitcast.91, bf16[2,64,16384]{2,1,0:T(8,128)(2,1)} %all-gather.2.cloned.1.call-done.k_ref.v_ref, bf16[2,64,16384]{2,1,0:T(8,128)(2,1)} %all-gather.2.cloned.1.call-done.k_ref.v_ref), custom_call_target="tpu_custom_call" | custom-call | tf_op jit(solution)/shard_map/pallas_call | solution.py:104
  174.0 1.4 reduce.5
  175.4 0.1 copy.71
  175.6 0.8 reshape.122
  176.4 4.2 %all-to-all-start.2 = ((bf16[4,2,4096]{2,1,0:T(2,128)(2,1)}), bf16[4,2,4096]{2,1,0:T(2,128)(2,1)S(1)}, u32[]{:S(2)}, u32[]{:S(2)}) async-start(bf16[4,2,4096]{2,1,0:T(2,128)(2,1)} %reshape.122), calls=%async_computation.2 | async-start | bytes 131072 | tf_op jit(solution)/shard_map/all_to_all | solution.py:168
  180.6 1.8 fusion.34
  182.4 0.1 reshape.121
  182.5 0.1 copy.61
  182.7 2.4 %all-to-all-done.2 = bf16[4,2,4096]{2,1,0:T(2,128)(2,1)S(1)} async-done(((bf16[4,2,4096]{2,1,0:T(2,128)(2,1)}), bf16[4,2,4096]{2,1,0:T(2,128)(2,1)S(1)}, u32[]{:S(2)}, u32[]{:S(2)}) %all-to-all-start.2) | async-done | bytes 65568 | tf_op jit(solution)/shard_map/all_to_all | solution.py:168
  185.1 0.1 reshape.123
  185.4 1.1 fusion
  186.5 10.1 %all-to-all-start.4 = ((bf16[4,64,1024]{2,1,0:T(8,128)(2,1)}), bf16[4,64,1024]{2,1,0:T(8,128)(2,1)S(1)}, u32[]{:S(2)}, u32[]{:S(2)}) async-start(bf16[4,64,1024]{2,1,0:T(8,128)(2,1)} %bitcast.28), calls=%async_computation.4 | async-start | bytes 1048576 | tf_op jit(solution)/shard_map/all_to_all | solution.py:189
  196.7 0.2 fusion.3
  197.1 7.5 %all-to-all-done.4 = bf16[4,64,1024]{2,1,0:T(8,128)(2,1)S(1)} async-done(((bf16[4,64,1024]{2,1,0:T(8,128)(2,1)}), bf16[4,64,1024]{2,1,0:T(8,128)(2,1)S(1)}, u32[]{:S(2)}, u32[]{:S(2)}) %all-to-all-start.4) | async-done | bytes 524320 | tf_op jit(solution)/shard_map/all_to_all | solution.py:189
  204.6 0.9 add_convert_fusion
  205.6 0.6 convolution_convert_fusion
  206.2 7.9 %all_to_all.71 = bf16[4,32,768]{2,1,0:T(8,128)(2,1)S(1)} all-to-all(bf16[4,32,768]{2,1,0:T(8,128)(2,1)S(1)} %bitcast.86), channel_id=1, replica_groups=mesh['sb'=4,'sy'=2,'sz'=8,'head'=4] {'head'}, dimensions={0} | all-to-all | bytes 393216 | tf_op jit(solution)/shard_map/all_to_all | solution.py:209
  214.1 0.7 copy.73
  (72 shorter events, 1.6 us)
Async XLA Ops:
  7.2 198.4 %copy-start = (bf16[1024,768]{1,0:T(8,128)(2,1)S(1)}, bf16[1024,768]{1,0:T(8,128)(2,1)}, u32[]{:S(2)}) copy-start(bf16[1024,768]{1,0:T(8,128)(2,1)} %param.22) | copy-start | bytes 4718596
  7.2 13.7 %copy-start.8 = (f32[8,256]{1,0:T(8,128)S(1)}, f32[8,256]{1,0:T(8,128)}, u32[]{:S(2)}) copy-start(f32[8,256]{1,0:T(8,128)} %param.19) | copy-start | bytes 24580
  7.2 14.5 %copy-start.3 = (bf16[256,512]{1,0:T(8,128)(2,1)S(1)}, bf16[256,512]{1,0:T(8,128)(2,1)}, u32[]{:S(2)}) copy-start(bf16[256,512]{1,0:T(8,128)(2,1)} %param.16) | copy-start | bytes 786436
  7.2 15.0 %copy-start.4 = (bf16[256,128]{1,0:T(8,128)(2,1)S(1)}, bf16[256,128]{1,0:T(8,128)(2,1)}, u32[]{:S(2)}) copy-start(bf16[256,128]{1,0:T(8,128)(2,1)} %param.17) | copy-start | bytes 196612
  7.2 123.0 %all-gather.2.cloned.1.call-start = ((), (), s32[]{:S(2)}) async-start(), calls=%async_computation.6 | async-start | bytes 4456448 | tf_op jit(solution)/shard_map/all_gather | solution.py:161
  9.4 27.8 %copy-start.7 = (bf16[256,256]{1,0:T(8,128)(2,1)S(1)}, bf16[256,256]{1,0:T(8,128)(2,1)}, u32[]{:S(2)}) copy-start(bf16[256,256]{1,0:T(8,128)(2,1)} %param.13) | copy-start | bytes 393220
  19.8 29.0 %copy-start.5 = (bf16[256,128]{1,0:T(8,128)(2,1)S(1)}, bf16[256,128]{1,0:T(8,128)(2,1)}, u32[]{:S(2)}) copy-start(bf16[256,128]{1,0:T(8,128)(2,1)} %param.18) | copy-start | bytes 196612
  22.4 7.1 %collective-permute-start.6 = (f32[8,128,64]{1,2,0:T(8,128)S(1)}, f32[8,128,64]{1,2,0:T(8,128)S(1)}, u32[]{:S(2)}, u32[]{:S(2)}) collective-permute-start(f32[8,128,64]{1,2,0:T(8,128)S(1)} %convolution_bitcast_fusion.2), channel_id=1, source_target_pairs={{0,4},{4,8},{8,12},{12,16},{16,20},{20,24},{24,28},{28,32},{32,36}... | collective-permute-start | bytes 786440 | tf_op jit(solution)/shard_map/ppermute | solution.py:54
  29.6 15.5 %collective-permute-start.7 = (f32[8,128,64]{1,2,0:T(8,128)S(1)}, f32[8,128,64]{1,2,0:T(8,128)S(1)}, u32[]{:S(2)}, u32[]{:S(2)}) collective-permute-start(f32[8,128,64]{1,2,0:T(8,128)S(1)} %broadcast_select_fusion), channel_id=1, source_target_pairs={{0,4},{4,8},{8,12},{12,16},{16,20},{20,24},{24,28},{28,32},{32,36}... | collective-permute-start | bytes 786440 | tf_op jit(solution)/shard_map/ppermute | solution.py:54
  33.7 11.3 %collective-permute-start = (f32[8]{0:T(128)S(1)}, f32[8]{0:T(128)S(1)}, u32[]{:S(2)}, u32[]{:S(2)}) collective-permute-start(f32[8]{0:T(128)S(1)} %exp.13), channel_id=1, source_target_pairs={{0,4},{4,8},{8,12},{12,16},{16,20},{20,24},{24,28},{28,32},{32,36}... | collective-permute-start | bytes 104 | tf_op jit(solution)/shard_map/ppermute | solution.py:54
  38.0 88.6 %all-to-all-start = ((bf16[256,4,64]{0,2,1:T(8,128)(2,1)}), bf16[256,4,64]{0,2,1:T(8,128)(2,1)S(1)}, u32[]{:S(2)}, u32[]{:S(2)}) async-start(bf16[256,4,64]{0,2,1:T(8,128)(2,1)} %bitcast), calls=%async_computation | async-start | bytes 262144 | tf_op jit(solution)/shard_map/all_to_all | solution.py:156
  45.1 14.1 %collective-permute-start.8 = (f32[8,128,64]{1,2,0:T(8,128)S(1)}, f32[8,128,64]{1,2,0:T(8,128)S(1)}, u32[]{:S(2)}, u32[]{:S(2)}) collective-permute-start(f32[8,128,64]{1,2,0:T(8,128)S(1)} %add_select_fusion.5), channel_id=1, source_target_pairs={{0,8},{4,12},{8,16},{12,20},{16,24},{20,28},{24,32},{28,36},{32,40... | collective-permute-start | bytes 786440 | tf_op jit(solution)/shard_map/ppermute | solution.py:54
  49.0 10.2 %collective-permute-start.1 = (f32[8]{0:T(128)S(1)}, f32[8]{0:T(128)S(1)}, u32[]{:S(2)}, u32[]{:S(2)}) collective-permute-start(f32[8]{0:T(128)S(1)} %broadcast_select_fusion.2), channel_id=1, source_target_pairs={{0,4},{4,8},{8,12},{12,16},{16,20},{20,24},{24,28},{28,32},{32,36}... | collective-permute-start | bytes 104 | tf_op jit(solution)/shard_map/ppermute | solution.py:54
  59.4 17.6 %collective-permute-start.9 = (f32[8,128,64]{1,2,0:T(8,128)S(1)}, f32[8,128,64]{1,2,0:T(8,128)S(1)}, u32[]{:S(2)}, u32[]{:S(2)}) collective-permute-start(f32[8,128,64]{1,2,0:T(8,128)S(1)} %add_select_fusion.4), channel_id=1, source_target_pairs={{0,16},{4,20},{8,24},{12,28},{16,32},{20,36},{24,40},{28,44},{32,4... | collective-permute-start | bytes 786440 | tf_op jit(solution)/shard_map/ppermute | solution.py:54
  70.1 6.9 %collective-permute-start.2 = (f32[8]{0:T(128)S(1)}, f32[8]{0:T(128)S(1)}, u32[]{:S(2)}, u32[]{:S(2)}) collective-permute-start(f32[8]{0:T(128)S(1)} %broadcast_select_fusion.1), channel_id=1, source_target_pairs={{0,8},{4,12},{8,16},{12,20},{16,24},{20,28},{24,32},{28,36},{32,40... | collective-permute-start | bytes 104 | tf_op jit(solution)/shard_map/ppermute | solution.py:54
  77.0 0.5 copy-start.9
  77.5 25.8 %collective-permute-start.10 = (f32[8,128,64]{1,2,0:T(8,128)S(1)}, f32[8,128,64]{1,2,0:T(8,128)S(1)}, u32[]{:S(2)}, u32[]{:S(2)}) collective-permute-start(f32[8,128,64]{1,2,0:T(8,128)S(1)} %add_select_fusion.3), channel_id=1, source_target_pairs={{0,32},{4,36},{8,40},{12,44},{16,48},{20,52},{24,56},{28,60},{32,6... | collective-permute-start | bytes 786440 | tf_op jit(solution)/shard_map/ppermute | solution.py:54
  86.8 1.5 copy-start.10
  88.4 41.6 %copy-start.6 = (bf16[256,128]{1,0:T(8,128)(2,1)S(1)}, bf16[256,128]{1,0:T(8,128)(2,1)}, u32[]{:S(2)}) copy-start(bf16[256,128]{1,0:T(8,128)(2,1)} %param.18) | copy-start | bytes 196612
  88.4 14.8 %collective-permute-start.3 = (f32[8]{0:T(128)S(1)}, f32[8]{0:T(128)S(1)}, u32[]{:S(2)}, u32[]{:S(2)}) collective-permute-start(f32[8]{0:T(128)S(1)} %copy-done.10), channel_id=1, source_target_pairs={{0,16},{4,20},{8,24},{12,28},{16,32},{20,36},{24,40},{28,44},{32,4... | collective-permute-start | bytes 104 | tf_op jit(solution)/shard_map/ppermute | solution.py:54
  103.3 21.3 %collective-permute-start.11 = (f32[8,128,64]{1,2,0:T(8,128)S(1)}, f32[8,128,64]{1,2,0:T(8,128)S(1)}, u32[]{:S(2)}, u32[]{:S(2)}) collective-permute-start(f32[8,128,64]{1,2,0:T(8,128)S(1)} %add_select_fusion.2), channel_id=1, source_target_pairs={{0,64},{4,68},{8,72},{12,76},{16,80},{20,84},{24,88},{28,92},{32,9... | collective-permute-start | bytes 786440 | tf_op jit(solution)/shard_map/ppermute | solution.py:54
  116.0 4.6 %collective-permute-start.4 = (f32[8]{0:T(128)S(1)}, f32[8]{0:T(128)S(1)}, u32[]{:S(2)}, u32[]{:S(2)}) collective-permute-start(f32[8]{0:T(128)S(1)} %broadcast_select_fusion.4), channel_id=1, source_target_pairs={{0,32},{4,36},{8,40},{12,44},{16,48},{20,52},{24,56},{28,60},{32,6... | collective-permute-start | bytes 104 | tf_op jit(solution)/shard_map/ppermute | solution.py:54
  120.6 6.0 %collective-permute-start.5 = (f32[8]{0:T(128)S(1)}, f32[8]{0:T(128)S(1)}, u32[]{:S(2)}, u32[]{:S(2)}) collective-permute-start(f32[8]{0:T(128)S(1)} %broadcast_select_fusion.5), channel_id=1, source_target_pairs={{0,64},{4,68},{8,72},{12,76},{16,80},{20,84},{24,88},{28,92},{32,9... | collective-permute-start | bytes 104 | tf_op jit(solution)/shard_map/ppermute | solution.py:54
  124.7 5.2 %collective-permute-start.12 = (f32[8,128,64]{1,2,0:T(8,128)S(1)}, f32[8,128,64]{1,2,0:T(8,128)S(1)}, u32[]{:S(2)}, u32[]{:S(2)}) collective-permute-start(f32[8,128,64]{1,2,0:T(8,128)S(1)} %add_select_fusion.1), channel_id=1, source_target_pairs={{0,128},{4,132},{8,136},{12,140},{16,144},{20,148},{24,152},{28,15... | collective-permute-start | bytes 786440 | tf_op jit(solution)/shard_map/ppermute | solution.py:54
  150.4 26.0 %all-to-all-start.3 = ((bf16[4,2,4096]{2,1,0:T(2,128)(2,1)}), bf16[4,2,4096]{2,1,0:T(2,128)(2,1)S(1)}, u32[]{:S(2)}, u32[]{:S(2)}) async-start(bf16[4,2,4096]{2,1,0:T(2,128)(2,1)} %reshape.120), calls=%async_computation.3 | async-start | bytes 131072 | tf_op jit(solution)/shard_map/all_to_all | solution.py:168
  176.4 8.7 %all-to-all-start.2 = ((bf16[4,2,4096]{2,1,0:T(2,128)(2,1)}), bf16[4,2,4096]{2,1,0:T(2,128)(2,1)S(1)}, u32[]{:S(2)}, u32[]{:S(2)}) async-start(bf16[4,2,4096]{2,1,0:T(2,128)(2,1)} %reshape.122), calls=%async_computation.2 | async-start | bytes 131072 | tf_op jit(solution)/shard_map/all_to_all | solution.py:168
  180.6 4.8 %copy-start.1 = (bf16[256,1024]{1,0:T(8,128)(2,1)S(1)}, bf16[256,1024]{1,0:T(8,128)(2,1)}, u32[]{:S(2)}) copy-start(bf16[256,1024]{1,0:T(8,128)(2,1)} %param.20) | copy-start | bytes 1572868
  182.7 14.0 %copy-start.11 = (s32[256]{0:T(256)S(1)}, s32[256]{0:T(256)}, u32[]{:S(2)}) copy-start(s32[256]{0:T(256)} %param.23) | copy-start | bytes 3076
  182.7 14.1 %copy-start.12 = (s32[64]{0:T(128)S(1)}, s32[64]{0:T(128)}, u32[]{:S(2)}) copy-start(s32[64]{0:T(128)} %get-tuple-element.8) | copy-start | bytes 772
  182.7 14.0 %copy-start.13 = (s32[64]{0:T(128)S(1)}, s32[64]{0:T(128)}, u32[]{:S(2)}) copy-start(s32[64]{0:T(128)} %get-tuple-element.9) | copy-start | bytes 772
  186.5 18.0 %all-to-all-start.4 = ((bf16[4,64,1024]{2,1,0:T(8,128)(2,1)}), bf16[4,64,1024]{2,1,0:T(8,128)(2,1)S(1)}, u32[]{:S(2)}, u32[]{:S(2)}) async-start(bf16[4,64,1024]{2,1,0:T(8,128)(2,1)} %bitcast.28), calls=%async_computation.4 | async-start | bytes 1048576 | tf_op jit(solution)/shard_map/all_to_all | solution.py:189
  205.5 9.2 %copy-start.2 = (bf16[64,1024]{1,0:T(8,128)(2,1)}, bf16[64,1024]{1,0:T(8,128)(2,1)S(1)}, u32[]{:S(2)}) copy-start(bf16[64,1024]{1,0:T(8,128)(2,1)S(1)} %add_convert_fusion) | copy-start | bytes 393220
Sparse Core Ops, SparseCore 0:
  21.0 102.5 all-gather.1

commit v12 on v10

--- a/solution.py
+++ b/solution.py
@@ -51,7 +51,12 @@
 
     def shifted(tree, distance):
         pairs = [(j, j + distance) for j in range(devices - distance)]
-        return jax.tree.map(lambda part: lax.ppermute(part, axis, pairs), tree)
+        return jax.tree.map(
+            lambda part: lax.ppermute(
+                part.astype(jnp.bfloat16) if part.ndim == 3 else part, axis, pairs
+            ).astype(part.dtype),
+            tree,
+        )
 
     decay, state = shifted((total_decay, local_state), 1)
     first = mine >= 1

time: 211 us -> 203 us (0.962)
  starting transfers between devices: 105 us -> 86.1 us
  waiting for transfers between devices: 24.4 us -> 34.8 us
    all_gather x1, waiting for transfers between devices: 0.02 us -> 21.4 us  [per_device(): gathered = lax.all_gather(pair_t, ('sy', 'sz'), axis=2, tiled=True)]
    ppermute x13, waiting for transfers between devices: 13.8 us -> 2.79 us  [shifted(): lax.ppermute(part.astype(jnp.bfloat16) if part.ndim == 3 else part, axis,...]
    all_to_all x1, starting transfers between devices: 12.2 us -> 3.33 us  [spread(): lax.all_to_all(split, 'sb', split_axis=split.ndim - 2, concat_axis=split....]
    ppermute x13, starting transfers between devices: 73.9 us -> 68.1 us  [shifted(): lax.ppermute(part.astype(jnp.bfloat16) if part.ndim == 3 else part, axis,...]
    all_to_all x1, starting transfers between devices: 10.4 us -> 5.94 us  [per_device(): lax.all_to_all(attended_one.reshape(-1, 1, HDIM), 'sb', split_axis=0, con...]
  transfers between devices with their start and end apart: 17 -> 17, of which waited for: 10 -> 5; matrix products, arithmetic and copies ran while one was open for 3% -> 4% of each run, Pallas kernels for 0% -> 0%
where the time goes in v12:
time: 203 us; the launch traced here: 202 us
  starting transfers between devices  86.1 us (42%)
  waiting for transfers between devices  34.8 us (17%)
  Pallas kernels  29.4 us (14%)
  blocking collectives  18.1 us (9%)
  between operations  14.6 us (7%)
  local copies, waits for them, and re-layouts  8.39 us (4%)
  matrix products  6.08 us (3%)
  other arithmetic  4.66 us (2%)
    ppermute x13, starting transfers between devices, shifted(): lax.ppermute(part.astype(jnp.bfloat16) if part.ndim == 3 else part, axis,...  68.1 us
    pallas_call x1, Pallas kernels, flash_one_head_t(): pl.pallas_call(kernel, out_shape=jax.ShapeDtypeStruct((width, row_count),...  29.4 us
    all_gather x1, waiting for transfers between devices, per_device(): gathered = lax.all_gather(pair_t, ('sy', 'sz'), axis=2, tiled=True)  21.4 us
    all_to_all x1, blocking collectives, spread(): lax.all_to_all(split, 'sb', split_axis=split.ndim - 2, concat_axis=split....  10.2 us
    all_to_all x1, starting transfers between devices, per_device(): lax.all_to_all(partial.reshape(owner_count, sub_rows, partial.shape[1]),...  8.75 us
    all_to_all x1, blocking collectives, per_device(): lax.all_to_all(packed, 'head', split_axis=0, concat_axis=0, tiled=True)  7.89 us
    all_to_all x1, waiting for transfers between devices, per_device(): lax.all_to_all(partial.reshape(owner_count, sub_rows, partial.shape[1]),...  7.46 us
    all_to_all x1, starting transfers between devices, per_device(): lax.all_to_all(attended_one.reshape(-1, 1, HDIM), 'sb', split_axis=0, con...  5.94 us
  transfers between devices with their start and end apart: 17, of which 5 were waited for; matrix products, arithmetic and copies ran while one was open for 4% of the time, Pallas kernels for 0%

profile of v12, /device:TPU:1, one launch (start us, length us, event | category | flops | bytes accessed | tf_op | source)
XLA Modules:
  0.0 202.2 jit_solution(17581025779005266990)
XLA Ops:
  7.2 0.0 all-gather.2.cloned.1.call-start
  7.3 1.1 copy.47
  8.4 1.0 copy.48
  9.5 10.2 %all_to_all.55 = bf16[2,256,4,64]{1,3,0,2:T(8,128)(2,1)S(1)} all-to-all(bf16[2,256,4,64]{1,3,0,2:T(8,128)(2,1)S(1)} %copy.49), channel_id=1, replica_groups=mesh['sb'=4,'sy'=2,'sz'=8,'head'=4] {'sb'}, dimensions={2} | all-to-all | bytes 524288 | tf_op jit(solution)/shard_map/all_to_all | solution.py:161
  19.7 0.2 copy.50
  19.9 0.9 reshape.103
  20.8 0.6 reduce-window.6
  21.4 0.2 slice_reduce_fusion
  21.6 0.1 exponential_bitcast_fusion
  21.7 0.2 slice_reduce_fusion.1
  21.9 3.5 %collective-permute-start = (f32[8]{0:T(128)S(1)}, f32[8]{0:T(128)S(1)}, u32[]{:S(2)}, u32[]{:S(2)}) collective-permute-start(f32[8]{0:T(128)S(1)} %exp.13), channel_id=1, source_target_pairs={{0,4},{4,8},{8,12},{12,16},{16,20},{20,24},{24,28},{28,32},{32,36}... | collective-permute-start | bytes 104 | tf_op jit(solution)/shard_map/ppermute | solution.py:55
  25.4 0.8 copy.45
  26.2 3.3 %all-to-all-start = ((bf16[256,4,64]{0,2,1:T(8,128)(2,1)}), bf16[256,4,64]{0,2,1:T(8,128)(2,1)S(1)}, u32[]{:S(2)}, u32[]{:S(2)}) async-start(bf16[256,4,64]{0,2,1:T(8,128)(2,1)} %bitcast), calls=%async_computation | async-start | bytes 262144 | tf_op jit(solution)/shard_map/all_to_all | solution.py:161
  29.5 0.1 copy.54
  29.7 0.1 exponential_bitcast_fusion.1
  29.8 0.2 fusion.3
  30.0 3.6 %collective-permute-start.6 = (bf16[8,128,64]{1,2,0:T(8,128)(2,1)S(1)}, bf16[8,128,64]{1,2,0:T(8,128)(2,1)S(1)}, u32[]{:S(2)}, u32[]{:S(2)}) collective-permute-start(bf16[8,128,64]{1,2,0:T(8,128)(2,1)S(1)} %fusion.3), channel_id=1, source_target_pairs={{0,4},{4,8},{8,12},{12,16},{16,20},{20,24},{24,28},{28,32},{32,36}... | collective-permute-start | bytes 393224 | tf_op jit(solution)/shard_map/ppermute | solution.py:55
  33.6 0.2 fusion.37
  33.8 1.7 collective-permute-done.6
  35.5 3.8 %collective-permute-start.7 = (bf16[8,128,64]{1,2,0:T(8,128)(2,1)S(1)}, bf16[8,128,64]{1,2,0:T(8,128)(2,1)S(1)}, u32[]{:S(2)}, u32[]{:S(2)}) collective-permute-start(bf16[8,128,64]{1,2,0:T(8,128)(2,1)S(1)} %fusion.11), channel_id=1, source_target_pairs={{0,4},{4,8},{8,12},{12,16},{16,20},{20,24},{24,28},{28,32},{32,36}... | collective-permute-start | bytes 393224 | tf_op jit(solution)/shard_map/ppermute | solution.py:55
  39.3 4.7 %collective-permute-start.1 = (f32[8]{0:T(128)S(1)}, f32[8]{0:T(128)S(1)}, u32[]{:S(2)}, u32[]{:S(2)}) collective-permute-start(f32[8]{0:T(128)S(1)} %broadcast_select_fusion.1), channel_id=1, source_target_pairs={{0,4},{4,8},{8,12},{12,16},{16,20},{20,24},{24,28},{28,32},{32,36}... | collective-permute-start | bytes 104 | tf_op jit(solution)/shard_map/ppermute | solution.py:55
  44.1 0.1 fusion.13
  44.2 5.5 %collective-permute-start.8 = (bf16[8,128,64]{1,2,0:T(8,128)(2,1)S(1)}, bf16[8,128,64]{1,2,0:T(8,128)(2,1)S(1)}, u32[]{:S(2)}, u32[]{:S(2)}) collective-permute-start(bf16[8,128,64]{1,2,0:T(8,128)(2,1)S(1)} %fusion.13), channel_id=1, source_target_pairs={{0,8},{4,12},{8,16},{12,20},{16,24},{20,28},{24,32},{28,36},{32,40... | collective-permute-start | bytes 393224 | tf_op jit(solution)/shard_map/ppermute | solution.py:55
  49.8 6.1 %collective-permute-start.2 = (f32[8]{0:T(128)S(1)}, f32[8]{0:T(128)S(1)}, u32[]{:S(2)}, u32[]{:S(2)}) collective-permute-start(f32[8]{0:T(128)S(1)} %broadcast_select_fusion), channel_id=1, source_target_pairs={{0,8},{4,12},{8,16},{12,20},{16,24},{20,28},{24,32},{28,36},{32,40... | collective-permute-start | bytes 104 | tf_op jit(solution)/shard_map/ppermute | solution.py:55
  55.8 0.2 fusion.35
  56.0 10.1 %collective-permute-start.9 = (bf16[8,128,64]{1,2,0:T(8,128)(2,1)S(1)}, bf16[8,128,64]{1,2,0:T(8,128)(2,1)S(1)}, u32[]{:S(2)}, u32[]{:S(2)}) collective-permute-start(bf16[8,128,64]{1,2,0:T(8,128)(2,1)S(1)} %fusion.35), channel_id=1, source_target_pairs={{0,16},{4,20},{8,24},{12,28},{16,32},{20,36},{24,40},{28,44},{32,4... | collective-permute-start | bytes 393224 | tf_op jit(solution)/shard_map/ppermute | solution.py:55
  66.1 7.0 %collective-permute-start.3 = (f32[8]{0:T(128)S(1)}, f32[8]{0:T(128)S(1)}, u32[]{:S(2)}, u32[]{:S(2)}) collective-permute-start(f32[8]{0:T(128)S(1)} %broadcast_select_fusion.2), channel_id=1, source_target_pairs={{0,16},{4,20},{8,24},{12,28},{16,32},{20,36},{24,40},{28,44},{32,4... | collective-permute-start | bytes 104 | tf_op jit(solution)/shard_map/ppermute | solution.py:55
  73.2 0.3 fusion.14
  73.5 6.5 %collective-permute-start.10 = (bf16[8,128,64]{1,2,0:T(8,128)(2,1)S(1)}, bf16[8,128,64]{1,2,0:T(8,128)(2,1)S(1)}, u32[]{:S(2)}, u32[]{:S(2)}) collective-permute-start(bf16[8,128,64]{1,2,0:T(8,128)(2,1)S(1)} %fusion.14), channel_id=1, source_target_pairs={{0,32},{4,36},{8,40},{12,44},{16,48},{20,52},{24,56},{28,60},{32,6... | collective-permute-start | bytes 393224 | tf_op jit(solution)/shard_map/ppermute | solution.py:55
  80.0 5.9 %collective-permute-start.4 = (f32[8]{0:T(128)S(1)}, f32[8]{0:T(128)S(1)}, u32[]{:S(2)}, u32[]{:S(2)}) collective-permute-start(f32[8]{0:T(128)S(1)} %broadcast_select_fusion.3), channel_id=1, source_target_pairs={{0,32},{4,36},{8,40},{12,44},{16,48},{20,52},{24,56},{28,60},{32,6... | collective-permute-start | bytes 104 | tf_op jit(solution)/shard_map/ppermute | solution.py:55
  85.9 0.3 fusion.36
  86.3 3.5 %collective-permute-start.11 = (bf16[8,128,64]{1,2,0:T(8,128)(2,1)S(1)}, bf16[8,128,64]{1,2,0:T(8,128)(2,1)S(1)}, u32[]{:S(2)}, u32[]{:S(2)}) collective-permute-start(bf16[8,128,64]{1,2,0:T(8,128)(2,1)S(1)} %get-tuple-element.2), channel_id=1, source_target_pairs={{0,64},{4,68},{8,72},{12,76},{16,80},{20,84},{24,88},{28,92},{32,9... | collective-permute-start | bytes 393224 | tf_op jit(solution)/shard_map/ppermute | solution.py:55
  89.8 3.3 %collective-permute-start.5 = (f32[8]{0:T(128)S(1)}, f32[8]{0:T(128)S(1)}, u32[]{:S(2)}, u32[]{:S(2)}) collective-permute-start(f32[8]{0:T(128)S(1)} %broadcast_select_fusion.4), channel_id=1, source_target_pairs={{0,64},{4,68},{8,72},{12,76},{16,80},{20,84},{24,88},{28,92},{32,9... | collective-permute-start | bytes 104 | tf_op jit(solution)/shard_map/ppermute | solution.py:55
  93.2 0.1 fusion.15
  93.3 4.5 %collective-permute-start.12 = (bf16[8,128,64]{1,2,0:T(8,128)(2,1)S(1)}, bf16[8,128,64]{1,2,0:T(8,128)(2,1)S(1)}, u32[]{:S(2)}, u32[]{:S(2)}) collective-permute-start(bf16[8,128,64]{1,2,0:T(8,128)(2,1)S(1)} %fusion.15), channel_id=1, source_target_pairs={{0,128},{4,132},{8,136},{12,140},{16,144},{20,148},{24,152},{28,15... | collective-permute-start | bytes 393224 | tf_op jit(solution)/shard_map/ppermute | solution.py:55
  97.8 0.1 copy.46
  98.0 0.7 copy.55
  98.6 1.1 collective-permute-done.12
  99.7 0.3 fusion.1
  100.0 0.7 multiply_reduce_fusion
  100.7 0.1 multiply_convert_fusion.2
  100.8 21.4 %all-gather.2.cloned.1.call-done.k_ref.v_ref = bf16[2,64,16384]{2,1,0:T(8,128)(2,1)} async-done(((bf16[2,64,1024]{2,1,0:T(8,128)(2,1)}), bf16[2,64,16384]{2,1,0:T(8,128)(2,1)}) %all-gather.2.cloned.1.call-update) | async-done | bytes 4194320 | tf_op jit(solution)/shard_map/all_gather | solution.py:166
  122.2 29.4 %shard_map.131 = bf16[64,1024]{1,0:T(8,128)(2,1)} custom-call(bf16[64,1024]{1,0:T(8,128)(2,1)} %bitcast.71, bf16[2,64,16384]{2,1,0:T(8,128)(2,1)} %all-gather.2.cloned.1.call-done.k_ref.v_ref, bf16[2,64,16384]{2,1,0:T(8,128)(2,1)} %all-gather.2.cloned.1.call-done.k_ref.v_ref), custom_call_target="tpu_custom_call" | custom-call | tf_op jit(solution)/shard_map/pallas_call | solution.py:109
  151.6 0.5 broadcast.86
  152.1 1.6 reduce.4
  153.7 0.2 copy.56
  153.9 0.9 reshape.116
  154.8 5.9 %all-to-all-start.2 = ((bf16[4,2,8192]{2,1,0:T(2,128)(2,1)}), bf16[4,2,8192]{2,1,0:T(2,128)(2,1)S(1)}, u32[]{:S(2)}, u32[]{:S(2)}) async-start(bf16[4,2,8192]{2,1,0:T(2,128)(2,1)} %reshape.116), calls=%async_computation.2 | async-start | bytes 262144 | tf_op jit(solution)/shard_map/all_to_all | solution.py:168
  160.7 1.7 fusion.38
  162.4 3.1 %all-to-all-done.2 = bf16[4,2,8192]{2,1,0:T(2,128)(2,1)S(1)} async-done(((bf16[4,2,8192]{2,1,0:T(2,128)(2,1)}), bf16[4,2,8192]{2,1,0:T(2,128)(2,1)S(1)}, u32[]{:S(2)}, u32[]{:S(2)}) %all-to-all-start.2) | async-done | bytes 131104 | tf_op jit(solution)/shard_map/all_to_all | solution.py:168
  165.6 0.3 reshape.117
  165.9 0.3 copy.52
  166.2 0.1 all_to_all.46
  166.3 2.2 %fusion = bf16[256,1024]{1,0:T(8,128)(2,1)} fusion(f32[256,1024]{1,0:T(8,128)S(1)} %fusion.38, bf16[256,256]{0,1:T(8,128)(2,1)S(1)} %bitcast.73, bf16[256,1024]{1,0:T(8,128)(2,1)} %param.20), kind=kOutput, calls=%fused_computation.2 | convolution fusion | flops 134742016 | bytes 2228224 | tf_op jit(solution)/shard_map/dot_general | solution.py:184
  168.5 8.7 %all-to-all-start.3 = ((bf16[4,64,1024]{2,1,0:T(8,128)(2,1)}), bf16[4,64,1024]{2,1,0:T(8,128)(2,1)S(1)}, u32[]{:S(2)}, u32[]{:S(2)}) async-start(bf16[4,64,1024]{2,1,0:T(8,128)(2,1)} %bitcast.24), calls=%async_computation.3 | async-start | bytes 1048576 | tf_op jit(solution)/shard_map/all_to_all | solution.py:187
  177.3 0.1 dynamic_slice.7
  177.3 0.2 fusion.4
  177.6 0.1 multiply_add_fusion
  177.6 7.5 %all-to-all-done.3 = bf16[4,64,1024]{2,1,0:T(8,128)(2,1)S(1)} async-done(((bf16[4,64,1024]{2,1,0:T(8,128)(2,1)}), bf16[4,64,1024]{2,1,0:T(8,128)(2,1)S(1)}, u32[]{:S(2)}, u32[]{:S(2)}) %all-to-all-start.3) | async-done | bytes 524320 | tf_op jit(solution)/shard_map/all_to_all | solution.py:187
  185.1 0.1 convert_reduce_fusion
  185.2 0.9 add_convert_fusion
  186.1 0.6 convolution_convert_fusion
  186.8 7.9 %all_to_all.56 = bf16[4,32,768]{2,1,0:T(8,128)(2,1)S(1)} all-to-all(bf16[4,32,768]{2,1,0:T(8,128)(2,1)S(1)} %bitcast.69), channel_id=1, replica_groups=mesh['sb'=4,'sy'=2,'sz'=8,'head'=4] {'head'}, dimensions={0} | all-to-all | bytes 393216 | tf_op jit(solution)/shard_map/all_to_all | solution.py:207
  194.7 0.7 copy.58
  (46 shorter events, 0.3 us)
Async XLA Ops:
  7.2 179.0 %copy-start = (bf16[1024,768]{1,0:T(8,128)(2,1)S(1)}, bf16[1024,768]{1,0:T(8,128)(2,1)}, u32[]{:S(2)}) copy-start(bf16[1024,768]{1,0:T(8,128)(2,1)} %param.22) | copy-start | bytes 4718596
  7.2 13.6 %copy-start.6 = (f32[8,256]{1,0:T(8,128)S(1)}, f32[8,256]{1,0:T(8,128)}, u32[]{:S(2)}) copy-start(f32[8,256]{1,0:T(8,128)} %param.19) | copy-start | bytes 24580
  7.2 18.2 %copy-start.5 = (bf16[256,256]{1,0:T(8,128)(2,1)S(1)}, bf16[256,256]{1,0:T(8,128)(2,1)}, u32[]{:S(2)}) copy-start(bf16[256,256]{1,0:T(8,128)(2,1)} %param.13) | copy-start | bytes 393220
  7.2 22.3 %copy-start.2 = (bf16[256,512]{1,0:T(8,128)(2,1)S(1)}, bf16[256,512]{1,0:T(8,128)(2,1)}, u32[]{:S(2)}) copy-start(bf16[256,512]{1,0:T(8,128)(2,1)} %param.16) | copy-start | bytes 786436
  7.2 115.0 %all-gather.2.cloned.1.call-start = ((), (), s32[]{:S(2)}) async-start(), calls=%async_computation.5 | async-start | bytes 4456448 | tf_op jit(solution)/shard_map/all_gather | solution.py:166
  8.4 21.4 %copy-start.3 = (bf16[256,128]{1,0:T(8,128)(2,1)S(1)}, bf16[256,128]{1,0:T(8,128)(2,1)}, u32[]{:S(2)}) copy-start(bf16[256,128]{1,0:T(8,128)(2,1)} %param.17) | copy-start | bytes 196612
  9.5 24.1 %copy-start.4 = (bf16[256,128]{1,0:T(8,128)(2,1)S(1)}, bf16[256,128]{1,0:T(8,128)(2,1)}, u32[]{:S(2)}) copy-start(bf16[256,128]{1,0:T(8,128)(2,1)} %param.18) | copy-start | bytes 196612
  21.9 17.4 %collective-permute-start = (f32[8]{0:T(128)S(1)}, f32[8]{0:T(128)S(1)}, u32[]{:S(2)}, u32[]{:S(2)}) collective-permute-start(f32[8]{0:T(128)S(1)} %exp.13), channel_id=1, source_target_pairs={{0,4},{4,8},{8,12},{12,16},{16,20},{20,24},{24,28},{28,32},{32,36}... | collective-permute-start | bytes 104 | tf_op jit(solution)/shard_map/ppermute | solution.py:55
  26.2 71.6 %all-to-all-start = ((bf16[256,4,64]{0,2,1:T(8,128)(2,1)}), bf16[256,4,64]{0,2,1:T(8,128)(2,1)S(1)}, u32[]{:S(2)}, u32[]{:S(2)}) async-start(bf16[256,4,64]{0,2,1:T(8,128)(2,1)} %bitcast), calls=%async_computation | async-start | bytes 262144 | tf_op jit(solution)/shard_map/all_to_all | solution.py:161
  30.0 5.5 %collective-permute-start.6 = (bf16[8,128,64]{1,2,0:T(8,128)(2,1)S(1)}, bf16[8,128,64]{1,2,0:T(8,128)(2,1)S(1)}, u32[]{:S(2)}, u32[]{:S(2)}) collective-permute-start(bf16[8,128,64]{1,2,0:T(8,128)(2,1)S(1)} %fusion.3), channel_id=1, source_target_pairs={{0,4},{4,8},{8,12},{12,16},{16,20},{20,24},{24,28},{28,32},{32,36}... | collective-permute-start | bytes 393224 | tf_op jit(solution)/shard_map/ppermute | solution.py:55
  35.5 8.6 %collective-permute-start.7 = (bf16[8,128,64]{1,2,0:T(8,128)(2,1)S(1)}, bf16[8,128,64]{1,2,0:T(8,128)(2,1)S(1)}, u32[]{:S(2)}, u32[]{:S(2)}) collective-permute-start(bf16[8,128,64]{1,2,0:T(8,128)(2,1)S(1)} %fusion.11), channel_id=1, source_target_pairs={{0,4},{4,8},{8,12},{12,16},{16,20},{20,24},{24,28},{28,32},{32,36}... | collective-permute-start | bytes 393224 | tf_op jit(solution)/shard_map/ppermute | solution.py:55
  39.3 10.4 %collective-permute-start.1 = (f32[8]{0:T(128)S(1)}, f32[8]{0:T(128)S(1)}, u32[]{:S(2)}, u32[]{:S(2)}) collective-permute-start(f32[8]{0:T(128)S(1)} %broadcast_select_fusion.1), channel_id=1, source_target_pairs={{0,4},{4,8},{8,12},{12,16},{16,20},{20,24},{24,28},{28,32},{32,36}... | collective-permute-start | bytes 104 | tf_op jit(solution)/shard_map/ppermute | solution.py:55
  44.2 11.6 %collective-permute-start.8 = (bf16[8,128,64]{1,2,0:T(8,128)(2,1)S(1)}, bf16[8,128,64]{1,2,0:T(8,128)(2,1)S(1)}, u32[]{:S(2)}, u32[]{:S(2)}) collective-permute-start(bf16[8,128,64]{1,2,0:T(8,128)(2,1)S(1)} %fusion.13), channel_id=1, source_target_pairs={{0,8},{4,12},{8,16},{12,20},{16,24},{20,28},{24,32},{28,36},{32,40... | collective-permute-start | bytes 393224 | tf_op jit(solution)/shard_map/ppermute | solution.py:55
  49.8 16.4 %collective-permute-start.2 = (f32[8]{0:T(128)S(1)}, f32[8]{0:T(128)S(1)}, u32[]{:S(2)}, u32[]{:S(2)}) collective-permute-start(f32[8]{0:T(128)S(1)} %broadcast_select_fusion), channel_id=1, source_target_pairs={{0,8},{4,12},{8,16},{12,20},{16,24},{20,28},{24,32},{28,36},{32,40... | collective-permute-start | bytes 104 | tf_op jit(solution)/shard_map/ppermute | solution.py:55
  56.0 17.2 %collective-permute-start.9 = (bf16[8,128,64]{1,2,0:T(8,128)(2,1)S(1)}, bf16[8,128,64]{1,2,0:T(8,128)(2,1)S(1)}, u32[]{:S(2)}, u32[]{:S(2)}) collective-permute-start(bf16[8,128,64]{1,2,0:T(8,128)(2,1)S(1)} %fusion.35), channel_id=1, source_target_pairs={{0,16},{4,20},{8,24},{12,28},{16,32},{20,36},{24,40},{28,44},{32,4... | collective-permute-start | bytes 393224 | tf_op jit(solution)/shard_map/ppermute | solution.py:55
  66.1 13.9 %collective-permute-start.3 = (f32[8]{0:T(128)S(1)}, f32[8]{0:T(128)S(1)}, u32[]{:S(2)}, u32[]{:S(2)}) collective-permute-start(f32[8]{0:T(128)S(1)} %broadcast_select_fusion.2), channel_id=1, source_target_pairs={{0,16},{4,20},{8,24},{12,28},{16,32},{20,36},{24,40},{28,44},{32,4... | collective-permute-start | bytes 104 | tf_op jit(solution)/shard_map/ppermute | solution.py:55
  73.5 12.4 %collective-permute-start.10 = (bf16[8,128,64]{1,2,0:T(8,128)(2,1)S(1)}, bf16[8,128,64]{1,2,0:T(8,128)(2,1)S(1)}, u32[]{:S(2)}, u32[]{:S(2)}) collective-permute-start(bf16[8,128,64]{1,2,0:T(8,128)(2,1)S(1)} %fusion.14), channel_id=1, source_target_pairs={{0,32},{4,36},{8,40},{12,44},{16,48},{20,52},{24,56},{28,60},{32,6... | collective-permute-start | bytes 393224 | tf_op jit(solution)/shard_map/ppermute | solution.py:55
  80.0 9.8 %collective-permute-start.4 = (f32[8]{0:T(128)S(1)}, f32[8]{0:T(128)S(1)}, u32[]{:S(2)}, u32[]{:S(2)}) collective-permute-start(f32[8]{0:T(128)S(1)} %broadcast_select_fusion.3), channel_id=1, source_target_pairs={{0,32},{4,36},{8,40},{12,44},{16,48},{20,52},{24,56},{28,60},{32,6... | collective-permute-start | bytes 104 | tf_op jit(solution)/shard_map/ppermute | solution.py:55
  86.3 6.9 %collective-permute-start.11 = (bf16[8,128,64]{1,2,0:T(8,128)(2,1)S(1)}, bf16[8,128,64]{1,2,0:T(8,128)(2,1)S(1)}, u32[]{:S(2)}, u32[]{:S(2)}) collective-permute-start(bf16[8,128,64]{1,2,0:T(8,128)(2,1)S(1)} %get-tuple-element.2), channel_id=1, source_target_pairs={{0,64},{4,68},{8,72},{12,76},{16,80},{20,84},{24,88},{28,92},{32,9... | collective-permute-start | bytes 393224 | tf_op jit(solution)/shard_map/ppermute | solution.py:55
  89.8 8.0 %collective-permute-start.5 = (f32[8]{0:T(128)S(1)}, f32[8]{0:T(128)S(1)}, u32[]{:S(2)}, u32[]{:S(2)}) collective-permute-start(f32[8]{0:T(128)S(1)} %broadcast_select_fusion.4), channel_id=1, source_target_pairs={{0,64},{4,68},{8,72},{12,76},{16,80},{20,84},{24,88},{28,92},{32,9... | collective-permute-start | bytes 104 | tf_op jit(solution)/shard_map/ppermute | solution.py:55
  93.3 6.4 %collective-permute-start.12 = (bf16[8,128,64]{1,2,0:T(8,128)(2,1)S(1)}, bf16[8,128,64]{1,2,0:T(8,128)(2,1)S(1)}, u32[]{:S(2)}, u32[]{:S(2)}) collective-permute-start(bf16[8,128,64]{1,2,0:T(8,128)(2,1)S(1)} %fusion.15), channel_id=1, source_target_pairs={{0,128},{4,132},{8,136},{12,140},{16,144},{20,148},{24,152},{28,15... | collective-permute-start | bytes 393224 | tf_op jit(solution)/shard_map/ppermute | solution.py:55
  154.8 10.8 %all-to-all-start.2 = ((bf16[4,2,8192]{2,1,0:T(2,128)(2,1)}), bf16[4,2,8192]{2,1,0:T(2,128)(2,1)S(1)}, u32[]{:S(2)}, u32[]{:S(2)}) async-start(bf16[4,2,8192]{2,1,0:T(2,128)(2,1)} %reshape.116), calls=%async_computation.2 | async-start | bytes 262144 | tf_op jit(solution)/shard_map/all_to_all | solution.py:168
  165.9 11.4 %copy-start.7 = (s32[256]{0:T(256)S(1)}, s32[256]{0:T(256)}, u32[]{:S(2)}) copy-start(s32[256]{0:T(256)} %param.23) | copy-start | bytes 3076
  168.5 16.6 %all-to-all-start.3 = ((bf16[4,64,1024]{2,1,0:T(8,128)(2,1)}), bf16[4,64,1024]{2,1,0:T(8,128)(2,1)S(1)}, u32[]{:S(2)}, u32[]{:S(2)}) async-start(bf16[4,64,1024]{2,1,0:T(8,128)(2,1)} %bitcast.24), calls=%async_computation.3 | async-start | bytes 1048576 | tf_op jit(solution)/shard_map/all_to_all | solution.py:187
  186.1 9.2 %copy-start.1 = (bf16[64,1024]{1,0:T(8,128)(2,1)}, bf16[64,1024]{1,0:T(8,128)(2,1)S(1)}, u32[]{:S(2)}) copy-start(bf16[64,1024]{1,0:T(8,128)(2,1)S(1)} %add_convert_fusion) | copy-start | bytes 393220
Sparse Core Ops, SparseCore 0:
  20.9 101.2 all-gather.1

commit v13 on v12

--- a/solution.py
+++ b/solution.py
@@ -45,7 +45,7 @@
 
 
 def pass_states(local_state, total_decay):
-    axis = ("sb", "sy", "sz")
+    axis = ("sx", "sy", "sh", "sz")
     devices = lax.axis_size(axis)
     mine = lax.axis_index(axis)
 
@@ -158,15 +158,15 @@
 
     def spread(part):
         split = part.reshape(part.shape[:-1] + (head_count, HDIM))
-        return lax.all_to_all(split, "sb", split_axis=split.ndim - 2, concat_axis=split.ndim - 3, tiled=True)
+        return lax.all_to_all(split, ("sy", "sh"), split_axis=split.ndim - 2, concat_axis=split.ndim - 3, tiled=True)
 
     query_heads = spread(queries)
     pair = spread(jnp.stack([key_rows, values]))
     pair_t = pair.reshape(2, -1, HDIM).transpose(0, 2, 1)
-    gathered = lax.all_gather(pair_t, ("sy", "sz"), axis=2, tiled=True)
+    gathered = lax.all_gather(pair_t, ("sx", "sz"), axis=2, tiled=True)
     attended_one = flash_one_head_t(query_heads.reshape(-1, HDIM).T, gathered).T
     attended = lax.all_to_all(
-        attended_one.reshape(-1, 1, HDIM), "sb", split_axis=0, concat_axis=1, tiled=True
+        attended_one.reshape(-1, 1, HDIM), ("sy", "sh"), split_axis=0, concat_axis=1, tiled=True
     ).reshape(row_count, head_count * HDIM)
     cumulative, inner_part, local_state, total_decay = chain_pieces(
         ssm_input, write_proj, read_proj, log_decay
@@ -212,12 +212,11 @@
 def solution(mesh):
     seq_count = mesh.shape["seq"]
     outer = math.gcd(seq_count, mesh.shape["head"])
-    middle = math.gcd(seq_count // outer, 2)
     split_mesh = Mesh(
-        mesh.devices.reshape(outer, middle, seq_count // outer // middle, mesh.shape["head"]),
-        ("sb", "sy", "sz", "head"),
-    )
-    seq = ("sb", "sy", "sz")
+        mesh.devices.reshape(outer, 2, 2, seq_count // outer // 4, mesh.shape["head"]),
+        ("sx", "sy", "sh", "sz", "head"),
+    )
+    seq = ("sx", "sy", "sh", "sz")
     in_specs = (
         P(seq, None),
         P(seq, "head"),
@@ -232,7 +231,7 @@
         P(),
         P(seq),
     )
-    out_specs = (P(("sb", "sy", "sz", "head"), None), P(seq, "head", None, None, None))
+    out_specs = (P(("sx", "sy", "sh", "sz", "head"), None), P(seq, "head", None, None, None))
     return jax.shard_map(
         per_device, mesh=split_mesh, in_specs=in_specs, out_specs=out_specs, check_vma=False
     )

time: 203 us -> 235 us (1.16)
  waiting for transfers between devices: 34.8 us -> 46.4 us
  blocking collectives: 18.1 us -> 29.4 us
  starting transfers between devices: 86.1 us -> 95 us
    ppermute x13, waiting for transfers between devices: 2.79 us -> 16.5 us  [shifted(): lax.ppermute(part.astype(jnp.bfloat16) if part.ndim == 3 else part, axis,...]
    all_to_all x1, blocking collectives: 10.2 us -> 21.5 us  [spread(): lax.all_to_all(split, ('sy', 'sh'), split_axis=split.ndim - 2, concat_axi...]
    ppermute x13, starting transfers between devices: 68.1 us -> 77.3 us  [shifted(): lax.ppermute(part.astype(jnp.bfloat16) if part.ndim == 3 else part, axis,...]
    all_gather x1, waiting for transfers between devices: 21.4 us -> 14.7 us  [per_device(): gathered = lax.all_gather(pair_t, ('sx', 'sz'), axis=2, tiled=True)]
    all_to_all x2, waiting for transfers between devices: 3.14 us -> 7.7 us  [the longest x1 7.69 us: per_device(): lax.all_to_all(attended_one.reshape(-1, 1, HDIM), ('sy', 'sh'), split_axi...]
    all_to_all x1, starting transfers between devices: 8.75 us -> 6.26 us  [per_device(): lax.all_to_all(partial.reshape(owner_count, sub_rows, partial.shape[1]),...]
  transfers between devices with their start and end apart: 17 -> 17, of which waited for: 5 -> 8; matrix products, arithmetic and copies ran while one was open for 4% -> 3% of each run, Pallas kernels for 0% -> 0%
where the time goes in v13:
time: 235 us; the launch traced here: 234 us
  starting transfers between devices  95 us (40%)
  waiting for transfers between devices  46.4 us (20%)
  blocking collectives  29.4 us (13%)
  Pallas kernels  29.4 us (13%)
  between operations  14.6 us (6%)
  local copies, waits for them, and re-layouts  8.39 us (4%)
  matrix products  6.08 us (3%)
  other arithmetic  4.65 us (2%)
    ppermute x13, starting transfers between devices, shifted(): lax.ppermute(part.astype(jnp.bfloat16) if part.ndim == 3 else part, axis,...  77.3 us
    pallas_call x1, Pallas kernels, flash_one_head_t(): pl.pallas_call(kernel, out_shape=jax.ShapeDtypeStruct((width, row_count),...  29.4 us
    all_to_all x1, blocking collectives, spread(): lax.all_to_all(split, ('sy', 'sh'), split_axis=split.ndim - 2, concat_axi...  21.5 us
    ppermute x13, waiting for transfers between devices, shifted(): lax.ppermute(part.astype(jnp.bfloat16) if part.ndim == 3 else part, axis,...  16.5 us
    all_gather x1, waiting for transfers between devices, per_device(): gathered = lax.all_gather(pair_t, ('sx', 'sz'), axis=2, tiled=True)  14.7 us
    all_to_all x1, starting transfers between devices, per_device(): lax.all_to_all(attended_one.reshape(-1, 1, HDIM), ('sy', 'sh'), split_axi...  8.14 us
    all_to_all x1, blocking collectives, per_device(): lax.all_to_all(packed, 'head', split_axis=0, concat_axis=0, tiled=True)  7.89 us
    all_to_all x1, waiting for transfers between devices, per_device(): lax.all_to_all(attended_one.reshape(-1, 1, HDIM), ('sy', 'sh'), split_axi...  7.69 us
  transfers between devices with their start and end apart: 17, of which 8 were waited for; matrix products, arithmetic and copies ran while one was open for 3% of the time, Pallas kernels for 0%

profile of v13, /device:TPU:1, one launch (start us, length us, event | category | flops | bytes accessed | tf_op | source)
XLA Modules:
  0.0 233.9 jit_solution(1871587745838356193)
XLA Ops:
  7.3 1.1 copy.47
  8.4 1.0 copy.48
  9.5 21.5 %all_to_all.55 = bf16[2,256,4,64]{1,3,0,2:T(8,128)(2,1)S(1)} all-to-all(bf16[2,256,4,64]{1,3,0,2:T(8,128)(2,1)S(1)} %copy.49), channel_id=1, replica_groups=mesh['sx'=4,'sy'=2,'sh'=2,'sz'=4,'head'=4] {'sy','sh'}, dimensions={2} | all-to-all | bytes 524288 | tf_op jit(solution)/shard_map/all_to_all | solution.py:161
  31.0 0.2 copy.50
  31.2 0.9 reshape.103
  32.1 0.6 reduce-window.6
  32.7 0.2 slice_reduce_fusion
  32.9 0.1 exponential_bitcast_fusion
  33.0 0.2 slice_reduce_fusion.1
  33.2 5.7 %collective-permute-start = (f32[8]{0:T(128)S(1)}, f32[8]{0:T(128)S(1)}, u32[]{:S(2)}, u32[]{:S(2)}) collective-permute-start(f32[8]{0:T(128)S(1)} %exp.13), channel_id=1, source_target_pairs={{0,4},{4,8},{8,12},{12,16},{16,20},{20,24},{24,28},{28,32},{32,36}... | collective-permute-start | bytes 104 | tf_op jit(solution)/shard_map/ppermute | solution.py:55
  38.9 0.8 copy.45
  39.7 3.3 %all-to-all-start = ((bf16[256,4,64]{0,2,1:T(8,128)(2,1)}), bf16[256,4,64]{0,2,1:T(8,128)(2,1)S(1)}, u32[]{:S(2)}, u32[]{:S(2)}) async-start(bf16[256,4,64]{0,2,1:T(8,128)(2,1)} %bitcast), calls=%async_computation | async-start | bytes 262144 | tf_op jit(solution)/shard_map/all_to_all | solution.py:161
  43.0 0.1 copy.54
  43.2 0.2 fusion.3
  43.5 2.7 %collective-permute-start.6 = (bf16[8,128,64]{1,2,0:T(8,128)(2,1)S(1)}, bf16[8,128,64]{1,2,0:T(8,128)(2,1)S(1)}, u32[]{:S(2)}, u32[]{:S(2)}) collective-permute-start(bf16[8,128,64]{1,2,0:T(8,128)(2,1)S(1)} %fusion.3), channel_id=1, source_target_pairs={{0,4},{4,8},{8,12},{12,16},{16,20},{20,24},{24,28},{28,32},{32,36}... | collective-permute-start | bytes 393224 | tf_op jit(solution)/shard_map/ppermute | solution.py:55
  46.2 0.2 fusion.37
  46.4 6.5 %collective-permute-done.6 = bf16[8,128,64]{1,2,0:T(8,128)(2,1)S(1)} collective-permute-done((bf16[8,128,64]{1,2,0:T(8,128)(2,1)S(1)}, bf16[8,128,64]{1,2,0:T(8,128)(2,1)S(1)}, u32[]{:S(2)}, u32[]{:S(2)}) %collective-permute-start.6) | collective-permute-done | bytes 131104 | tf_op jit(solution)/shard_map/ppermute | solution.py:55
  53.0 4.9 %collective-permute-start.7 = (bf16[8,128,64]{1,2,0:T(8,128)(2,1)S(1)}, bf16[8,128,64]{1,2,0:T(8,128)(2,1)S(1)}, u32[]{:S(2)}, u32[]{:S(2)}) collective-permute-start(bf16[8,128,64]{1,2,0:T(8,128)(2,1)S(1)} %fusion.11), channel_id=1, source_target_pairs={{0,4},{4,8},{8,12},{12,16},{16,20},{20,24},{24,28},{28,32},{32,36}... | collective-permute-start | bytes 393224 | tf_op jit(solution)/shard_map/ppermute | solution.py:55
  57.9 4.9 %collective-permute-start.1 = (f32[8]{0:T(128)S(1)}, f32[8]{0:T(128)S(1)}, u32[]{:S(2)}, u32[]{:S(2)}) collective-permute-start(f32[8]{0:T(128)S(1)} %broadcast_select_fusion.1), channel_id=1, source_target_pairs={{0,4},{4,8},{8,12},{12,16},{16,20},{20,24},{24,28},{28,32},{32,36}... | collective-permute-start | bytes 104 | tf_op jit(solution)/shard_map/ppermute | solution.py:55
  62.8 0.5 collective-permute-done.7
  63.3 0.1 fusion.13
  63.4 10.4 %collective-permute-start.8 = (bf16[8,128,64]{1,2,0:T(8,128)(2,1)S(1)}, bf16[8,128,64]{1,2,0:T(8,128)(2,1)S(1)}, u32[]{:S(2)}, u32[]{:S(2)}) collective-permute-start(bf16[8,128,64]{1,2,0:T(8,128)(2,1)S(1)} %fusion.13), channel_id=1, source_target_pairs={{0,8},{4,12},{8,16},{12,20},{16,24},{20,28},{24,32},{28,36},{32,40... | collective-permute-start | bytes 393224 | tf_op jit(solution)/shard_map/ppermute | solution.py:55
  73.8 1.9 collective-permute-start.2
  75.7 4.4 %collective-permute-done.8 = bf16[8,128,64]{1,2,0:T(8,128)(2,1)S(1)} collective-permute-done((bf16[8,128,64]{1,2,0:T(8,128)(2,1)S(1)}, bf16[8,128,64]{1,2,0:T(8,128)(2,1)S(1)}, u32[]{:S(2)}, u32[]{:S(2)}) %collective-permute-start.8) | collective-permute-done | bytes 131104 | tf_op jit(solution)/shard_map/ppermute | solution.py:55
  80.1 0.2 fusion.35
  80.3 10.3 %collective-permute-start.9 = (bf16[8,128,64]{1,2,0:T(8,128)(2,1)S(1)}, bf16[8,128,64]{1,2,0:T(8,128)(2,1)S(1)}, u32[]{:S(2)}, u32[]{:S(2)}) collective-permute-start(bf16[8,128,64]{1,2,0:T(8,128)(2,1)S(1)} %fusion.35), channel_id=1, source_target_pairs={{0,16},{4,20},{8,24},{12,28},{16,32},{20,36},{24,40},{28,44},{32,4... | collective-permute-start | bytes 393224 | tf_op jit(solution)/shard_map/ppermute | solution.py:55
  90.6 6.5 %collective-permute-start.3 = (f32[8]{0:T(128)S(1)}, f32[8]{0:T(128)S(1)}, u32[]{:S(2)}, u32[]{:S(2)}) collective-permute-start(f32[8]{0:T(128)S(1)} %broadcast_select_fusion.2), channel_id=1, source_target_pairs={{0,16},{4,20},{8,24},{12,28},{16,32},{20,36},{24,40},{28,44},{32,4... | collective-permute-start | bytes 104 | tf_op jit(solution)/shard_map/ppermute | solution.py:55
  97.1 0.3 fusion.14
  97.4 8.7 %collective-permute-start.10 = (bf16[8,128,64]{1,2,0:T(8,128)(2,1)S(1)}, bf16[8,128,64]{1,2,0:T(8,128)(2,1)S(1)}, u32[]{:S(2)}, u32[]{:S(2)}) collective-permute-start(bf16[8,128,64]{1,2,0:T(8,128)(2,1)S(1)} %fusion.14), channel_id=1, source_target_pairs={{0,32},{4,36},{8,40},{12,44},{16,48},{20,52},{24,56},{28,60},{32,6... | collective-permute-start | bytes 393224 | tf_op jit(solution)/shard_map/ppermute | solution.py:55
  106.2 8.0 %collective-permute-start.4 = (f32[8]{0:T(128)S(1)}, f32[8]{0:T(128)S(1)}, u32[]{:S(2)}, u32[]{:S(2)}) collective-permute-start(f32[8]{0:T(128)S(1)} %broadcast_select_fusion.3), channel_id=1, source_target_pairs={{0,32},{4,36},{8,40},{12,44},{16,48},{20,52},{24,56},{28,60},{32,6... | collective-permute-start | bytes 104 | tf_op jit(solution)/shard_map/ppermute | solution.py:55
  114.1 0.3 fusion.36
  114.5 5.2 %collective-permute-start.11 = (bf16[8,128,64]{1,2,0:T(8,128)(2,1)S(1)}, bf16[8,128,64]{1,2,0:T(8,128)(2,1)S(1)}, u32[]{:S(2)}, u32[]{:S(2)}) collective-permute-start(bf16[8,128,64]{1,2,0:T(8,128)(2,1)S(1)} %get-tuple-element.2), channel_id=1, source_target_pairs={{0,64},{4,68},{8,72},{12,76},{16,80},{20,84},{24,88},{28,92},{32,9... | collective-permute-start | bytes 393224 | tf_op jit(solution)/shard_map/ppermute | solution.py:55
  119.7 2.7 %collective-permute-start.5 = (f32[8]{0:T(128)S(1)}, f32[8]{0:T(128)S(1)}, u32[]{:S(2)}, u32[]{:S(2)}) collective-permute-start(f32[8]{0:T(128)S(1)} %broadcast_select_fusion.4), channel_id=1, source_target_pairs={{0,64},{4,68},{8,72},{12,76},{16,80},{20,84},{24,88},{28,92},{32,9... | collective-permute-start | bytes 104 | tf_op jit(solution)/shard_map/ppermute | solution.py:55
  122.4 0.4 collective-permute-done.11
  122.9 0.1 fusion.15
  123.0 5.5 %collective-permute-start.12 = (bf16[8,128,64]{1,2,0:T(8,128)(2,1)S(1)}, bf16[8,128,64]{1,2,0:T(8,128)(2,1)S(1)}, u32[]{:S(2)}, u32[]{:S(2)}) collective-permute-start(bf16[8,128,64]{1,2,0:T(8,128)(2,1)S(1)} %fusion.15), channel_id=1, source_target_pairs={{0,128},{4,132},{8,136},{12,140},{16,144},{20,148},{24,152},{28,15... | collective-permute-start | bytes 393224 | tf_op jit(solution)/shard_map/ppermute | solution.py:55
  128.5 0.1 copy.46
  128.6 0.7 copy.55
  129.3 4.6 %collective-permute-done.12 = bf16[8,128,64]{1,2,0:T(8,128)(2,1)S(1)} collective-permute-done((bf16[8,128,64]{1,2,0:T(8,128)(2,1)S(1)}, bf16[8,128,64]{1,2,0:T(8,128)(2,1)S(1)}, u32[]{:S(2)}, u32[]{:S(2)}) %collective-permute-start.12) | collective-permute-done | bytes 131104 | tf_op jit(solution)/shard_map/ppermute | solution.py:55
  133.9 0.3 fusion.1
  134.2 0.7 multiply_reduce_fusion
  135.0 14.7 %all-gather.2.cloned.1.call-done.k_ref.v_ref = bf16[2,64,16384]{2,1,0:T(8,128)(2,1)} async-done(((bf16[2,64,1024]{2,1,0:T(8,128)(2,1)}), bf16[2,64,16384]{2,1,0:T(8,128)(2,1)}) %all-gather.2.cloned.1.call-update) | async-done | bytes 4194320 | tf_op jit(solution)/shard_map/all_gather | solution.py:166
  149.7 29.4 %shard_map.131 = bf16[64,1024]{1,0:T(8,128)(2,1)} custom-call(bf16[64,1024]{1,0:T(8,128)(2,1)} %bitcast.71, bf16[2,64,16384]{2,1,0:T(8,128)(2,1)} %all-gather.2.cloned.1.call-done.k_ref.v_ref, bf16[2,64,16384]{2,1,0:T(8,128)(2,1)} %all-gather.2.cloned.1.call-done.k_ref.v_ref), custom_call_target="tpu_custom_call" | custom-call | tf_op jit(solution)/shard_map/pallas_call | solution.py:109
  179.1 0.5 broadcast.86
  179.6 1.6 reduce.4
  181.2 0.2 copy.56
  181.3 0.9 reshape.116
  182.3 8.1 %all-to-all-start.2 = ((bf16[4,2,8192]{2,1,0:T(2,128)(2,1)}), bf16[4,2,8192]{2,1,0:T(2,128)(2,1)S(1)}, u32[]{:S(2)}, u32[]{:S(2)}) async-start(bf16[4,2,8192]{2,1,0:T(2,128)(2,1)} %reshape.116), calls=%async_computation.2 | async-start | bytes 262144 | tf_op jit(solution)/shard_map/all_to_all | solution.py:168
  190.4 1.7 fusion.38
  192.1 7.7 %all-to-all-done.2 = bf16[4,2,8192]{2,1,0:T(2,128)(2,1)S(1)} async-done(((bf16[4,2,8192]{2,1,0:T(2,128)(2,1)}), bf16[4,2,8192]{2,1,0:T(2,128)(2,1)S(1)}, u32[]{:S(2)}, u32[]{:S(2)}) %all-to-all-start.2) | async-done | bytes 131104 | tf_op jit(solution)/shard_map/all_to_all | solution.py:168
  199.8 0.3 reshape.117
  200.1 0.3 copy.52
  200.4 0.1 all_to_all.46
  200.6 2.2 fusion
  202.7 6.3 %all-to-all-start.3 = ((bf16[4,64,1024]{2,1,0:T(8,128)(2,1)}), bf16[4,64,1024]{2,1,0:T(8,128)(2,1)S(1)}, u32[]{:S(2)}, u32[]{:S(2)}) async-start(bf16[4,64,1024]{2,1,0:T(8,128)(2,1)} %bitcast.24), calls=%async_computation.3 | async-start | bytes 1048576 | tf_op jit(solution)/shard_map/all_to_all | solution.py:187
  209.0 0.1 dynamic_slice.7
  209.1 0.2 fusion.4
  209.3 0.1 multiply_add_fusion
  209.4 7.5 %all-to-all-done.3 = bf16[4,64,1024]{2,1,0:T(8,128)(2,1)S(1)} async-done(((bf16[4,64,1024]{2,1,0:T(8,128)(2,1)}), bf16[4,64,1024]{2,1,0:T(8,128)(2,1)S(1)}, u32[]{:S(2)}, u32[]{:S(2)}) %all-to-all-start.3) | async-done | bytes 524320 | tf_op jit(solution)/shard_map/all_to_all | solution.py:187
  216.8 0.1 convert_reduce_fusion
  216.9 0.9 add_convert_fusion
  217.9 0.6 convolution_convert_fusion
  218.5 7.9 %all_to_all.56 = bf16[4,32,768]{2,1,0:T(8,128)(2,1)S(1)} all-to-all(bf16[4,32,768]{2,1,0:T(8,128)(2,1)S(1)} %bitcast.69), channel_id=1, replica_groups=mesh['sx'=4,'sy'=2,'sh'=2,'sz'=4,'head'=4] {'head'}, dimensions={0} | all-to-all | bytes 393216 | tf_op jit(solution)/shard_map/all_to_all | solution.py:207
  226.4 0.7 copy.58
  (46 shorter events, 0.5 us)
Async XLA Ops:
  7.2 210.7 %copy-start = (bf16[1024,768]{1,0:T(8,128)(2,1)S(1)}, bf16[1024,768]{1,0:T(8,128)(2,1)}, u32[]{:S(2)}) copy-start(bf16[1024,768]{1,0:T(8,128)(2,1)} %param.22) | copy-start | bytes 4718596
  7.2 25.0 %copy-start.6 = (f32[8,256]{1,0:T(8,128)S(1)}, f32[8,256]{1,0:T(8,128)}, u32[]{:S(2)}) copy-start(f32[8,256]{1,0:T(8,128)} %param.19) | copy-start | bytes 24580
  7.2 31.7 %copy-start.5 = (bf16[256,256]{1,0:T(8,128)(2,1)S(1)}, bf16[256,256]{1,0:T(8,128)(2,1)}, u32[]{:S(2)}) copy-start(bf16[256,256]{1,0:T(8,128)(2,1)} %param.13) | copy-start | bytes 393220
  7.2 35.8 %copy-start.2 = (bf16[256,512]{1,0:T(8,128)(2,1)S(1)}, bf16[256,512]{1,0:T(8,128)(2,1)}, u32[]{:S(2)}) copy-start(bf16[256,512]{1,0:T(8,128)(2,1)} %param.16) | copy-start | bytes 786436
  7.2 142.5 %all-gather.2.cloned.1.call-start = ((), (), s32[]{:S(2)}) async-start(), calls=%async_computation.5 | async-start | bytes 4456448 | tf_op jit(solution)/shard_map/all_gather | solution.py:166
  8.4 34.8 %copy-start.3 = (bf16[256,128]{1,0:T(8,128)(2,1)S(1)}, bf16[256,128]{1,0:T(8,128)(2,1)}, u32[]{:S(2)}) copy-start(bf16[256,128]{1,0:T(8,128)(2,1)} %param.17) | copy-start | bytes 196612
  9.5 36.7 %copy-start.4 = (bf16[256,128]{1,0:T(8,128)(2,1)S(1)}, bf16[256,128]{1,0:T(8,128)(2,1)}, u32[]{:S(2)}) copy-start(bf16[256,128]{1,0:T(8,128)(2,1)} %param.18) | copy-start | bytes 196612
  33.2 24.7 %collective-permute-start = (f32[8]{0:T(128)S(1)}, f32[8]{0:T(128)S(1)}, u32[]{:S(2)}, u32[]{:S(2)}) collective-permute-start(f32[8]{0:T(128)S(1)} %exp.13), channel_id=1, source_target_pairs={{0,4},{4,8},{8,12},{12,16},{16,20},{20,24},{24,28},{28,32},{32,36}... | collective-permute-start | bytes 104 | tf_op jit(solution)/shard_map/ppermute | solution.py:55
  39.7 88.8 %all-to-all-start = ((bf16[256,4,64]{0,2,1:T(8,128)(2,1)}), bf16[256,4,64]{0,2,1:T(8,128)(2,1)S(1)}, u32[]{:S(2)}, u32[]{:S(2)}) async-start(bf16[256,4,64]{0,2,1:T(8,128)(2,1)} %bitcast), calls=%async_computation | async-start | bytes 262144 | tf_op jit(solution)/shard_map/all_to_all | solution.py:161
  43.5 9.5 %collective-permute-start.6 = (bf16[8,128,64]{1,2,0:T(8,128)(2,1)S(1)}, bf16[8,128,64]{1,2,0:T(8,128)(2,1)S(1)}, u32[]{:S(2)}, u32[]{:S(2)}) collective-permute-start(bf16[8,128,64]{1,2,0:T(8,128)(2,1)S(1)} %fusion.3), channel_id=1, source_target_pairs={{0,4},{4,8},{8,12},{12,16},{16,20},{20,24},{24,28},{28,32},{32,36}... | collective-permute-start | bytes 393224 | tf_op jit(solution)/shard_map/ppermute | solution.py:55
  53.0 10.3 %collective-permute-start.7 = (bf16[8,128,64]{1,2,0:T(8,128)(2,1)S(1)}, bf16[8,128,64]{1,2,0:T(8,128)(2,1)S(1)}, u32[]{:S(2)}, u32[]{:S(2)}) collective-permute-start(bf16[8,128,64]{1,2,0:T(8,128)(2,1)S(1)} %fusion.11), channel_id=1, source_target_pairs={{0,4},{4,8},{8,12},{12,16},{16,20},{20,24},{24,28},{28,32},{32,36}... | collective-permute-start | bytes 393224 | tf_op jit(solution)/shard_map/ppermute | solution.py:55
  57.9 15.9 %collective-permute-start.1 = (f32[8]{0:T(128)S(1)}, f32[8]{0:T(128)S(1)}, u32[]{:S(2)}, u32[]{:S(2)}) collective-permute-start(f32[8]{0:T(128)S(1)} %broadcast_select_fusion.1), channel_id=1, source_target_pairs={{0,4},{4,8},{8,12},{12,16},{16,20},{20,24},{24,28},{28,32},{32,36}... | collective-permute-start | bytes 104 | tf_op jit(solution)/shard_map/ppermute | solution.py:55
  63.4 16.7 %collective-permute-start.8 = (bf16[8,128,64]{1,2,0:T(8,128)(2,1)S(1)}, bf16[8,128,64]{1,2,0:T(8,128)(2,1)S(1)}, u32[]{:S(2)}, u32[]{:S(2)}) collective-permute-start(bf16[8,128,64]{1,2,0:T(8,128)(2,1)S(1)} %fusion.13), channel_id=1, source_target_pairs={{0,8},{4,12},{8,16},{12,20},{16,24},{20,28},{24,32},{28,36},{32,40... | collective-permute-start | bytes 393224 | tf_op jit(solution)/shard_map/ppermute | solution.py:55
  73.8 16.8 %collective-permute-start.2 = (f32[8]{0:T(128)S(1)}, f32[8]{0:T(128)S(1)}, u32[]{:S(2)}, u32[]{:S(2)}) collective-permute-start(f32[8]{0:T(128)S(1)} %broadcast_select_fusion), channel_id=1, source_target_pairs={{0,8},{4,12},{8,16},{12,20},{16,24},{20,28},{24,32},{28,36},{32,40... | collective-permute-start | bytes 104 | tf_op jit(solution)/shard_map/ppermute | solution.py:55
  80.3 16.8 %collective-permute-start.9 = (bf16[8,128,64]{1,2,0:T(8,128)(2,1)S(1)}, bf16[8,128,64]{1,2,0:T(8,128)(2,1)S(1)}, u32[]{:S(2)}, u32[]{:S(2)}) collective-permute-start(bf16[8,128,64]{1,2,0:T(8,128)(2,1)S(1)} %fusion.35), channel_id=1, source_target_pairs={{0,16},{4,20},{8,24},{12,28},{16,32},{20,36},{24,40},{28,44},{32,4... | collective-permute-start | bytes 393224 | tf_op jit(solution)/shard_map/ppermute | solution.py:55
  90.6 15.6 %collective-permute-start.3 = (f32[8]{0:T(128)S(1)}, f32[8]{0:T(128)S(1)}, u32[]{:S(2)}, u32[]{:S(2)}) collective-permute-start(f32[8]{0:T(128)S(1)} %broadcast_select_fusion.2), channel_id=1, source_target_pairs={{0,16},{4,20},{8,24},{12,28},{16,32},{20,36},{24,40},{28,44},{32,4... | collective-permute-start | bytes 104 | tf_op jit(solution)/shard_map/ppermute | solution.py:55
  97.4 16.7 %collective-permute-start.10 = (bf16[8,128,64]{1,2,0:T(8,128)(2,1)S(1)}, bf16[8,128,64]{1,2,0:T(8,128)(2,1)S(1)}, u32[]{:S(2)}, u32[]{:S(2)}) collective-permute-start(bf16[8,128,64]{1,2,0:T(8,128)(2,1)S(1)} %fusion.14), channel_id=1, source_target_pairs={{0,32},{4,36},{8,40},{12,44},{16,48},{20,52},{24,56},{28,60},{32,6... | collective-permute-start | bytes 393224 | tf_op jit(solution)/shard_map/ppermute | solution.py:55
  106.2 13.5 %collective-permute-start.4 = (f32[8]{0:T(128)S(1)}, f32[8]{0:T(128)S(1)}, u32[]{:S(2)}, u32[]{:S(2)}) collective-permute-start(f32[8]{0:T(128)S(1)} %broadcast_select_fusion.3), channel_id=1, source_target_pairs={{0,32},{4,36},{8,40},{12,44},{16,48},{20,52},{24,56},{28,60},{32,6... | collective-permute-start | bytes 104 | tf_op jit(solution)/shard_map/ppermute | solution.py:55
  114.5 8.4 %collective-permute-start.11 = (bf16[8,128,64]{1,2,0:T(8,128)(2,1)S(1)}, bf16[8,128,64]{1,2,0:T(8,128)(2,1)S(1)}, u32[]{:S(2)}, u32[]{:S(2)}) collective-permute-start(bf16[8,128,64]{1,2,0:T(8,128)(2,1)S(1)} %get-tuple-element.2), channel_id=1, source_target_pairs={{0,64},{4,68},{8,72},{12,76},{16,80},{20,84},{24,88},{28,92},{32,9... | collective-permute-start | bytes 393224 | tf_op jit(solution)/shard_map/ppermute | solution.py:55
  119.7 8.7 %collective-permute-start.5 = (f32[8]{0:T(128)S(1)}, f32[8]{0:T(128)S(1)}, u32[]{:S(2)}, u32[]{:S(2)}) collective-permute-start(f32[8]{0:T(128)S(1)} %broadcast_select_fusion.4), channel_id=1, source_target_pairs={{0,64},{4,68},{8,72},{12,76},{16,80},{20,84},{24,88},{28,92},{32,9... | collective-permute-start | bytes 104 | tf_op jit(solution)/shard_map/ppermute | solution.py:55
  123.0 10.9 %collective-permute-start.12 = (bf16[8,128,64]{1,2,0:T(8,128)(2,1)S(1)}, bf16[8,128,64]{1,2,0:T(8,128)(2,1)S(1)}, u32[]{:S(2)}, u32[]{:S(2)}) collective-permute-start(bf16[8,128,64]{1,2,0:T(8,128)(2,1)S(1)} %fusion.15), channel_id=1, source_target_pairs={{0,128},{4,132},{8,136},{12,140},{16,144},{20,148},{24,152},{28,15... | collective-permute-start | bytes 393224 | tf_op jit(solution)/shard_map/ppermute | solution.py:55
  182.3 17.5 %all-to-all-start.2 = ((bf16[4,2,8192]{2,1,0:T(2,128)(2,1)}), bf16[4,2,8192]{2,1,0:T(2,128)(2,1)S(1)}, u32[]{:S(2)}, u32[]{:S(2)}) async-start(bf16[4,2,8192]{2,1,0:T(2,128)(2,1)} %reshape.116), calls=%async_computation.2 | async-start | bytes 262144 | tf_op jit(solution)/shard_map/all_to_all | solution.py:168
  200.1 8.9 %copy-start.7 = (s32[256]{0:T(256)S(1)}, s32[256]{0:T(256)}, u32[]{:S(2)}) copy-start(s32[256]{0:T(256)} %param.23) | copy-start | bytes 3076
  202.7 14.1 %all-to-all-start.3 = ((bf16[4,64,1024]{2,1,0:T(8,128)(2,1)}), bf16[4,64,1024]{2,1,0:T(8,128)(2,1)S(1)}, u32[]{:S(2)}, u32[]{:S(2)}) async-start(bf16[4,64,1024]{2,1,0:T(8,128)(2,1)} %bitcast.24), calls=%async_computation.3 | async-start | bytes 1048576 | tf_op jit(solution)/shard_map/all_to_all | solution.py:187
  217.9 9.2 %copy-start.1 = (bf16[64,1024]{1,0:T(8,128)(2,1)}, bf16[64,1024]{1,0:T(8,128)(2,1)S(1)}, u32[]{:S(2)}) copy-start(bf16[64,1024]{1,0:T(8,128)(2,1)S(1)} %add_convert_fusion) | copy-start | bytes 393220
Sparse Core Ops, SparseCore 0:
  32.3 117.3 all-gather.1

commit v14 on v12

--- a/solution.py
+++ b/solution.py
@@ -164,15 +164,17 @@
     pair = spread(jnp.stack([key_rows, values]))
     pair_t = pair.reshape(2, -1, HDIM).transpose(0, 2, 1)
     gathered = lax.all_gather(pair_t, ("sy", "sz"), axis=2, tiled=True)
+    cumulative, inner_part, local_state, total_decay = chain_pieces(
+        ssm_input, write_proj, read_proj, log_decay
+    )
+    entering = pass_states(local_state, total_decay)
+    ssm_mix = chain_output(cumulative, inner_part, entering, read_proj)
+    ssm_part = jnp.dot(ssm_mix, ssm_project, preferred_element_type=jnp.float32)
+    gathered, ssm_part = lax.optimization_barrier((gathered, ssm_part))
     attended_one = flash_one_head_t(query_heads.reshape(-1, HDIM).T, gathered).T
     attended = lax.all_to_all(
         attended_one.reshape(-1, 1, HDIM), "sb", split_axis=0, concat_axis=1, tiled=True
     ).reshape(row_count, head_count * HDIM)
-    cumulative, inner_part, local_state, total_decay = chain_pieces(
-        ssm_input, write_proj, read_proj, log_decay
-    )
-    entering = pass_states(local_state, total_decay)
-    ssm_mix = chain_output(cumulative, inner_part, entering, read_proj)
     owner_count = lax.axis_size("head")
     own_index = lax.axis_index("head")
     sub_rows = row_count // owner_count
@@ -182,7 +184,7 @@
     slot_ids = jnp.arange(slot_count, dtype=jnp.float32)
     partial = (
         jnp.dot(attended, attn_project, preferred_element_type=jnp.float32)
-        + jnp.dot(ssm_mix, ssm_project, preferred_element_type=jnp.float32)
+        + ssm_part
     ).astype(jnp.bfloat16)
     pieces = lax.all_to_all(
         partial.reshape(owner_count, sub_rows, partial.shape[1]),

time: 203 us -> 202 us (level)
    unnamed x25 -> x27, local copies, waits for them, and re-layouts: 5.84 us -> 6.27 us
  transfers between devices with their start and end apart: 17 -> 17, of which waited for: 5 -> 4; matrix products, arithmetic and copies ran while one was open for 4% -> 3% of each run, Pallas kernels for 0% -> 0%
where the time goes in v14:
time: 202 us; the launch traced here: 201 us
  starting transfers between devices  84.2 us (42%)
  waiting for transfers between devices  36.1 us (18%)
  Pallas kernels  29.4 us (15%)
  blocking collectives  18.1 us (9%)
  between operations  14.6 us (7%)
  local copies, waits for them, and re-layouts  8.83 us (4%)
  matrix products  4.85 us (2%)
  other arithmetic  4.66 us (2%)
    ppermute x13, starting transfers between devices, shifted(): lax.ppermute(part.astype(jnp.bfloat16) if part.ndim == 3 else part, axis,...  66.5 us
    pallas_call x1, Pallas kernels, flash_one_head_t(): pl.pallas_call(kernel, out_shape=jax.ShapeDtypeStruct((width, row_count),...  29.4 us
    all_gather x1, waiting for transfers between devices, per_device(): gathered = lax.all_gather(pair_t, ('sy', 'sz'), axis=2, tiled=True)  22.6 us
    all_to_all x1, blocking collectives, spread(): lax.all_to_all(split, 'sb', split_axis=split.ndim - 2, concat_axis=split....  10.2 us
    all_to_all x1, starting transfers between devices, per_device(): lax.all_to_all(partial.reshape(owner_count, sub_rows, partial.shape[1]),...  9.39 us
    all_to_all x1, blocking collectives, per_device(): lax.all_to_all(packed, 'head', split_axis=0, concat_axis=0, tiled=True)  7.9 us
    all_to_all x1, waiting for transfers between devices, per_device(): lax.all_to_all(partial.reshape(owner_count, sub_rows, partial.shape[1]),...  7.46 us
    unnamed x27, local copies, waits for them, and re-layouts  6.27 us
  transfers between devices with their start and end apart: 17, of which 4 were waited for; matrix products, arithmetic and copies ran while one was open for 3% of the time, Pallas kernels for 0%

profile of v14, /device:TPU:1, one launch (start us, length us, event | category | flops | bytes accessed | tf_op | source)
XLA Modules:
  0.0 200.7 jit_solution(4061613049049405530)
XLA Ops:
  7.2 0.0 all-gather.2.cloned.1.call-start
  7.3 1.1 copy.47
  8.4 1.0 copy.48
  9.5 10.2 %all_to_all.55 = bf16[2,256,4,64]{1,3,0,2:T(8,128)(2,1)S(1)} all-to-all(bf16[2,256,4,64]{1,3,0,2:T(8,128)(2,1)S(1)} %copy.49), channel_id=1, replica_groups=mesh['sb'=4,'sy'=2,'sz'=8,'head'=4] {'sb'}, dimensions={2} | all-to-all | bytes 524288 | tf_op jit(solution)/shard_map/all_to_all | solution.py:161
  19.7 0.2 copy.50
  19.9 0.9 reshape.103
  20.8 0.6 reduce-window.6
  21.4 0.2 slice_reduce_fusion
  21.6 0.1 copy.51
  21.8 0.1 exponential_bitcast_fusion
  21.8 0.2 slice_reduce_fusion.1
  22.0 0.1 exponential_bitcast_fusion.1
  22.1 0.2 fusion.3
  22.3 3.5 %collective-permute-start.6 = (bf16[8,128,64]{1,2,0:T(8,128)(2,1)S(1)}, bf16[8,128,64]{1,2,0:T(8,128)(2,1)S(1)}, u32[]{:S(2)}, u32[]{:S(2)}) collective-permute-start(bf16[8,128,64]{1,2,0:T(8,128)(2,1)S(1)} %fusion.3), channel_id=1, source_target_pairs={{0,4},{4,8},{8,12},{12,16},{16,20},{20,24},{24,28},{28,32},{32,36}... | collective-permute-start | bytes 393224 | tf_op jit(solution)/shard_map/ppermute | solution.py:55
  25.9 3.5 %collective-permute-start = (f32[8]{0:T(128)S(1)}, f32[8]{0:T(128)S(1)}, u32[]{:S(2)}, u32[]{:S(2)}) collective-permute-start(f32[8]{0:T(128)S(1)} %exp.13), channel_id=1, source_target_pairs={{0,4},{4,8},{8,12},{12,16},{16,20},{20,24},{24,28},{28,32},{32,36}... | collective-permute-start | bytes 104 | tf_op jit(solution)/shard_map/ppermute | solution.py:55
  29.5 0.8 copy.45
  30.2 3.3 %all-to-all-start = ((bf16[256,4,64]{0,2,1:T(8,128)(2,1)}), bf16[256,4,64]{0,2,1:T(8,128)(2,1)S(1)}, u32[]{:S(2)}, u32[]{:S(2)}) async-start(bf16[256,4,64]{0,2,1:T(8,128)(2,1)} %bitcast), calls=%async_computation | async-start | bytes 262144 | tf_op jit(solution)/shard_map/all_to_all | solution.py:161
  33.6 0.2 fusion.37
  33.9 3.6 %collective-permute-start.7 = (bf16[8,128,64]{1,2,0:T(8,128)(2,1)S(1)}, bf16[8,128,64]{1,2,0:T(8,128)(2,1)S(1)}, u32[]{:S(2)}, u32[]{:S(2)}) collective-permute-start(bf16[8,128,64]{1,2,0:T(8,128)(2,1)S(1)} %fusion.11), channel_id=1, source_target_pairs={{0,4},{4,8},{8,12},{12,16},{16,20},{20,24},{24,28},{28,32},{32,36}... | collective-permute-start | bytes 393224 | tf_op jit(solution)/shard_map/ppermute | solution.py:55
  37.4 4.7 %collective-permute-start.1 = (f32[8]{0:T(128)S(1)}, f32[8]{0:T(128)S(1)}, u32[]{:S(2)}, u32[]{:S(2)}) collective-permute-start(f32[8]{0:T(128)S(1)} %broadcast_select_fusion.1), channel_id=1, source_target_pairs={{0,4},{4,8},{8,12},{12,16},{16,20},{20,24},{24,28},{28,32},{32,36}... | collective-permute-start | bytes 104 | tf_op jit(solution)/shard_map/ppermute | solution.py:55
  42.2 0.1 fusion.13
  42.3 3.9 %collective-permute-start.8 = (bf16[8,128,64]{1,2,0:T(8,128)(2,1)S(1)}, bf16[8,128,64]{1,2,0:T(8,128)(2,1)S(1)}, u32[]{:S(2)}, u32[]{:S(2)}) collective-permute-start(bf16[8,128,64]{1,2,0:T(8,128)(2,1)S(1)} %fusion.13), channel_id=1, source_target_pairs={{0,8},{4,12},{8,16},{12,20},{16,24},{20,28},{24,32},{28,36},{32,40... | collective-permute-start | bytes 393224 | tf_op jit(solution)/shard_map/ppermute | solution.py:55
  46.2 4.4 %collective-permute-start.2 = (f32[8]{0:T(128)S(1)}, f32[8]{0:T(128)S(1)}, u32[]{:S(2)}, u32[]{:S(2)}) collective-permute-start(f32[8]{0:T(128)S(1)} %broadcast_select_fusion), channel_id=1, source_target_pairs={{0,8},{4,12},{8,16},{12,20},{16,24},{20,28},{24,32},{28,36},{32,40... | collective-permute-start | bytes 104 | tf_op jit(solution)/shard_map/ppermute | solution.py:55
  50.7 0.2 fusion.35
  50.9 7.6 %collective-permute-start.9 = (bf16[8,128,64]{1,2,0:T(8,128)(2,1)S(1)}, bf16[8,128,64]{1,2,0:T(8,128)(2,1)S(1)}, u32[]{:S(2)}, u32[]{:S(2)}) collective-permute-start(bf16[8,128,64]{1,2,0:T(8,128)(2,1)S(1)} %fusion.35), channel_id=1, source_target_pairs={{0,16},{4,20},{8,24},{12,28},{16,32},{20,36},{24,40},{28,44},{32,4... | collective-permute-start | bytes 393224 | tf_op jit(solution)/shard_map/ppermute | solution.py:55
  58.5 9.5 %collective-permute-start.3 = (f32[8]{0:T(128)S(1)}, f32[8]{0:T(128)S(1)}, u32[]{:S(2)}, u32[]{:S(2)}) collective-permute-start(f32[8]{0:T(128)S(1)} %broadcast_select_fusion.2), channel_id=1, source_target_pairs={{0,16},{4,20},{8,24},{12,28},{16,32},{20,36},{24,40},{28,44},{32,4... | collective-permute-start | bytes 104 | tf_op jit(solution)/shard_map/ppermute | solution.py:55
  68.0 0.3 fusion.14
  68.3 8.9 %collective-permute-start.10 = (bf16[8,128,64]{1,2,0:T(8,128)(2,1)S(1)}, bf16[8,128,64]{1,2,0:T(8,128)(2,1)S(1)}, u32[]{:S(2)}, u32[]{:S(2)}) collective-permute-start(bf16[8,128,64]{1,2,0:T(8,128)(2,1)S(1)} %fusion.14), channel_id=1, source_target_pairs={{0,32},{4,36},{8,40},{12,44},{16,48},{20,52},{24,56},{28,60},{32,6... | collective-permute-start | bytes 393224 | tf_op jit(solution)/shard_map/ppermute | solution.py:55
  77.3 6.3 %collective-permute-start.4 = (f32[8]{0:T(128)S(1)}, f32[8]{0:T(128)S(1)}, u32[]{:S(2)}, u32[]{:S(2)}) collective-permute-start(f32[8]{0:T(128)S(1)} %broadcast_select_fusion.3), channel_id=1, source_target_pairs={{0,32},{4,36},{8,40},{12,44},{16,48},{20,52},{24,56},{28,60},{32,6... | collective-permute-start | bytes 104 | tf_op jit(solution)/shard_map/ppermute | solution.py:55
  83.6 0.3 fusion.36
  84.0 3.6 %collective-permute-start.11 = (bf16[8,128,64]{1,2,0:T(8,128)(2,1)S(1)}, bf16[8,128,64]{1,2,0:T(8,128)(2,1)S(1)}, u32[]{:S(2)}, u32[]{:S(2)}) collective-permute-start(bf16[8,128,64]{1,2,0:T(8,128)(2,1)S(1)} %get-tuple-element.6), channel_id=1, source_target_pairs={{0,64},{4,68},{8,72},{12,76},{16,80},{20,84},{24,88},{28,92},{32,9... | collective-permute-start | bytes 393224 | tf_op jit(solution)/shard_map/ppermute | solution.py:55
  87.6 2.3 %collective-permute-start.5 = (f32[8]{0:T(128)S(1)}, f32[8]{0:T(128)S(1)}, u32[]{:S(2)}, u32[]{:S(2)}) collective-permute-start(f32[8]{0:T(128)S(1)} %broadcast_select_fusion.4), channel_id=1, source_target_pairs={{0,64},{4,68},{8,72},{12,76},{16,80},{20,84},{24,88},{28,92},{32,9... | collective-permute-start | bytes 104 | tf_op jit(solution)/shard_map/ppermute | solution.py:55
  89.9 0.1 fusion.15
  90.0 4.5 %collective-permute-start.12 = (bf16[8,128,64]{1,2,0:T(8,128)(2,1)S(1)}, bf16[8,128,64]{1,2,0:T(8,128)(2,1)S(1)}, u32[]{:S(2)}, u32[]{:S(2)}) collective-permute-start(bf16[8,128,64]{1,2,0:T(8,128)(2,1)S(1)} %fusion.15), channel_id=1, source_target_pairs={{0,128},{4,132},{8,136},{12,140},{16,144},{20,148},{24,152},{28,15... | collective-permute-start | bytes 393224 | tf_op jit(solution)/shard_map/ppermute | solution.py:55
  94.6 0.1 copy.46
  94.7 0.7 copy.55
  95.3 1.1 collective-permute-done.12
  96.4 0.3 fusion.1
  96.7 0.7 multiply_reduce_fusion
  97.5 0.1 multiply_convert_fusion.2
  97.5 0.4 copy-done.1
  98.0 0.5 fusion.38
  98.4 22.6 %all-gather.2.cloned.1.call-done.k_ref.v_ref = bf16[2,64,16384]{2,1,0:T(8,128)(2,1)} async-done(((bf16[2,64,1024]{2,1,0:T(8,128)(2,1)}), bf16[2,64,16384]{2,1,0:T(8,128)(2,1)}) %all-gather.2.cloned.1.call-update) | async-done | bytes 4194320 | tf_op jit(solution)/shard_map/all_gather | solution.py:166
  121.1 29.4 %shard_map.131 = bf16[64,1024]{1,0:T(8,128)(2,1)} custom-call(bf16[64,1024]{1,0:T(8,128)(2,1)} %bitcast.71, bf16[2,64,16384]{2,1,0:T(8,128)(2,1)} %all-gather.2.cloned.1.call-done.k_ref.v_ref, bf16[2,64,16384]{2,1,0:T(8,128)(2,1)} %all-gather.2.cloned.1.call-done.k_ref.v_ref), custom_call_target="tpu_custom_call" | custom-call | tf_op jit(solution)/shard_map/pallas_call | solution.py:109
  150.5 0.5 broadcast.86
  151.0 1.6 reduce.4
  152.6 0.2 copy.56
  152.7 0.9 reshape.116
  153.7 5.0 %all-to-all-start.2 = ((bf16[4,2,8192]{2,1,0:T(2,128)(2,1)}), bf16[4,2,8192]{2,1,0:T(2,128)(2,1)S(1)}, u32[]{:S(2)}, u32[]{:S(2)}) async-start(bf16[4,2,8192]{2,1,0:T(2,128)(2,1)} %reshape.116), calls=%async_computation.2 | async-start | bytes 262144 | tf_op jit(solution)/shard_map/all_to_all | solution.py:175
  158.6 4.8 %all-to-all-done.2 = bf16[4,2,8192]{2,1,0:T(2,128)(2,1)S(1)} async-done(((bf16[4,2,8192]{2,1,0:T(2,128)(2,1)}), bf16[4,2,8192]{2,1,0:T(2,128)(2,1)S(1)}, u32[]{:S(2)}, u32[]{:S(2)}) %all-to-all-start.2) | async-done | bytes 131104 | tf_op jit(solution)/shard_map/all_to_all | solution.py:175
  163.5 0.3 reshape.117
  163.8 0.3 copy.53
  164.1 0.1 all_to_all.46
  164.2 2.2 %fusion = bf16[256,1024]{1,0:T(8,128)(2,1)} fusion(f32[256,1024]{1,0:T(8,128)S(1)} %fusion.38, bf16[256,256]{0,1:T(8,128)(2,1)S(1)} %bitcast.73, bf16[256,1024]{1,0:T(8,128)(2,1)} %param.20), kind=kOutput, calls=%fused_computation.2 | convolution fusion | flops 134742016 | bytes 2228224 | tf_op jit(solution)/shard_map/dot_general | solution.py:186
  166.4 9.4 %all-to-all-start.3 = ((bf16[4,64,1024]{2,1,0:T(8,128)(2,1)}), bf16[4,64,1024]{2,1,0:T(8,128)(2,1)S(1)}, u32[]{:S(2)}, u32[]{:S(2)}) async-start(bf16[4,64,1024]{2,1,0:T(8,128)(2,1)} %bitcast.24), calls=%async_computation.3 | async-start | bytes 1048576 | tf_op jit(solution)/shard_map/all_to_all | solution.py:189
  175.8 0.1 dynamic_slice.7
  175.9 0.2 fusion.4
  176.1 0.1 multiply_add_fusion
  176.2 7.5 %all-to-all-done.3 = bf16[4,64,1024]{2,1,0:T(8,128)(2,1)S(1)} async-done(((bf16[4,64,1024]{2,1,0:T(8,128)(2,1)}), bf16[4,64,1024]{2,1,0:T(8,128)(2,1)S(1)}, u32[]{:S(2)}, u32[]{:S(2)}) %all-to-all-start.3) | async-done | bytes 524320 | tf_op jit(solution)/shard_map/all_to_all | solution.py:189
  183.6 0.1 convert_reduce_fusion
  183.7 0.9 add_convert_fusion
  184.7 0.6 convolution_convert_fusion
  185.3 7.9 %all_to_all.56 = bf16[4,32,768]{2,1,0:T(8,128)(2,1)S(1)} all-to-all(bf16[4,32,768]{2,1,0:T(8,128)(2,1)S(1)} %bitcast.69), channel_id=1, replica_groups=mesh['sb'=4,'sy'=2,'sz'=8,'head'=4] {'head'}, dimensions={0} | all-to-all | bytes 393216 | tf_op jit(solution)/shard_map/all_to_all | solution.py:209
  193.2 0.7 copy.58
  (48 shorter events, 0.3 us)
Async XLA Ops:
  7.2 177.5 %copy-start = (bf16[1024,768]{1,0:T(8,128)(2,1)S(1)}, bf16[1024,768]{1,0:T(8,128)(2,1)}, u32[]{:S(2)}) copy-start(bf16[1024,768]{1,0:T(8,128)(2,1)} %param.22) | copy-start | bytes 4718596
  7.2 13.6 %copy-start.7 = (f32[8,256]{1,0:T(8,128)S(1)}, f32[8,256]{1,0:T(8,128)}, u32[]{:S(2)}) copy-start(f32[8,256]{1,0:T(8,128)} %param.19) | copy-start | bytes 24580
  7.2 14.4 %copy-start.3 = (bf16[256,512]{1,0:T(8,128)(2,1)S(1)}, bf16[256,512]{1,0:T(8,128)(2,1)}, u32[]{:S(2)}) copy-start(bf16[256,512]{1,0:T(8,128)(2,1)} %param.16) | copy-start | bytes 786436
  7.2 14.9 %copy-start.4 = (bf16[256,128]{1,0:T(8,128)(2,1)S(1)}, bf16[256,128]{1,0:T(8,128)(2,1)}, u32[]{:S(2)}) copy-start(bf16[256,128]{1,0:T(8,128)(2,1)} %param.17) | copy-start | bytes 196612
  7.2 113.9 %all-gather.2.cloned.1.call-start = ((), (), s32[]{:S(2)}) async-start(), calls=%async_computation.5 | async-start | bytes 4456448 | tf_op jit(solution)/shard_map/all_gather | solution.py:166
  8.4 21.1 %copy-start.6 = (bf16[256,256]{1,0:T(8,128)(2,1)S(1)}, bf16[256,256]{1,0:T(8,128)(2,1)}, u32[]{:S(2)}) copy-start(bf16[256,256]{1,0:T(8,128)(2,1)} %param.13) | copy-start | bytes 393220
  9.5 24.1 %copy-start.5 = (bf16[256,128]{1,0:T(8,128)(2,1)S(1)}, bf16[256,128]{1,0:T(8,128)(2,1)}, u32[]{:S(2)}) copy-start(bf16[256,128]{1,0:T(8,128)(2,1)} %param.18) | copy-start | bytes 196612
  22.3 11.5 %collective-permute-start.6 = (bf16[8,128,64]{1,2,0:T(8,128)(2,1)S(1)}, bf16[8,128,64]{1,2,0:T(8,128)(2,1)S(1)}, u32[]{:S(2)}, u32[]{:S(2)}) collective-permute-start(bf16[8,128,64]{1,2,0:T(8,128)(2,1)S(1)} %fusion.3), channel_id=1, source_target_pairs={{0,4},{4,8},{8,12},{12,16},{16,20},{20,24},{24,28},{28,32},{32,36}... | collective-permute-start | bytes 393224 | tf_op jit(solution)/shard_map/ppermute | solution.py:55
  25.9 11.5 %collective-permute-start = (f32[8]{0:T(128)S(1)}, f32[8]{0:T(128)S(1)}, u32[]{:S(2)}, u32[]{:S(2)}) collective-permute-start(f32[8]{0:T(128)S(1)} %exp.13), channel_id=1, source_target_pairs={{0,4},{4,8},{8,12},{12,16},{16,20},{20,24},{24,28},{28,32},{32,36}... | collective-permute-start | bytes 104 | tf_op jit(solution)/shard_map/ppermute | solution.py:55
  30.2 64.3 %all-to-all-start = ((bf16[256,4,64]{0,2,1:T(8,128)(2,1)}), bf16[256,4,64]{0,2,1:T(8,128)(2,1)S(1)}, u32[]{:S(2)}, u32[]{:S(2)}) async-start(bf16[256,4,64]{0,2,1:T(8,128)(2,1)} %bitcast), calls=%async_computation | async-start | bytes 262144 | tf_op jit(solution)/shard_map/all_to_all | solution.py:161
  33.9 8.3 %collective-permute-start.7 = (bf16[8,128,64]{1,2,0:T(8,128)(2,1)S(1)}, bf16[8,128,64]{1,2,0:T(8,128)(2,1)S(1)}, u32[]{:S(2)}, u32[]{:S(2)}) collective-permute-start(bf16[8,128,64]{1,2,0:T(8,128)(2,1)S(1)} %fusion.11), channel_id=1, source_target_pairs={{0,4},{4,8},{8,12},{12,16},{16,20},{20,24},{24,28},{28,32},{32,36}... | collective-permute-start | bytes 393224 | tf_op jit(solution)/shard_map/ppermute | solution.py:55
  37.4 8.8 %collective-permute-start.1 = (f32[8]{0:T(128)S(1)}, f32[8]{0:T(128)S(1)}, u32[]{:S(2)}, u32[]{:S(2)}) collective-permute-start(f32[8]{0:T(128)S(1)} %broadcast_select_fusion.1), channel_id=1, source_target_pairs={{0,4},{4,8},{8,12},{12,16},{16,20},{20,24},{24,28},{28,32},{32,36}... | collective-permute-start | bytes 104 | tf_op jit(solution)/shard_map/ppermute | solution.py:55
  42.3 8.4 %collective-permute-start.8 = (bf16[8,128,64]{1,2,0:T(8,128)(2,1)S(1)}, bf16[8,128,64]{1,2,0:T(8,128)(2,1)S(1)}, u32[]{:S(2)}, u32[]{:S(2)}) collective-permute-start(bf16[8,128,64]{1,2,0:T(8,128)(2,1)S(1)} %fusion.13), channel_id=1, source_target_pairs={{0,8},{4,12},{8,16},{12,20},{16,24},{20,28},{24,32},{28,36},{32,40... | collective-permute-start | bytes 393224 | tf_op jit(solution)/shard_map/ppermute | solution.py:55
  46.2 12.3 %collective-permute-start.2 = (f32[8]{0:T(128)S(1)}, f32[8]{0:T(128)S(1)}, u32[]{:S(2)}, u32[]{:S(2)}) collective-permute-start(f32[8]{0:T(128)S(1)} %broadcast_select_fusion), channel_id=1, source_target_pairs={{0,8},{4,12},{8,16},{12,20},{16,24},{20,28},{24,32},{28,36},{32,40... | collective-permute-start | bytes 104 | tf_op jit(solution)/shard_map/ppermute | solution.py:55
  50.9 17.2 %collective-permute-start.9 = (bf16[8,128,64]{1,2,0:T(8,128)(2,1)S(1)}, bf16[8,128,64]{1,2,0:T(8,128)(2,1)S(1)}, u32[]{:S(2)}, u32[]{:S(2)}) collective-permute-start(bf16[8,128,64]{1,2,0:T(8,128)(2,1)S(1)} %fusion.35), channel_id=1, source_target_pairs={{0,16},{4,20},{8,24},{12,28},{16,32},{20,36},{24,40},{28,44},{32,4... | collective-permute-start | bytes 393224 | tf_op jit(solution)/shard_map/ppermute | solution.py:55
  58.5 18.7 %collective-permute-start.3 = (f32[8]{0:T(128)S(1)}, f32[8]{0:T(128)S(1)}, u32[]{:S(2)}, u32[]{:S(2)}) collective-permute-start(f32[8]{0:T(128)S(1)} %broadcast_select_fusion.2), channel_id=1, source_target_pairs={{0,16},{4,20},{8,24},{12,28},{16,32},{20,36},{24,40},{28,44},{32,4... | collective-permute-start | bytes 104 | tf_op jit(solution)/shard_map/ppermute | solution.py:55
  68.3 15.3 %collective-permute-start.10 = (bf16[8,128,64]{1,2,0:T(8,128)(2,1)S(1)}, bf16[8,128,64]{1,2,0:T(8,128)(2,1)S(1)}, u32[]{:S(2)}, u32[]{:S(2)}) collective-permute-start(bf16[8,128,64]{1,2,0:T(8,128)(2,1)S(1)} %fusion.14), channel_id=1, source_target_pairs={{0,32},{4,36},{8,40},{12,44},{16,48},{20,52},{24,56},{28,60},{32,6... | collective-permute-start | bytes 393224 | tf_op jit(solution)/shard_map/ppermute | solution.py:55
  77.3 10.3 %collective-permute-start.4 = (f32[8]{0:T(128)S(1)}, f32[8]{0:T(128)S(1)}, u32[]{:S(2)}, u32[]{:S(2)}) collective-permute-start(f32[8]{0:T(128)S(1)} %broadcast_select_fusion.3), channel_id=1, source_target_pairs={{0,32},{4,36},{8,40},{12,44},{16,48},{20,52},{24,56},{28,60},{32,6... | collective-permute-start | bytes 104 | tf_op jit(solution)/shard_map/ppermute | solution.py:55
  84.0 5.9 %collective-permute-start.11 = (bf16[8,128,64]{1,2,0:T(8,128)(2,1)S(1)}, bf16[8,128,64]{1,2,0:T(8,128)(2,1)S(1)}, u32[]{:S(2)}, u32[]{:S(2)}) collective-permute-start(bf16[8,128,64]{1,2,0:T(8,128)(2,1)S(1)} %get-tuple-element.6), channel_id=1, source_target_pairs={{0,64},{4,68},{8,72},{12,76},{16,80},{20,84},{24,88},{28,92},{32,9... | collective-permute-start | bytes 393224 | tf_op jit(solution)/shard_map/ppermute | solution.py:55
  87.6 6.9 %collective-permute-start.5 = (f32[8]{0:T(128)S(1)}, f32[8]{0:T(128)S(1)}, u32[]{:S(2)}, u32[]{:S(2)}) collective-permute-start(f32[8]{0:T(128)S(1)} %broadcast_select_fusion.4), channel_id=1, source_target_pairs={{0,64},{4,68},{8,72},{12,76},{16,80},{20,84},{24,88},{28,92},{32,9... | collective-permute-start | bytes 104 | tf_op jit(solution)/shard_map/ppermute | solution.py:55
  90.0 6.4 %collective-permute-start.12 = (bf16[8,128,64]{1,2,0:T(8,128)(2,1)S(1)}, bf16[8,128,64]{1,2,0:T(8,128)(2,1)S(1)}, u32[]{:S(2)}, u32[]{:S(2)}) collective-permute-start(bf16[8,128,64]{1,2,0:T(8,128)(2,1)S(1)} %fusion.15), channel_id=1, source_target_pairs={{0,128},{4,132},{8,136},{12,140},{16,144},{20,148},{24,152},{28,15... | collective-permute-start | bytes 393224 | tf_op jit(solution)/shard_map/ppermute | solution.py:55
  96.7 1.2 copy-start.1
  153.7 9.8 %all-to-all-start.2 = ((bf16[4,2,8192]{2,1,0:T(2,128)(2,1)}), bf16[4,2,8192]{2,1,0:T(2,128)(2,1)S(1)}, u32[]{:S(2)}, u32[]{:S(2)}) async-start(bf16[4,2,8192]{2,1,0:T(2,128)(2,1)} %reshape.116), calls=%async_computation.2 | async-start | bytes 262144 | tf_op jit(solution)/shard_map/all_to_all | solution.py:175
  163.8 12.0 %copy-start.8 = (s32[256]{0:T(256)S(1)}, s32[256]{0:T(256)}, u32[]{:S(2)}) copy-start(s32[256]{0:T(256)} %param.23) | copy-start | bytes 3076
  166.4 17.2 %all-to-all-start.3 = ((bf16[4,64,1024]{2,1,0:T(8,128)(2,1)}), bf16[4,64,1024]{2,1,0:T(8,128)(2,1)S(1)}, u32[]{:S(2)}, u32[]{:S(2)}) async-start(bf16[4,64,1024]{2,1,0:T(8,128)(2,1)} %bitcast.24), calls=%async_computation.3 | async-start | bytes 1048576 | tf_op jit(solution)/shard_map/all_to_all | solution.py:189
  184.7 9.2 %copy-start.2 = (bf16[64,1024]{1,0:T(8,128)(2,1)}, bf16[64,1024]{1,0:T(8,128)(2,1)S(1)}, u32[]{:S(2)}) copy-start(bf16[64,1024]{1,0:T(8,128)(2,1)S(1)} %add_convert_fusion) | copy-start | bytes 393220
Sparse Core Ops, SparseCore 0:
  20.9 100.0 all-gather.1
